TPU v7x, 128 devices: a whole 4x4x4 slice. The times are simulated.
128 devices in a mesh: req: 32 (over z, x, core), seq: 4 (over y).
Axes of the slice: x: 4, y: 4, z: 4, core: 2. Of those that a mesh axis runs over, the one named last changes fastest.
Arguments:
- x_in: bfloat16 [65536, 2560], P(('req', 'seq')), may hold values from -6 to 6
- bc_in: bfloat16 [65536, 256], P(('req', 'seq')), may hold values from -6 to 6
- z_in: bfloat16 [65536, 2560], P(('req', 'seq')), may hold values from -6 to 6
- dt_raw: bfloat16 [65536, 40], P(('req', 'seq')), may hold values from -3 to 22
- conv_weight: float32 [4, 2816], replicated, may hold values from -3 to 3
- conv_bias: float32 [2816], replicated, may hold values from -0.5 to 0.5
- dt_bias: float32 [40], replicated, may hold values from -5 to -4
- a_log: float32 [40], replicated, may hold values from -3.95 to 1.17
- d_skip: float32 [40], replicated, may hold values from 0.5 to 2
- norm_gain: float32 [2560], replicated, may hold values from 0.1 to 1.9
- w_out: bfloat16 [2560, 2560], replicated, may hold values from -0.125 to 0.125
- prompt_stretches: int32 [64], replicated, may hold values from 1 to 16, as said below
Outputs:
- mixed_out: bfloat16 [65536, 2560], P(('req', 'seq'))
- end_states: float32 [256, 40, 64, 128], P('req', 'seq')
Inputs may be any that keep to these rules, and one draw needn't show every extreme that they name: `prompt_stretches`: the lengths sum to 256; the last prompt is exactly 16 stretches long and none is longer.
All inputs are finite; a program needn't handle non-finite values.
Results may differ from a plain program's by a relative error of at most 0.0073.
Values may be sent and summed in bfloat16 or wider, within the bound.
No kernel may reach another device: no remote copies, remote signals or barrier semaphores. Data moves between devices by JAX's collectives and lax.ppermute only.
A program may use at most 448 MiB of HBM per device.

v0:
```python
import jax
import jax.numpy as jnp
from jax import lax
from jax.sharding import PartitionSpec as P

N = 128
STRETCH = 256


def from_behind(value, axis, steps):
    count = lax.axis_size(axis)
    leading, last = (max(0, -steps), min(count, count - steps))
    return lax.ppermute(value, axis, [(source, source + steps) for source in range(leading, last)])


def carried_in(part, axis, combine, identity):
    place = lax.axis_index(axis)
    gathered = jax.tree.map(lambda a: lax.all_gather(a, axis), part)
    state = jax.tree.map(lambda a, e: jnp.zeros_like(a) + jnp.asarray(e, a.dtype), part, identity)

    def one(step, state):
        return combine(
            state, jax.tree.map(lambda a: lax.dynamic_index_in_dim(a, step, 0, False), gathered)
        )

    return lax.fori_loop(0, place, one, state)


def stretch_flags(prompt_stretches, stretch_ids):
    firsts = jnp.cumsum(prompt_stretches) - prompt_stretches
    last_stretches = firsts + prompt_stretches - 1
    starts = jnp.any(stretch_ids[:, None] == firsts[None, :], axis=1)
    finals = jnp.any(stretch_ids[:, None] == last_stretches[None, :], axis=1)
    return (starts, finals)


def causal_conv(row_block, history, weight, conv_bias, starts):
    conv_span = weight.shape[0]
    length = row_block.shape[0]
    extended = jnp.concatenate([history, row_block], axis=0)
    in_stretch = jnp.arange(length, dtype=jnp.int32) % STRETCH
    start_rows = jnp.repeat(starts, STRETCH)
    running = conv_bias[None, :]
    for offset in range(conv_span):
        lag_rows = conv_span - 1 - offset
        shifted = extended[offset : offset + length].astype(jnp.float32)
        usable = jnp.logical_not((in_stretch < lag_rows) & start_rows)
        running = running + weight[offset][None, :] * jnp.where(usable[:, None], shifted, 0.0)
    return jax.nn.silu(running).astype(jnp.bfloat16)


def local_stretch(x_stretch, bc_stretch, dt_stretch, dt_bias, a_log):
    state_size = bc_stretch.shape[1] // 2
    b_mat = bc_stretch[:, :state_size]
    c_mat = bc_stretch[:, state_size:]
    step_size = jax.nn.softplus(dt_stretch.astype(jnp.float32) + dt_bias[None, :])
    log_decay = jnp.cumsum(-jnp.exp(a_log)[None, :] * step_size, axis=0)
    scores = jnp.dot(c_mat, b_mat.T, preferred_element_type=jnp.float32)
    stretch_len = scores.shape[0]
    causal = jnp.arange(stretch_len)[:, None] >= jnp.arange(stretch_len)[None, :]
    by_head = log_decay.T
    segment = by_head[:, :, None] - by_head[:, None, :]
    decay_mask = jnp.where(causal[None], jnp.exp(jnp.where(causal[None], segment, 0.0)), 0.0)
    mixing = (scores[None] * decay_mask * step_size.T[:, None, :]).astype(jnp.bfloat16)
    y_diag = jnp.einsum("htu,uhp->thp", mixing, x_stretch, preferred_element_type=jnp.float32)
    tail_weight = jnp.exp(log_decay[-1][None, :] - log_decay) * step_size
    weighted_x = (x_stretch.astype(jnp.float32) * tail_weight[:, :, None]).astype(jnp.bfloat16)
    stretch_state = jnp.einsum("uhp,un->hpn", weighted_x, b_mat, preferred_element_type=jnp.float32)
    return (y_diag, stretch_state, log_decay)


def finish_stretch(y_diag, log_decay, state_in, x_stretch, c_mat, z_stretch, d_skip, norm_gain):
    state_low = state_in.astype(jnp.bfloat16)
    y_off = jnp.exp(log_decay)[:, :, None] * jnp.einsum(
        "tn,hpn->thp", c_mat, state_low, preferred_element_type=jnp.float32
    )
    mixed_rows = y_diag + y_off + d_skip[None, :, None] * x_stretch.astype(jnp.float32)
    mixed_rows = mixed_rows.reshape(mixed_rows.shape[0], -1)
    gated_rows = mixed_rows * jax.nn.silu(z_stretch.astype(jnp.float32))
    inv_rms = lax.rsqrt(jnp.mean(gated_rows * gated_rows, axis=-1, keepdims=True) + 1e-05)
    return (gated_rows * inv_rms * norm_gain[None, :]).astype(jnp.bfloat16)


def chain_states(earlier, later):
    return (earlier[0] * later[0], later[0][:, None, None] * earlier[1] + later[1])


def per_device(
    x_in,
    bc_in,
    z_in,
    dt_raw,
    conv_weight,
    conv_bias,
    dt_bias,
    a_log,
    d_skip,
    norm_gain,
    w_out,
    prompt_stretches,
):
    x_rows, bc_rows, z_rows, dt_rows = (
        lax.all_to_all(x_in, "req", split_axis=0, concat_axis=0, tiled=True),
        lax.all_to_all(bc_in, "req", split_axis=0, concat_axis=0, tiled=True),
        lax.all_to_all(z_in, "req", split_axis=0, concat_axis=0, tiled=True),
        lax.all_to_all(dt_raw, "req", split_axis=0, concat_axis=0, tiled=True),
    )
    row_count = x_rows.shape[0]
    inner_width = x_rows.shape[1]
    head_count = a_log.shape[0]
    head_dim = inner_width // head_count
    stretch_count = row_count // STRETCH
    conv_span = conv_weight.shape[0]
    device = lax.axis_index(("req", "seq"))
    stretch_ids = device * stretch_count + jnp.arange(stretch_count, dtype=jnp.int32)
    starts, finals = stretch_flags(prompt_stretches, stretch_ids)
    edge_x, edge_bc = from_behind(
        (x_rows[row_count - conv_span + 1 :], bc_rows[row_count - conv_span + 1 :]),
        ("req", "seq"),
        1,
    )
    conv_x = causal_conv(
        x_rows, edge_x, conv_weight[:, :inner_width], conv_bias[:inner_width], starts
    )
    conv_bc = causal_conv(
        bc_rows, edge_bc, conv_weight[:, inner_width:], conv_bias[inner_width:], starts
    )
    x_heads = conv_x.reshape(stretch_count, STRETCH, head_count, head_dim)
    bc_stretches = conv_bc.reshape(stretch_count, STRETCH, 2 * N)
    dt_stretches = dt_rows.reshape(stretch_count, STRETCH, head_count)

    def stretch_work(element):
        return local_stretch(element[0], element[1], element[2], dt_bias, a_log)

    y_diag, stretch_state, log_decay = lax.map(stretch_work, (x_heads, bc_stretches, dt_stretches))
    carried = jnp.where(starts[:, None], 0.0, jnp.exp(log_decay[:, -1, :]))
    total_gain = jnp.ones((head_count,), jnp.float32)
    total_state = jnp.zeros((head_count, head_dim, N), jnp.float32)
    for stretch in range(stretch_count):
        total_gain, total_state = chain_states(
            (total_gain, total_state), (carried[stretch], stretch_state[stretch])
        )
    identity = (
        jnp.ones((head_count,), jnp.float32),
        jnp.zeros((head_count, head_dim, N), jnp.float32),
    )
    incoming = carried_in((total_gain, total_state), ("req", "seq"), chain_states, identity)
    state_prev = incoming[1]
    normed_parts = []
    ending_parts = []
    for stretch in range(stretch_count):
        state_in = jnp.where(starts[stretch], jnp.zeros_like(state_prev), state_prev)
        z_stretch = z_rows[stretch * STRETCH : (stretch + 1) * STRETCH]
        normed_parts.append(
            finish_stretch(
                y_diag[stretch],
                log_decay[stretch],
                state_in,
                x_heads[stretch],
                bc_stretches[stretch, :, N:],
                z_stretch,
                d_skip,
                norm_gain,
            )
        )
        state_out = (
            jnp.exp(log_decay[stretch, -1])[:, None, None] * state_in + stretch_state[stretch]
        )
        ending_parts.append(jnp.where(finals[stretch], state_out, jnp.zeros_like(state_out)))
        state_prev = state_out
    normed = jnp.concatenate(normed_parts, axis=0)
    endings = lax.all_to_all(
        jnp.stack(ending_parts, axis=0), "seq", split_axis=1, concat_axis=0, tiled=True
    )
    projected = jnp.dot(normed, w_out, preferred_element_type=jnp.float32).astype(jnp.bfloat16)
    mixed_out = lax.all_to_all(projected, "req", split_axis=0, concat_axis=0, tiled=True)
    return (mixed_out, endings)


def solution(mesh):
    placed = (
        P(("req", "seq"), None),
        P(("req", "seq"), None),
        P(("req", "seq"), None),
        P(("req", "seq"), None),
        P(),
        P(),
        P(),
        P(),
        P(),
        P(),
        P(),
        P(),
    )
    return jax.shard_map(
        per_device,
        mesh=mesh,
        in_specs=placed,
        out_specs=(P(("req", "seq"), None), P("req", "seq", None, None)),
        check_vma=False,
    )
```

profile of v0, /device:TPU:1, one launch (start us, length us, event | category | flops | bytes accessed | tf_op | source)
XLA Modules:
  0.0 788.2 jit_solution(1823685997956062627)
XLA Ops:
  8.3 16.5 %all_to_all.72 = bf16[32,2,320]{2,1,0:T(2,128)(2,1)S(1)} all-to-all(bf16[32,2,320]{2,1,0:T(2,128)(2,1)S(1)} %reshape.277), channel_id=1, replica_groups=mesh['req'=32,'seq'=4] {'req'}, dimensions={0} | all-to-all | bytes 81920 | tf_op jit(solution)/shard_map/all_to_all | solution.py:106
  24.8 12.9 %all_to_all.73 = bf16[32,16,256]{2,1,0:T(8,128)(2,1)S(1)} all-to-all(bf16[32,16,256]{2,1,0:T(8,128)(2,1)} %bitcast.232), channel_id=1, replica_groups=mesh['req'=32,'seq'=4] {'req'}, dimensions={0} | all-to-all | bytes 524288 | tf_op jit(solution)/shard_map/all_to_all | solution.py:104
  37.7 4.0 all-to-all-start
  42.4 3.2 collective-permute-start.1
  46.1 29.6 %all-to-all-done = bf16[32,16,2560]{2,1,0:T(8,128)(2,1)S(1)} async-done(((bf16[32,16,2560]{2,1,0:T(8,128)(2,1)}), bf16[32,16,2560]{2,1,0:T(8,128)(2,1)S(1)}, u32[]{:S(2)}, u32[]{:S(2)}) %all-to-all-start) | async-done | bytes 2621472 | tf_op jit(solution)/shard_map/all_to_all | solution.py:103
  75.7 3.2 collective-permute-start
  79.7 4.7 collective-permute-done
  84.4 9.7 %multiply_convert_fusion.6 = bf16[512,2560]{1,0:T(8,128)(2,1)S(1)} fusion(bf16[512,2560]{1,0:T(8,128)(2,1)} %bitcast.218, bf16[3,2560]{1,0:T(4,128)(2,1)S(1)} %collective-permute-done, f32[2560]{0:T(1024)S(1)} %get-tuple-element.197, f32[2560]{0:T(1024)S(1)} %get-tuple-element.198, f32[2560]{0:T(1024)S(1)} %get-tuple-element.199, ...), kind=kLoop, calls=%fused_computation.47 | loop fusion | flops 39321600 | bytes 5311488 | tf_op jit(solution)/shard_map/convert_element_type | solution.py:49
  94.2 1.4 copy-done
  95.6 4.4 reshape.266
  100.1 5.2 copy.80
  105.3 16.8 %while.28 = (s32[]{:T(128)}, f32[2,256,40,64]{1,3,2,0:T(8,128)}, f32[2,40,64,128]{3,2,1,0:T(8,128)}, f32[2,256,40]{1,2,0:T(8,128)S(1)}, bf16[2,256,40,64]{1,3,2,...) while((s32[]{:T(128)}, f32[2,256,40,64]{1,3,2,0:T(8,128)}, ...), condition=%wide.region_5.6_spmd, body=%wide.region_2.0_spmd.sunk | while | flops 539379840 | bytes 29302236 | solution.py:135
  106.8 4.7 bitcast_dynamic-update-slice_fusion.4
  112.1 1.5 copy-done.6
  115.2 4.7 bitcast_dynamic-update-slice_fusion.4
  120.5 1.5 copy-done.6
  122.3 3.0 multiply_add_fusion
  125.4 5.5 all-to-all-start.3
  131.5 47.4 %all-to-all-done.3 = bf16[32,16,2560]{2,1,0:T(8,128)(2,1)} async-done(((bf16[32,16,2560]{2,1,0:T(8,128)(2,1)}), bf16[32,16,2560]{2,1,0:T(8,128)(2,1)}, u32[]{:S(2)}, u32[]{:S(2)}) %all-to-all-start.3) | async-done | bytes 2621472 | tf_op jit(solution)/shard_map/all_to_all | solution.py:105
  178.9 3.9 slice_convert_fusion.2
  182.8 3.9 reshape.257
  187.1 6.0 copy.85
  193.1 5.0 reshape.260
  198.1 6.4 copy.89
  204.4 3.0 slice_convert_fusion.3
  207.4 3.5 copy.82
  210.9 2.1 copy.86
  213.0 46.3 %all-gather = f32[128,1,40]{2,1,0:T(1,128)S(1)} all-gather(f32[1,1,40]{2,1,0:T(1,128)S(1)} %get-tuple-element.255), channel_id=1, replica_groups=mesh['req'=32,'seq'=4] {'req','seq'}, dimensions={0}, use_global_device_ids=true | all-gather | bytes 20640 | tf_op jit(solution)/shard_map/all_gather | solution.py:18
  259.5 229.7 %all-gather.3.cloned.1.call-done = f32[128,40,64,128]{3,2,1,0:T(8,128)} async-done(((f32[1,40,64,128]{3,2,1,0:T(8,128)}), f32[128,40,64,128]{3,2,1,0:T(8,128)}) %all-gather.3.cloned.1.call-update) | async-done | bytes 167772176 | tf_op jit(solution)/shard_map/all_gather | solution.py:18
  489.4 6.5 while.29
  489.4 1.6 bitcast_add_fusion.7
  491.0 1.6 bitcast_add_fusion.7
  492.7 1.6 bitcast_add_fusion.7
  494.3 1.6 bitcast_add_fusion.7
  495.9 2.8 fusion.52
  498.7 1.5 select_bitcast_fusion
  500.2 2.6 fusion.53
  504.6 1.7 copy.90
  506.3 8.7 %all-to-all-start.5 = ((f32[2,40,64,128]{3,2,0,1:T(8,128)}), f32[2,40,64,128]{3,2,0,1:T(8,128)}, u32[]{:S(2)}, u32[]{:S(2)}) async-start(f32[2,40,64,128]{3,2,0,1:T(8,128)} %copy.90), calls=%async_computation.5 | async-start | bytes 5242880 | tf_op jit(solution)/shard_map/all_to_all | solution.py:172
  515.0 9.6 %multiply_reduce_fusion.1 = (f32[256]{0:T(256)S(1)}, f32[256,40,64]{0,2,1:T(8,128)}, f32[256]{0:T(256)S(1)}, f32[256,40,64]{0,2,1:T(8,128)}) fusion(f32[256,40,64]{0,2,1:T(8,128)} %copy.85, f32[256,40,64]{0,2,1:T(8,128)S(1)} %bitcast.220, f32[40]{0:T(128)S(1)} %copy-done.15, f32[256,40,64]{0,2,1:T(8,128)} %fusion.52, f32[256,40]{0,1:T(8,128)S(1)} %get-tuple-element.246, ...), kind=kLoop, calls=%fused_computation.79 | loop fusion | flops 14417408 | bytes 26298528 | tf_op jit(solution)/shard_map/reduce_sum | solution.py:80
  524.6 3.2 copy.83
  527.8 3.4 copy.87
  531.2 4.3 fusion.48
  535.6 11.0 %convolution_convert_fusion = bf16[512,2560]{1,0:T(8,128)(2,1)} fusion(bf16[2560,2560]{1,0:T(8,128)(2,1)} %param.26, bf16[256,2560]{1,0:T(8,128)(2,1)S(1)} %get-tuple-element.253, bf16[256,2560]{1,0:T(8,128)(2,1)S(1)} %get-tuple-element.252), kind=kOutput, calls=%fused_computation.48 | convolution fusion | flops 6717440000 | bytes 18350080 | tf_op jit(solution)/shard_map/dot_general | solution.py:175
  546.6 199.3 %all-to-all-start.4 = ((bf16[32,16,2560]{2,1,0:T(8,128)(2,1)}), bf16[32,16,2560]{2,1,0:T(8,128)(2,1)S(1)}, u32[]{:S(2)}, u32[]{:S(2)}) async-start(bf16[32,16,2560]{2,1,0:T(8,128)(2,1)} %bitcast.227), calls=%async_computation.4 | async-start | bytes 5242880 | tf_op jit(solution)/shard_map/all_to_all | solution.py:176
  745.9 3.6 copy.91
  749.4 30.4 %all-to-all-done.4 = bf16[32,16,2560]{2,1,0:T(8,128)(2,1)S(1)} async-done(((bf16[32,16,2560]{2,1,0:T(8,128)(2,1)}), bf16[32,16,2560]{2,1,0:T(8,128)(2,1)S(1)}, u32[]{:S(2)}, u32[]{:S(2)}) %all-to-all-start.4) | async-done | bytes 2621472 | tf_op jit(solution)/shard_map/all_to_all | solution.py:176
  779.8 1.5 copy.134
  (103 shorter events, 10.6 us)
Async XLA Ops:
  37.7 4.1 copy-start.14
  37.7 4.7 copy-start.16
  37.7 4.7 copy-start.11
  37.7 8.1 %copy-start.12 = (f32[2816]{0:T(1024)S(1)}, f32[2816]{0:T(1024)}, u32[]{:S(2)}) copy-start(f32[2816]{0:T(1024)} %param.21) | copy-start | bytes 33796
  37.7 38.0 %all-to-all-start = ((bf16[32,16,2560]{2,1,0:T(8,128)(2,1)}), bf16[32,16,2560]{2,1,0:T(8,128)(2,1)S(1)}, u32[]{:S(2)}, u32[]{:S(2)}) async-start(bf16[32,16,2560]{2,1,0:T(8,128)(2,1)} %bitcast.225), calls=%async_computation | async-start | bytes 5242880 | tf_op jit(solution)/shard_map/all_to_all | solution.py:103
  41.7 447.5 %all-gather.3.cloned.1.call-start = ((), (), s32[]{:S(2)}) async-start(), calls=%async_computation.6 | async-start | bytes 169082880 | tf_op jit(solution)/shard_map/all_gather | solution.py:18
  42.4 36.5 %collective-permute-start.1 = (bf16[3,256]{1,0:T(4,128)(2,1)S(1)}, bf16[3,256]{1,0:T(4,128)(2,1)S(1)}, u32[]{:S(2)}, u32[]{:S(2)}) collective-permute-start(bf16[3,256]{1,0:T(4,128)(2,1)S(1)} %slice.206), channel_id=1, source_target_pairs={{0,1},{1,2},{2,3},{3,4},{4,5},{5,6},{6,7},{7,8},{8,9},{9,10},{10,1... | collective-permute-start | bytes 4616 | tf_op jit(solution)/shard_map/ppermute | solution.py:13
  75.7 8.8 %copy-start.4 = (bf16[32,16,2560]{2,1,0:T(8,128)(2,1)}, bf16[32,16,2560]{2,1,0:T(8,128)(2,1)S(1)}, u32[]{:S(2)}) copy-start(bf16[32,16,2560]{2,1,0:T(8,128)(2,1)S(1)} %all-to-all-done) | copy-start | bytes 7864324
  75.7 8.7 %collective-permute-start = (bf16[3,2560]{1,0:T(4,128)(2,1)S(1)}, bf16[3,2560]{1,0:T(4,128)(2,1)S(1)}, u32[]{:S(2)}, u32[]{:S(2)}) collective-permute-start(bf16[3,2560]{1,0:T(4,128)(2,1)S(1)} %slice.201), channel_id=1, source_target_pairs={{0,1},{1,2},{2,3},{3,4},{4,5},{5,6},{6,7},{7,8},{8,9},{9,10},{10,1... | collective-permute-start | bytes 46088 | tf_op jit(solution)/shard_map/ppermute | solution.py:13
  94.2 1.5 copy-start
  100.1 5.2 copy-start.10
  106.8 4.7 copy-start.5
  112.1 1.5 copy-start.6
  115.2 4.7 copy-start.5
  120.5 1.5 copy-start.6
  125.4 53.6 %all-to-all-start.3 = ((bf16[32,16,2560]{2,1,0:T(8,128)(2,1)}), bf16[32,16,2560]{2,1,0:T(8,128)(2,1)}, u32[]{:S(2)}, u32[]{:S(2)}) async-start(bf16[32,16,2560]{2,1,0:T(8,128)(2,1)} %bitcast.38), calls=%async_computation.3 | async-start | bytes 5242880 | tf_op jit(solution)/shard_map/all_to_all | solution.py:105
  182.8 4.3 copy-start.2
  198.1 6.4 copy-start.1
  207.4 3.5 copy-start.8
  495.9 2.8 copy-start.7
  506.3 8.7 %copy-start.9 = (f32[256,2560]{0,1:T(8,128)S(1)}, f32[256,2560]{0,1:T(8,128)}, u32[]{:S(2)}) copy-start(f32[256,2560]{0,1:T(8,128)} %copy.82) | copy-start | bytes 7864324
  506.3 8.7 %copy-start.15 = (f32[40]{0:T(128)S(1)}, f32[40]{0:T(128)}, u32[]{:S(2)}) copy-start(f32[40]{0:T(128)} %param.24) | copy-start | bytes 484
  506.3 40.3 %all-to-all-start.5 = ((f32[2,40,64,128]{3,2,0,1:T(8,128)}), f32[2,40,64,128]{3,2,0,1:T(8,128)}, u32[]{:S(2)}, u32[]{:S(2)}) async-start(f32[2,40,64,128]{3,2,0,1:T(8,128)} %copy.90), calls=%async_computation.5 | async-start | bytes 5242880 | tf_op jit(solution)/shard_map/all_to_all | solution.py:172
  527.8 3.4 copy-start.3
  527.8 3.4 copy-start.13
  546.6 233.2 %all-to-all-start.4 = ((bf16[32,16,2560]{2,1,0:T(8,128)(2,1)}), bf16[32,16,2560]{2,1,0:T(8,128)(2,1)S(1)}, u32[]{:S(2)}, u32[]{:S(2)}) async-start(bf16[32,16,2560]{2,1,0:T(8,128)(2,1)} %bitcast.227), calls=%async_computation.4 | async-start | bytes 5242880 | tf_op jit(solution)/shard_map/all_to_all | solution.py:176
Sparse Core Ops, SparseCore 0:
  125.5 363.6 all-gather.2
where the time goes:
time: 795 us; the launch traced here: 788 us
  waiting for transfers between devices  342 us (43%)
  starting transfers between devices  224 us (28%)
  blocking collectives  75.7 us (10%)
  local copies, waits for them, and re-layouts  58.3 us (7%)
  other arithmetic  46.5 us (6%)
  matrix products  27.2 us (3%)
  between operations  14.4 us (2%)
    all_gather x1, waiting for transfers between devices, carried_in(): gathered = jax.tree.map(lambda a: lax.all_gather(a, axis), part)  230 us
    all_to_all x1, starting transfers between devices, per_device(): lax.all_to_all(projected, 'req', split_axis=0, concat_axis=0, tiled=True)  199 us
    all_to_all x1, waiting for transfers between devices, per_device(): lax.all_to_all(z_in, 'req', split_axis=0, concat_axis=0, tiled=True)  47.4 us
    all_gather x1, blocking collectives, carried_in(): gathered = jax.tree.map(lambda a: lax.all_gather(a, axis), part)  46.3 us
    all_to_all x1, waiting for transfers between devices, per_device(): lax.all_to_all(projected, 'req', split_axis=0, concat_axis=0, tiled=True)  30.4 us
    all_to_all x1, waiting for transfers between devices, per_device(): lax.all_to_all(x_in, 'req', split_axis=0, concat_axis=0, tiled=True)  29.6 us
    convert_element_type x4, local copies, waits for them, and re-layouts, finish_stretch(): gated_rows = mixed_rows * jax.nn.silu(z_stretch.astype(jnp.float32))  21.3 us
    all_to_all x1, blocking collectives, per_device(): lax.all_to_all(dt_raw, 'req', split_axis=0, concat_axis=0, tiled=True)  16.5 us
  transfers between devices with their start and end apart: 7, of which 5 were waited for; matrix products, arithmetic and copies ran while one was open for 9% of the time, Pallas kernels for 0%

commit v1 on v0

--- a/solution.py
+++ b/solution.py
@@ -13,17 +13,20 @@
     return lax.ppermute(value, axis, [(source, source + steps) for source in range(leading, last)])
 
 
-def carried_in(part, axis, combine, identity):
-    place = lax.axis_index(axis)
-    gathered = jax.tree.map(lambda a: lax.all_gather(a, axis), part)
-    state = jax.tree.map(lambda a, e: jnp.zeros_like(a) + jnp.asarray(e, a.dtype), part, identity)
-
-    def one(step, state):
-        return combine(
-            state, jax.tree.map(lambda a: lax.dynamic_index_in_dim(a, step, 0, False), gathered)
-        )
-
-    return lax.fori_loop(0, place, one, state)
+LMAX_CH = 16
+
+
+def carried_in(part, axis, combine, window):
+    first = min(4, window)
+    pieces = [from_behind(part, axis, k) for k in range(1, first + 1)]
+    state = pieces[-1]
+    for piece in reversed(pieces[:-1]):
+        state = combine(state, piece)
+    cover = first
+    while cover < window:
+        state = combine(from_behind(state, axis, cover), state)
+        cover *= 2
+    return state
 
 
 def stretch_flags(prompt_stretches, stretch_ids):
@@ -140,11 +143,8 @@
         total_gain, total_state = chain_states(
             (total_gain, total_state), (carried[stretch], stretch_state[stretch])
         )
-    identity = (
-        jnp.ones((head_count,), jnp.float32),
-        jnp.zeros((head_count, head_dim, N), jnp.float32),
-    )
-    incoming = carried_in((total_gain, total_state), ("req", "seq"), chain_states, identity)
+    window = -(-(LMAX_CH - 1) // stretch_count)
+    incoming = carried_in((total_gain, total_state), ("req", "seq"), chain_states, window)
     state_prev = incoming[1]
     normed_parts = []
     ending_parts = []

time: 795 us -> 364 us (0.46)
  waiting for transfers between devices: 342 us -> 119 us
  starting transfers between devices: 224 us -> 81.7 us
  blocking collectives: 75.7 us -> 29.4 us
  between operations: 14.4 us -> 1.14 us
    all_gather x1 -> x0, waiting for transfers between devices: 230 us -> none  [carried_in(): gathered = jax.tree.map(lambda a: lax.all_gather(a, axis), part)]
    all_to_all x1, starting transfers between devices: 199 us -> 10.1 us  [per_device(): lax.all_to_all(projected, 'req', split_axis=0, concat_axis=0, tiled=True)]
    ppermute x2 -> x11, waiting for transfers between devices: 4.69 us -> 58.6 us  [from_behind(): lax.ppermute(value, axis, [(source, source + steps) for source in range(l...]
    ppermute x2 -> x11, starting transfers between devices: 6.41 us -> 56.1 us  [from_behind(): lax.ppermute(value, axis, [(source, source + steps) for source in range(l...]
    all_to_all x1, waiting for transfers between devices: 47.4 us -> 0.01 us  [per_device(): lax.all_to_all(z_in, 'req', split_axis=0, concat_axis=0, tiled=True)]
    all_gather x1 -> x0, blocking collectives: 46.3 us -> none  [carried_in(): gathered = jax.tree.map(lambda a: lax.all_gather(a, axis), part)]
  transfers between devices with their start and end apart: 7 -> 15, of which waited for: 5 -> 7; matrix products, arithmetic and copies ran while one was open for 9% -> 31% of each run, Pallas kernels for 0% -> 0%
where the time goes in v1:
time: 364 us; the launch traced here: 361 us
  waiting for transfers between devices  119 us (33%)
  starting transfers between devices  81.7 us (22%)
  local copies, waits for them, and re-layouts  55.5 us (15%)
  other arithmetic  46 us (13%)
  blocking collectives  29.4 us (8%)
  matrix products  28.2 us (8%)
    ppermute x11, waiting for transfers between devices, from_behind(): lax.ppermute(value, axis, [(source, source + steps) for source in range(l...  58.6 us
    ppermute x11, starting transfers between devices, from_behind(): lax.ppermute(value, axis, [(source, source + steps) for source in range(l...  56.1 us
    all_to_all x1, waiting for transfers between devices, per_device(): lax.all_to_all(projected, 'req', split_axis=0, concat_axis=0, tiled=True)  30.4 us
    all_to_all x1, waiting for transfers between devices, per_device(): lax.all_to_all(x_in, 'req', split_axis=0, concat_axis=0, tiled=True)  29.7 us
    convert_element_type x4, local copies, waits for them, and re-layouts, finish_stretch(): gated_rows = mixed_rows * jax.nn.silu(z_stretch.astype(jnp.float32))  19.9 us
    all_to_all x1, blocking collectives, per_device(): lax.all_to_all(dt_raw, 'req', split_axis=0, concat_axis=0, tiled=True)  16.5 us
    all_to_all x1, blocking collectives, per_device(): lax.all_to_all(bc_in, 'req', split_axis=0, concat_axis=0, tiled=True)  12.9 us
    dot_general x1, matrix products, per_device(): jnp.dot(normed, w_out, preferred_element_type=jnp.float32)  11 us
  transfers between devices with their start and end apart: 15, of which 7 were waited for; matrix products, arithmetic and copies ran while one was open for 31% of the time, Pallas kernels for 0%

profile of v1, /device:TPU:1, one launch (start us, length us, event | category | flops | bytes accessed | tf_op | source)
XLA Modules:
  0.0 360.8 jit_solution(13563285232511800863)
XLA Ops:
  1.7 16.5 %all_to_all.72 = bf16[32,2,320]{2,1,0:T(2,128)(2,1)S(1)} all-to-all(bf16[32,2,320]{2,1,0:T(2,128)(2,1)S(1)} %reshape.275), channel_id=1, replica_groups=mesh['req'=32,'seq'=4] {'req'}, dimensions={0} | all-to-all | bytes 81920 | tf_op jit(solution)/shard_map/all_to_all | solution.py:109
  18.2 12.9 %all_to_all.73 = bf16[32,16,256]{2,1,0:T(8,128)(2,1)S(1)} all-to-all(bf16[32,16,256]{2,1,0:T(8,128)(2,1)} %bitcast.233), channel_id=1, replica_groups=mesh['req'=32,'seq'=4] {'req'}, dimensions={0} | all-to-all | bytes 524288 | tf_op jit(solution)/shard_map/all_to_all | solution.py:107
  31.1 4.0 %all-to-all-start = ((bf16[32,16,2560]{2,1,0:T(8,128)(2,1)}), bf16[32,16,2560]{2,1,0:T(8,128)(2,1)S(1)}, u32[]{:S(2)}, u32[]{:S(2)}) async-start(bf16[32,16,2560]{2,1,0:T(8,128)(2,1)} %bitcast.225), calls=%async_computation | async-start | bytes 5242880 | tf_op jit(solution)/shard_map/all_to_all | solution.py:106
  35.9 3.2 collective-permute-start.1
  39.5 29.7 %all-to-all-done = bf16[32,16,2560]{2,1,0:T(8,128)(2,1)S(1)} async-done(((bf16[32,16,2560]{2,1,0:T(8,128)(2,1)}), bf16[32,16,2560]{2,1,0:T(8,128)(2,1)S(1)}, u32[]{:S(2)}, u32[]{:S(2)}) %all-to-all-start) | async-done | bytes 2621472 | tf_op jit(solution)/shard_map/all_to_all | solution.py:106
  69.2 6.9 %all-to-all-start.3 = ((bf16[32,16,2560]{2,1,0:T(8,128)(2,1)}), bf16[32,16,2560]{2,1,0:T(8,128)(2,1)}, u32[]{:S(2)}, u32[]{:S(2)}) async-start(bf16[32,16,2560]{2,1,0:T(8,128)(2,1)} %bitcast.226), calls=%async_computation.3 | async-start | bytes 5242880 | tf_op jit(solution)/shard_map/all_to_all | solution.py:108
  76.1 3.2 collective-permute-start
  80.2 2.8 collective-permute-done
  82.9 10.0 %multiply_convert_fusion.6 = bf16[512,2560]{1,0:T(8,128)(2,1)S(1)} fusion(bf16[512,2560]{1,0:T(8,128)(2,1)} %bitcast.218, bf16[3,2560]{1,0:T(4,128)(2,1)S(1)} %collective-permute-done, f32[2560]{0:T(1024)S(1)} %get-tuple-element.152, f32[2560]{0:T(1024)S(1)} %get-tuple-element.153, f32[2560]{0:T(1024)S(1)} %get-tuple-element.154, ...), kind=kLoop, calls=%fused_computation.45 | loop fusion | flops 39321600 | bytes 5311488 | tf_op jit(solution)/shard_map/convert_element_type | solution.py:52
  94.4 4.4 %reshape.264 = bf16[2,256,40,64]{3,2,1,0:T(8,128)(2,1)} reshape(bf16[512,2560]{1,0:T(8,128)(2,1)S(1)} %multiply_convert_fusion.6) | data formatting | bytes 5242880 | tf_op jit(solution)/shard_map/reshape | solution.py:131
  98.9 5.2 %copy.80 = bf16[2,256,40,64]{1,3,2,0:T(8,128)(2,1)S(1)} copy(bf16[2,256,40,64]{3,2,1,0:T(8,128)(2,1)} %reshape.264) | data formatting | bytes 5242880 | tf_op jit(solution)/shard_map/while | solution.py:138
  104.1 16.7 %while.16 = (s32[]{:T(128)}, f32[2,256,40,64]{1,3,2,0:T(8,128)}, f32[2,40,64,128]{3,2,1,0:T(8,128)}, f32[2,256,40]{1,2,0:T(8,128)S(1)}, bf16[2,256,40,64]{1,3,2,...) while((s32[]{:T(128)}, f32[2,256,40,64]{1,3,2,0:T(8,128)}, ...), condition=%wide.region_5.6_spmd, body=%wide.region_2.0_spmd.sunk | while | flops 539379840 | bytes 29302236 | solution.py:138
  105.6 4.7 %bitcast_dynamic-update-slice_fusion.4 = f32[2,256,40,64]{1,3,2,0:T(8,128)} fusion(f32[2,256,40,64]{1,3,2,0:T(8,128)} %get-tuple-element.288, s32[]{:T(128)} %get-tuple-element.287, f32[40,256]{1,0:T(8,128)S(1)} %get-tuple-element.273, f32[40,256]{1,0:T(8,128)S(1)} %get-tuple-element.274, f32[256,256]{1,0:T(8,128)S(1)} %fusion.97, ...), kind=kOutput, calls=%fused_computation.8.clone.1 | convolution fusion | flops 351272960 | bytes 4383744 | tf_op jit(solution)/shard_map/while/body/eval_jaxpr/htu,uhp->thp/dot_general | solution.py:68
  114.0 4.7 %bitcast_dynamic-update-slice_fusion.4 = f32[2,256,40,64]{1,3,2,0:T(8,128)} fusion(f32[2,256,40,64]{1,3,2,0:T(8,128)} %get-tuple-element.288, s32[]{:T(128)} %get-tuple-element.287, f32[40,256]{1,0:T(8,128)S(1)} %get-tuple-element.273, f32[40,256]{1,0:T(8,128)S(1)} %get-tuple-element.274, f32[256,256]{1,0:T(8,128)S(1)} %fusion.97, ...), kind=kOutput, calls=%fused_computation.8.clone.1 | convolution fusion | flops 351272960 | bytes 4383744 | tf_op jit(solution)/shard_map/while/body/eval_jaxpr/htu,uhp->thp/dot_general | solution.py:68
  121.0 3.0 bitcast_add_fusion.3
  124.1 29.3 %collective-permute-start.6 = (f32[40,64,128]{2,1,0:T(8,128)}, f32[40,64,128]{2,1,0:T(8,128)}, u32[]{:S(2)}, u32[]{:S(2)}) collective-permute-start(f32[40,64,128]{2,1,0:T(8,128)} %bitcast_add_fusion.3), channel_id=1, source_target_pairs={{0,4},{1,5},{2,6},{3,7},{4,8},{5,9},{6,10},{7,11},{8,12},{9,13},{1... | collective-permute-start | bytes 3932168 | tf_op jit(solution)/shard_map/ppermute | solution.py:13
  153.3 1.9 collective-permute-start.7
  155.3 1.9 collective-permute-start.8
  157.2 3.1 collective-permute-start.9
  161.0 3.9 %slice_convert_fusion.2 = (f32[16,16,2560]{2,1,0:T(8,128)S(1)}, f32[16,16,2560]{2,1,0:T(8,128)}) fusion(bf16[32,16,2560]{2,1,0:T(8,128)(2,1)} %all-to-all-done.3), kind=kLoop, calls=%fused_computation.82 | loop fusion | flops 1310720 | bytes 7864320 | tf_op jit(solution)/shard_map/convert_element_type | solution.py:82
  164.9 5.7 %collective-permute-start.3 = (f32[40]{0:T(128)S(1)}, f32[40]{0:T(128)S(1)}, u32[]{:S(2)}, u32[]{:S(2)}) collective-permute-start(f32[40]{0:T(128)S(1)} %get-tuple-element.199), channel_id=1, source_target_pairs={{0,3},{1,4},{2,5},{3,6},{4,7},{5,8},{6,9},{7,10},{8,11},{9,12},{10... | collective-permute-start | bytes 488 | tf_op jit(solution)/shard_map/ppermute | solution.py:13
  170.5 2.9 reshape.257
  173.4 6.0 %copy.85 = f32[256,40,64]{0,2,1:T(8,128)} copy(f32[256,40,64]{2,1,0:T(8,128)} %reshape.257) | data formatting | bytes 5242880 | tf_op jit(solution)/shard_map/convert_element_type | solution.py:82
  179.5 35.2 %collective-permute-done.3 = f32[40]{0:T(128)S(1)} collective-permute-done((f32[40]{0:T(128)S(1)}, f32[40]{0:T(128)S(1)}, u32[]{:S(2)}, u32[]{:S(2)}) %collective-permute-start.3) | collective-permute-done | bytes 192 | tf_op jit(solution)/shard_map/ppermute | solution.py:13
  214.6 2.1 collective-permute-start.4
  216.7 4.9 %reshape.260 = f32[256,40,64]{2,1,0:T(8,128)} reshape(f32[16,16,2560]{2,1,0:T(8,128)} %get-tuple-element.190) | data formatting | bytes 5242880 | tf_op jit(solution)/shard_map/convert_element_type | solution.py:82
  221.6 6.0 %copy.89 = f32[256,40,64]{0,2,1:T(8,128)} copy(f32[256,40,64]{2,1,0:T(8,128)} %reshape.260) | data formatting | bytes 5242880 | tf_op jit(solution)/shard_map/convert_element_type | solution.py:82
  227.7 11.4 %collective-permute-done.4 = f32[40]{0:T(128)S(1)} collective-permute-done((f32[40]{0:T(128)S(1)}, f32[40]{0:T(128)S(1)}, u32[]{:S(2)}, u32[]{:S(2)}) %collective-permute-start.4) | collective-permute-done | bytes 192 | tf_op jit(solution)/shard_map/ppermute | solution.py:13
  241.2 4.0 %collective-permute-done.5 = f32[40]{0:T(128)S(1)} collective-permute-done((f32[40]{0:T(128)S(1)}, f32[40]{0:T(128)S(1)}, u32[]{:S(2)}, u32[]{:S(2)}) %collective-permute-start.5) | collective-permute-done | bytes 192 | tf_op jit(solution)/shard_map/ppermute | solution.py:13
  245.2 1.9 collective-permute-start.2
  247.2 3.9 %multiply_add_fusion = f32[40,64,128]{2,1,0:T(8,128)} fusion(f32[40,64,128]{2,1,0:T(8,128)} %collective-permute-done.9, f32[40,64,128]{2,1,0:T(8,128)} %collective-permute-done.8, f32[40,64,128]{2,1,0:T(8,128)} %collective-permute-done.7, f32[40,64,128]{2,1,0:T(8,128)} %collective-permute-done.6, f32[40]{0:T(128)S(1)} %collective-permute-done.3, ...), kind=kLoop, calls=%fused_computation.93 | loop fusion | flops 1966080 | bytes 6554080 | tf_op jit(solution)/shard_map/add | solution.py:88
  251.1 1.9 collective-permute-start.10
  253.1 3.1 slice_convert_fusion.3
  256.1 3.3 copy.82
  259.4 3.2 copy.86
  262.6 5.3 %collective-permute-done.10 = f32[40,64,128]{2,1,0:T(8,128)} collective-permute-done((f32[40,64,128]{2,1,0:T(8,128)}, f32[40,64,128]{2,1,0:T(8,128)}, u32[]{:S(2)}, u32[]{:S(2)}) %collective-permute-start.10) | collective-permute-done | bytes 1310752 | tf_op jit(solution)/shard_map/ppermute | solution.py:13
  267.9 3.7 %select_bitcast_fusion = (f32[1,40,64,128]{3,2,0,1:T(8,128)S(1)}, f32[40,64,128]{2,1,0:T(8,128)S(1)}) fusion(pred[]{:T(512)} %bitcast.48, f32[2,40,64,128]{3,2,1,0:T(8,128)} %get-tuple-element.112, f32[40,64,128]{2,1,0:T(8,128)} %multiply_add_fusion, f32[40,64,128]{2,1,0:T(8,128)} %collective-permute-done.10, f32[40]{0:T(128)S(1)} %multiply_multiply_fusion, ...), kind=kLoop, calls=%fused_computation.91 | loop fusion | flops 1966080 | bytes 6553922 | tf_op jit(solution)/shard_map/stack | solution.py:173
  271.6 2.9 fusion.53
  277.6 4.6 %all-to-all-start.5 = ((f32[2,40,64,128]{3,2,0,1:T(8,128)}), f32[2,40,64,128]{3,2,0,1:T(8,128)}, u32[]{:S(2)}, u32[]{:S(2)}) async-start(f32[2,40,64,128]{3,2,0,1:T(8,128)} %pad_maximum_fusion.1), calls=%async_computation.5 | async-start | bytes 5242880 | tf_op jit(solution)/shard_map/all_to_all | solution.py:172
  282.2 3.5 fusion.54
  285.7 7.6 %multiply_reduce_fusion.1 = (f32[256]{0:T(256)S(1)}, f32[256,40,64]{0,2,1:T(8,128)}, f32[256]{0:T(256)S(1)}, f32[256,40,64]{0,2,1:T(8,128)}) fusion(f32[256,40,64]{0,2,1:T(8,128)} %copy.85, f32[256,40,64]{0,2,1:T(8,128)S(1)} %bitcast.220, f32[40]{0:T(128)S(1)} %copy-done.13, f32[256,40,64]{0,2,1:T(8,128)S(1)} %fusion.54, ...), kind=kLoop, calls=%fused_computation.77 | loop fusion | flops 14417408 | bytes 26298528 | tf_op jit(solution)/shard_map/reduce_sum | solution.py:83
  293.3 3.2 copy.83
  296.6 3.2 copy.87
  299.8 4.3 %fusion.48 = (bf16[256,2560]{1,0:T(8,128)(2,1)S(1)}, bf16[256,2560]{1,0:T(8,128)(2,1)S(1)}) fusion(f32[256,2560]{1,0:T(8,128)} %copy.83, f32[16,16,2560]{2,1,0:T(8,128)S(1)} %get-tuple-element.189, f32[2560]{0:T(1024)S(1)} %copy-done.11, f32[256]{0:T(256)S(1)} %add_rsqrt_fusion.1, f32[256]{0:T(256)S(1)} %add_rsqrt_fusion, f32[256,2560]{1,0:T(8,128)} %copy.87, ...), kind=kLoop, calls=%fused_computation.78 | loop fusion | flops 10485760 | bytes 13119488 | tf_op jit(solution)/shard_map/convert_element_type | solution.py:84
  304.2 11.0 %convolution_convert_fusion = bf16[512,2560]{1,0:T(8,128)(2,1)} fusion(bf16[2560,2560]{1,0:T(8,128)(2,1)} %param.24, bf16[256,2560]{1,0:T(8,128)(2,1)S(1)} %get-tuple-element.198, bf16[256,2560]{1,0:T(8,128)(2,1)S(1)} %get-tuple-element.197), kind=kOutput, calls=%fused_computation.46 | convolution fusion | flops 6717440000 | bytes 18350080 | tf_op jit(solution)/shard_map/dot_general | solution.py:175
  315.2 10.1 %all-to-all-start.4 = ((bf16[32,16,2560]{2,1,0:T(8,128)(2,1)}), bf16[32,16,2560]{2,1,0:T(8,128)(2,1)S(1)}, u32[]{:S(2)}, u32[]{:S(2)}) async-start(bf16[32,16,2560]{2,1,0:T(8,128)(2,1)} %bitcast.228), calls=%async_computation.4 | async-start | bytes 5242880 | tf_op jit(solution)/shard_map/all_to_all | solution.py:176
  325.3 3.6 copy.91
  328.9 30.4 %all-to-all-done.4 = bf16[32,16,2560]{2,1,0:T(8,128)(2,1)S(1)} async-done(((bf16[32,16,2560]{2,1,0:T(8,128)(2,1)}), bf16[32,16,2560]{2,1,0:T(8,128)(2,1)S(1)}, u32[]{:S(2)}, u32[]{:S(2)}) %all-to-all-start.4) | async-done | bytes 2621472 | tf_op jit(solution)/shard_map/all_to_all | solution.py:176
  (105 shorter events, 19.3 us)
Async XLA Ops:
  31.1 4.0 %copy-start.12 = (s32[64]{0:T(128)S(1)}, s32[64]{0:T(128)}, u32[]{:S(2)}) copy-start(s32[64]{0:T(128)} %param.25) | copy-start | bytes 772
  31.1 4.7 %copy-start.14 = (f32[40]{0:T(128)S(1)}, f32[40]{0:T(128)}, u32[]{:S(2)}) copy-start(f32[40]{0:T(128)} %param.21) | copy-start | bytes 484
  31.1 4.7 %copy-start.9 = (f32[4,2816]{1,0:T(4,128)S(1)}, f32[4,2816]{1,0:T(4,128)}, u32[]{:S(2)}) copy-start(f32[4,2816]{1,0:T(4,128)} %param.18) | copy-start | bytes 135172
  31.1 8.1 %copy-start.10 = (f32[2816]{0:T(1024)S(1)}, f32[2816]{0:T(1024)}, u32[]{:S(2)}) copy-start(f32[2816]{0:T(1024)} %param.19) | copy-start | bytes 33796
  31.1 38.0 %all-to-all-start = ((bf16[32,16,2560]{2,1,0:T(8,128)(2,1)}), bf16[32,16,2560]{2,1,0:T(8,128)(2,1)S(1)}, u32[]{:S(2)}, u32[]{:S(2)}) async-start(bf16[32,16,2560]{2,1,0:T(8,128)(2,1)} %bitcast.225), calls=%async_computation | async-start | bytes 5242880 | tf_op jit(solution)/shard_map/all_to_all | solution.py:106
  35.9 43.5 %collective-permute-start.1 = (bf16[3,256]{1,0:T(4,128)(2,1)S(1)}, bf16[3,256]{1,0:T(4,128)(2,1)S(1)}, u32[]{:S(2)}, u32[]{:S(2)}) collective-permute-start(bf16[3,256]{1,0:T(4,128)(2,1)S(1)} %slice.206), channel_id=1, source_target_pairs={{0,1},{1,2},{2,3},{3,4},{4,5},{5,6},{6,7},{7,8},{8,9},{9,10},{10,1... | collective-permute-start | bytes 4616 | tf_op jit(solution)/shard_map/ppermute | solution.py:13
  69.1 7.0 %copy-start.2 = (bf16[32,16,2560]{2,1,0:T(8,128)(2,1)}, bf16[32,16,2560]{2,1,0:T(8,128)(2,1)S(1)}, u32[]{:S(2)}) copy-start(bf16[32,16,2560]{2,1,0:T(8,128)(2,1)S(1)} %all-to-all-done) | copy-start | bytes 7864324
  69.2 91.8 %all-to-all-start.3 = ((bf16[32,16,2560]{2,1,0:T(8,128)(2,1)}), bf16[32,16,2560]{2,1,0:T(8,128)(2,1)}, u32[]{:S(2)}, u32[]{:S(2)}) async-start(bf16[32,16,2560]{2,1,0:T(8,128)(2,1)} %bitcast.226), calls=%async_computation.3 | async-start | bytes 5242880 | tf_op jit(solution)/shard_map/all_to_all | solution.py:108
  76.1 6.8 %collective-permute-start = (bf16[3,2560]{1,0:T(4,128)(2,1)S(1)}, bf16[3,2560]{1,0:T(4,128)(2,1)S(1)}, u32[]{:S(2)}, u32[]{:S(2)}) collective-permute-start(bf16[3,2560]{1,0:T(4,128)(2,1)S(1)} %slice.201), channel_id=1, source_target_pairs={{0,1},{1,2},{2,3},{3,4},{4,5},{5,6},{6,7},{7,8},{8,9},{9,10},{10,1... | collective-permute-start | bytes 46088 | tf_op jit(solution)/shard_map/ppermute | solution.py:13
  92.9 1.5 copy-start
  98.9 5.2 %copy-start.8 = (f32[40]{0:T(128)S(1)}, f32[40]{0:T(128)}, u32[]{:S(2)}) copy-start(f32[40]{0:T(128)} %param.20) | copy-start | bytes 484
  105.6 4.7 %copy-start.3 = (f32[2,40,64,128]{3,2,1,0:T(8,128)S(1)}, f32[2,40,64,128]{3,2,1,0:T(8,128)}, u32[]{:S(2)}) copy-start(f32[2,40,64,128]{3,2,1,0:T(8,128)} %get-tuple-element.289) | copy-start | bytes 7864324 | tf_op jit(solution)/shard_map/while
  110.9 1.5 copy-start.4
  114.0 4.7 %copy-start.3 = (f32[2,40,64,128]{3,2,1,0:T(8,128)S(1)}, f32[2,40,64,128]{3,2,1,0:T(8,128)}, u32[]{:S(2)}) copy-start(f32[2,40,64,128]{3,2,1,0:T(8,128)} %get-tuple-element.289) | copy-start | bytes 7864324 | tf_op jit(solution)/shard_map/while
  119.2 1.5 copy-start.4
  124.1 123.1 %collective-permute-start.6 = (f32[40,64,128]{2,1,0:T(8,128)}, f32[40,64,128]{2,1,0:T(8,128)}, u32[]{:S(2)}, u32[]{:S(2)}) collective-permute-start(f32[40,64,128]{2,1,0:T(8,128)} %bitcast_add_fusion.3), channel_id=1, source_target_pairs={{0,4},{1,5},{2,6},{3,7},{4,8},{5,9},{6,10},{7,11},{8,12},{9,13},{1... | collective-permute-start | bytes 3932168 | tf_op jit(solution)/shard_map/ppermute | solution.py:13
  153.3 93.8 %collective-permute-start.7 = (f32[40,64,128]{2,1,0:T(8,128)}, f32[40,64,128]{2,1,0:T(8,128)}, u32[]{:S(2)}, u32[]{:S(2)}) collective-permute-start(f32[40,64,128]{2,1,0:T(8,128)} %bitcast_add_fusion.3), channel_id=1, source_target_pairs={{0,3},{1,4},{2,5},{3,6},{4,7},{5,8},{6,9},{7,10},{8,11},{9,12},{10... | collective-permute-start | bytes 3932168 | tf_op jit(solution)/shard_map/ppermute | solution.py:13
  155.3 91.9 %collective-permute-start.8 = (f32[40,64,128]{2,1,0:T(8,128)}, f32[40,64,128]{2,1,0:T(8,128)}, u32[]{:S(2)}, u32[]{:S(2)}) collective-permute-start(f32[40,64,128]{2,1,0:T(8,128)} %bitcast_add_fusion.3), channel_id=1, source_target_pairs={{0,2},{1,3},{2,4},{3,5},{4,6},{5,7},{6,8},{7,9},{8,10},{9,11},{10,... | collective-permute-start | bytes 3932168 | tf_op jit(solution)/shard_map/ppermute | solution.py:13
  157.2 90.0 %collective-permute-start.9 = (f32[40,64,128]{2,1,0:T(8,128)}, f32[40,64,128]{2,1,0:T(8,128)}, u32[]{:S(2)}, u32[]{:S(2)}) collective-permute-start(f32[40,64,128]{2,1,0:T(8,128)} %bitcast_add_fusion.3), channel_id=1, source_target_pairs={{0,1},{1,2},{2,3},{3,4},{4,5},{5,6},{6,7},{7,8},{8,9},{9,10},{10,1... | collective-permute-start | bytes 3932168 | tf_op jit(solution)/shard_map/ppermute | solution.py:13
  164.9 49.8 %collective-permute-start.3 = (f32[40]{0:T(128)S(1)}, f32[40]{0:T(128)S(1)}, u32[]{:S(2)}, u32[]{:S(2)}) collective-permute-start(f32[40]{0:T(128)S(1)} %get-tuple-element.199), channel_id=1, source_target_pairs={{0,3},{1,4},{2,5},{3,6},{4,7},{5,8},{6,9},{7,10},{8,11},{9,12},{10... | collective-permute-start | bytes 488 | tf_op jit(solution)/shard_map/ppermute | solution.py:13
  214.6 24.5 %collective-permute-start.4 = (f32[40]{0:T(128)S(1)}, f32[40]{0:T(128)S(1)}, u32[]{:S(2)}, u32[]{:S(2)}) collective-permute-start(f32[40]{0:T(128)S(1)} %get-tuple-element.199), channel_id=1, source_target_pairs={{0,2},{1,3},{2,4},{3,5},{4,6},{5,7},{6,8},{7,9},{8,10},{9,11},{10,... | collective-permute-start | bytes 488 | tf_op jit(solution)/shard_map/ppermute | solution.py:13
  239.1 6.1 %collective-permute-start.5 = (f32[40]{0:T(128)S(1)}, f32[40]{0:T(128)S(1)}, u32[]{:S(2)}, u32[]{:S(2)}) collective-permute-start(f32[40]{0:T(128)S(1)} %get-tuple-element.199), channel_id=1, source_target_pairs={{0,1},{1,2},{2,3},{3,4},{4,5},{5,6},{6,7},{7,8},{8,9},{9,10},{10,1... | collective-permute-start | bytes 488 | tf_op jit(solution)/shard_map/ppermute | solution.py:13
  241.2 11.8 %copy-start.1 = (bf16[512,2560]{1,0:T(8,128)(2,1)S(1)}, bf16[512,2560]{1,0:T(8,128)(2,1)}, u32[]{:S(2)}) copy-start(bf16[512,2560]{1,0:T(8,128)(2,1)} %copy-done) | copy-start | bytes 7864324
  245.2 17.4 %collective-permute-start.2 = (f32[40]{0:T(128)S(1)}, f32[40]{0:T(128)S(1)}, u32[]{:S(2)}, u32[]{:S(2)}) collective-permute-start(f32[40]{0:T(128)S(1)} %get-tuple-element.199), channel_id=1, source_target_pairs={{0,4},{1,5},{2,6},{3,7},{4,8},{5,9},{6,10},{7,11},{8,12},{9,13},{1... | collective-permute-start | bytes 488 | tf_op jit(solution)/shard_map/ppermute | solution.py:13
  251.1 16.8 %collective-permute-start.10 = (f32[40,64,128]{2,1,0:T(8,128)}, f32[40,64,128]{2,1,0:T(8,128)}, u32[]{:S(2)}, u32[]{:S(2)}) collective-permute-start(f32[40,64,128]{2,1,0:T(8,128)} %multiply_add_fusion), channel_id=1, source_target_pairs={{0,4},{1,5},{2,6},{3,7},{4,8},{5,9},{6,10},{7,11},{8,12},{9,13},{1... | collective-permute-start | bytes 3932168 | tf_op jit(solution)/shard_map/ppermute | solution.py:13
  271.6 2.9 copy-start.5
  277.6 37.6 %all-to-all-start.5 = ((f32[2,40,64,128]{3,2,0,1:T(8,128)}), f32[2,40,64,128]{3,2,0,1:T(8,128)}, u32[]{:S(2)}, u32[]{:S(2)}) async-start(f32[2,40,64,128]{3,2,0,1:T(8,128)} %pad_maximum_fusion.1), calls=%async_computation.5 | async-start | bytes 5242880 | tf_op jit(solution)/shard_map/all_to_all | solution.py:172
  282.2 3.5 copy-start.6
  282.2 3.5 copy-start.7
  282.2 3.5 copy-start.13
  296.6 3.2 copy-start.11
  315.2 44.1 %all-to-all-start.4 = ((bf16[32,16,2560]{2,1,0:T(8,128)(2,1)}), bf16[32,16,2560]{2,1,0:T(8,128)(2,1)S(1)}, u32[]{:S(2)}, u32[]{:S(2)}) async-start(bf16[32,16,2560]{2,1,0:T(8,128)(2,1)} %bitcast.228), calls=%async_computation.4 | async-start | bytes 5242880 | tf_op jit(solution)/shard_map/all_to_all | solution.py:176

commit v2 on v1

--- a/solution.py
+++ b/solution.py
@@ -16,17 +16,32 @@
 LMAX_CH = 16
 
 
-def carried_in(part, axis, combine, window):
-    first = min(4, window)
-    pieces = [from_behind(part, axis, k) for k in range(1, first + 1)]
-    state = pieces[-1]
-    for piece in reversed(pieces[:-1]):
-        state = combine(state, piece)
-    cover = first
-    while cover < window:
-        state = combine(from_behind(state, axis, cover), state)
-        cover *= 2
-    return state
+def chain_flat(earlier, later):
+    return (earlier[0] * later[0], later[0][:, None] * earlier[1] + later[1])
+
+
+def carried_in(gain, state, window):
+    groups = lax.axis_size("seq")
+    heads = gain.shape[0]
+    share = heads // groups
+    cells = state.shape[1] * state.shape[2]
+    packed = jnp.concatenate(
+        [state.reshape(heads, cells), jnp.broadcast_to(gain[:, None], (heads, 128))], axis=1
+    )
+    mine = lax.all_to_all(packed, "seq", split_axis=0, concat_axis=0, tiled=True)
+    mine = mine.reshape(groups, share, cells + 128)
+    parts = [(mine[k, :, cells], mine[k, :, :cells]) for k in range(groups)]
+    prefixes = [(jnp.ones((share,), jnp.float32), jnp.zeros((share, cells), jnp.float32))]
+    for k in range(groups):
+        prefixes.append(chain_flat(prefixes[-1], parts[k]))
+    whole = prefixes[-1]
+    reach = -(-window // groups)
+    behind = from_behind(whole, "req", reach)
+    for step in range(reach - 1, 0, -1):
+        behind = chain_flat(behind, from_behind(whole, "req", step))
+    incoming = jnp.stack([chain_flat(behind, prefixes[k])[1] for k in range(groups)], axis=0)
+    incoming = lax.all_to_all(incoming, "seq", split_axis=0, concat_axis=0, tiled=True)
+    return incoming.reshape(state.shape)
 
 
 def stretch_flags(prompt_stretches, stretch_ids):
@@ -144,8 +159,7 @@
             (total_gain, total_state), (carried[stretch], stretch_state[stretch])
         )
     window = -(-(LMAX_CH - 1) // stretch_count)
-    incoming = carried_in((total_gain, total_state), ("req", "seq"), chain_states, window)
-    state_prev = incoming[1]
+    state_prev = carried_in(total_gain, total_state, window)
     normed_parts = []
     ending_parts = []
     for stretch in range(stretch_count):

time: 364 us -> 368 us (1.011)
  starting transfers between devices: 81.7 us -> 41.7 us
  blocking collectives: 29.4 us -> 57.3 us
  local copies, waits for them, and re-layouts: 55.5 us -> 66.8 us
  waiting for transfers between devices: 119 us -> 124 us
    ppermute x11 -> x5, waiting for transfers between devices: 58.6 us -> 5.59 us  [from_behind(): lax.ppermute(value, axis, [(source, source + steps) for source in range(l...]
    ppermute x11 -> x5, starting transfers between devices: 56.1 us -> 17.3 us  [from_behind(): lax.ppermute(value, axis, [(source, source + steps) for source in range(l...]
    all_to_all x0 -> x1, blocking collectives: none -> 27.9 us  [carried_in(): lax.all_to_all(packed, 'seq', split_axis=0, concat_axis=0, tiled=True)]
    all_to_all x1, waiting for transfers between devices: 0.01 us -> 24.9 us  [per_device(): lax.all_to_all(z_in, 'req', split_axis=0, concat_axis=0, tiled=True)]
    all_to_all x0 -> x1, waiting for transfers between devices: none -> 17 us  [carried_in(): lax.all_to_all(incoming, 'seq', split_axis=0, concat_axis=0, tiled=True)]
    all_to_all x1, waiting for transfers between devices: 0.01 us -> 16.7 us  [per_device(): lax.all_to_all(jnp.stack(ending_parts, axis=0), 'seq', split_axis=1, conc...]
    another operation x3 -> x1, other arithmetic: 6.83 us -> 0.25 us  [per_device(): jnp.stack(ending_parts, axis=0)]
    all_to_all x1, starting transfers between devices: 10.1 us -> 4.11 us  [per_device(): lax.all_to_all(projected, 'req', split_axis=0, concat_axis=0, tiled=True)]
  transfers between devices with their start and end apart: 15 -> 10, of which waited for: 7 -> 7; matrix products, arithmetic and copies ran while one was open for 31% -> 15% of each run, Pallas kernels for 0% -> 0%
where the time goes in v2:
time: 368 us; the launch traced here: 365 us
  waiting for transfers between devices  124 us (34%)
  local copies, waits for them, and re-layouts  66.8 us (18%)
  blocking collectives  57.3 us (16%)
  other arithmetic  48.4 us (13%)
  starting transfers between devices  41.7 us (11%)
  matrix products  25.2 us (7%)
    all_to_all x1, waiting for transfers between devices, per_device(): lax.all_to_all(projected, 'req', split_axis=0, concat_axis=0, tiled=True)  30.4 us
    all_to_all x1, waiting for transfers between devices, per_device(): lax.all_to_all(x_in, 'req', split_axis=0, concat_axis=0, tiled=True)  29.7 us
    all_to_all x1, blocking collectives, carried_in(): lax.all_to_all(packed, 'seq', split_axis=0, concat_axis=0, tiled=True)  27.9 us
    all_to_all x1, waiting for transfers between devices, per_device(): lax.all_to_all(z_in, 'req', split_axis=0, concat_axis=0, tiled=True)  24.9 us
    convert_element_type x4, local copies, waits for them, and re-layouts, finish_stretch(): gated_rows = mixed_rows * jax.nn.silu(z_stretch.astype(jnp.float32))  20.1 us
    ppermute x5, starting transfers between devices, from_behind(): lax.ppermute(value, axis, [(source, source + steps) for source in range(l...  17.3 us
    all_to_all x1, waiting for transfers between devices, carried_in(): lax.all_to_all(incoming, 'seq', split_axis=0, concat_axis=0, tiled=True)  17 us
    all_to_all x1, waiting for transfers between devices, per_device(): lax.all_to_all(jnp.stack(ending_parts, axis=0), 'seq', split_axis=1, conc...  16.7 us
  transfers between devices with their start and end apart: 10, of which 7 were waited for; matrix products, arithmetic and copies ran while one was open for 15% of the time, Pallas kernels for 0%

profile of v2, /device:TPU:1, one launch (start us, length us, event | category | flops | bytes accessed | tf_op | source)
XLA Modules:
  0.0 364.9 jit_solution(10509877049277878437)
XLA Ops:
  1.7 16.5 %all_to_all.83 = bf16[32,2,320]{2,1,0:T(2,128)(2,1)S(1)} all-to-all(bf16[32,2,320]{2,1,0:T(2,128)(2,1)S(1)} %reshape.368), channel_id=1, replica_groups=mesh['req'=32,'seq'=4] {'req'}, dimensions={0} | all-to-all | bytes 81920 | tf_op jit(solution)/shard_map/all_to_all | solution.py:124
  18.2 12.9 %all_to_all.84 = bf16[32,16,256]{2,1,0:T(8,128)(2,1)S(1)} all-to-all(bf16[32,16,256]{2,1,0:T(8,128)(2,1)} %bitcast.247), channel_id=1, replica_groups=mesh['req'=32,'seq'=4] {'req'}, dimensions={0} | all-to-all | bytes 524288 | tf_op jit(solution)/shard_map/all_to_all | solution.py:122
  31.1 4.0 %all-to-all-start = ((bf16[32,16,2560]{2,1,0:T(8,128)(2,1)}), bf16[32,16,2560]{2,1,0:T(8,128)(2,1)S(1)}, u32[]{:S(2)}, u32[]{:S(2)}) async-start(bf16[32,16,2560]{2,1,0:T(8,128)(2,1)} %bitcast.239), calls=%async_computation | async-start | bytes 5242880 | tf_op jit(solution)/shard_map/all_to_all | solution.py:121
  35.9 3.2 collective-permute-start.1
  39.5 29.7 %all-to-all-done = bf16[32,16,2560]{2,1,0:T(8,128)(2,1)S(1)} async-done(((bf16[32,16,2560]{2,1,0:T(8,128)(2,1)}), bf16[32,16,2560]{2,1,0:T(8,128)(2,1)S(1)}, u32[]{:S(2)}, u32[]{:S(2)}) %all-to-all-start) | async-done | bytes 2621472 | tf_op jit(solution)/shard_map/all_to_all | solution.py:121
  69.2 3.2 collective-permute-start
  73.2 4.7 %collective-permute-done = bf16[3,2560]{1,0:T(4,128)(2,1)S(1)} collective-permute-done((bf16[3,2560]{1,0:T(4,128)(2,1)S(1)}, bf16[3,2560]{1,0:T(4,128)(2,1)S(1)}, u32[]{:S(2)}, u32[]{:S(2)}) %collective-permute-start) | collective-permute-done | bytes 15392 | tf_op jit(solution)/shard_map/ppermute | solution.py:13
  77.9 10.0 %multiply_convert_fusion.6 = bf16[512,2560]{1,0:T(8,128)(2,1)S(1)} fusion(bf16[512,2560]{1,0:T(8,128)(2,1)} %bitcast.231, bf16[3,2560]{1,0:T(4,128)(2,1)S(1)} %collective-permute-done, f32[2560]{0:T(1024)S(1)} %get-tuple-element.156, f32[2560]{0:T(1024)S(1)} %get-tuple-element.157, f32[2560]{0:T(1024)S(1)} %get-tuple-element.158, ...), kind=kLoop, calls=%fused_computation.45 | loop fusion | flops 39321600 | bytes 5311488 | tf_op jit(solution)/shard_map/convert_element_type | solution.py:67
  89.3 4.4 %reshape.341 = bf16[2,256,40,64]{3,2,1,0:T(8,128)(2,1)} reshape(bf16[512,2560]{1,0:T(8,128)(2,1)S(1)} %multiply_convert_fusion.6) | data formatting | bytes 5242880 | tf_op jit(solution)/shard_map/reshape | solution.py:146
  93.8 5.2 %copy.84 = bf16[2,256,40,64]{1,3,2,0:T(8,128)(2,1)S(1)} copy(bf16[2,256,40,64]{3,2,1,0:T(8,128)(2,1)} %reshape.341) | data formatting | bytes 5242880 | tf_op jit(solution)/shard_map/while | solution.py:153
  99.0 16.5 %while.16 = (s32[]{:T(128)}, f32[2,256,40,64]{1,3,2,0:T(8,128)}, f32[2,40,64,128]{3,2,1,0:T(8,128)}, f32[2,256,40]{1,2,0:T(8,128)S(1)}, bf16[2,256,40,64]{1,3,2,...) while((s32[]{:T(128)}, f32[2,256,40,64]{1,3,2,0:T(8,128)}, ...), condition=%wide.region_5.6_spmd, body=%wide.region_2.0_spmd.sunk | while | flops 539379840 | bytes 29302244 | solution.py:153
  100.5 4.7 %bitcast_dynamic-update-slice_fusion.4 = f32[2,256,40,64]{1,3,2,0:T(8,128)} fusion(f32[2,256,40,64]{1,3,2,0:T(8,128)} %get-tuple-element.308, s32[]{:T(128)S(6)} %copy.123, f32[40,256]{1,0:T(8,128)S(1)} %get-tuple-element.293, f32[40,256]{1,0:T(8,128)S(1)} %get-tuple-element.294, f32[256,256]{1,0:T(8,128)S(1)} %fusion.103, ...), kind=kOutput, calls=%fused_computation.8.clone.1 | convolution fusion | flops 351272960 | bytes 4383744 | tf_op jit(solution)/shard_map/while/body/eval_jaxpr/htu,uhp->thp/dot_general | solution.py:83
  108.8 4.7 %bitcast_dynamic-update-slice_fusion.4 = f32[2,256,40,64]{1,3,2,0:T(8,128)} fusion(f32[2,256,40,64]{1,3,2,0:T(8,128)} %get-tuple-element.308, s32[]{:T(128)S(6)} %copy.123, f32[40,256]{1,0:T(8,128)S(1)} %get-tuple-element.293, f32[40,256]{1,0:T(8,128)S(1)} %get-tuple-element.294, f32[256,256]{1,0:T(8,128)S(1)} %fusion.103, ...), kind=kOutput, calls=%fused_computation.8.clone.1 | convolution fusion | flops 351272960 | bytes 4383744 | tf_op jit(solution)/shard_map/while/body/eval_jaxpr/htu,uhp->thp/dot_general | solution.py:83
  116.2 3.0 fusion.84
  120.7 1.6 squeeze.84
  122.2 1.9 multiply_add_fusion
  124.4 27.9 %all_to_all.85 = f32[4,10,8320]{2,1,0:T(8,128)S(1)} all-to-all(f32[4,10,8320]{2,1,0:T(8,128)S(1)} %pad_maximum_fusion.2), channel_id=1, replica_groups=mesh['req'=32,'seq'=4] {'seq'}, dimensions={0} | all-to-all | bytes 2662400 | tf_op jit(solution)/shard_map/all_to_all | solution.py:31
  152.3 6.6 %all-to-all-start.5 = ((bf16[32,16,2560]{2,1,0:T(8,128)(2,1)}), bf16[32,16,2560]{2,1,0:T(8,128)(2,1)}, u32[]{:S(2)}, u32[]{:S(2)}) async-start(bf16[32,16,2560]{2,1,0:T(8,128)(2,1)} %bitcast.240), calls=%async_computation.5 | async-start | bytes 5242880 | tf_op jit(solution)/shard_map/all_to_all | solution.py:123
  160.7 3.5 collective-permute-start.4
  164.2 3.9 %collective-permute-start.3 = (f32[10,8192]{1,0:T(8,128)}, f32[10,8192]{1,0:T(8,128)}, u32[]{:S(2)}, u32[]{:S(2)}) collective-permute-start(f32[10,8192]{1,0:T(8,128)} %get-tuple-element.194), channel_id=1, source_target_pairs={{0,8},{4,12},{8,16},{12,20},{16,24},{20,28},{24,32},{28,36},{32,40... | collective-permute-start | bytes 983048 | tf_op jit(solution)/shard_map/ppermute | solution.py:13
  168.1 24.9 %all-to-all-done.5 = bf16[32,16,2560]{2,1,0:T(8,128)(2,1)} async-done(((bf16[32,16,2560]{2,1,0:T(8,128)(2,1)}), bf16[32,16,2560]{2,1,0:T(8,128)(2,1)}, u32[]{:S(2)}, u32[]{:S(2)}) %all-to-all-start.5) | async-done | bytes 2621472 | tf_op jit(solution)/shard_map/all_to_all | solution.py:123
  193.0 3.9 %slice_convert_fusion.2 = (f32[16,16,2560]{2,1,0:T(8,128)S(1)}, f32[16,16,2560]{2,1,0:T(8,128)}) fusion(bf16[32,16,2560]{2,1,0:T(8,128)(2,1)} %all-to-all-done.5), kind=kLoop, calls=%fused_computation.85 | loop fusion | flops 1310720 | bytes 7864320 | tf_op jit(solution)/shard_map/convert_element_type | solution.py:97
  196.9 3.1 reshape.334
  200.0 6.0 %copy.89 = f32[256,40,64]{0,2,1:T(8,128)} copy(f32[256,40,64]{2,1,0:T(8,128)} %reshape.334) | data formatting | bytes 5242880 | tf_op jit(solution)/shard_map/convert_element_type | solution.py:97
  206.0 4.9 %reshape.337 = f32[256,40,64]{2,1,0:T(8,128)} reshape(f32[16,16,2560]{2,1,0:T(8,128)} %get-tuple-element.205) | data formatting | bytes 5242880 | tf_op jit(solution)/shard_map/convert_element_type | solution.py:97
  211.0 6.0 %copy.93 = f32[256,40,64]{0,2,1:T(8,128)} copy(f32[256,40,64]{2,1,0:T(8,128)} %reshape.337) | data formatting | bytes 5242880 | tf_op jit(solution)/shard_map/convert_element_type | solution.py:97
  217.0 3.5 collective-permute-start.2
  225.6 4.7 %all-to-all-start.4 = ((f32[4,10,8192]{2,1,0:T(8,128)}), f32[4,10,8192]{2,1,0:T(8,128)}, u32[]{:S(2)}, u32[]{:S(2)}) async-start(f32[4,10,8192]{2,1,0:T(8,128)} %pad_maximum_fusion.3), calls=%async_computation.4 | async-start | bytes 4194304 | tf_op jit(solution)/shard_map/all_to_all | solution.py:43
  230.4 3.0 slice_convert_fusion.3
  233.4 3.3 copy.86
  236.8 2.1 copy.90
  239.7 17.0 %all-to-all-done.4 = f32[4,10,8192]{2,1,0:T(8,128)} async-done(((f32[4,10,8192]{2,1,0:T(8,128)}), f32[4,10,8192]{2,1,0:T(8,128)}, u32[]{:S(2)}, u32[]{:S(2)}) %all-to-all-start.4) | async-done | bytes 1310752 | tf_op jit(solution)/shard_map/all_to_all | solution.py:43
  256.7 3.6 fusion.80
  260.3 1.6 convert_element_type.121
  261.9 2.1 fusion.61
  265.3 3.0 broadcast_select_fusion.1
  270.2 6.8 %multiply_reduce_fusion.1 = (f32[256]{0:T(256)S(1)}, f32[256,40,64]{0,2,1:T(8,128)}, f32[256]{0:T(256)S(1)}, f32[256,40,64]{0,2,1:T(8,128)}) fusion(f32[256,40,64]{0,2,1:T(8,128)} %copy.89, f32[256,40,64]{0,2,1:T(8,128)S(1)} %bitcast.233, f32[40]{0:T(128)S(1)} %copy-done.21, f32[256,40,64]{0,2,1:T(8,128)S(1)} %copy-done.11, f32[256,40]{0,1:T(8,128)S(1)} %copy-done.14, ...), kind=kLoop, calls=%fused_computation.77 | loop fusion | flops 14417408 | bytes 26298528 | tf_op jit(solution)/shard_map/reduce_sum | solution.py:98
  277.0 3.2 copy.87
  280.2 3.2 copy.91
  283.4 2.8 add_select_fusion
  286.5 1.7 copy.94
  288.2 5.0 %all-to-all-start.7 = ((f32[2,40,64,128]{3,2,0,1:T(8,128)}), f32[2,40,64,128]{3,2,0,1:T(8,128)}, u32[]{:S(2)}, u32[]{:S(2)}) async-start(f32[2,40,64,128]{3,2,0,1:T(8,128)} %copy.94), calls=%async_computation.7 | async-start | bytes 5242880 | tf_op jit(solution)/shard_map/all_to_all | solution.py:186
  293.2 4.3 %fusion.48 = (bf16[256,2560]{1,0:T(8,128)(2,1)S(1)}, bf16[256,2560]{1,0:T(8,128)(2,1)S(1)}) fusion(f32[256,2560]{1,0:T(8,128)} %copy.87, f32[16,16,2560]{2,1,0:T(8,128)S(1)} %copy-done.3, f32[2560]{0:T(1024)S(1)} %copy-done.19, f32[256]{0:T(256)S(1)} %add_rsqrt_fusion.1, f32[256]{0:T(256)S(1)} %add_rsqrt_fusion, f32[256,2560]{1,0:T(8,128)} %copy.91, ...), kind=kLoop, calls=%fused_computation.78 | loop fusion | flops 10485760 | bytes 13119488 | tf_op jit(solution)/shard_map/convert_element_type | solution.py:99
  297.6 11.0 %convolution_convert_fusion = bf16[512,2560]{1,0:T(8,128)(2,1)} fusion(bf16[2560,2560]{1,0:T(8,128)(2,1)} %param.24, bf16[256,2560]{1,0:T(8,128)(2,1)S(1)} %get-tuple-element.217, bf16[256,2560]{1,0:T(8,128)(2,1)S(1)} %get-tuple-element.216), kind=kOutput, calls=%fused_computation.46 | convolution fusion | flops 6717440000 | bytes 18350080 | tf_op jit(solution)/shard_map/dot_general | solution.py:189
  308.6 16.7 %all-to-all-done.7 = f32[2,40,64,128]{3,2,0,1:T(8,128)} async-done(((f32[2,40,64,128]{3,2,0,1:T(8,128)}), f32[2,40,64,128]{3,2,0,1:T(8,128)}, u32[]{:S(2)}, u32[]{:S(2)}) %all-to-all-start.7) | async-done | bytes 2621472 | tf_op jit(solution)/shard_map/all_to_all | solution.py:186
  325.3 4.1 %all-to-all-start.6 = ((bf16[32,16,2560]{2,1,0:T(8,128)(2,1)}), bf16[32,16,2560]{2,1,0:T(8,128)(2,1)S(1)}, u32[]{:S(2)}, u32[]{:S(2)}) async-start(bf16[32,16,2560]{2,1,0:T(8,128)(2,1)} %bitcast.242), calls=%async_computation.6 | async-start | bytes 5242880 | tf_op jit(solution)/shard_map/all_to_all | solution.py:190
  329.5 3.6 copy.95
  333.0 30.4 %all-to-all-done.6 = bf16[32,16,2560]{2,1,0:T(8,128)(2,1)S(1)} async-done(((bf16[32,16,2560]{2,1,0:T(8,128)(2,1)}), bf16[32,16,2560]{2,1,0:T(8,128)(2,1)S(1)}, u32[]{:S(2)}, u32[]{:S(2)}) %all-to-all-start.6) | async-done | bytes 2621472 | tf_op jit(solution)/shard_map/all_to_all | solution.py:190
  (127 shorter events, 26.4 us)
Async XLA Ops:
  31.1 4.0 %copy-start.20 = (s32[64]{0:T(128)S(1)}, s32[64]{0:T(128)}, u32[]{:S(2)}) copy-start(s32[64]{0:T(128)} %param.25) | copy-start | bytes 772
  31.1 4.7 %copy-start.22 = (f32[40]{0:T(128)S(1)}, f32[40]{0:T(128)}, u32[]{:S(2)}) copy-start(f32[40]{0:T(128)} %param.21) | copy-start | bytes 484
  31.1 4.7 %copy-start.17 = (f32[4,2816]{1,0:T(4,128)S(1)}, f32[4,2816]{1,0:T(4,128)}, u32[]{:S(2)}) copy-start(f32[4,2816]{1,0:T(4,128)} %param.18) | copy-start | bytes 135172
  31.1 8.1 %copy-start.18 = (f32[2816]{0:T(1024)S(1)}, f32[2816]{0:T(1024)}, u32[]{:S(2)}) copy-start(f32[2816]{0:T(1024)} %param.19) | copy-start | bytes 33796
  31.1 38.0 %all-to-all-start = ((bf16[32,16,2560]{2,1,0:T(8,128)(2,1)}), bf16[32,16,2560]{2,1,0:T(8,128)(2,1)S(1)}, u32[]{:S(2)}, u32[]{:S(2)}) async-start(bf16[32,16,2560]{2,1,0:T(8,128)(2,1)} %bitcast.239), calls=%async_computation | async-start | bytes 5242880 | tf_op jit(solution)/shard_map/all_to_all | solution.py:121
  35.9 36.5 %collective-permute-start.1 = (bf16[3,256]{1,0:T(4,128)(2,1)S(1)}, bf16[3,256]{1,0:T(4,128)(2,1)S(1)}, u32[]{:S(2)}, u32[]{:S(2)}) collective-permute-start(bf16[3,256]{1,0:T(4,128)(2,1)S(1)} %slice.238), channel_id=1, source_target_pairs={{0,1},{1,2},{2,3},{3,4},{4,5},{5,6},{6,7},{7,8},{8,9},{9,10},{10,1... | collective-permute-start | bytes 4616 | tf_op jit(solution)/shard_map/ppermute | solution.py:13
  69.1 8.8 %copy-start.5 = (bf16[32,16,2560]{2,1,0:T(8,128)(2,1)}, bf16[32,16,2560]{2,1,0:T(8,128)(2,1)S(1)}, u32[]{:S(2)}) copy-start(bf16[32,16,2560]{2,1,0:T(8,128)(2,1)S(1)} %all-to-all-done) | copy-start | bytes 7864324
  69.2 8.7 %collective-permute-start = (bf16[3,2560]{1,0:T(4,128)(2,1)S(1)}, bf16[3,2560]{1,0:T(4,128)(2,1)S(1)}, u32[]{:S(2)}, u32[]{:S(2)}) collective-permute-start(bf16[3,2560]{1,0:T(4,128)(2,1)S(1)} %slice.233), channel_id=1, source_target_pairs={{0,1},{1,2},{2,3},{3,4},{4,5},{5,6},{6,7},{7,8},{8,9},{9,10},{10,1... | collective-permute-start | bytes 46088 | tf_op jit(solution)/shard_map/ppermute | solution.py:13
  87.9 1.5 copy-start
  93.8 5.2 %copy-start.16 = (f32[40]{0:T(128)S(1)}, f32[40]{0:T(128)}, u32[]{:S(2)}) copy-start(f32[40]{0:T(128)} %param.20) | copy-start | bytes 484
  100.5 4.7 %copy-start.6 = (f32[2,40,64,128]{3,2,1,0:T(8,128)S(1)}, f32[2,40,64,128]{3,2,1,0:T(8,128)}, u32[]{:S(2)}) copy-start(f32[2,40,64,128]{3,2,1,0:T(8,128)} %get-tuple-element.309) | copy-start | bytes 7864324 | tf_op jit(solution)/shard_map/while
  105.8 1.5 copy-start.7
  108.8 4.7 %copy-start.6 = (f32[2,40,64,128]{3,2,1,0:T(8,128)S(1)}, f32[2,40,64,128]{3,2,1,0:T(8,128)}, u32[]{:S(2)}) copy-start(f32[2,40,64,128]{3,2,1,0:T(8,128)} %get-tuple-element.309) | copy-start | bytes 7864324 | tf_op jit(solution)/shard_map/while
  114.0 1.5 copy-start.7
  115.5 0.7 copy-start.12
  152.3 7.4 %copy-start.4 = (f32[4,10,8320]{2,1,0:T(8,128)}, f32[4,10,8320]{2,1,0:T(8,128)S(1)}, u32[]{:S(2)}) copy-start(f32[4,10,8320]{2,1,0:T(8,128)S(1)} %all_to_all.85) | copy-start | bytes 3993604
  152.3 40.7 %all-to-all-start.5 = ((bf16[32,16,2560]{2,1,0:T(8,128)(2,1)}), bf16[32,16,2560]{2,1,0:T(8,128)(2,1)}, u32[]{:S(2)}, u32[]{:S(2)}) async-start(bf16[32,16,2560]{2,1,0:T(8,128)(2,1)} %bitcast.240), calls=%async_computation.5 | async-start | bytes 5242880 | tf_op jit(solution)/shard_map/all_to_all | solution.py:123
  160.7 60.7 %collective-permute-start.4 = (f32[10,8192]{1,0:T(8,128)}, f32[10,8192]{1,0:T(8,128)}, u32[]{:S(2)}, u32[]{:S(2)}) collective-permute-start(f32[10,8192]{1,0:T(8,128)} %get-tuple-element.194), channel_id=1, source_target_pairs={{0,4},{4,8},{8,12},{12,16},{16,20},{20,24},{24,28},{28,32},{32,36}... | collective-permute-start | bytes 983048 | tf_op jit(solution)/shard_map/ppermute | solution.py:13
  164.2 57.1 %collective-permute-start.3 = (f32[10,8192]{1,0:T(8,128)}, f32[10,8192]{1,0:T(8,128)}, u32[]{:S(2)}, u32[]{:S(2)}) collective-permute-start(f32[10,8192]{1,0:T(8,128)} %get-tuple-element.194), channel_id=1, source_target_pairs={{0,8},{4,12},{8,16},{12,20},{16,24},{20,28},{24,32},{28,36},{32,40... | collective-permute-start | bytes 983048 | tf_op jit(solution)/shard_map/ppermute | solution.py:13
  196.9 3.1 copy-start.2
  217.0 4.4 %collective-permute-start.2 = (f32[10]{0:T(128)S(1)}, f32[10]{0:T(128)S(1)}, u32[]{:S(2)}, u32[]{:S(2)}) collective-permute-start(f32[10]{0:T(128)S(1)} %get-tuple-element.191), channel_id=1, source_target_pairs={{0,4},{4,8},{8,12},{12,16},{16,20},{20,24},{24,28},{28,32},{32,36}... | collective-permute-start | bytes 128 | tf_op jit(solution)/shard_map/ppermute | solution.py:13
  225.6 4.7 %copy-start.1 = (bf16[512,2560]{1,0:T(8,128)(2,1)S(1)}, bf16[512,2560]{1,0:T(8,128)(2,1)}, u32[]{:S(2)}) copy-start(bf16[512,2560]{1,0:T(8,128)(2,1)} %copy-done) | copy-start | bytes 7864324
  225.6 31.0 %all-to-all-start.4 = ((f32[4,10,8192]{2,1,0:T(8,128)}), f32[4,10,8192]{2,1,0:T(8,128)}, u32[]{:S(2)}, u32[]{:S(2)}) async-start(f32[4,10,8192]{2,1,0:T(8,128)} %pad_maximum_fusion.3), calls=%async_computation.4 | async-start | bytes 4194304 | tf_op jit(solution)/shard_map/all_to_all | solution.py:43
  233.4 3.3 copy-start.8
  256.7 5.3 %copy-start.13 = (bf16[2,256,256]{2,1,0:T(8,128)(2,1)S(1)}, bf16[2,256,256]{2,1,0:T(8,128)(2,1)}, u32[]{:S(2)}) copy-start(bf16[2,256,256]{2,1,0:T(8,128)(2,1)} %copy-done.12) | copy-start | bytes 786436
  265.3 4.4 %copy-start.10 = (f32[256,2560]{0,1:T(8,128)S(1)}, f32[256,2560]{0,1:T(8,128)}, u32[]{:S(2)}) copy-start(f32[256,2560]{0,1:T(8,128)} %copy.90) | copy-start | bytes 7864324
  265.3 4.4 %copy-start.11 = (f32[256,40,64]{0,2,1:T(8,128)S(1)}, f32[256,40,64]{0,2,1:T(8,128)}, u32[]{:S(2)}) copy-start(f32[256,40,64]{0,2,1:T(8,128)} %fusion.61) | copy-start | bytes 7864324
  268.4 1.8 copy-start.9
  268.4 1.8 copy-start.14
  268.4 1.8 copy-start.15
  268.4 1.8 copy-start.21
  288.2 5.0 %copy-start.3 = (f32[16,16,2560]{2,1,0:T(8,128)S(1)}, f32[16,16,2560]{2,1,0:T(8,128)}, u32[]{:S(2)}) copy-start(f32[16,16,2560]{2,1,0:T(8,128)} %copy-done.2) | copy-start | bytes 7864324
  288.2 5.0 %copy-start.19 = (f32[2560]{0:T(1024)S(1)}, f32[2560]{0:T(1024)}, u32[]{:S(2)}) copy-start(f32[2560]{0:T(1024)} %param.23) | copy-start | bytes 30724
  288.2 37.2 %all-to-all-start.7 = ((f32[2,40,64,128]{3,2,0,1:T(8,128)}), f32[2,40,64,128]{3,2,0,1:T(8,128)}, u32[]{:S(2)}, u32[]{:S(2)}) async-start(f32[2,40,64,128]{3,2,0,1:T(8,128)} %copy.94), calls=%async_computation.7 | async-start | bytes 5242880 | tf_op jit(solution)/shard_map/all_to_all | solution.py:186
  325.3 38.1 %all-to-all-start.6 = ((bf16[32,16,2560]{2,1,0:T(8,128)(2,1)}), bf16[32,16,2560]{2,1,0:T(8,128)(2,1)S(1)}, u32[]{:S(2)}, u32[]{:S(2)}) async-start(bf16[32,16,2560]{2,1,0:T(8,128)(2,1)} %bitcast.242), calls=%async_computation.6 | async-start | bytes 5242880 | tf_op jit(solution)/shard_map/all_to_all | solution.py:190

commit v3 on v2

--- a/solution.py
+++ b/solution.py
@@ -87,14 +87,17 @@
     return (y_diag, stretch_state, log_decay)
 
 
-def finish_stretch(y_diag, log_decay, state_in, x_stretch, c_mat, z_stretch, d_skip, norm_gain):
+def finish_stretch(y_diag, log_decay, state_in, x_stretch, c_mat, d_skip):
     state_low = state_in.astype(jnp.bfloat16)
     y_off = jnp.exp(log_decay)[:, :, None] * jnp.einsum(
         "tn,hpn->thp", c_mat, state_low, preferred_element_type=jnp.float32
     )
     mixed_rows = y_diag + y_off + d_skip[None, :, None] * x_stretch.astype(jnp.float32)
-    mixed_rows = mixed_rows.reshape(mixed_rows.shape[0], -1)
-    gated_rows = mixed_rows * jax.nn.silu(z_stretch.astype(jnp.float32))
+    return mixed_rows.reshape(mixed_rows.shape[0], -1).astype(jnp.bfloat16)
+
+
+def gate_and_norm(mixed_rows, z_rows, norm_gain):
+    gated_rows = mixed_rows.astype(jnp.float32) * jax.nn.silu(z_rows.astype(jnp.float32))
     inv_rms = lax.rsqrt(jnp.mean(gated_rows * gated_rows, axis=-1, keepdims=True) + 1e-05)
     return (gated_rows * inv_rms * norm_gain[None, :]).astype(jnp.bfloat16)
 
@@ -117,14 +120,15 @@
     w_out,
     prompt_stretches,
 ):
-    x_rows, bc_rows, z_rows, dt_rows = (
-        lax.all_to_all(x_in, "req", split_axis=0, concat_axis=0, tiled=True),
-        lax.all_to_all(bc_in, "req", split_axis=0, concat_axis=0, tiled=True),
-        lax.all_to_all(z_in, "req", split_axis=0, concat_axis=0, tiled=True),
-        lax.all_to_all(dt_raw, "req", split_axis=0, concat_axis=0, tiled=True),
-    )
+    inner_width = x_in.shape[1]
+    bc_width = bc_in.shape[1]
+    joined = lax.all_to_all(
+        jnp.concatenate([x_in, bc_in, dt_raw], axis=1), "req", split_axis=0, concat_axis=0, tiled=True
+    )
+    x_rows = joined[:, :inner_width]
+    bc_rows = joined[:, inner_width : inner_width + bc_width]
+    dt_rows = joined[:, inner_width + bc_width :]
     row_count = x_rows.shape[0]
-    inner_width = x_rows.shape[1]
     head_count = a_log.shape[0]
     head_dim = inner_width // head_count
     stretch_count = row_count // STRETCH
@@ -164,7 +168,6 @@
     ending_parts = []
     for stretch in range(stretch_count):
         state_in = jnp.where(starts[stretch], jnp.zeros_like(state_prev), state_prev)
-        z_stretch = z_rows[stretch * STRETCH : (stretch + 1) * STRETCH]
         normed_parts.append(
             finish_stretch(
                 y_diag[stretch],
@@ -172,9 +175,7 @@
                 state_in,
                 x_heads[stretch],
                 bc_stretches[stretch, :, N:],
-                z_stretch,
                 d_skip,
-                norm_gain,
             )
         )
         state_out = (
@@ -182,12 +183,13 @@
         )
         ending_parts.append(jnp.where(finals[stretch], state_out, jnp.zeros_like(state_out)))
         state_prev = state_out
-    normed = jnp.concatenate(normed_parts, axis=0)
+    mixed_stream = jnp.concatenate(normed_parts, axis=0)
     endings = lax.all_to_all(
         jnp.stack(ending_parts, axis=0), "seq", split_axis=1, concat_axis=0, tiled=True
     )
-    projected = jnp.dot(normed, w_out, preferred_element_type=jnp.float32).astype(jnp.bfloat16)
-    mixed_out = lax.all_to_all(projected, "req", split_axis=0, concat_axis=0, tiled=True)
+    mixed_tokens = lax.all_to_all(mixed_stream, "req", split_axis=0, concat_axis=0, tiled=True)
+    normed = gate_and_norm(mixed_tokens, z_in, norm_gain)
+    mixed_out = jnp.dot(normed, w_out, preferred_element_type=jnp.float32).astype(jnp.bfloat16)
     return (mixed_out, endings)
 
 

time: 368 us -> 301 us (0.82)
  blocking collectives: 57.3 us -> 26.4 us
  local copies, waits for them, and re-layouts: 66.8 us -> 47.8 us
  waiting for transfers between devices: 124 us -> 112 us
  other arithmetic: 48.4 us -> 44.1 us
    all_to_all x2 -> x0, blocking collectives: 29.4 us -> none  [the longest x1 16.5 us: per_device(): lax.all_to_all(dt_raw, 'req', split_axis=0, concat_axis=0, tiled=True)]
    all_to_all x3 -> x2, waiting for transfers between devices: 85 us -> 66.4 us  [the longest x1 36 us: per_device(): lax.all_to_all(jnp.concatenate([x_in, bc_in, dt_raw], axis=1), 'req', spl...]
    convert_element_type x4 -> x2, local copies, waits for them, and re-layouts: 20.1 us -> 3.15 us  [finish_stretch(): return mixed_rows.reshape(mixed_rows.shape[0], -1).astype(jnp.bfloat16)]
    all_to_all x1, waiting for transfers between devices: 16.7 us -> 8.16 us  [per_device(): lax.all_to_all(jnp.stack(ending_parts, axis=0), 'seq', split_axis=1, conc...]
    all_to_all x1, waiting for transfers between devices: 17 us -> 24.9 us  [carried_in(): lax.all_to_all(incoming, 'seq', split_axis=0, concat_axis=0, tiled=True)]
    ppermute x5, waiting for transfers between devices: 5.59 us -> 12.3 us  [from_behind(): lax.ppermute(value, axis, [(source, source + steps) for source in range(l...]
    concatenate x0 -> x2, other arithmetic: none -> 6.64 us  [the longest x1 3.66 us: per_device(): jnp.concatenate([x_in, bc_in, dt_raw], axis=1)]
    reshape x2 -> x0, local copies, waits for them, and re-layouts: 6.41 us -> none  [finish_stretch(): mixed_rows = mixed_rows.reshape(mixed_rows.shape[0], -1)]
  transfers between devices with their start and end apart: 10 -> 9, of which waited for: 7 -> 6; matrix products, arithmetic and copies ran while one was open for 15% -> 12% of each run, Pallas kernels for 0% -> 0%
where the time goes in v3:
time: 301 us; the launch traced here: 298 us
  waiting for transfers between devices  112 us (37%)
  local copies, waits for them, and re-layouts  47.8 us (16%)
  other arithmetic  44.1 us (15%)
  starting transfers between devices  43.2 us (14%)
  blocking collectives  26.4 us (9%)
  matrix products  24 us (8%)
    all_to_all x1, waiting for transfers between devices, per_device(): lax.all_to_all(jnp.concatenate([x_in, bc_in, dt_raw], axis=1), 'req', spl...  36 us
    all_to_all x1, waiting for transfers between devices, per_device(): lax.all_to_all(mixed_stream, 'req', split_axis=0, concat_axis=0, tiled=True)  30.4 us
    all_to_all x1, blocking collectives, carried_in(): lax.all_to_all(packed, 'seq', split_axis=0, concat_axis=0, tiled=True)  26.4 us
    all_to_all x1, waiting for transfers between devices, carried_in(): lax.all_to_all(incoming, 'seq', split_axis=0, concat_axis=0, tiled=True)  24.9 us
    ppermute x5, starting transfers between devices, from_behind(): lax.ppermute(value, axis, [(source, source + steps) for source in range(l...  15.6 us
    ppermute x5, waiting for transfers between devices, from_behind(): lax.ppermute(value, axis, [(source, source + steps) for source in range(l...  12.3 us
    convert_element_type x2, other arithmetic, causal_conv(): return jax.nn.silu(running).astype(jnp.bfloat16)  11.6 us
    dot_general x1, matrix products, per_device(): jnp.dot(normed, w_out, preferred_element_type=jnp.float32)  11.3 us
  transfers between devices with their start and end apart: 9, of which 6 were waited for; matrix products, arithmetic and copies ran while one was open for 12% of the time, Pallas kernels for 0%

profile of v3, /device:TPU:1, one launch (start us, length us, event | category | flops | bytes accessed | tf_op | source)
XLA Modules:
  0.0 298.4 jit_solution(233902081133677068)
XLA Ops:
  1.5 3.7 %pad_maximum_fusion = bf16[512,2856]{1,0:T(8,128)(2,1)} fusion(bf16[512,40]{1,0:T(8,128)(2,1)S(1)} %copy.72, bf16[512,256]{1,0:T(8,128)(2,1)} %param.15, bf16[512,2560]{1,0:T(8,128)(2,1)} %param.14), kind=kLoop, calls=%fused_computation.57 | loop fusion | flops 8773632 | bytes 5849088 | tf_op jit(solution)/shard_map/concatenate | solution.py:126
  5.2 9.6 %all-to-all-start = ((bf16[32,16,2856]{2,1,0:T(8,128)(2,1)}), bf16[32,16,2856]{2,1,0:T(8,128)(2,1)S(1)}, u32[]{:S(2)}, u32[]{:S(2)}) async-start(bf16[32,16,2856]{2,1,0:T(8,128)(2,1)} %bitcast.198), calls=%async_computation | async-start | bytes 6029312 | tf_op jit(solution)/shard_map/all_to_all | solution.py:125
  17.2 36.0 %all-to-all-done = bf16[32,16,2856]{2,1,0:T(8,128)(2,1)S(1)} async-done(((bf16[32,16,2856]{2,1,0:T(8,128)(2,1)}), bf16[32,16,2856]{2,1,0:T(8,128)(2,1)S(1)}, u32[]{:S(2)}, u32[]{:S(2)}) %all-to-all-start) | async-done | bytes 2924576 | tf_op jit(solution)/shard_map/all_to_all | solution.py:125
  53.8 3.2 %collective-permute-start.1 = (bf16[3,256]{1,0:T(4,128)(2,1)}, bf16[3,256]{1,0:T(4,128)(2,1)}, u32[]{:S(2)}, u32[]{:S(2)}) collective-permute-start(bf16[3,256]{1,0:T(4,128)(2,1)} %slice.243), channel_id=1, source_target_pairs={{0,1},{1,2},{2,3},{3,4},{4,5},{5,6},{6,7},{7,8},{8,9},{9,10},{10,1... | collective-permute-start | bytes 4616 | tf_op jit(solution)/shard_map/ppermute | solution.py:13
  57.8 1.7 slice.238
  60.1 3.2 %collective-permute-start = (bf16[3,2560]{1,0:T(4,128)(2,1)}, bf16[3,2560]{1,0:T(4,128)(2,1)S(1)}, u32[]{:S(2)}, u32[]{:S(2)}) collective-permute-start(bf16[3,2560]{1,0:T(4,128)(2,1)} %slice.237), channel_id=1, source_target_pairs={{0,1},{1,2},{2,3},{3,4},{4,5},{5,6},{6,7},{7,8},{8,9},{9,10},{10,1... | collective-permute-start | bytes 46088 | tf_op jit(solution)/shard_map/ppermute | solution.py:13
  63.4 1.6 multiply_convert_fusion.9
  65.0 2.3 collective-permute-done
  67.4 9.9 %multiply_convert_fusion.7 = bf16[512,2560]{1,0:T(8,128)(2,1)S(1)} fusion(bf16[512,2560]{1,0:T(8,128)(2,1)} %slice.238, bf16[3,2560]{1,0:T(4,128)(2,1)S(1)} %collective-permute-done, f32[2560]{0:T(1024)S(1)} %get-tuple-element.156, f32[2560]{0:T(1024)S(1)} %get-tuple-element.157, f32[2560]{0:T(1024)S(1)} %get-tuple-element.158, ...), kind=kLoop, calls=%fused_computation.53 | loop fusion | flops 39321600 | bytes 5311488 | tf_op jit(solution)/shard_map/convert_element_type | solution.py:67
  77.3 1.5 copy-done
  78.8 4.4 %reshape.309 = bf16[2,256,40,64]{3,2,1,0:T(8,128)(2,1)} reshape(bf16[512,2560]{1,0:T(8,128)(2,1)S(1)} %multiply_convert_fusion.7) | data formatting | bytes 5242880 | tf_op jit(solution)/shard_map/reshape | solution.py:150
  83.2 5.2 %copy.75 = bf16[2,256,40,64]{1,3,2,0:T(8,128)(2,1)S(1)} copy(bf16[2,256,40,64]{3,2,1,0:T(8,128)(2,1)} %reshape.309) | data formatting | bytes 5242880 | tf_op jit(solution)/shard_map/while | solution.py:157
  88.4 16.7 %while.16 = (s32[]{:T(128)}, f32[2,256,40,64]{1,3,2,0:T(8,128)}, f32[2,40,64,128]{3,2,1,0:T(8,128)}, f32[2,256,40]{1,2,0:T(8,128)S(1)}, bf16[2,256,40,64]{1,3,2,...) while((s32[]{:T(128)}, f32[2,256,40,64]{1,3,2,0:T(8,128)}, ...), condition=%wide.region_5.6_spmd, body=%wide.region_2.0_spmd.sunk | while | flops 539379840 | bytes 29302236 | solution.py:157
  90.0 4.7 %bitcast_dynamic-update-slice_fusion.4 = f32[2,256,40,64]{1,3,2,0:T(8,128)} fusion(f32[2,256,40,64]{1,3,2,0:T(8,128)} %get-tuple-element.302, s32[]{:T(128)} %get-tuple-element.301, f32[40,256]{1,0:T(8,128)S(1)} %get-tuple-element.287, f32[40,256]{1,0:T(8,128)S(1)} %get-tuple-element.288, f32[256,256]{1,0:T(8,128)S(1)} %fusion.92, ...), kind=kOutput, calls=%fused_computation.8.clone.1 | convolution fusion | flops 351272960 | bytes 4383744 | tf_op jit(solution)/shard_map/while/body/eval_jaxpr/htu,uhp->thp/dot_general | solution.py:83
  95.2 1.5 copy-done.7
  98.4 4.7 %bitcast_dynamic-update-slice_fusion.4 = f32[2,256,40,64]{1,3,2,0:T(8,128)} fusion(f32[2,256,40,64]{1,3,2,0:T(8,128)} %get-tuple-element.302, s32[]{:T(128)} %get-tuple-element.301, f32[40,256]{1,0:T(8,128)S(1)} %get-tuple-element.287, f32[40,256]{1,0:T(8,128)S(1)} %get-tuple-element.288, f32[256,256]{1,0:T(8,128)S(1)} %fusion.92, ...), kind=kOutput, calls=%fused_computation.8.clone.1 | convolution fusion | flops 351272960 | bytes 4383744 | tf_op jit(solution)/shard_map/while/body/eval_jaxpr/htu,uhp->thp/dot_general | solution.py:83
  103.6 1.5 copy-done.7
  105.9 3.1 %fusion.73 = (f32[1,40,64,128]{3,2,1,0:T(8,128)}, f32[1,40,64,128]{3,2,1,0:T(8,128)S(1)}) fusion(f32[2,40,64,128]{3,2,1,0:T(8,128)} %get-tuple-element.112), kind=kLoop, calls=%fused_computation.150 | loop fusion | bytes 5242880 | tf_op jit(solution)/shard_map/slice | solution.py:163
  110.4 1.6 squeeze.85
  112.5 1.9 multiply_add_fusion
  114.6 26.4 %all_to_all.50 = f32[4,10,8320]{2,1,0:T(8,128)S(1)} all-to-all(f32[4,10,8320]{2,1,0:T(8,128)S(1)} %pad_maximum_fusion.4), channel_id=1, replica_groups=mesh['req'=32,'seq'=4] {'seq'}, dimensions={0} | all-to-all | bytes 2662400 | tf_op jit(solution)/shard_map/all_to_all | solution.py:31
  141.4 1.8 collective-permute-start.3
  143.2 5.5 %collective-permute-start.4 = (f32[10,8192]{1,0:T(8,128)S(1)}, f32[10,8192]{1,0:T(8,128)S(1)}, u32[]{:S(2)}, u32[]{:S(2)}) collective-permute-start(f32[10,8192]{1,0:T(8,128)S(1)} %get-tuple-element.192), channel_id=1, source_target_pairs={{0,4},{4,8},{8,12},{12,16},{16,20},{20,24},{24,28},{28,32},{32,36}... | collective-permute-start | bytes 983048 | tf_op jit(solution)/shard_map/ppermute | solution.py:13
  148.7 1.9 collective-permute-start.2
  150.6 10.0 %collective-permute-done.2 = f32[10]{0:T(128)S(1)} collective-permute-done((f32[10]{0:T(128)S(1)}, f32[10]{0:T(128)S(1)}, u32[]{:S(2)}, u32[]{:S(2)}) %collective-permute-start.2) | collective-permute-done | bytes 72 | tf_op jit(solution)/shard_map/ppermute | solution.py:13
  161.0 1.5 pad_maximum_fusion.5
  162.5 3.7 %all-to-all-start.2 = ((f32[4,10,8192]{2,1,0:T(8,128)}), f32[4,10,8192]{2,1,0:T(8,128)S(1)}, u32[]{:S(2)}, u32[]{:S(2)}) async-start(f32[4,10,8192]{2,1,0:T(8,128)} %pad_maximum_fusion.5), calls=%async_computation.2 | async-start | bytes 4194304 | tf_op jit(solution)/shard_map/all_to_all | solution.py:43
  167.1 24.9 %all-to-all-done.2 = f32[4,10,8192]{2,1,0:T(8,128)S(1)} async-done(((f32[4,10,8192]{2,1,0:T(8,128)}), f32[4,10,8192]{2,1,0:T(8,128)S(1)}, u32[]{:S(2)}, u32[]{:S(2)}) %all-to-all-start.2) | async-done | bytes 1310752 | tf_op jit(solution)/shard_map/all_to_all | solution.py:43
  192.0 2.7 fusion.70
  194.7 2.9 select_n.131
  197.6 2.1 broadcast_select_fusion.1
  199.7 1.5 add_select_fusion
  201.5 1.7 copy.81
  203.3 5.0 %all-to-all-start.4 = ((f32[2,40,64,128]{3,2,0,1:T(8,128)}), f32[2,40,64,128]{3,2,0,1:T(8,128)}, u32[]{:S(2)}, u32[]{:S(2)}) async-start(f32[2,40,64,128]{3,2,0,1:T(8,128)} %copy.81), calls=%async_computation.4 | async-start | bytes 5242880 | tf_op jit(solution)/shard_map/all_to_all | solution.py:187
  208.3 3.0 %slice_convert_fusion.1 = (f32[256,2560]{1,0:T(8,128)}, f32[256,2560]{1,0:T(8,128)}) fusion(bf16[512,2560]{1,0:T(8,128)(2,1)S(1)} %copy-done.1), kind=kLoop, calls=%fused_computation.75 | loop fusion | flops 1310720 | bytes 7864320 | tf_op jit(solution)/shard_map/convert_element_type | solution.py:95
  211.3 3.4 %copy.77 = f32[256,2560]{0,1:T(8,128)} copy(f32[256,2560]{1,0:T(8,128)} %get-tuple-element.200) | data formatting | bytes 5242880 | tf_op jit(solution)/shard_map/convert_element_type | solution.py:95
  214.7 2.1 copy.78
  216.8 1.7 convert_element_type.115
  221.2 4.8 %fusion.38 = (bf16[256,40,64]{0,2,1:T(8,128)(2,1)S(1)}, bf16[256,40,64]{0,2,1:T(8,128)(2,1)S(1)}) fusion(f32[256,40,64]{0,2,1:T(8,128)S(1)} %bitcast.199, f32[256,40,64]{0,2,1:T(8,128)S(1)} %fusion.52, f32[2,256,40,64]{1,3,2,0:T(8,128)} %get-tuple-element.110, f32[40]{0:T(128)S(1)} %copy-done.20, f32[256,40]{0,1:T(8,128)S(1)} %get-tuple-element.206, ...), kind=kLoop, calls=%fused_computation.68 | loop fusion | flops 6553600 | bytes 18432160 | tf_op jit(solution)/shard_map/convert_element_type | solution.py:96
  226.1 1.6 copy.79
  227.6 1.6 copy.80
  229.2 3.0 pad_maximum_fusion.2
  232.2 8.2 %all-to-all-done.4 = f32[2,40,64,128]{3,2,0,1:T(8,128)} async-done(((f32[2,40,64,128]{3,2,0,1:T(8,128)}), f32[2,40,64,128]{3,2,0,1:T(8,128)}, u32[]{:S(2)}, u32[]{:S(2)}) %all-to-all-start.4) | async-done | bytes 2621472 | tf_op jit(solution)/shard_map/all_to_all | solution.py:187
  240.3 9.3 %all-to-all-start.3 = ((bf16[32,16,2560]{2,1,0:T(8,128)(2,1)}), bf16[32,16,2560]{2,1,0:T(8,128)(2,1)S(1)}, u32[]{:S(2)}, u32[]{:S(2)}) async-start(bf16[32,16,2560]{2,1,0:T(8,128)(2,1)} %bitcast.45), calls=%async_computation.3 | async-start | bytes 5242880 | tf_op jit(solution)/shard_map/all_to_all | solution.py:190
  249.7 3.6 %copy.82 = f32[4,2,10,64,128]{4,3,2,1,0:T(8,128)} copy(f32[4,2,10,64,128]{4,3,1,2,0:T(8,128)} %bitcast.50) | data formatting | bytes 5242880 | tf_op jit(solution)/shard_map/all_to_all | solution.py:187
  253.3 30.4 %all-to-all-done.3 = bf16[32,16,2560]{2,1,0:T(8,128)(2,1)S(1)} async-done(((bf16[32,16,2560]{2,1,0:T(8,128)(2,1)}), bf16[32,16,2560]{2,1,0:T(8,128)(2,1)S(1)}, u32[]{:S(2)}, u32[]{:S(2)}) %all-to-all-start.3) | async-done | bytes 2621472 | tf_op jit(solution)/shard_map/all_to_all | solution.py:190
  283.6 3.5 %multiply_reduce_fusion = (f32[512]{0:T(512)S(1)}, f32[512,2560]{1,0:T(8,128)S(1)}) fusion(bf16[512,2560]{1,0:T(8,128)(2,1)} %param.16, bf16[32,16,2560]{2,1,0:T(8,128)(2,1)S(1)} %all-to-all-done.3), kind=kLoop, calls=%fused_computation.52 | loop fusion | flops 11795968 | bytes 10487808 | tf_op jit(solution)/shard_map/reduce_sum | solution.py:101
  287.2 11.3 %convolution_convert_fusion = bf16[512,2560]{1,0:T(8,128)(2,1)} fusion(bf16[2560,2560]{1,0:T(8,128)(2,1)} %param.24, f32[512,2560]{1,0:T(8,128)S(1)} %get-tuple-element.184, f32[2560]{0:T(1024)S(1)} %copy-done.21, f32[512]{0:T(512)S(1)} %add_rsqrt_fusion), kind=kOutput, calls=%fused_computation.54 | convolution fusion | flops 6716129280 | bytes 20983808 | tf_op jit(solution)/shard_map/dot_general | solution.py:192
  (119 shorter events, 16.9 us)
Async XLA Ops:
  5.2 9.6 %copy-start.19 = (s32[64]{0:T(128)S(1)}, s32[64]{0:T(128)}, u32[]{:S(2)}) copy-start(s32[64]{0:T(128)} %param.25) | copy-start | bytes 772
  5.2 10.8 %copy-start.22 = (f32[40]{0:T(128)S(1)}, f32[40]{0:T(128)}, u32[]{:S(2)}) copy-start(f32[40]{0:T(128)} %param.21) | copy-start | bytes 484
  5.2 11.4 %copy-start.14 = (f32[4,2816]{1,0:T(4,128)S(1)}, f32[4,2816]{1,0:T(4,128)}, u32[]{:S(2)}) copy-start(f32[4,2816]{1,0:T(4,128)} %param.18) | copy-start | bytes 135172
  5.2 52.0 %copy-start.15 = (f32[2816]{0:T(1024)S(1)}, f32[2816]{0:T(1024)}, u32[]{:S(2)}) copy-start(f32[2816]{0:T(1024)} %param.19) | copy-start | bytes 33796
  5.2 48.0 %all-to-all-start = ((bf16[32,16,2856]{2,1,0:T(8,128)(2,1)}), bf16[32,16,2856]{2,1,0:T(8,128)(2,1)S(1)}, u32[]{:S(2)}, u32[]{:S(2)}) async-start(bf16[32,16,2856]{2,1,0:T(8,128)(2,1)} %bitcast.198), calls=%async_computation | async-start | bytes 6029312 | tf_op jit(solution)/shard_map/all_to_all | solution.py:125
  15.9 41.3 %copy-start.16 = (pred[2]{0:T(512)(128)(4,1)}, pred[2]{0:T(512)(128)(4,1)S(1)}, u32[]{:S(2)}) copy-start(pred[2]{0:T(512)(128)(4,1)S(1)} %get-tuple-element.162) | copy-start | bytes 10
  53.8 9.6 %collective-permute-start.1 = (bf16[3,256]{1,0:T(4,128)(2,1)}, bf16[3,256]{1,0:T(4,128)(2,1)}, u32[]{:S(2)}, u32[]{:S(2)}) collective-permute-start(bf16[3,256]{1,0:T(4,128)(2,1)} %slice.243), channel_id=1, source_target_pairs={{0,1},{1,2},{2,3},{3,4},{4,5},{5,6},{6,7},{7,8},{8,9},{9,10},{10,1... | collective-permute-start | bytes 4616 | tf_op jit(solution)/shard_map/ppermute | solution.py:13
  60.1 7.3 %collective-permute-start = (bf16[3,2560]{1,0:T(4,128)(2,1)}, bf16[3,2560]{1,0:T(4,128)(2,1)S(1)}, u32[]{:S(2)}, u32[]{:S(2)}) collective-permute-start(bf16[3,2560]{1,0:T(4,128)(2,1)} %slice.237), channel_id=1, source_target_pairs={{0,1},{1,2},{2,3},{3,4},{4,5},{5,6},{6,7},{7,8},{8,9},{9,10},{10,1... | collective-permute-start | bytes 46088 | tf_op jit(solution)/shard_map/ppermute | solution.py:13
  77.3 1.5 copy-start
  83.2 5.2 %copy-start.13 = (f32[40]{0:T(128)S(1)}, f32[40]{0:T(128)}, u32[]{:S(2)}) copy-start(f32[40]{0:T(128)} %param.20) | copy-start | bytes 484
  90.0 4.7 %copy-start.6 = (f32[2,40,64,128]{3,2,1,0:T(8,128)S(1)}, f32[2,40,64,128]{3,2,1,0:T(8,128)}, u32[]{:S(2)}) copy-start(f32[2,40,64,128]{3,2,1,0:T(8,128)} %get-tuple-element.303) | copy-start | bytes 7864324 | tf_op jit(solution)/shard_map/while
  95.2 1.5 copy-start.7
  98.3 4.7 %copy-start.6 = (f32[2,40,64,128]{3,2,1,0:T(8,128)S(1)}, f32[2,40,64,128]{3,2,1,0:T(8,128)}, u32[]{:S(2)}) copy-start(f32[2,40,64,128]{3,2,1,0:T(8,128)} %get-tuple-element.303) | copy-start | bytes 7864324 | tf_op jit(solution)/shard_map/while
  103.6 1.5 copy-start.7
  105.2 0.7 copy-start.11
  108.9 3.3 %copy-start.17 = (pred[2]{0:T(512)(128)(4,1)S(1)}, pred[2]{0:T(512)(128)(4,1)}, u32[]{:S(2)}) copy-start(pred[2]{0:T(512)(128)(4,1)} %copy-done.16) | copy-start | bytes 10
  141.4 19.2 %collective-permute-start.3 = (f32[10,8192]{1,0:T(8,128)S(1)}, f32[10,8192]{1,0:T(8,128)S(1)}, u32[]{:S(2)}, u32[]{:S(2)}) collective-permute-start(f32[10,8192]{1,0:T(8,128)S(1)} %get-tuple-element.192), channel_id=1, source_target_pairs={{0,8},{4,12},{8,16},{12,20},{16,24},{20,28},{24,32},{28,36},{32,40... | collective-permute-start | bytes 983048 | tf_op jit(solution)/shard_map/ppermute | solution.py:13
  143.2 17.4 %collective-permute-start.4 = (f32[10,8192]{1,0:T(8,128)S(1)}, f32[10,8192]{1,0:T(8,128)S(1)}, u32[]{:S(2)}, u32[]{:S(2)}) collective-permute-start(f32[10,8192]{1,0:T(8,128)S(1)} %get-tuple-element.192), channel_id=1, source_target_pairs={{0,4},{4,8},{8,12},{12,16},{16,20},{20,24},{24,28},{28,32},{32,36}... | collective-permute-start | bytes 983048 | tf_op jit(solution)/shard_map/ppermute | solution.py:13
  148.7 11.9 %collective-permute-start.2 = (f32[10]{0:T(128)S(1)}, f32[10]{0:T(128)S(1)}, u32[]{:S(2)}, u32[]{:S(2)}) collective-permute-start(f32[10]{0:T(128)S(1)} %get-tuple-element.189), channel_id=1, source_target_pairs={{0,4},{4,8},{8,12},{12,16},{16,20},{20,24},{24,28},{28,32},{32,36}... | collective-permute-start | bytes 128 | tf_op jit(solution)/shard_map/ppermute | solution.py:13
  162.5 3.8 %copy-start.18 = (pred[2]{0:T(512)(128)(4,1)S(1)}, pred[2]{0:T(512)(128)(4,1)}, u32[]{:S(2)}) copy-start(pred[2]{0:T(512)(128)(4,1)} %get-tuple-element.161) | copy-start | bytes 10
  162.5 29.5 %all-to-all-start.2 = ((f32[4,10,8192]{2,1,0:T(8,128)}), f32[4,10,8192]{2,1,0:T(8,128)S(1)}, u32[]{:S(2)}, u32[]{:S(2)}) async-start(f32[4,10,8192]{2,1,0:T(8,128)} %pad_maximum_fusion.5), calls=%async_computation.2 | async-start | bytes 4194304 | tf_op jit(solution)/shard_map/all_to_all | solution.py:43
  194.7 2.9 copy-start.8
  199.7 1.8 copy-start.2
  203.3 5.0 %copy-start.1 = (bf16[512,2560]{1,0:T(8,128)(2,1)S(1)}, bf16[512,2560]{1,0:T(8,128)(2,1)}, u32[]{:S(2)}) copy-start(bf16[512,2560]{1,0:T(8,128)(2,1)} %copy-done) | copy-start | bytes 7864324
  203.3 37.1 %all-to-all-start.4 = ((f32[2,40,64,128]{3,2,0,1:T(8,128)}), f32[2,40,64,128]{3,2,0,1:T(8,128)}, u32[]{:S(2)}, u32[]{:S(2)}) async-start(f32[2,40,64,128]{3,2,0,1:T(8,128)} %copy.81), calls=%async_computation.4 | async-start | bytes 5242880 | tf_op jit(solution)/shard_map/all_to_all | solution.py:187
  211.3 3.4 %copy-start.9 = (f32[256,2560]{1,0:T(8,128)S(1)}, f32[256,2560]{1,0:T(8,128)}, u32[]{:S(2)}) copy-start(f32[256,2560]{1,0:T(8,128)} %get-tuple-element.201) | copy-start | bytes 7864324
  214.7 3.8 %copy-start.12 = (bf16[2,256,256]{2,1,0:T(8,128)(2,1)S(1)}, bf16[2,256,256]{2,1,0:T(8,128)(2,1)}, u32[]{:S(2)}) copy-start(bf16[2,256,256]{2,1,0:T(8,128)(2,1)} %copy-done.11) | copy-start | bytes 786436
  216.8 2.3 copy-start.3
  218.6 1.9 copy-start.5
  219.1 2.1 copy-start.4
  219.1 2.1 copy-start.20
  227.6 1.6 copy-start.10
  240.3 43.3 %all-to-all-start.3 = ((bf16[32,16,2560]{2,1,0:T(8,128)(2,1)}), bf16[32,16,2560]{2,1,0:T(8,128)(2,1)S(1)}, u32[]{:S(2)}, u32[]{:S(2)}) async-start(bf16[32,16,2560]{2,1,0:T(8,128)(2,1)} %bitcast.45), calls=%async_computation.3 | async-start | bytes 5242880 | tf_op jit(solution)/shard_map/all_to_all | solution.py:190
  253.3 33.9 %copy-start.21 = (f32[2560]{0:T(1024)S(1)}, f32[2560]{0:T(1024)}, u32[]{:S(2)}) copy-start(f32[2560]{0:T(1024)} %param.23) | copy-start | bytes 30724

commit v4 on v3

--- a/solution.py
+++ b/solution.py
@@ -67,12 +67,21 @@
     return jax.nn.silu(running).astype(jnp.bfloat16)
 
 
-def local_stretch(x_stretch, bc_stretch, dt_stretch, dt_bias, a_log):
+def stretch_summary(x_stretch, bc_stretch, dt_stretch, dt_bias, a_log):
+    state_size = bc_stretch.shape[1] // 2
+    b_mat = bc_stretch[:, :state_size]
+    step_size = jax.nn.softplus(dt_stretch.astype(jnp.float32) + dt_bias[None, :])
+    log_decay = jnp.cumsum(-jnp.exp(a_log)[None, :] * step_size, axis=0)
+    tail_weight = jnp.exp(log_decay[-1][None, :] - log_decay) * step_size
+    weighted_x = (x_stretch.astype(jnp.float32) * tail_weight[:, :, None]).astype(jnp.bfloat16)
+    stretch_state = jnp.einsum("uhp,un->hpn", weighted_x, b_mat, preferred_element_type=jnp.float32)
+    return (step_size, log_decay, stretch_state)
+
+
+def stretch_diag(x_stretch, bc_stretch, step_size, log_decay):
     state_size = bc_stretch.shape[1] // 2
     b_mat = bc_stretch[:, :state_size]
     c_mat = bc_stretch[:, state_size:]
-    step_size = jax.nn.softplus(dt_stretch.astype(jnp.float32) + dt_bias[None, :])
-    log_decay = jnp.cumsum(-jnp.exp(a_log)[None, :] * step_size, axis=0)
     scores = jnp.dot(c_mat, b_mat.T, preferred_element_type=jnp.float32)
     stretch_len = scores.shape[0]
     causal = jnp.arange(stretch_len)[:, None] >= jnp.arange(stretch_len)[None, :]
@@ -80,11 +89,7 @@
     segment = by_head[:, :, None] - by_head[:, None, :]
     decay_mask = jnp.where(causal[None], jnp.exp(jnp.where(causal[None], segment, 0.0)), 0.0)
     mixing = (scores[None] * decay_mask * step_size.T[:, None, :]).astype(jnp.bfloat16)
-    y_diag = jnp.einsum("htu,uhp->thp", mixing, x_stretch, preferred_element_type=jnp.float32)
-    tail_weight = jnp.exp(log_decay[-1][None, :] - log_decay) * step_size
-    weighted_x = (x_stretch.astype(jnp.float32) * tail_weight[:, :, None]).astype(jnp.bfloat16)
-    stretch_state = jnp.einsum("uhp,un->hpn", weighted_x, b_mat, preferred_element_type=jnp.float32)
-    return (y_diag, stretch_state, log_decay)
+    return jnp.einsum("htu,uhp->thp", mixing, x_stretch, preferred_element_type=jnp.float32)
 
 
 def finish_stretch(y_diag, log_decay, state_in, x_stretch, c_mat, d_skip):
@@ -151,10 +156,17 @@
     bc_stretches = conv_bc.reshape(stretch_count, STRETCH, 2 * N)
     dt_stretches = dt_rows.reshape(stretch_count, STRETCH, head_count)
 
-    def stretch_work(element):
-        return local_stretch(element[0], element[1], element[2], dt_bias, a_log)
-
-    y_diag, stretch_state, log_decay = lax.map(stretch_work, (x_heads, bc_stretches, dt_stretches))
+    summaries = [
+        stretch_summary(x_heads[c], bc_stretches[c], dt_stretches[c], dt_bias, a_log)
+        for c in range(stretch_count)
+    ]
+    step_size = jnp.stack([s[0] for s in summaries], axis=0)
+    log_decay = jnp.stack([s[1] for s in summaries], axis=0)
+    stretch_state = jnp.stack([s[2] for s in summaries], axis=0)
+    y_diag = [
+        stretch_diag(x_heads[c], bc_stretches[c], step_size[c], log_decay[c])
+        for c in range(stretch_count)
+    ]
     carried = jnp.where(starts[:, None], 0.0, jnp.exp(log_decay[:, -1, :]))
     total_gain = jnp.ones((head_count,), jnp.float32)
     total_state = jnp.zeros((head_count, head_dim, N), jnp.float32)

time: 301 us -> 278 us (0.924)
  local copies, waits for them, and re-layouts: 47.8 us -> 28.3 us
  other arithmetic: 44.1 us -> 35.2 us
  matrix products: 24 us -> 27.5 us
  blocking collectives: 26.4 us -> 29.5 us
    while x10 -> x0, local copies, waits for them, and re-layouts: 8.27 us -> none  [the longest x2 5.28 us: per_device(): lax.map(stretch_work, (x_heads, bc_stretches, dt_stretches))]
    convert_element_type x2 -> x0, other arithmetic: 7.85 us -> none  [the longest x1 4.81 us: finish_stretch(): return mixed_rows.reshape(mixed_rows.shape[0], -1).astype(jnp.bfloat16)]
    convert_element_type x2 -> x0, local copies, waits for them, and re-layouts: 5.47 us -> none  [finish_stretch(): x_stretch.astype(jnp.float32)]
    reshape x1 -> x0, local copies, waits for them, and re-layouts: 4.42 us -> none  [per_device(): x_heads = conv_x.reshape(stretch_count, STRETCH, head_count, head_dim)]
    another operation x1 -> x3, other arithmetic: 0.32 us -> 3.99 us  [per_device(): jnp.stack(ending_parts, axis=0)]
    select_n x2 -> x0, other arithmetic: 3.6 us -> none  [per_device(): jnp.where(finals[stretch], state_out, jnp.zeros_like(state_out))]
    squeeze x4 -> x0, local copies, waits for them, and re-layouts: 3.11 us -> none  [the longest x2 3.08 us: per_device(): stretch_state[stretch]]
    all_to_all x1, blocking collectives: 26.4 us -> 29.5 us  [carried_in(): lax.all_to_all(packed, 'seq', split_axis=0, concat_axis=0, tiled=True)]
  transfers between devices with their start and end apart: 9 -> 9, of which waited for: 6 -> 5; matrix products, arithmetic and copies ran while one was open for 12% -> 12% of each run, Pallas kernels for 0% -> 0%
where the time goes in v4:
time: 278 us; the launch traced here: 276 us
  waiting for transfers between devices  110 us (40%)
  starting transfers between devices  44.3 us (16%)
  other arithmetic  35.2 us (13%)
  blocking collectives  29.5 us (11%)
  local copies, waits for them, and re-layouts  28.3 us (10%)
  matrix products  27.5 us (10%)
    all_to_all x1, waiting for transfers between devices, per_device(): lax.all_to_all(jnp.concatenate([x_in, bc_in, dt_raw], axis=1), 'req', spl...  35.9 us
    all_to_all x1, waiting for transfers between devices, per_device(): lax.all_to_all(mixed_stream, 'req', split_axis=0, concat_axis=0, tiled=True)  30.4 us
    all_to_all x1, blocking collectives, carried_in(): lax.all_to_all(packed, 'seq', split_axis=0, concat_axis=0, tiled=True)  29.5 us
    all_to_all x1, waiting for transfers between devices, carried_in(): lax.all_to_all(incoming, 'seq', split_axis=0, concat_axis=0, tiled=True)  22.7 us
    ppermute x5, starting transfers between devices, from_behind(): lax.ppermute(value, axis, [(source, source + steps) for source in range(l...  14.4 us
    all_to_all x1, starting transfers between devices, per_device(): lax.all_to_all(mixed_stream, 'req', split_axis=0, concat_axis=0, tiled=True)  12 us
    convert_element_type x2, other arithmetic, causal_conv(): return jax.nn.silu(running).astype(jnp.bfloat16)  11.7 us
    dot_general x1, matrix products, per_device(): jnp.dot(normed, w_out, preferred_element_type=jnp.float32)  11.3 us
  transfers between devices with their start and end apart: 9, of which 5 were waited for; matrix products, arithmetic and copies ran while one was open for 12% of the time, Pallas kernels for 0%

profile of v4, /device:TPU:1, one launch (start us, length us, event | category | flops | bytes accessed | tf_op | source)
XLA Modules:
  0.0 275.6 jit_solution(551171012262628597)
XLA Ops:
  0.6 0.9 copy.169
  1.5 3.7 %pad_maximum_fusion = bf16[512,2856]{1,0:T(8,128)(2,1)} fusion(bf16[512,40]{1,0:T(8,128)(2,1)S(1)} %copy.169, bf16[512,256]{1,0:T(8,128)(2,1)} %param.13, bf16[512,2560]{1,0:T(8,128)(2,1)} %param.12), kind=kLoop, calls=%fused_computation.32 | loop fusion | flops 8773632 | bytes 5849088 | tf_op jit(solution)/shard_map/concatenate | solution.py:131
  5.2 9.6 %all-to-all-start = ((bf16[32,16,2856]{2,1,0:T(8,128)(2,1)}), bf16[32,16,2856]{2,1,0:T(8,128)(2,1)S(1)}, u32[]{:S(2)}, u32[]{:S(2)}) async-start(bf16[32,16,2856]{2,1,0:T(8,128)(2,1)} %bitcast.158), calls=%async_computation | async-start | bytes 6029312 | tf_op jit(solution)/shard_map/all_to_all | solution.py:130
  17.3 35.9 %all-to-all-done = bf16[32,16,2856]{2,1,0:T(8,128)(2,1)S(1)} async-done(((bf16[32,16,2856]{2,1,0:T(8,128)(2,1)}), bf16[32,16,2856]{2,1,0:T(8,128)(2,1)S(1)}, u32[]{:S(2)}, u32[]{:S(2)}) %all-to-all-start) | async-done | bytes 2924576 | tf_op jit(solution)/shard_map/all_to_all | solution.py:130
  55.0 0.7 copy_bitcast_fusion
  56.7 0.7 copy_bitcast_fusion.1
  57.6 3.2 %collective-permute-start.1 = (bf16[3,256]{1,0:T(4,128)(2,1)}, bf16[3,256]{1,0:T(4,128)(2,1)}, u32[]{:S(2)}, u32[]{:S(2)}) collective-permute-start(bf16[3,256]{1,0:T(4,128)(2,1)} %slice.254), channel_id=1, source_target_pairs={{0,1},{1,2},{2,3},{3,4},{4,5},{5,6},{6,7},{7,8},{8,9},{9,10},{10,1... | collective-permute-start | bytes 4616 | tf_op jit(solution)/shard_map/ppermute | solution.py:13
  60.8 3.2 %collective-permute-start = (bf16[3,2560]{1,0:T(4,128)(2,1)S(1)}, bf16[3,2560]{1,0:T(4,128)(2,1)S(1)}, u32[]{:S(2)}, u32[]{:S(2)}) collective-permute-start(bf16[3,2560]{1,0:T(4,128)(2,1)S(1)} %slice.247), channel_id=1, source_target_pairs={{0,1},{1,2},{2,3},{3,4},{4,5},{5,6},{6,7},{7,8},{8,9},{9,10},{10,1... | collective-permute-start | bytes 46088 | tf_op jit(solution)/shard_map/ppermute | solution.py:13
  64.2 0.8 bitcast_exponential_fusion
  65.0 1.1 slice_bitcast_fusion.8
  66.1 1.7 slice.248
  67.8 0.7 mul.399
  68.5 1.7 multiply_convert_fusion.11
  70.2 10.0 %multiply_convert_fusion.5 = bf16[512,2560]{1,0:T(8,128)(2,1)S(1)} fusion(bf16[512,2560]{1,0:T(8,128)(2,1)} %slice.248, bf16[3,2560]{1,0:T(4,128)(2,1)S(1)} %collective-permute-done, f32[2560]{0:T(1024)S(1)} %get-tuple-element.7, f32[2560]{0:T(1024)S(1)} %get-tuple-element.8, f32[2560]{0:T(1024)S(1)} %get-tuple-element.9, f32[2560]{0:T(1024)S(1)} %get-tuple-element.6, ...), kind=kLoop, calls=%fused_computation.22 | loop fusion | flops 39321600 | bytes 5311488 | tf_op jit(solution)/shard_map/convert_element_type | solution.py:67
  80.2 1.7 fusion.87
  81.8 1.7 copy.170
  83.6 1.5 copy.177
  85.6 0.8 copy-done.6
  86.3 2.0 multiply_add_fusion.1
  88.4 1.5 concatenate.21
  90.1 29.5 %all_to_all.50 = f32[4,10,8320]{2,1,0:T(8,128)S(1)} all-to-all(f32[4,10,8320]{2,1,0:T(8,128)S(1)} %pad_maximum_fusion.4), channel_id=1, replica_groups=mesh['req'=32,'seq'=4] {'seq'}, dimensions={0} | all-to-all | bytes 2662400 | tf_op jit(solution)/shard_map/all_to_all | solution.py:31
  119.9 1.3 collective-permute-start.3
  121.3 4.7 %collective-permute-start.4 = (f32[10,8192]{1,0:T(8,128)S(1)}, f32[10,8192]{1,0:T(8,128)S(1)}, u32[]{:S(2)}, u32[]{:S(2)}) collective-permute-start(f32[10,8192]{1,0:T(8,128)S(1)} %get-tuple-element.23), channel_id=1, source_target_pairs={{0,4},{4,8},{8,12},{12,16},{16,20},{20,24},{24,28},{28,32},{32,36}... | collective-permute-start | bytes 983048 | tf_op jit(solution)/shard_map/ppermute | solution.py:13
  126.0 1.9 collective-permute-start.2
  127.9 10.7 %collective-permute-done.2 = f32[10]{0:T(128)S(1)} collective-permute-done((f32[10]{0:T(128)S(1)}, f32[10]{0:T(128)S(1)}, u32[]{:S(2)}, u32[]{:S(2)}) %collective-permute-start.2) | collective-permute-done | bytes 72 | tf_op jit(solution)/shard_map/ppermute | solution.py:13
  139.0 1.5 pad_maximum_fusion.5
  140.5 3.6 %all-to-all-start.2 = ((f32[4,10,8192]{2,1,0:T(8,128)}), f32[4,10,8192]{2,1,0:T(8,128)S(1)}, u32[]{:S(2)}, u32[]{:S(2)}) async-start(f32[4,10,8192]{2,1,0:T(8,128)} %pad_maximum_fusion.5), calls=%async_computation.2 | async-start | bytes 4194304 | tf_op jit(solution)/shard_map/all_to_all | solution.py:43
  145.5 22.7 %all-to-all-done.2 = f32[4,10,8192]{2,1,0:T(8,128)S(1)} async-done(((f32[4,10,8192]{2,1,0:T(8,128)}), f32[4,10,8192]{2,1,0:T(8,128)S(1)}, u32[]{:S(2)}, u32[]{:S(2)}) %all-to-all-start.2) | async-done | bytes 1310752 | tf_op jit(solution)/shard_map/all_to_all | solution.py:43
  168.2 2.6 fusion.83
  170.8 2.8 %select_n.127 = f32[40,64,128]{2,1,0:T(8,128)} reshape(f32[4,10,8192]{2,1,0:T(8,128)} %get-tuple-element.17) | data formatting | bytes 2621440 | tf_op jit(solution)/shard_map/jit(_where)/select_n | solution.py:182
  173.6 2.3 select_bitcast_fusion.1
  175.9 1.5 select_bitcast_fusion
  177.6 1.7 copy.180
  179.3 4.7 %all-to-all-start.4 = ((f32[2,40,64,128]{3,2,0,1:T(8,128)}), f32[2,40,64,128]{3,2,0,1:T(8,128)}, u32[]{:S(2)}, u32[]{:S(2)}) async-start(f32[2,40,64,128]{3,2,0,1:T(8,128)} %copy.180), calls=%async_computation.4 | async-start | bytes 5242880 | tf_op jit(solution)/shard_map/all_to_all | solution.py:199
  184.1 2.4 convert_element_type.110
  186.5 1.6 fusion.45
  188.1 5.7 %fusion.20 = bf16[256,40,64]{0,2,1:T(8,128)(2,1)} fusion(bf16[256,40,64]{0,2,1:T(8,128)(2,1)S(1)} %bitcast.160, f32[256,40,64]{0,2,1:T(8,128)S(1)} %fusion.45, f32[40,256]{1,0:T(8,128)} %get-tuple-element.67, f32[40,256]{1,0:T(8,128)} %get-tuple-element.37, f32[256,256]{1,0:T(8,128)S(1)} %fusion.46, pred[256,256]{1,0:T(8,128)(4,1)S(1)} %iota_compare_fusion, ...), kind=kOutput, calls=%fused_computation.35 | convolution fusion | flops 355205120 | bytes 5693600 | tf_op jit(solution)/shard_map/htu,uhp->thp/dot_general | solution.py:92
  193.8 1.6 copy.178
  195.5 1.2 fusion.34
  196.7 4.8 %fusion.23 = bf16[256,40,64]{0,2,1:T(8,128)(2,1)} fusion(bf16[256,40,64]{0,2,1:T(8,128)(2,1)S(1)} %bitcast.162, f32[256,40,64]{0,2,1:T(8,128)S(1)} %fusion.34, f32[40,256]{1,0:T(8,128)S(1)} %copy-done.11, f32[40,256]{1,0:T(8,128)S(1)} %copy-done.9, f32[256,256]{1,0:T(8,128)S(1)} %fusion.43, pred[256,256]{1,0:T(8,128)(4,1)S(1)} %iota_compare_fusion, ...), kind=kOutput, calls=%fused_computation.38 | convolution fusion | flops 355205120 | bytes 5693600 | tf_op jit(solution)/shard_map/htu,uhp->thp/dot_general | solution.py:92
  201.5 1.6 copy.179
  203.1 1.7 pad_maximum_fusion.2
  204.8 10.1 %all-to-all-done.4 = f32[2,40,64,128]{3,2,0,1:T(8,128)} async-done(((f32[2,40,64,128]{3,2,0,1:T(8,128)}), f32[2,40,64,128]{3,2,0,1:T(8,128)}, u32[]{:S(2)}, u32[]{:S(2)}) %all-to-all-start.4) | async-done | bytes 2621472 | tf_op jit(solution)/shard_map/all_to_all | solution.py:199
  214.9 12.0 %all-to-all-start.3 = ((bf16[32,16,2560]{2,1,0:T(8,128)(2,1)}), bf16[32,16,2560]{2,1,0:T(8,128)(2,1)S(1)}, u32[]{:S(2)}, u32[]{:S(2)}) async-start(bf16[32,16,2560]{2,1,0:T(8,128)(2,1)} %bitcast.41), calls=%async_computation.3 | async-start | bytes 5242880 | tf_op jit(solution)/shard_map/all_to_all | solution.py:202
  226.9 3.6 %copy.181 = f32[4,2,10,64,128]{4,3,2,1,0:T(8,128)} copy(f32[4,2,10,64,128]{4,3,1,2,0:T(8,128)} %bitcast.49) | data formatting | bytes 5242880 | tf_op jit(solution)/shard_map/all_to_all | solution.py:199
  230.4 30.4 %all-to-all-done.3 = bf16[32,16,2560]{2,1,0:T(8,128)(2,1)S(1)} async-done(((bf16[32,16,2560]{2,1,0:T(8,128)(2,1)}), bf16[32,16,2560]{2,1,0:T(8,128)(2,1)S(1)}, u32[]{:S(2)}, u32[]{:S(2)}) %all-to-all-start.3) | async-done | bytes 2621472 | tf_op jit(solution)/shard_map/all_to_all | solution.py:202
  260.8 3.5 %multiply_reduce_fusion = (f32[512]{0:T(512)S(1)}, f32[512,2560]{1,0:T(8,128)S(1)}) fusion(bf16[512,2560]{1,0:T(8,128)(2,1)} %param.14, bf16[32,16,2560]{2,1,0:T(8,128)(2,1)S(1)} %all-to-all-done.3), kind=kLoop, calls=%fused_computation.11 | loop fusion | flops 11795968 | bytes 10487808 | tf_op jit(solution)/shard_map/reduce_sum | solution.py:106
  264.3 11.3 %convolution_convert_fusion = bf16[512,2560]{1,0:T(8,128)(2,1)} fusion(bf16[2560,2560]{1,0:T(8,128)(2,1)} %param.22, f32[512,2560]{1,0:T(8,128)S(1)} %get-tuple-element.15, f32[2560]{0:T(1024)S(1)} %copy-done.17, f32[512]{0:T(512)S(1)} %add_rsqrt_fusion), kind=kOutput, calls=%fused_computation.25 | convolution fusion | flops 6716129280 | bytes 20983808 | tf_op jit(solution)/shard_map/dot_general | solution.py:204
  (93 shorter events, 8.9 us)
Async XLA Ops:
  5.2 9.6 %copy-start.16 = (s32[64]{0:T(128)S(1)}, s32[64]{0:T(128)}, u32[]{:S(2)}) copy-start(s32[64]{0:T(128)} %param.23) | copy-start | bytes 772
  5.2 10.2 %copy-start.12 = (f32[2816]{0:T(1024)S(1)}, f32[2816]{0:T(1024)}, u32[]{:S(2)}) copy-start(f32[2816]{0:T(1024)} %param.17) | copy-start | bytes 33796
  5.2 10.8 %copy-start.8 = (f32[4,2816]{1,0:T(4,128)S(1)}, f32[4,2816]{1,0:T(4,128)}, u32[]{:S(2)}) copy-start(f32[4,2816]{1,0:T(4,128)} %param.16) | copy-start | bytes 135172
  5.2 10.9 %copy-start.18 = (f32[40]{0:T(128)S(1)}, f32[40]{0:T(128)}, u32[]{:S(2)}) copy-start(f32[40]{0:T(128)} %param.19) | copy-start | bytes 484
  5.2 48.8 %copy-start.13 = (f32[40]{0:T(128)S(1)}, f32[40]{0:T(128)}, u32[]{:S(2)}) copy-start(f32[40]{0:T(128)} %param.18) | copy-start | bytes 484
  5.2 48.0 %all-to-all-start = ((bf16[32,16,2856]{2,1,0:T(8,128)(2,1)}), bf16[32,16,2856]{2,1,0:T(8,128)(2,1)S(1)}, u32[]{:S(2)}, u32[]{:S(2)}) async-start(bf16[32,16,2856]{2,1,0:T(8,128)(2,1)} %bitcast.158), calls=%async_computation | async-start | bytes 6029312 | tf_op jit(solution)/shard_map/all_to_all | solution.py:130
  57.6 10.9 %collective-permute-start.1 = (bf16[3,256]{1,0:T(4,128)(2,1)}, bf16[3,256]{1,0:T(4,128)(2,1)}, u32[]{:S(2)}, u32[]{:S(2)}) collective-permute-start(bf16[3,256]{1,0:T(4,128)(2,1)} %slice.254), channel_id=1, source_target_pairs={{0,1},{1,2},{2,3},{3,4},{4,5},{5,6},{6,7},{7,8},{8,9},{9,10},{10,1... | collective-permute-start | bytes 4616 | tf_op jit(solution)/shard_map/ppermute | solution.py:13
  60.8 9.4 %collective-permute-start = (bf16[3,2560]{1,0:T(4,128)(2,1)S(1)}, bf16[3,2560]{1,0:T(4,128)(2,1)S(1)}, u32[]{:S(2)}, u32[]{:S(2)}) collective-permute-start(bf16[3,2560]{1,0:T(4,128)(2,1)S(1)} %slice.247), channel_id=1, source_target_pairs={{0,1},{1,2},{2,3},{3,4},{4,5},{5,6},{6,7},{7,8},{8,9},{9,10},{10,1... | collective-permute-start | bytes 46088 | tf_op jit(solution)/shard_map/ppermute | solution.py:13
  81.8 1.7 copy-start.2
  83.5 2.0 copy-start.3
  83.5 2.0 copy-start.14
  83.6 2.0 copy-start.15
  85.0 1.3 copy-start.6
  85.6 2.8 %copy-start = (f32[40,64,128]{2,1,0:T(8,128)}, f32[40,64,128]{2,1,0:T(8,128)S(1)}, u32[]{:S(2)}) copy-start(f32[40,64,128]{2,1,0:T(8,128)S(1)} %fusion.30) | copy-start | bytes 3932164
  119.9 18.7 %collective-permute-start.3 = (f32[10,8192]{1,0:T(8,128)S(1)}, f32[10,8192]{1,0:T(8,128)S(1)}, u32[]{:S(2)}, u32[]{:S(2)}) collective-permute-start(f32[10,8192]{1,0:T(8,128)S(1)} %get-tuple-element.23), channel_id=1, source_target_pairs={{0,8},{4,12},{8,16},{12,20},{16,24},{20,28},{24,32},{28,36},{32,40... | collective-permute-start | bytes 983048 | tf_op jit(solution)/shard_map/ppermute | solution.py:13
  121.3 17.4 %collective-permute-start.4 = (f32[10,8192]{1,0:T(8,128)S(1)}, f32[10,8192]{1,0:T(8,128)S(1)}, u32[]{:S(2)}, u32[]{:S(2)}) collective-permute-start(f32[10,8192]{1,0:T(8,128)S(1)} %get-tuple-element.23), channel_id=1, source_target_pairs={{0,4},{4,8},{8,12},{12,16},{16,20},{20,24},{24,28},{28,32},{32,36}... | collective-permute-start | bytes 983048 | tf_op jit(solution)/shard_map/ppermute | solution.py:13
  126.0 12.6 %collective-permute-start.2 = (f32[10]{0:T(128)S(1)}, f32[10]{0:T(128)S(1)}, u32[]{:S(2)}, u32[]{:S(2)}) collective-permute-start(f32[10]{0:T(128)S(1)} %get-tuple-element.20), channel_id=1, source_target_pairs={{0,4},{4,8},{8,12},{12,16},{16,20},{20,24},{24,28},{28,32},{32,36}... | collective-permute-start | bytes 128 | tf_op jit(solution)/shard_map/ppermute | solution.py:13
  140.5 27.8 %all-to-all-start.2 = ((f32[4,10,8192]{2,1,0:T(8,128)}), f32[4,10,8192]{2,1,0:T(8,128)S(1)}, u32[]{:S(2)}, u32[]{:S(2)}) async-start(f32[4,10,8192]{2,1,0:T(8,128)} %pad_maximum_fusion.5), calls=%async_computation.2 | async-start | bytes 4194304 | tf_op jit(solution)/shard_map/all_to_all | solution.py:43
  170.8 2.8 %copy-start.1 = (f32[40,64,128]{2,1,0:T(8,128)S(1)}, f32[40,64,128]{2,1,0:T(8,128)}, u32[]{:S(2)}) copy-start(f32[40,64,128]{2,1,0:T(8,128)} %copy-done) | copy-start | bytes 3932164
  173.6 2.3 copy-start.5
  179.3 35.5 %all-to-all-start.4 = ((f32[2,40,64,128]{3,2,0,1:T(8,128)}), f32[2,40,64,128]{3,2,0,1:T(8,128)}, u32[]{:S(2)}, u32[]{:S(2)}) async-start(f32[2,40,64,128]{3,2,0,1:T(8,128)} %copy.180), calls=%async_computation.4 | async-start | bytes 5242880 | tf_op jit(solution)/shard_map/all_to_all | solution.py:199
  184.0 4.0 %copy-start.4 = (bf16[256,2560]{0,1:T(8,128)(2,1)S(1)}, bf16[256,2560]{0,1:T(8,128)(2,1)}, u32[]{:S(2)}) copy-start(bf16[256,2560]{0,1:T(8,128)(2,1)} %copy-done.3) | copy-start | bytes 3932164
  184.1 4.0 %copy-start.19 = (f32[40]{0:T(128)S(1)}, f32[40]{0:T(128)}, u32[]{:S(2)}) copy-start(f32[40]{0:T(128)} %param.20) | copy-start | bytes 484
  195.4 1.3 copy-start.7
  195.4 1.3 copy-start.9
  195.4 1.3 copy-start.10
  195.4 1.3 copy-start.11
  214.9 45.9 %all-to-all-start.3 = ((bf16[32,16,2560]{2,1,0:T(8,128)(2,1)}), bf16[32,16,2560]{2,1,0:T(8,128)(2,1)S(1)}, u32[]{:S(2)}, u32[]{:S(2)}) async-start(bf16[32,16,2560]{2,1,0:T(8,128)(2,1)} %bitcast.41), calls=%async_computation.3 | async-start | bytes 5242880 | tf_op jit(solution)/shard_map/all_to_all | solution.py:202
  230.4 33.9 %copy-start.17 = (f32[2560]{0:T(1024)S(1)}, f32[2560]{0:T(1024)}, u32[]{:S(2)}) copy-start(f32[2560]{0:T(1024)} %param.21) | copy-start | bytes 30724

commit v5 on v4

--- a/solution.py
+++ b/solution.py
@@ -125,84 +125,106 @@
     w_out,
     prompt_stretches,
 ):
-    inner_width = x_in.shape[1]
-    bc_width = bc_in.shape[1]
-    joined = lax.all_to_all(
-        jnp.concatenate([x_in, bc_in, dt_raw], axis=1), "req", split_axis=0, concat_axis=0, tiled=True
-    )
-    x_rows = joined[:, :inner_width]
-    bc_rows = joined[:, inner_width : inner_width + bc_width]
-    dt_rows = joined[:, inner_width + bc_width :]
-    row_count = x_rows.shape[0]
+    n_req = lax.axis_size("req")
+    n_seq = lax.axis_size("seq")
+    tok_rows, inner_width = x_in.shape
     head_count = a_log.shape[0]
     head_dim = inner_width // head_count
+    share = head_count // n_seq
+    width = share * head_dim
+    chunk = tok_rows // n_req
+    bc_width = bc_in.shape[1]
+    state_size = bc_width // 2
+    conv_span = conv_weight.shape[0]
+    group = lax.axis_index("seq")
+    block = lax.axis_index("req")
+
+    x_parts = x_in.reshape(n_req, chunk, n_seq, width)
+    dt_parts = dt_raw.reshape(n_req, chunk, n_seq, share)
+    bc_parts = jnp.broadcast_to(
+        bc_in.reshape(n_req, chunk, 1, bc_width), (n_req, chunk, n_seq, bc_width)
+    )
+    outbound = jnp.concatenate([x_parts, bc_parts, dt_parts], axis=3)
+    outbound = outbound.transpose(0, 2, 1, 3).reshape(n_req * n_seq, chunk, -1)
+    inbound = lax.all_to_all(outbound, ("req", "seq"), 0, 0, tiled=True)
+    inbound = inbound.reshape(n_req, n_seq, chunk, -1).transpose(1, 0, 2, 3)
+    inbound = inbound.reshape(n_seq * tok_rows, -1)
+    x_rows = inbound[:, :width]
+    bc_rows = inbound[:, width : width + bc_width]
+    dt_rows = inbound[:, width + bc_width :]
+
+    row_count = x_rows.shape[0]
     stretch_count = row_count // STRETCH
-    conv_span = conv_weight.shape[0]
-    device = lax.axis_index(("req", "seq"))
-    stretch_ids = device * stretch_count + jnp.arange(stretch_count, dtype=jnp.int32)
+    stretch_ids = block * stretch_count + jnp.arange(stretch_count, dtype=jnp.int32)
     starts, finals = stretch_flags(prompt_stretches, stretch_ids)
     edge_x, edge_bc = from_behind(
-        (x_rows[row_count - conv_span + 1 :], bc_rows[row_count - conv_span + 1 :]),
-        ("req", "seq"),
-        1,
-    )
-    conv_x = causal_conv(
-        x_rows, edge_x, conv_weight[:, :inner_width], conv_bias[:inner_width], starts
-    )
+        (x_rows[row_count - conv_span + 1 :], bc_rows[row_count - conv_span + 1 :]), "req", 1
+    )
+    weight_x = lax.dynamic_slice_in_dim(conv_weight, group * width, width, axis=1)
+    bias_x = lax.dynamic_slice_in_dim(conv_bias, group * width, width, axis=0)
+    conv_x = causal_conv(x_rows, edge_x, weight_x, bias_x, starts)
     conv_bc = causal_conv(
         bc_rows, edge_bc, conv_weight[:, inner_width:], conv_bias[inner_width:], starts
     )
-    x_heads = conv_x.reshape(stretch_count, STRETCH, head_count, head_dim)
-    bc_stretches = conv_bc.reshape(stretch_count, STRETCH, 2 * N)
-    dt_stretches = dt_rows.reshape(stretch_count, STRETCH, head_count)
-
-    summaries = [
-        stretch_summary(x_heads[c], bc_stretches[c], dt_stretches[c], dt_bias, a_log)
-        for c in range(stretch_count)
-    ]
-    step_size = jnp.stack([s[0] for s in summaries], axis=0)
-    log_decay = jnp.stack([s[1] for s in summaries], axis=0)
-    stretch_state = jnp.stack([s[2] for s in summaries], axis=0)
-    y_diag = [
-        stretch_diag(x_heads[c], bc_stretches[c], step_size[c], log_decay[c])
-        for c in range(stretch_count)
-    ]
+    bias_dt = lax.dynamic_slice_in_dim(dt_bias, group * share, share)
+    rate_log = lax.dynamic_slice_in_dim(a_log, group * share, share)
+    skip = lax.dynamic_slice_in_dim(d_skip, group * share, share)
+
+    x_heads = conv_x.reshape(stretch_count, STRETCH, share, head_dim)
+    bcs = conv_bc.reshape(stretch_count, STRETCH, bc_width)
+    b_mat = bcs[:, :, :state_size]
+    c_mat = bcs[:, :, state_size:]
+    dts = dt_rows.reshape(stretch_count, STRETCH, share)
+    step_size = jax.nn.softplus(dts.astype(jnp.float32) + bias_dt[None, None, :])
+    log_decay = jnp.cumsum(-jnp.exp(rate_log)[None, None, :] * step_size, axis=1)
+    tail_weight = jnp.exp(log_decay[:, -1:, :] - log_decay) * step_size
+    weighted_x = (x_heads.astype(jnp.float32) * tail_weight[..., None]).astype(jnp.bfloat16)
+    stretch_state = jnp.einsum(
+        "cuhp,cun->chpn", weighted_x, b_mat, preferred_element_type=jnp.float32
+    )
     carried = jnp.where(starts[:, None], 0.0, jnp.exp(log_decay[:, -1, :]))
-    total_gain = jnp.ones((head_count,), jnp.float32)
-    total_state = jnp.zeros((head_count, head_dim, N), jnp.float32)
+    total = (jnp.ones((share,), jnp.float32), jnp.zeros((share, head_dim, N), jnp.float32))
     for stretch in range(stretch_count):
-        total_gain, total_state = chain_states(
-            (total_gain, total_state), (carried[stretch], stretch_state[stretch])
-        )
-    window = -(-(LMAX_CH - 1) // stretch_count)
-    state_prev = carried_in(total_gain, total_state, window)
-    normed_parts = []
+        total = chain_states(total, (carried[stretch], stretch_state[stretch]))
+    reach = -(-(LMAX_CH - 1) // stretch_count)
+    behind = from_behind(total, "req", reach)
+    for step in range(reach - 1, 0, -1):
+        behind = chain_states(behind, from_behind(total, "req", step))
+    state_prev = behind[1]
+
+    scores = jnp.einsum("ctn,cun->ctu", c_mat, b_mat, preferred_element_type=jnp.float32)
+    causal = jnp.arange(STRETCH)[:, None] >= jnp.arange(STRETCH)[None, :]
+    by_head = log_decay.transpose(0, 2, 1)
+    segment = by_head[:, :, :, None] - by_head[:, :, None, :]
+    decay_mask = jnp.where(causal, jnp.exp(jnp.where(causal, segment, 0.0)), 0.0)
+    mixing = (
+        scores[:, None] * decay_mask * step_size.transpose(0, 2, 1)[:, :, None, :]
+    ).astype(jnp.bfloat16)
+    y_diag = jnp.einsum("chtu,cuhp->cthp", mixing, x_heads, preferred_element_type=jnp.float32)
+
+    state_ins = []
     ending_parts = []
     for stretch in range(stretch_count):
         state_in = jnp.where(starts[stretch], jnp.zeros_like(state_prev), state_prev)
-        normed_parts.append(
-            finish_stretch(
-                y_diag[stretch],
-                log_decay[stretch],
-                state_in,
-                x_heads[stretch],
-                bc_stretches[stretch, :, N:],
-                d_skip,
-            )
-        )
+        state_ins.append(state_in)
         state_out = (
             jnp.exp(log_decay[stretch, -1])[:, None, None] * state_in + stretch_state[stretch]
         )
         ending_parts.append(jnp.where(finals[stretch], state_out, jnp.zeros_like(state_out)))
         state_prev = state_out
-    mixed_stream = jnp.concatenate(normed_parts, axis=0)
-    endings = lax.all_to_all(
-        jnp.stack(ending_parts, axis=0), "seq", split_axis=1, concat_axis=0, tiled=True
-    )
-    mixed_tokens = lax.all_to_all(mixed_stream, "req", split_axis=0, concat_axis=0, tiled=True)
+    state_low = jnp.stack(state_ins, axis=0).astype(jnp.bfloat16)
+    y_off = jnp.exp(log_decay)[..., None] * jnp.einsum(
+        "ctn,chpn->cthp", c_mat, state_low, preferred_element_type=jnp.float32
+    )
+    mixed = y_diag + y_off + skip[None, None, :, None] * x_heads.astype(jnp.float32)
+    mixed = mixed.reshape(n_seq, n_req, chunk, width).astype(jnp.bfloat16)
+    mixed = mixed.transpose(1, 0, 2, 3).reshape(n_req * n_seq, chunk, width)
+    back = lax.all_to_all(mixed, ("req", "seq"), 0, 0, tiled=True)
+    back = back.reshape(n_req, n_seq, chunk, width).transpose(0, 2, 1, 3)
+    mixed_tokens = back.reshape(tok_rows, inner_width)
     normed = gate_and_norm(mixed_tokens, z_in, norm_gain)
     mixed_out = jnp.dot(normed, w_out, preferred_element_type=jnp.float32).astype(jnp.bfloat16)
-    return (mixed_out, endings)
+    return (mixed_out, jnp.stack(ending_parts, axis=0))
 
 
 def solution(mesh):

time: 278 us -> 238 us (0.86)
  blocking collectives: 29.5 us -> 0 us
  local copies, waits for them, and re-layouts: 28.3 us -> 55 us
  waiting for transfers between devices: 110 us -> 85.6 us
  starting transfers between devices: 44.3 us -> 32.1 us
  other arithmetic: 35.2 us -> 39 us
  matrix products: 27.5 us -> 23.9 us
    all_to_all x1 -> x0, blocking collectives: 29.5 us -> none  [carried_in(): lax.all_to_all(packed, 'seq', split_axis=0, concat_axis=0, tiled=True)]
    all_to_all x4 -> x2, waiting for transfers between devices: 99.1 us -> 81.1 us  [the longest x1 47.9 us: per_device(): inbound = lax.all_to_all(outbound, ('req', 'seq'), 0, 0, tiled=True)]
    convert_element_type x3 -> x4, local copies, waits for them, and re-layouts: 5.6 us -> 22.7 us  [the longest x2 18 us: per_device(): mixed = mixed.reshape(n_seq, n_req, chunk, width).astype(jnp.bfloat16)]
    unnamed x1 -> x14, other arithmetic: 0.12 us -> 14.3 us
    all_to_all x4 -> x2, starting transfers between devices: 29.9 us -> 19.6 us  [the longest x1 12 us: per_device(): inbound = lax.all_to_all(outbound, ('req', 'seq'), 0, 0, tiled=True)]
    reshape x0 -> x4, local copies, waits for them, and re-layouts: none -> 9.09 us  [the longest x2 7.95 us: per_device(): x_parts = x_in.reshape(n_req, chunk, n_seq, width)]
    ppermute x5, waiting for transfers between devices: 10.7 us -> 4.48 us  [from_behind(): lax.ppermute(value, axis, [(source, source + steps) for source in range(l...]
    unnamed x43 -> x26, local copies, waits for them, and re-layouts: 2.01 us -> 7.98 us
  transfers between devices with their start and end apart: 9 -> 7, of which waited for: 5 -> 3; matrix products, arithmetic and copies ran while one was open for 12% -> 7% of each run, Pallas kernels for 0% -> 0%
where the time goes in v5:
time: 238 us; the launch traced here: 237 us
  waiting for transfers between devices  85.6 us (36%)
  local copies, waits for them, and re-layouts  55 us (23%)
  other arithmetic  39 us (16%)
  starting transfers between devices  32.1 us (13%)
  matrix products  23.9 us (10%)
    all_to_all x1, waiting for transfers between devices, per_device(): inbound = lax.all_to_all(outbound, ('req', 'seq'), 0, 0, tiled=True)  47.9 us
    all_to_all x1, waiting for transfers between devices, per_device(): back = lax.all_to_all(mixed, ('req', 'seq'), 0, 0, tiled=True)  33.1 us
    convert_element_type x2, local copies, waits for them, and re-layouts, per_device(): mixed = mixed.reshape(n_seq, n_req, chunk, width).astype(jnp.bfloat16)  18 us
    unnamed x14, other arithmetic  14.3 us
    dot_general x1, matrix products, per_device(): jnp.dot(normed, w_out, preferred_element_type=jnp.float32)  13.5 us
    ppermute x5, starting transfers between devices, from_behind(): lax.ppermute(value, axis, [(source, source + steps) for source in range(l...  12.6 us
    all_to_all x1, starting transfers between devices, per_device(): inbound = lax.all_to_all(outbound, ('req', 'seq'), 0, 0, tiled=True)  12 us
    convert_element_type x2, other arithmetic, causal_conv(): return jax.nn.silu(running).astype(jnp.bfloat16)  10.6 us
  transfers between devices with their start and end apart: 7, of which 3 were waited for; matrix products, arithmetic and copies ran while one was open for 7% of the time, Pallas kernels for 0%

profile of v5, /device:TPU:1, one launch (start us, length us, event | category | flops | bytes accessed | tf_op | source)
XLA Modules:
  0.0 236.7 jit_solution(2782362693071388390)
XLA Ops:
  0.6 5.7 %reshape.225 = bf16[32,16,4,640]{3,2,1,0:T(4,128)(2,1)} reshape(bf16[512,2560]{1,0:T(8,128)(2,1)} %param.12) | data formatting | bytes 5242880 | tf_op jit(solution)/shard_map/reshape | solution.py:142
  6.3 2.2 copy.86
  8.9 0.9 copy.87
  9.7 1.0 broadcast_in_dim.135
  10.8 2.4 pad_maximum_fusion
  13.2 12.0 %all-to-all-start = ((bf16[128,16,906]{2,1,0:T(8,128)(2,1)}), bf16[128,16,906]{2,1,0:T(8,128)(2,1)}, u32[]{:S(2)}, u32[]{:S(2)}) async-start(bf16[128,16,906]{2,1,0:T(8,128)(2,1)} %bitcast.245), calls=%async_computation | async-start | bytes 8388608 | tf_op jit(solution)/shard_map/all_to_all | solution.py:149
  25.8 0.8 dynamic_slice.15
  27.4 0.9 dynamic-slice_reduce_fusion.3
  29.2 0.8 fusion.80
  30.0 47.9 %all-to-all-done = bf16[128,16,906]{2,1,0:T(8,128)(2,1)} async-done(((bf16[128,16,906]{2,1,0:T(8,128)(2,1)}), bf16[128,16,906]{2,1,0:T(8,128)(2,1)}, u32[]{:S(2)}, u32[]{:S(2)}) %all-to-all-start) | async-done | bytes 3711008 | tf_op jit(solution)/shard_map/all_to_all | solution.py:149
  77.9 2.6 %copy.88 = bf16[4,32,16,906]{3,2,1,0:T(8,128)(2,1)S(1)} copy(bf16[4,32,16,906]{3,2,0,1:T(8,128)(2,1)} %bitcast.5) | data formatting | bytes 7421952 | tf_op jit(solution)/shard_map/transpose | solution.py:150
  80.7 1.8 copy-done
  83.0 4.6 %reduce-window.18 = f32[8,10,2,128]{3,1,2,0:T(8,128)S(1)} reduce-window(f32[8,10,2,128]{3,1,2,0:T(8,128)S(1)} %copy.91, f32[]{:T(128)} %constant.65.clone.1), window={size=1x1x1x128 pad=0_0x0_0x0_0x127_0}, to_apply=%region_2.3 | reduce-window | flops 2600960 | bytes 163844 | tf_op jit(solution)/shard_map/reduce-window.1
  88.6 2.5 %collective-permute-start.1 = (bf16[3,256]{1,0:T(4,128)(2,1)S(1)}, bf16[3,256]{1,0:T(4,128)(2,1)S(1)}, u32[]{:S(2)}, u32[]{:S(2)}) collective-permute-start(bf16[3,256]{1,0:T(4,128)(2,1)S(1)} %slice.282), channel_id=1, source_target_pairs={{0,4},{4,8},{8,12},{12,16},{16,20},{20,24},{24,28},{28,32},{32,36}... | collective-permute-start | bytes 4616 | tf_op jit(solution)/shard_map/ppermute | solution.py:13
  91.2 2.0 slice.277
  93.9 1.3 slice.283
  95.2 1.9 collective-permute-start
  97.2 4.6 %multiply_convert_fusion.7 = bf16[2048,256]{1,0:T(8,128)(2,1)} fusion(bf16[2048,256]{1,0:T(8,128)(2,1)S(1)} %slice.283, bf16[3,256]{1,0:T(4,128)(2,1)S(1)} %collective-permute-done.1, f32[256]{0:T(256)S(1)} %bitcast.262, f32[256]{0:T(256)S(1)} %bitcast.263, f32[256]{0:T(256)S(1)} %bitcast.261, f32[256]{0:T(256)S(1)} %bitcast.260, f32[256]{0:T(256)S(1)} %slice.220, ...), kind=kLoop, calls=%fused_computation.37 | loop fusion | flops 15728640 | bytes 2112000 | tf_op jit(solution)/shard_map/convert_element_type | solution.py:67
  101.8 6.0 %multiply_convert_fusion.3 = bf16[2048,640]{1,0:T(8,128)(2,1)S(1)} fusion(bf16[2048,640]{1,0:T(8,128)(2,1)S(1)} %slice.277, bf16[3,640]{1,0:T(4,128)(2,1)S(1)} %collective-permute-done, f32[640]{0:T(1024)S(1)} %get-tuple-element.13, f32[640]{0:T(1024)S(1)} %get-tuple-element.11, f32[640]{0:T(1024)S(1)} %get-tuple-element.12, f32[640]{0:T(1024)S(1)} %get-tuple-element.10, ...), kind=kLoop, calls=%fused_computation.23 | loop fusion | flops 39321600 | bytes 5267712 | tf_op jit(solution)/shard_map/convert_element_type | solution.py:67
  107.7 2.6 %copy.89 = bf16[2048,640]{0,1:T(8,128)(2,1)} copy(bf16[2048,640]{1,0:T(8,128)(2,1)S(1)} %multiply_convert_fusion.3) | data formatting | bytes 5242880 | tf_op jit(solution)/shard_map/convert_element_type | solution.py:67
  110.4 2.7 %copy.111 = bf16[80,8,8,256]{3,2,1,0:T(8,128)(2,1)S(1)} copy(bf16[80,8,8,256]{3,1,2,0:T(8,128)(2,1)} %bitcast.246) | data formatting | bytes 5242880
  113.1 0.9 fusion.16
  114.2 2.6 %collective-permute-start.3 = (f32[10,64,128]{2,1,0:T(8,128)S(1)}, f32[10,64,128]{2,1,0:T(8,128)S(1)}, u32[]{:S(2)}, u32[]{:S(2)}) collective-permute-start(f32[10,64,128]{2,1,0:T(8,128)S(1)} %multiply_add_fusion.7), channel_id=1, source_target_pairs={{0,8},{4,12},{8,16},{12,20},{16,24},{20,28},{24,32},{28,36},{32,40... | collective-permute-start | bytes 983048 | tf_op jit(solution)/shard_map/ppermute | solution.py:13
  116.8 3.5 %collective-permute-start.4 = (f32[10,64,128]{2,1,0:T(8,128)S(1)}, f32[10,64,128]{2,1,0:T(8,128)S(1)}, u32[]{:S(2)}, u32[]{:S(2)}) collective-permute-start(f32[10,64,128]{2,1,0:T(8,128)S(1)} %multiply_add_fusion.7), channel_id=1, source_target_pairs={{0,4},{4,8},{8,12},{12,16},{16,20},{20,24},{24,28},{28,32},{32,36}... | collective-permute-start | bytes 983048 | tf_op jit(solution)/shard_map/ppermute | solution.py:13
  120.6 2.1 collective-permute-start.2
  123.3 4.5 %collective-permute-done.2 = f32[10]{0:T(128)S(1)} collective-permute-done((f32[10]{0:T(128)S(1)}, f32[10]{0:T(128)S(1)}, u32[]{:S(2)}, u32[]{:S(2)}) %collective-permute-start.2) | collective-permute-done | bytes 72 | tf_op jit(solution)/shard_map/ppermute | solution.py:13
  127.8 0.8 bitcast_dynamic-update-slice_fusion.8
  128.6 1.4 bitcast_dynamic-update-slice_fusion.7
  130.6 1.3 bitcast_dynamic-update-slice_fusion.6
  132.6 1.3 bitcast_dynamic-update-slice_fusion.5
  134.5 1.3 bitcast_dynamic-update-slice_fusion.4
  136.5 1.4 bitcast_dynamic-update-slice_fusion.3
  138.6 1.3 bitcast_dynamic-update-slice_fusion.2
  139.9 0.7 fusion.44
  140.6 1.5 bitcast_dynamic-update-slice_fusion.1
  142.1 1.5 copy-done.4
  144.3 0.8 fusion.26
  145.1 8.3 %fusion.9 = bf16[8,256,10,64]{1,3,2,0:T(8,128)(2,1)S(1)} fusion(f32[8,256,10,64]{1,3,2,0:T(8,128)S(1)} %fusion.26, f32[10]{0:T(128)S(1)} %dynamic_slice.19, f32[8,256,10]{1,2,0:T(8,128)S(1)} %copy.99, f32[8,10,256]{2,1,0:T(8,128)S(1)} %copy.97, f32[8,10,256]{2,1,0:T(8,128)S(1)} %copy.95, f32[8,256,256]{2,1,0:T(8,128)S(1)} %fusion.29, ...), kind=kOutput, calls=%fused_computation.14 | convolution fusion | flops 710410240 | bytes 12894248 | tf_op jit(solution)/shard_map/chtu,cuhp->cthp/dot_general | solution.py:203
  153.4 8.5 %copy.104 = bf16[8,256,10,64]{3,2,1,0:T(8,128)(2,1)} copy(bf16[8,256,10,64]{1,3,2,0:T(8,128)(2,1)S(1)} %fusion.9) | data formatting | bytes 5242880 | tf_op jit(solution)/shard_map/convert_element_type | solution.py:220
  161.9 9.4 %convert_element_type.90 = bf16[4,32,16,640]{3,2,1,0:T(8,128)(2,1)S(1)} reshape(bf16[8,256,10,64]{3,2,1,0:T(8,128)(2,1)} %copy.104) | data formatting | bytes 5242880 | tf_op jit(solution)/shard_map/convert_element_type | solution.py:220
  171.4 1.9 copy.105
  173.3 7.6 %all-to-all-start.1 = ((bf16[128,16,640]{2,1,0:T(8,128)(2,1)}), bf16[128,16,640]{2,1,0:T(8,128)(2,1)S(1)}, u32[]{:S(2)}, u32[]{:S(2)}) async-start(bf16[128,16,640]{2,1,0:T(8,128)(2,1)} %bitcast.59), calls=%async_computation.1 | async-start | bytes 5242880 | tf_op jit(solution)/shard_map/all_to_all | solution.py:222
  180.9 3.0 %bitcast_dynamic-update-slice_fusion = f32[8,10,64,128]{3,2,1,0:T(8,128)} fusion(f32[8,10,64,128]{3,2,1,0:T(8,128)} %copy-done.4, f32[8,10,64,128]{3,2,1,0:T(8,128)} %copy-done.1, f32[10,64,128]{2,1,0:T(8,128)S(1)} %get-tuple-element.17, f32[10]{0:T(128)S(1)} %get-tuple-element.2, pred[]{:T(512)} %bitcast.76, pred[]{:T(512)} %bitcast.56), kind=kLoop, calls=%fused_computation.59 | loop fusion | flops 327680 | bytes 984104 | tf_op jit(solution)/shard_map/stack | solution.py:227
  183.9 33.1 %all-to-all-done.1 = bf16[128,16,640]{2,1,0:T(8,128)(2,1)S(1)} async-done(((bf16[128,16,640]{2,1,0:T(8,128)(2,1)}), bf16[128,16,640]{2,1,0:T(8,128)(2,1)S(1)}, u32[]{:S(2)}, u32[]{:S(2)}) %all-to-all-start.1) | async-done | bytes 2621472 | tf_op jit(solution)/shard_map/all_to_all | solution.py:222
  217.7 2.1 copy.106
  220.1 1.4 copy-done.3
  221.5 1.7 multiply_reduce_fusion
  223.3 13.5 %convolution_convert_fusion = bf16[512,2560]{1,0:T(8,128)(2,1)} fusion(bf16[2560,2560]{1,0:T(8,128)(2,1)} %param.22, f32[2560]{0:T(1024)S(1)} %copy-done.7, f32[512]{0:T(512)S(1)} %add_rsqrt_fusion, f32[512,2560]{1,0:T(8,128)S(1)} %bitcast.238, bf16[512,2560]{1,0:T(8,128)(2,1)S(1)} %copy-done.3), kind=kOutput, calls=%fused_computation.24 | convolution fusion | flops 6723993600 | bytes 23605248 | tf_op jit(solution)/shard_map/dot_general | solution.py:226
  (78 shorter events, 11.0 us)
Async XLA Ops:
  6.3 2.2 copy-start.5
  13.1 13.4 %copy-start.6 = (s32[64]{0:T(128)S(1)}, s32[64]{0:T(128)}, u32[]{:S(2)}) copy-start(s32[64]{0:T(128)} %param.23) | copy-start | bytes 772
  13.1 14.1 %copy-start.8 = (f32[40]{0:T(128)S(1)}, f32[40]{0:T(128)}, u32[]{:S(2)}) copy-start(f32[40]{0:T(128)} %param.18) | copy-start | bytes 484
  13.1 14.1 %copy-start.9 = (f32[40]{0:T(128)S(1)}, f32[40]{0:T(128)}, u32[]{:S(2)}) copy-start(f32[40]{0:T(128)} %param.20) | copy-start | bytes 484
  13.2 15.2 %copy-start.10 = (f32[40]{0:T(128)S(1)}, f32[40]{0:T(128)}, u32[]{:S(2)}) copy-start(f32[40]{0:T(128)} %param.19) | copy-start | bytes 484
  13.2 64.8 %all-to-all-start = ((bf16[128,16,906]{2,1,0:T(8,128)(2,1)}), bf16[128,16,906]{2,1,0:T(8,128)(2,1)}, u32[]{:S(2)}, u32[]{:S(2)}) async-start(bf16[128,16,906]{2,1,0:T(8,128)(2,1)} %bitcast.245), calls=%async_computation | async-start | bytes 8388608 | tf_op jit(solution)/shard_map/all_to_all | solution.py:149
  80.6 1.9 copy-start
  88.6 8.6 %collective-permute-start.1 = (bf16[3,256]{1,0:T(4,128)(2,1)S(1)}, bf16[3,256]{1,0:T(4,128)(2,1)S(1)}, u32[]{:S(2)}, u32[]{:S(2)}) collective-permute-start(bf16[3,256]{1,0:T(4,128)(2,1)S(1)} %slice.282), channel_id=1, source_target_pairs={{0,4},{4,8},{8,12},{12,16},{16,20},{20,24},{24,28},{28,32},{32,36}... | collective-permute-start | bytes 4616 | tf_op jit(solution)/shard_map/ppermute | solution.py:13
  95.2 6.5 %collective-permute-start = (bf16[3,640]{1,0:T(4,128)(2,1)S(1)}, bf16[3,640]{1,0:T(4,128)(2,1)S(1)}, u32[]{:S(2)}, u32[]{:S(2)}) collective-permute-start(bf16[3,640]{1,0:T(4,128)(2,1)S(1)} %slice.276), channel_id=1, source_target_pairs={{0,4},{4,8},{8,12},{12,16},{16,20},{20,24},{24,28},{28,32},{32,36}... | collective-permute-start | bytes 11528 | tf_op jit(solution)/shard_map/ppermute | solution.py:13
  110.4 2.7 %copy-start.2 = (bf16[2048,256]{1,0:T(8,128)(2,1)S(1)}, bf16[2048,256]{1,0:T(8,128)(2,1)}, u32[]{:S(2)}) copy-start(bf16[2048,256]{1,0:T(8,128)(2,1)} %multiply_convert_fusion.7) | copy-start | bytes 3145732
  113.9 26.7 %copy-start.1 = (f32[8,10,64,128]{3,2,1,0:T(8,128)}, f32[8,10,64,128]{3,2,1,0:T(8,128)S(1)}, u32[]{:S(2)}) copy-start(f32[8,10,64,128]{3,2,1,0:T(8,128)S(1)} %fusion.16) | copy-start | bytes 7864324
  114.2 13.6 %collective-permute-start.3 = (f32[10,64,128]{2,1,0:T(8,128)S(1)}, f32[10,64,128]{2,1,0:T(8,128)S(1)}, u32[]{:S(2)}, u32[]{:S(2)}) collective-permute-start(f32[10,64,128]{2,1,0:T(8,128)S(1)} %multiply_add_fusion.7), channel_id=1, source_target_pairs={{0,8},{4,12},{8,16},{12,20},{16,24},{20,28},{24,32},{28,36},{32,40... | collective-permute-start | bytes 983048 | tf_op jit(solution)/shard_map/ppermute | solution.py:13
  116.8 11.0 %collective-permute-start.4 = (f32[10,64,128]{2,1,0:T(8,128)S(1)}, f32[10,64,128]{2,1,0:T(8,128)S(1)}, u32[]{:S(2)}, u32[]{:S(2)}) collective-permute-start(f32[10,64,128]{2,1,0:T(8,128)S(1)} %multiply_add_fusion.7), channel_id=1, source_target_pairs={{0,4},{4,8},{8,12},{12,16},{16,20},{20,24},{24,28},{28,32},{32,36}... | collective-permute-start | bytes 983048 | tf_op jit(solution)/shard_map/ppermute | solution.py:13
  120.6 7.1 %collective-permute-start.2 = (f32[10]{0:T(128)S(1)}, f32[10]{0:T(128)S(1)}, u32[]{:S(2)}, u32[]{:S(2)}) collective-permute-start(f32[10]{0:T(128)S(1)} %get-tuple-element.38), channel_id=1, source_target_pairs={{0,4},{4,8},{8,12},{12,16},{16,20},{20,24},{24,28},{28,32},{32,36}... | collective-permute-start | bytes 128 | tf_op jit(solution)/shard_map/ppermute | solution.py:13
  142.1 1.5 copy-start.4
  173.3 43.7 %all-to-all-start.1 = ((bf16[128,16,640]{2,1,0:T(8,128)(2,1)}), bf16[128,16,640]{2,1,0:T(8,128)(2,1)S(1)}, u32[]{:S(2)}, u32[]{:S(2)}) async-start(bf16[128,16,640]{2,1,0:T(8,128)(2,1)} %bitcast.59), calls=%async_computation.1 | async-start | bytes 5242880 | tf_op jit(solution)/shard_map/all_to_all | solution.py:222
  219.8 1.7 copy-start.3
  221.5 1.8 copy-start.7

commit v6 on v5

--- a/solution.py
+++ b/solution.py
@@ -139,15 +139,12 @@
     group = lax.axis_index("seq")
     block = lax.axis_index("req")
 
-    x_parts = x_in.reshape(n_req, chunk, n_seq, width)
-    dt_parts = dt_raw.reshape(n_req, chunk, n_seq, share)
-    bc_parts = jnp.broadcast_to(
-        bc_in.reshape(n_req, chunk, 1, bc_width), (n_req, chunk, n_seq, bc_width)
-    )
-    outbound = jnp.concatenate([x_parts, bc_parts, dt_parts], axis=3)
-    outbound = outbound.transpose(0, 2, 1, 3).reshape(n_req * n_seq, chunk, -1)
-    inbound = lax.all_to_all(outbound, ("req", "seq"), 0, 0, tiled=True)
-    inbound = inbound.reshape(n_req, n_seq, chunk, -1).transpose(1, 0, 2, 3)
+    x_slabs = jnp.stack([x_in[:, g * width : (g + 1) * width] for g in range(n_seq)], axis=0)
+    dt_slabs = jnp.stack([dt_raw[:, g * share : (g + 1) * share] for g in range(n_seq)], axis=0)
+    bc_slabs = jnp.broadcast_to(bc_in[None], (n_seq, tok_rows, bc_width))
+    outbound = jnp.concatenate([x_slabs, bc_slabs, dt_slabs], axis=2)
+    outbound = outbound.reshape(n_seq * n_req, chunk, -1)
+    inbound = lax.all_to_all(outbound, ("seq", "req"), 0, 0, tiled=True)
     inbound = inbound.reshape(n_seq * tok_rows, -1)
     x_rows = inbound[:, :width]
     bc_rows = inbound[:, width : width + bc_width]
@@ -213,15 +210,25 @@
         ending_parts.append(jnp.where(finals[stretch], state_out, jnp.zeros_like(state_out)))
         state_prev = state_out
     state_low = jnp.stack(state_ins, axis=0).astype(jnp.bfloat16)
-    y_off = jnp.exp(log_decay)[..., None] * jnp.einsum(
-        "ctn,chpn->cthp", c_mat, state_low, preferred_element_type=jnp.float32
-    )
-    mixed = y_diag + y_off + skip[None, None, :, None] * x_heads.astype(jnp.float32)
-    mixed = mixed.reshape(n_seq, n_req, chunk, width).astype(jnp.bfloat16)
-    mixed = mixed.transpose(1, 0, 2, 3).reshape(n_req * n_seq, chunk, width)
-    back = lax.all_to_all(mixed, ("req", "seq"), 0, 0, tiled=True)
-    back = back.reshape(n_req, n_seq, chunk, width).transpose(0, 2, 1, 3)
-    mixed_tokens = back.reshape(tok_rows, inner_width)
+    state_low = state_low.reshape(stretch_count, width, N)
+    y_off = jnp.repeat(jnp.exp(log_decay), head_dim, axis=-1) * jnp.einsum(
+        "ctn,cqn->ctq", c_mat, state_low, preferred_element_type=jnp.float32
+    )
+    y_diag = jnp.concatenate(
+        [
+            jnp.einsum(
+                "ctu,cup->ctp", mixing[:, h], x_heads[:, :, h], preferred_element_type=jnp.float32
+            )
+            for h in range(share)
+        ],
+        axis=-1,
+    )
+    x_flat = conv_x.reshape(stretch_count, STRETCH, width).astype(jnp.float32)
+    mixed = y_diag + y_off + jnp.repeat(skip, head_dim)[None, None, :] * x_flat
+    mixed = mixed.astype(jnp.bfloat16).reshape(n_seq * n_req, chunk, width)
+    back = lax.all_to_all(mixed, ("seq", "req"), 0, 0, tiled=True)
+    back = back.reshape(n_seq, tok_rows, width)
+    mixed_tokens = jnp.concatenate([back[g] for g in range(n_seq)], axis=1)
     normed = gate_and_norm(mixed_tokens, z_in, norm_gain)
     mixed_out = jnp.dot(normed, w_out, preferred_element_type=jnp.float32).astype(jnp.bfloat16)
     return (mixed_out, jnp.stack(ending_parts, axis=0))

time: 238 us -> 220 us (0.924)
  local copies, waits for them, and re-layouts: 55 us -> 34.8 us
  other arithmetic: 39 us -> 46.4 us
  waiting for transfers between devices: 85.6 us -> 81.2 us
    convert_element_type x3 -> x2, local copies, waits for them, and re-layouts: 20 us -> 7.61 us  [the longest x1 4.41 us: per_device(): mixed = mixed.astype(jnp.bfloat16).reshape(n_seq * n_req, chunk, width)]
    reshape x4 -> x0, local copies, waits for them, and re-layouts: 9.09 us -> none  [the longest x2 7.95 us: per_device(): x_parts = x_in.reshape(n_req, chunk, n_seq, width)]
    convert_element_type x1 -> x2, other arithmetic: 0.64 us -> 7.77 us  [the longest x1 7.29 us: per_device(): mixing = (scores[:, None] * decay_mask * step_size.transpose(0, 2, 1)[:,...]
    transpose x3 -> x0, local copies, waits for them, and re-layouts: 4.57 us -> none  [the longest x1 2.63 us: per_device(): inbound = inbound.reshape(n_req, n_seq, chunk, -1).transpose(1, 0, 2, 3)]
    another operation x7 -> x15, other arithmetic: 5.69 us -> 10.2 us
    ppermute x5, waiting for transfers between devices: 4.48 us -> 0.01 us  [from_behind(): lax.ppermute(value, axis, [(source, source + steps) for source in range(l...]
    another operation x6 -> x9, local copies, waits for them, and re-layouts: 0.22 us -> 3.3 us  [the longest x1 1.92 us: per_device(): jnp.stack([x_in[:, g * width:(g + 1) * width] for g in range(n_seq)], axi...]
    unnamed x14 -> x9, other arithmetic: 14.3 us -> 11.4 us
  transfers between devices with their start and end apart: 7 -> 7, of which waited for: 3 -> 2; matrix products, arithmetic and copies ran while one was open for 7% -> 21% of each run, Pallas kernels for 0% -> 0%
where the time goes in v6:
time: 220 us; the launch traced here: 219 us
  waiting for transfers between devices  81.2 us (37%)
  other arithmetic  46.4 us (21%)
  local copies, waits for them, and re-layouts  34.8 us (16%)
  starting transfers between devices  31.2 us (14%)
  matrix products  24.4 us (11%)
    all_to_all x1, waiting for transfers between devices, per_device(): inbound = lax.all_to_all(outbound, ('seq', 'req'), 0, 0, tiled=True)  47.6 us
    all_to_all x1, waiting for transfers between devices, per_device(): back = lax.all_to_all(mixed, ('seq', 'req'), 0, 0, tiled=True)  33.7 us
    dot_general x1, matrix products, per_device(): jnp.dot(normed, w_out, preferred_element_type=jnp.float32)  13.8 us
    ppermute x5, starting transfers between devices, from_behind(): lax.ppermute(value, axis, [(source, source + steps) for source in range(l...  12.7 us
    all_to_all x1, starting transfers between devices, per_device(): inbound = lax.all_to_all(outbound, ('seq', 'req'), 0, 0, tiled=True)  12 us
    unnamed x9, other arithmetic  11.4 us
    another operation x14, other arithmetic  10.2 us
    convert_element_type x2, other arithmetic, causal_conv(): return jax.nn.silu(running).astype(jnp.bfloat16)  9.14 us
  transfers between devices with their start and end apart: 7, of which 2 were waited for; matrix products, arithmetic and copies ran while one was open for 21% of the time, Pallas kernels for 0%

profile of v6, /device:TPU:1, one launch (start us, length us, event | category | flops | bytes accessed | tf_op | source)
XLA Modules:
  0.0 219.3 jit_solution(11047734494180563551)
XLA Ops:
  0.6 0.9 slice_bitcast_fusion.35
  1.8 1.9 slice_bitcast_fusion.23
  3.8 2.3 %pad_maximum_fusion = bf16[4,512,906]{2,1,0:T(8,128)(2,1)} fusion(bf16[4,512,10]{2,1,0:T(8,128)(2,1)S(1)} %copy.127, bf16[4,512,256]{2,1,0:T(8,128)(2,1)S(1)} %broadcast_in_dim.137, bf16[1,512,640]{2,1,0:T(8,128)(2,1)S(1)} %get-tuple-element.48, bf16[1,512,640]{2,1,0:T(8,128)(2,1)S(1)} %get-tuple-element.49, bf16[1,512,640]{2,1,0:T(8,128)(2,1)S(1)} %get-tuple-element.47, ...), kind=kLoop, calls=%fused_computation.16 | loop fusion | flops 22265856 | bytes 7421952 | tf_op jit(solution)/shard_map/concatenate | solution.py:145
  6.2 12.0 %all-to-all-start = ((bf16[128,16,906]{2,1,0:T(8,128)(2,1)}), bf16[128,16,906]{2,1,0:T(8,128)(2,1)}, u32[]{:S(2)}, u32[]{:S(2)}) async-start(bf16[128,16,906]{2,1,0:T(8,128)(2,1)} %bitcast.301), calls=%async_computation | async-start | bytes 8388608 | tf_op jit(solution)/shard_map/all_to_all | solution.py:147
  18.2 0.7 slice.311
  19.5 0.8 dynamic_slice.17
  20.5 0.9 dynamic-slice_reduce_fusion.3
  21.6 0.7 fusion.58
  22.3 0.8 fusion.57
  23.2 47.6 %all-to-all-done = bf16[128,16,906]{2,1,0:T(8,128)(2,1)} async-done(((bf16[128,16,906]{2,1,0:T(8,128)(2,1)}), bf16[128,16,906]{2,1,0:T(8,128)(2,1)}, u32[]{:S(2)}, u32[]{:S(2)}) %all-to-all-start) | async-done | bytes 3711008 | tf_op jit(solution)/shard_map/all_to_all | solution.py:147
  70.7 1.1 slice.416
  73.0 4.6 %reduce-window.18 = f32[8,10,2,128]{3,1,2,0:T(8,128)S(1)} reduce-window(f32[8,10,2,128]{3,1,2,0:T(8,128)S(1)} %copy.129, f32[]{:T(128)} %constant.62.clone.1), window={size=1x1x1x128 pad=0_0x0_0x0_0x127_0}, to_apply=%region_2.3 | reduce-window | flops 2600960 | bytes 163844 | tf_op jit(solution)/shard_map/reduce-window.1
  78.7 3.1 %collective-permute-start = (bf16[3,256]{1,0:T(4,128)(2,1)S(1)}, bf16[3,256]{1,0:T(4,128)(2,1)S(1)}, u32[]{:S(2)}, u32[]{:S(2)}) collective-permute-start(bf16[3,256]{1,0:T(4,128)(2,1)S(1)} %slice.408), channel_id=1, source_target_pairs={{0,4},{4,8},{8,12},{12,16},{16,20},{20,24},{24,28},{28,32},{32,36}... | collective-permute-start | bytes 4616 | tf_op jit(solution)/shard_map/ppermute | solution.py:13
  82.1 1.3 slice.409
  83.4 2.0 slice.421
  85.4 0.7 slice.420
  86.1 1.9 collective-permute-start.1
  88.1 2.2 collective-permute-start.2
  90.3 3.2 %multiply_convert_fusion.5 = bf16[2048,256]{1,0:T(8,128)(2,1)S(1)} fusion(bf16[2048,256]{1,0:T(8,128)(2,1)S(1)} %slice.409, bf16[3,256]{1,0:T(4,128)(2,1)S(1)} %collective-permute-done, f32[256]{0:T(256)S(1)} %bitcast.333, f32[256]{0:T(256)S(1)} %bitcast.331, f32[256]{0:T(256)S(1)} %bitcast.332, f32[256]{0:T(256)S(1)} %bitcast.330, f32[256]{0:T(256)S(1)} %slice.311, ...), kind=kLoop, calls=%fused_computation.26 | loop fusion | flops 15728640 | bytes 2112000 | tf_op jit(solution)/shard_map/convert_element_type | solution.py:67
  93.4 1.0 copy-done.2
  94.8 7.3 %multiply_convert_fusion = bf16[8,10,256,256]{3,2,0,1:T(8,128)(2,1)} fusion(f32[8,10,256]{2,0,1:T(8,128)S(1)} %get-tuple-element.51, f32[8,10,256]{2,0,1:T(8,128)S(1)} %bitcast.317, f32[8,256,256]{2,1,0:T(8,128)S(1)} %fusion.17, pred[256,256]{1,0:T(8,128)(4,1)S(1)} %iota_compare_fusion), kind=kLoop, calls=%fused_computation | loop fusion | flops 31457280 | bytes 12812288 | tf_op jit(solution)/shard_map/convert_element_type | solution.py:199
  102.1 6.0 %multiply_convert_fusion.3 = bf16[2048,640]{1,0:T(8,128)(2,1)S(1)} fusion(bf16[2048,640]{1,0:T(8,128)(2,1)S(1)} %slice.421, bf16[3,640]{1,0:T(4,128)(2,1)S(1)} %collective-permute-done.1, f32[640]{0:T(1024)S(1)} %get-tuple-element.13, f32[640]{0:T(1024)S(1)} %get-tuple-element.11, f32[640]{0:T(1024)S(1)} %get-tuple-element.12, ...), kind=kLoop, calls=%fused_computation.14 | loop fusion | flops 39321600 | bytes 5267712 | tf_op jit(solution)/shard_map/convert_element_type | solution.py:67
  108.1 2.6 %copy.133 = bf16[2048,640]{0,1:T(8,128)(2,1)} copy(bf16[2048,640]{1,0:T(8,128)(2,1)S(1)} %multiply_convert_fusion.3) | data formatting | bytes 5242880 | tf_op jit(solution)/shard_map/convert_element_type | solution.py:67
  110.7 2.8 %copy.166 = bf16[80,8,8,256]{3,2,1,0:T(8,128)(2,1)S(1)} copy(bf16[80,8,8,256]{3,1,2,0:T(8,128)(2,1)} %bitcast.305) | data formatting | bytes 5242880
  113.5 0.9 fusion.56
  114.9 0.8 fusion.9
  115.8 1.0 multiply_add_fusion.7
  116.8 2.0 collective-permute-start.4
  118.8 3.5 %collective-permute-start.3 = (f32[10,64,128]{2,1,0:T(8,128)}, f32[10,64,128]{2,1,0:T(8,128)S(1)}, u32[]{:S(2)}, u32[]{:S(2)}) collective-permute-start(f32[10,64,128]{2,1,0:T(8,128)} %multiply_add_fusion.7), channel_id=1, source_target_pairs={{0,8},{4,12},{8,16},{12,20},{16,24},{20,28},{24,32},{28,36},{32,40... | collective-permute-start | bytes 983048 | tf_op jit(solution)/shard_map/ppermute | solution.py:13
  126.4 2.2 %copy-done.5 = f32[8,256,640]{1,2,0:T(8,128)} copy-done((f32[8,256,640]{1,2,0:T(8,128)}, f32[8,256,640]{1,2,0:T(8,128)S(1)}, u32[]{:S(2)}) %copy-start.5) | copy-done | bytes 5242904
  128.6 3.2 %copy.149 = f32[8,256,640]{1,2,0:T(8,128)} copy(bf16[8,256,640]{2,1,0:T(8,128)(2,1)S(1)} %bitcast.298) | data formatting | bytes 7864320 | tf_op jit(solution)/shard_map/convert_element_type | solution.py:226
  131.8 2.7 %convolution_dynamic-update-slice_fusion = f32[8,256,640]{1,2,0:T(8,128)} fusion(f32[8,256,640]{1,2,0:T(8,128)} %copy-done.5, bf16[8,10,256,256]{3,2,0,1:T(8,128)(2,1)} %multiply_convert_fusion, bf16[8,256,1,64]{1,0,3,2:T(8,128)(2,1)} %get-tuple-element.36), kind=kOutput, calls=%fused_computation.29 | convolution fusion | flops 67108864 | bytes 1835008 | tf_op jit(solution)/shard_map/ctu,cup->ctp/dot_general | solution.py:219
  135.2 2.7 %bitcast_dynamic-update-slice_fusion.7 = (f32[8,10,64,128]{3,2,1,0:T(8,128)S(1)}, f32[10,64,128]{2,1,0:T(8,128)S(1)}) fusion(pred[]{:T(512)} %bitcast.86, f32[8,10,64,128]{3,2,1,0:T(8,128)} %copy-done, f32[10,64,128]{2,1,0:T(8,128)S(1)} %collective-permute-done.4, f32[10,64,128]{2,1,0:T(8,128)S(1)} %collective-permute-done.3, ...), kind=kLoop, calls=%fused_computation.78 | loop fusion | flops 491519 | bytes 1638482
  138.7 1.3 bitcast_dynamic-update-slice_fusion.6
  140.7 1.9 bitcast_dynamic-update-slice_fusion.5
  143.3 1.4 bitcast_dynamic-update-slice_fusion.4
  145.4 1.4 bitcast_dynamic-update-slice_fusion.3
  147.5 1.3 bitcast_dynamic-update-slice_fusion.2
  149.4 1.3 bitcast_dynamic-update-slice_fusion.1
  151.5 0.8 copy-done.9
  152.3 2.7 %fusion.6 = bf16[8,256,640]{1,2,0:T(8,128)(2,1)} fusion(f32[8,256,640]{1,2,0:T(8,128)S(1)} %copy-done.6, f32[8,256,640]{1,2,0:T(8,128)S(1)} %bitcast.300, f32[640]{0:T(1024)S(1)} %mul.410, f32[8,256,10]{1,2,0:T(8,128)S(1)} %copy.144, bf16[8,640,128]{2,1,0:T(8,128)(2,1)S(1)} %bitcast_dynamic-update-slice_fusion.8, bf16[8,256,256]{2,1,0:T(8,128)(2,1)S(1)} %bitcast.308), kind=kOutput, calls=%fused_computation.10 | convolution fusion | flops 342097920 | bytes 15077376 | tf_op jit(solution)/shard_map/ctn,cqn->ctq/dot_general | solution.py:214
  155.0 4.4 %copy.150 = bf16[8,256,640]{2,1,0:T(8,128)(2,1)} copy(bf16[8,256,640]{1,2,0:T(8,128)(2,1)} %fusion.6) | data formatting | bytes 5242880 | tf_op jit(solution)/shard_map/convert_element_type | solution.py:228
  159.4 6.5 %all-to-all-start.1 = ((bf16[128,16,640]{2,1,0:T(8,128)(2,1)}), bf16[128,16,640]{2,1,0:T(8,128)(2,1)}, u32[]{:S(2)}, u32[]{:S(2)}) async-start(bf16[128,16,640]{2,1,0:T(8,128)(2,1)} %bitcast.304), calls=%async_computation.1 | async-start | bytes 5242880 | tf_op jit(solution)/shard_map/all_to_all | solution.py:229
  165.9 2.1 bitcast_dynamic-update-slice_fusion
  168.0 33.7 %all-to-all-done.1 = bf16[128,16,640]{2,1,0:T(8,128)(2,1)} async-done(((bf16[128,16,640]{2,1,0:T(8,128)(2,1)}), bf16[128,16,640]{2,1,0:T(8,128)(2,1)}, u32[]{:S(2)}, u32[]{:S(2)}) %all-to-all-start.1) | async-done | bytes 2621472 | tf_op jit(solution)/shard_map/all_to_all | solution.py:229
  201.7 1.9 fusion.55
  203.6 1.9 multiply_reduce_fusion
  205.5 13.8 %convolution_convert_fusion = bf16[512,2560]{1,0:T(8,128)(2,1)} fusion(bf16[2560,2560]{1,0:T(8,128)(2,1)} %param.22, f32[2560]{0:T(1024)S(1)} %copy-done.11, f32[512]{0:T(512)S(1)} %add_rsqrt_fusion, bf16[512,2560]{1,0:T(8,128)(2,1)S(1)} %copy-done.7, bf16[512,640]{1,0:T(8,128)(2,1)S(1)} %bitcast.312, bf16[512,640]{1,0:T(8,128)(2,1)S(1)} %bitcast.314, ...), kind=kOutput, calls=%fused_computation.15 | convolution fusion | flops 6734479360 | bytes 20983808 | tf_op jit(solution)/shard_map/dot_general | solution.py:233
  (113 shorter events, 14.3 us)
Async XLA Ops:
  0.6 3.1 %copy-start.8 = (bf16[512,256]{1,0:T(8,128)(2,1)S(1)}, bf16[512,256]{1,0:T(8,128)(2,1)}, u32[]{:S(2)}) copy-start(bf16[512,256]{1,0:T(8,128)(2,1)} %param.13) | copy-start | bytes 786436
  6.2 12.7 %copy-start.10 = (s32[64]{0:T(128)S(1)}, s32[64]{0:T(128)}, u32[]{:S(2)}) copy-start(s32[64]{0:T(128)} %param.23) | copy-start | bytes 772
  6.2 14.1 %copy-start.12 = (f32[40]{0:T(128)S(1)}, f32[40]{0:T(128)}, u32[]{:S(2)}) copy-start(f32[40]{0:T(128)} %param.18) | copy-start | bytes 484
  6.2 14.1 %copy-start.13 = (f32[40]{0:T(128)S(1)}, f32[40]{0:T(128)}, u32[]{:S(2)}) copy-start(f32[40]{0:T(128)} %param.20) | copy-start | bytes 484
  6.2 15.3 %copy-start.14 = (f32[40]{0:T(128)S(1)}, f32[40]{0:T(128)}, u32[]{:S(2)}) copy-start(f32[40]{0:T(128)} %param.19) | copy-start | bytes 484
  6.2 64.5 %all-to-all-start = ((bf16[128,16,906]{2,1,0:T(8,128)(2,1)}), bf16[128,16,906]{2,1,0:T(8,128)(2,1)}, u32[]{:S(2)}, u32[]{:S(2)}) async-start(bf16[128,16,906]{2,1,0:T(8,128)(2,1)} %bitcast.301), calls=%async_computation | async-start | bytes 8388608 | tf_op jit(solution)/shard_map/all_to_all | solution.py:147
  78.7 11.6 %collective-permute-start = (bf16[3,256]{1,0:T(4,128)(2,1)S(1)}, bf16[3,256]{1,0:T(4,128)(2,1)S(1)}, u32[]{:S(2)}, u32[]{:S(2)}) collective-permute-start(bf16[3,256]{1,0:T(4,128)(2,1)S(1)} %slice.408), channel_id=1, source_target_pairs={{0,4},{4,8},{8,12},{12,16},{16,20},{20,24},{24,28},{28,32},{32,36}... | collective-permute-start | bytes 4616 | tf_op jit(solution)/shard_map/ppermute | solution.py:13
  86.1 16.0 %collective-permute-start.1 = (bf16[3,640]{1,0:T(4,128)(2,1)S(1)}, bf16[3,640]{1,0:T(4,128)(2,1)S(1)}, u32[]{:S(2)}, u32[]{:S(2)}) collective-permute-start(bf16[3,640]{1,0:T(4,128)(2,1)S(1)} %slice.420), channel_id=1, source_target_pairs={{0,4},{4,8},{8,12},{12,16},{16,20},{20,24},{24,28},{28,32},{32,36}... | collective-permute-start | bytes 11528 | tf_op jit(solution)/shard_map/ppermute | solution.py:13
  88.1 46.4 %collective-permute-start.2 = (f32[10]{0:T(128)S(1)}, f32[10]{0:T(128)S(1)}, u32[]{:S(2)}, u32[]{:S(2)}) collective-permute-start(f32[10]{0:T(128)S(1)} %get-tuple-element.60), channel_id=1, source_target_pairs={{0,4},{4,8},{8,12},{12,16},{16,20},{20,24},{24,28},{28,32},{32,36}... | collective-permute-start | bytes 128 | tf_op jit(solution)/shard_map/ppermute | solution.py:13
  93.4 1.0 copy-start.2
  110.7 11.6 %slice-start.2 = ((s8[10485760]{0:T(1024)(128)(4,1)}), s8[2097152]{0:T(1024)(128)(4,1)S(1)}, s32[]{:S(2)}) async-start(s8[10485760]{0:T(1024)(128)(4,1)} %bitcast.302), calls=%async_computation.4 | async-start | bytes 4194304
  113.5 1.4 copy-start.3
  113.5 8.9 %slice-start.3 = ((s8[10485760]{0:T(1024)(128)(4,1)}), s8[4194304]{0:T(1024)(128)(4,1)S(1)}, s32[]{:S(2)}) async-start(s8[10485760]{0:T(1024)(128)(4,1)} %bitcast.302), calls=%async_computation.5 | async-start | bytes 8388608
  114.9 7.5 %slice-start.4 = ((s8[10485760]{0:T(1024)(128)(4,1)}), s8[4194304]{0:T(1024)(128)(4,1)S(1)}, s32[]{:S(2)}) async-start(s8[10485760]{0:T(1024)(128)(4,1)} %bitcast.302), calls=%async_computation.6 | async-start | bytes 8388608
  115.8 8.4 %copy-start = (f32[8,10,64,128]{3,2,1,0:T(8,128)}, f32[8,10,64,128]{3,2,1,0:T(8,128)S(1)}, u32[]{:S(2)}) copy-start(f32[8,10,64,128]{3,2,1,0:T(8,128)S(1)} %fusion.9) | copy-start | bytes 7864324
  116.8 17.7 %collective-permute-start.4 = (f32[10,64,128]{2,1,0:T(8,128)}, f32[10,64,128]{2,1,0:T(8,128)S(1)}, u32[]{:S(2)}, u32[]{:S(2)}) collective-permute-start(f32[10,64,128]{2,1,0:T(8,128)} %multiply_add_fusion.7), channel_id=1, source_target_pairs={{0,4},{4,8},{8,12},{12,16},{16,20},{20,24},{24,28},{28,32},{32,36}... | collective-permute-start | bytes 983048 | tf_op jit(solution)/shard_map/ppermute | solution.py:13
  118.8 15.7 %collective-permute-start.3 = (f32[10,64,128]{2,1,0:T(8,128)}, f32[10,64,128]{2,1,0:T(8,128)S(1)}, u32[]{:S(2)}, u32[]{:S(2)}) collective-permute-start(f32[10,64,128]{2,1,0:T(8,128)} %multiply_add_fusion.7), channel_id=1, source_target_pairs={{0,8},{4,12},{8,16},{12,20},{16,24},{20,28},{24,32},{28,36},{32,40... | collective-permute-start | bytes 983048 | tf_op jit(solution)/shard_map/ppermute | solution.py:13
  126.4 2.2 %copy-start.5 = (f32[8,256,640]{1,2,0:T(8,128)}, f32[8,256,640]{1,2,0:T(8,128)S(1)}, u32[]{:S(2)}) copy-start(f32[8,256,640]{1,2,0:T(8,128)S(1)} %convolution_dynamic-update-slice_fusion.1) | copy-start | bytes 15728644
  131.8 6.8 %copy-start.1 = (f32[8,10,64,128]{3,2,1,0:T(8,128)S(1)}, f32[8,10,64,128]{3,2,1,0:T(8,128)}, u32[]{:S(2)}) copy-start(f32[8,10,64,128]{3,2,1,0:T(8,128)} %copy-done) | copy-start | bytes 7864324
  135.2 17.0 %slice-start = ((s8[5242880]{0:T(1024)(128)(4,1)}), s8[4194304]{0:T(1024)(128)(4,1)S(1)}, s32[]{:S(2)}) async-start(s8[5242880]{0:T(1024)(128)(4,1)} %bitcast.299), calls=%async_computation.2 | async-start | bytes 8388608
  140.6 11.6 %copy-start.4 = (bf16[2048,256]{1,0:T(8,128)(2,1)S(1)}, bf16[2048,256]{1,0:T(8,128)(2,1)}, u32[]{:S(2)}) copy-start(bf16[2048,256]{1,0:T(8,128)(2,1)} %copy-done.2) | copy-start | bytes 3145732
  140.7 11.6 %copy-start.6 = (f32[8,256,640]{1,2,0:T(8,128)S(1)}, f32[8,256,640]{1,2,0:T(8,128)}, u32[]{:S(2)}) copy-start(f32[8,256,640]{1,2,0:T(8,128)} %convolution_dynamic-update-slice_fusion) | copy-start | bytes 15728644
  143.3 9.0 %slice-start.1 = ((s8[5242880]{0:T(1024)(128)(4,1)}), s8[1048576]{0:T(1024)(128)(4,1)S(1)}, s32[]{:S(2)}) async-start(s8[5242880]{0:T(1024)(128)(4,1)} %bitcast.299), calls=%async_computation.3 | async-start | bytes 2097152
  150.7 1.5 copy-start.9
  159.4 42.3 %all-to-all-start.1 = ((bf16[128,16,640]{2,1,0:T(8,128)(2,1)}), bf16[128,16,640]{2,1,0:T(8,128)(2,1)}, u32[]{:S(2)}, u32[]{:S(2)}) async-start(bf16[128,16,640]{2,1,0:T(8,128)(2,1)} %bitcast.304), calls=%async_computation.1 | async-start | bytes 5242880 | tf_op jit(solution)/shard_map/all_to_all | solution.py:229
  168.0 35.6 %copy-start.7 = (bf16[512,2560]{1,0:T(8,128)(2,1)S(1)}, bf16[512,2560]{1,0:T(8,128)(2,1)}, u32[]{:S(2)}) copy-start(bf16[512,2560]{1,0:T(8,128)(2,1)} %param.14) | copy-start | bytes 7864324
  168.0 37.5 %copy-start.11 = (f32[2560]{0:T(1024)S(1)}, f32[2560]{0:T(1024)}, u32[]{:S(2)}) copy-start(f32[2560]{0:T(1024)} %param.21) | copy-start | bytes 30724

commit v7 on v6

--- a/solution.py
+++ b/solution.py
@@ -199,16 +199,25 @@
     ).astype(jnp.bfloat16)
     y_diag = jnp.einsum("chtu,cuhp->cthp", mixing, x_heads, preferred_element_type=jnp.float32)
 
-    state_ins = []
-    ending_parts = []
+    keep = jnp.where(starts, 0.0, 1.0)
+    gains = jnp.exp(log_decay[:, -1, :])
+    rows = []
+    weights = [jnp.zeros((share,), jnp.float32)] * stretch_count + [jnp.ones((share,), jnp.float32)]
     for stretch in range(stretch_count):
-        state_in = jnp.where(starts[stretch], jnp.zeros_like(state_prev), state_prev)
-        state_ins.append(state_in)
-        state_out = (
-            jnp.exp(log_decay[stretch, -1])[:, None, None] * state_in + stretch_state[stretch]
-        )
-        ending_parts.append(jnp.where(finals[stretch], state_out, jnp.zeros_like(state_out)))
-        state_prev = state_out
+        if stretch > 0:
+            weights = [w * gains[stretch - 1] for w in weights]
+            weights[stretch - 1] = weights[stretch - 1] + 1.0
+        weights = [w * keep[stretch] for w in weights]
+        rows.append(jnp.stack(weights, axis=0))
+    mix = jnp.stack(rows, axis=0)
+    sources = jnp.concatenate([stretch_state, state_prev[None]], axis=0)
+    state_in_all = jnp.einsum(
+        "ckh,khpn->chpn", mix, sources, precision=lax.Precision.HIGHEST,
+        preferred_element_type=jnp.float32,
+    )
+    state_out_all = gains[:, :, None, None] * state_in_all + stretch_state
+    endings = jnp.where(finals[:, None, None, None], state_out_all, 0.0)
+    state_ins = [state_in_all[c] for c in range(stretch_count)]
     state_low = jnp.stack(state_ins, axis=0).astype(jnp.bfloat16)
     state_low = state_low.reshape(stretch_count, width, N)
     y_off = jnp.repeat(jnp.exp(log_decay), head_dim, axis=-1) * jnp.einsum(
@@ -231,7 +240,7 @@
     mixed_tokens = jnp.concatenate([back[g] for g in range(n_seq)], axis=1)
     normed = gate_and_norm(mixed_tokens, z_in, norm_gain)
     mixed_out = jnp.dot(normed, w_out, preferred_element_type=jnp.float32).astype(jnp.bfloat16)
-    return (mixed_out, jnp.stack(ending_parts, axis=0))
+    return (mixed_out, endings)
 
 
 def solution(mesh):

time: 220 us -> 239 us (1.086)
  other arithmetic: 46.4 us -> 55.8 us
  matrix products: 24.4 us -> 30.5 us
  local copies, waits for them, and re-layouts: 34.8 us -> 40.4 us
  waiting for transfers between devices: 81.2 us -> 77.9 us
    mul x0 -> x6, other arithmetic: none -> 23.8 us  [per_device(): weights = [w * keep[stretch] for w in weights]]
    unnamed x9 -> x3, other arithmetic: 11.4 us -> 0.01 us
    another operation x15 -> x6, other arithmetic: 12.2 us -> 5.03 us
    dot_general x0 -> x1, matrix products: none -> 6.24 us  [per_device(): jnp.einsum('ckh,khpn->chpn', mix, sources, precision=lax.Precision.HIGHES...]
    select_n x1 -> x2, other arithmetic: 0.07 us -> 3.93 us  [the longest x1 3.93 us: per_device(): endings = jnp.where(finals[:, None, None, None], state_out_all, 0.0)]
    unnamed x50 -> x45, local copies, waits for them, and re-layouts: 7.25 us -> 7.41 us
  transfers between devices with their start and end apart: 7 -> 7, of which waited for: 2 -> 2; matrix products, arithmetic and copies ran while one was open for 21% -> 24% of each run, Pallas kernels for 0% -> 0%
where the time goes in v7:
time: 239 us; the launch traced here: 238 us
  waiting for transfers between devices  77.9 us (33%)
  other arithmetic  55.8 us (23%)
  local copies, waits for them, and re-layouts  40.4 us (17%)
  starting transfers between devices  31.1 us (13%)
  matrix products  30.5 us (13%)
    all_to_all x1, waiting for transfers between devices, per_device(): inbound = lax.all_to_all(outbound, ('seq', 'req'), 0, 0, tiled=True)  46.1 us
    all_to_all x1, waiting for transfers between devices, per_device(): back = lax.all_to_all(mixed, ('seq', 'req'), 0, 0, tiled=True)  31.8 us
    mul x6, other arithmetic, per_device(): weights = [w * keep[stretch] for w in weights]  23.8 us
    dot_general x1, matrix products, per_device(): jnp.dot(normed, w_out, preferred_element_type=jnp.float32)  13.8 us
    ppermute x5, starting transfers between devices, from_behind(): lax.ppermute(value, axis, [(source, source + steps) for source in range(l...  12.6 us
    all_to_all x1, starting transfers between devices, per_device(): inbound = lax.all_to_all(outbound, ('seq', 'req'), 0, 0, tiled=True)  12 us
    convert_element_type x2, other arithmetic, causal_conv(): return jax.nn.silu(running).astype(jnp.bfloat16)  9.1 us
    unnamed x45, local copies, waits for them, and re-layouts  7.41 us
  transfers between devices with their start and end apart: 7, of which 2 were waited for; matrix products, arithmetic and copies ran while one was open for 24% of the time, Pallas kernels for 0%

profile of v7, /device:TPU:1, one launch (start us, length us, event | category | flops | bytes accessed | tf_op | source)
XLA Modules:
  0.0 237.6 jit_solution(10740968753257977385)
XLA Ops:
  0.6 0.9 slice_bitcast_fusion.35
  1.8 1.9 slice_bitcast_fusion.23
  3.8 2.4 %pad_maximum_fusion = bf16[4,512,906]{2,1,0:T(8,128)(2,1)} fusion(bf16[4,512,10]{2,1,0:T(8,128)(2,1)S(1)} %copy.142, bf16[4,512,256]{2,1,0:T(8,128)(2,1)S(1)} %broadcast_in_dim.157, bf16[1,512,640]{2,1,0:T(8,128)(2,1)S(1)} %get-tuple-element.67, bf16[1,512,640]{2,1,0:T(8,128)(2,1)S(1)} %get-tuple-element.68, bf16[1,512,640]{2,1,0:T(8,128)(2,1)S(1)} %get-tuple-element.66, ...), kind=kLoop, calls=%fused_computation.18 | loop fusion | flops 22265856 | bytes 7421952 | tf_op jit(solution)/shard_map/concatenate | solution.py:145
  6.2 12.0 %all-to-all-start = ((bf16[128,16,906]{2,1,0:T(8,128)(2,1)}), bf16[128,16,906]{2,1,0:T(8,128)(2,1)}, u32[]{:S(2)}, u32[]{:S(2)}) async-start(bf16[128,16,906]{2,1,0:T(8,128)(2,1)} %bitcast.282), calls=%async_computation | async-start | bytes 8388608 | tf_op jit(solution)/shard_map/all_to_all | solution.py:147
  18.2 0.7 slice.189
  19.5 0.8 dynamic_slice.17
  20.6 0.7 fusion.68
  22.7 0.9 dynamic-slice_reduce_fusion.3
  23.8 0.8 fusion.67
  24.7 46.1 %all-to-all-done = bf16[128,16,906]{2,1,0:T(8,128)(2,1)} async-done(((bf16[128,16,906]{2,1,0:T(8,128)(2,1)}), bf16[128,16,906]{2,1,0:T(8,128)(2,1)}, u32[]{:S(2)}, u32[]{:S(2)}) %all-to-all-start) | async-done | bytes 3711008 | tf_op jit(solution)/shard_map/all_to_all | solution.py:147
  70.8 1.1 slice.502
  72.3 4.6 %reduce-window.18 = f32[8,10,2,128]{3,1,2,0:T(8,128)S(1)} reduce-window(f32[8,10,2,128]{3,1,2,0:T(8,128)S(1)} %copy.144, f32[]{:T(128)} %constant.65.clone.1), window={size=1x1x1x128 pad=0_0x0_0x0_0x127_0}, to_apply=%region_2.3 | reduce-window | flops 2600960 | bytes 163844 | tf_op jit(solution)/shard_map/reduce-window.1
  77.5 1.3 slice.495
  78.8 0.7 slice.494
  79.5 3.5 %slice.507 = bf16[2048,640]{1,0:T(8,128)(2,1)} slice(bf16[2048,906]{1,0:T(8,128)(2,1)} %bitcast.11), slice={[0:2048], [0:640]} | slice | bytes 5242880 | tf_op jit(solution)/shard_map/slice | solution.py:149
  82.9 0.7 slice.506
  84.1 4.5 %multiply_multiply_fusion.6 = (f32[1,10]{1,0:T(1,128)S(1)}, f32[1,10]{1,0:T(1,128)S(1)}, f32[1,10]{1,0:T(1,128)S(1)}, f32[1,10]{1,0:T(1,128)S(1)}, f32[1,10]{1,0...) fusion(f32[]{:T(128)} %bitcast.79, f32[8,10]{1,0:T(8,128)S(1)} %get-tuple-element.92, f32[]{:T(128)} %bitcast.77, ...), kind=kLoop, calls=%fused_computation.158 | loop fusion | flops 150 | bytes 592 | tf_op jit(solution)/shard_map/mul | solution.py:210
  88.6 4.5 %broadcast_multiply_fusion = (f32[1,10]{1,0:T(1,128)S(1)}, f32[1,10]{1,0:T(1,128)S(1)}, f32[1,10]{1,0:T(1,128)S(1)}, f32[1,10]{1,0:T(1,128)S(1)}, f32[1,10]{1,0:...) fusion(f32[]{:T(128)} %bitcast.79, f32[8,10]{1,0:T(8,128)S(1)} %get-tuple-element.92, f32[]{:T(128)} %bitcast.77, ...), kind=kLoop, calls=%fused_computation.198 | loop fusion | flops 140 | bytes 592 | tf_op jit(solution)/shard_map/mul | solution.py:210
  93.1 5.1 %multiply_multiply_fusion = (f32[1,10]{1,0:T(1,128)S(1)}, f32[1,10]{1,0:T(1,128)S(1)}, f32[1,10]{1,0:T(1,128)S(1)}, f32[1,10]{1,0:T(1,128)S(1)}, f32[1,10]{1,0:T...) fusion(f32[]{:T(128)} %bitcast.79, f32[8,10]{1,0:T(8,128)S(1)} %get-tuple-element.92, f32[]{:T(128)} %bitcast.77, ...), kind=kLoop, calls=%fused_computation.151 | loop fusion | flops 140 | bytes 592 | tf_op jit(solution)/shard_map/mul | solution.py:210
  98.3 3.1 %collective-permute-start = (bf16[3,256]{1,0:T(4,128)(2,1)S(1)}, bf16[3,256]{1,0:T(4,128)(2,1)S(1)}, u32[]{:S(2)}, u32[]{:S(2)}) collective-permute-start(bf16[3,256]{1,0:T(4,128)(2,1)S(1)} %slice.494), channel_id=1, source_target_pairs={{0,4},{4,8},{8,12},{12,16},{16,20},{20,24},{24,28},{28,32},{32,36}... | collective-permute-start | bytes 4616 | tf_op jit(solution)/shard_map/ppermute | solution.py:13
  101.4 1.9 collective-permute-start.1
  103.4 2.2 collective-permute-start.2
  105.7 3.8 %multiply_multiply_fusion.1 = (f32[1,10]{1,0:T(1,128)S(1)}, f32[1,10]{1,0:T(1,128)S(1)}, f32[1,10]{1,0:T(1,128)S(1)}, f32[1,10]{1,0:T(1,128)S(1)}, f32[1,10]{1,0...) fusion(f32[]{:T(128)} %bitcast.79, ...), kind=kLoop, calls=%fused_computation.153 | loop fusion | flops 210 | bytes 744 | tf_op jit(solution)/shard_map/mul | solution.py:210
  109.7 3.3 %multiply_multiply_fusion.2 = (f32[1,10]{1,0:T(1,128)S(1)}, f32[1,10]{1,0:T(1,128)S(1)}, f32[1,10]{1,0:T(1,128)S(1)}, f32[1,10]{1,0:T(1,128)S(1)}, f32[1,10]{1,0...) fusion(f32[]{:T(128)} %bitcast.79, f32[8,10]{1,0:T(8,128)S(1)} %get-tuple-element.92, ...), kind=kLoop, calls=%fused_computation.154 | loop fusion | flops 180 | bytes 620 | tf_op jit(solution)/shard_map/mul | solution.py:210
  112.9 2.6 %multiply_multiply_fusion.3 = (f32[1,10]{1,0:T(1,128)S(1)}, f32[1,10]{1,0:T(1,128)S(1)}, f32[1,10]{1,0:T(1,128)S(1)}, f32[1,10]{1,0:T(1,128)S(1)}) fusion(f32[]{:T(128)} %bitcast.79, f32[8,10]{1,0:T(8,128)S(1)} %get-tuple-element.92, f32[]{:T(128)} %bitcast.77, f32[]{:T(128)} %bitcast.75, f32[]{:T(128)} %bitcast.73, f32[1,10]{1,0:T(1,128)S(1)} %get-tuple-element.21), kind=kLoop, calls=%fused_computation.155 | loop fusion | flops 90 | bytes 376 | tf_op jit(solution)/shard_map/mul | solution.py:210
  116.3 3.2 %multiply_convert_fusion.5 = bf16[2048,256]{1,0:T(8,128)(2,1)S(1)} fusion(bf16[2048,256]{1,0:T(8,128)(2,1)S(1)} %slice.495, bf16[3,256]{1,0:T(4,128)(2,1)S(1)} %collective-permute-done, f32[256]{0:T(256)S(1)} %bitcast.317, f32[256]{0:T(256)S(1)} %bitcast.315, f32[256]{0:T(256)S(1)} %bitcast.316, f32[256]{0:T(256)S(1)} %bitcast.314, f32[256]{0:T(256)S(1)} %slice.189, ...), kind=kLoop, calls=%fused_computation.33 | loop fusion | flops 15728640 | bytes 2112000 | tf_op jit(solution)/shard_map/convert_element_type | solution.py:67
  120.5 7.2 %multiply_convert_fusion = bf16[8,10,256,256]{3,2,0,1:T(8,128)(2,1)} fusion(f32[8,10,256]{2,0,1:T(8,128)S(1)} %get-tuple-element.70, f32[8,10,256]{2,0,1:T(8,128)S(1)} %bitcast.301, f32[8,256,256]{2,1,0:T(8,128)S(1)} %fusion.21, pred[256,256]{1,0:T(8,128)(4,1)S(1)} %iota_compare_fusion), kind=kLoop, calls=%fused_computation | loop fusion | flops 31457280 | bytes 12812288 | tf_op jit(solution)/shard_map/convert_element_type | solution.py:199
  127.7 5.9 %multiply_convert_fusion.3 = bf16[2048,640]{1,0:T(8,128)(2,1)S(1)} fusion(bf16[2048,640]{1,0:T(8,128)(2,1)S(1)} %copy-done.2, bf16[3,640]{1,0:T(4,128)(2,1)S(1)} %collective-permute-done.1, f32[640]{0:T(1024)S(1)} %get-tuple-element.5, f32[640]{0:T(1024)S(1)} %get-tuple-element.3, f32[640]{0:T(1024)S(1)} %get-tuple-element.4, f32[640]{0:T(1024)S(1)} %get-tuple-element.2, ...), kind=kLoop, calls=%fused_computation.16 | loop fusion | flops 39321600 | bytes 5267712 | tf_op jit(solution)/shard_map/convert_element_type | solution.py:67
  133.6 3.0 %copy.148 = bf16[2048,640]{0,1:T(8,128)(2,1)} copy(bf16[2048,640]{1,0:T(8,128)(2,1)S(1)} %multiply_convert_fusion.3) | data formatting | bytes 5242880 | tf_op jit(solution)/shard_map/convert_element_type | solution.py:67
  136.6 2.8 %copy.192 = bf16[80,8,8,256]{3,2,1,0:T(8,128)(2,1)S(1)} copy(bf16[80,8,8,256]{3,1,2,0:T(8,128)(2,1)} %bitcast.286) | data formatting | bytes 5242880
  139.4 0.9 fusion.66
  140.8 0.8 fusion.13
  141.7 1.0 fusion.26
  142.6 1.9 collective-permute-start.4
  144.6 3.5 %collective-permute-start.3 = (f32[10,64,128]{2,1,0:T(8,128)}, f32[10,64,128]{2,1,0:T(8,128)S(1)}, u32[]{:S(2)}, u32[]{:S(2)}) collective-permute-start(f32[10,64,128]{2,1,0:T(8,128)} %fusion.26), channel_id=1, source_target_pairs={{0,8},{4,12},{8,16},{12,20},{16,24},{20,28},{24,32},{28,36},{32,40... | collective-permute-start | bytes 983048 | tf_op jit(solution)/shard_map/ppermute | solution.py:13
  152.1 2.3 copy-done.6
  154.4 4.9 %copy.174 = f32[8,256,640]{1,2,0:T(8,128)} copy(bf16[8,256,640]{2,1,0:T(8,128)(2,1)} %bitcast.279) | data formatting | bytes 7864320 | tf_op jit(solution)/shard_map/convert_element_type | solution.py:235
  159.3 2.5 %convolution_dynamic-update-slice_fusion = f32[8,256,640]{1,2,0:T(8,128)} fusion(f32[8,256,640]{1,2,0:T(8,128)} %copy-done.6, bf16[8,10,256,256]{3,2,0,1:T(8,128)(2,1)} %multiply_convert_fusion, bf16[8,256,1,64]{1,0,3,2:T(8,128)(2,1)} %get-tuple-element.55), kind=kOutput, calls=%fused_computation.36 | convolution fusion | flops 67108864 | bytes 1835008 | tf_op jit(solution)/shard_map/ctu,cup->ctp/dot_general | solution.py:228
  162.3 6.2 %fusion.7 = f32[10,64,128,8]{2,3,1,0:T(8,128)S(1)} fusion(f32[9,10,64,128]{3,2,1,0:T(8,128)S(1)} %pad_maximum_fusion.1, f32[8,9,10]{1,0,2:T(8,128)S(1)} %stack.87), kind=kOutput, calls=%fused_computation.11 | convolution fusion | flops 70778880 | bytes 5573440 | tf_op jit(solution)/shard_map/ckh,khpn->chpn/dot_general | solution.py:214
  168.6 1.5 copy-done
  170.6 2.7 %fusion.6 = bf16[8,256,640]{1,2,0:T(8,128)(2,1)} fusion(f32[8,256,640]{1,2,0:T(8,128)S(1)} %bitcast.291, f32[8,256,640]{1,2,0:T(8,128)S(1)} %bitcast.281, f32[640]{0:T(1024)S(1)} %mul.1182, f32[8,256,10]{1,2,0:T(8,128)S(1)} %copy.159, bf16[8,640,128]{2,1,0:T(8,128)(2,1)S(1)} %bitcast.292, bf16[8,256,256]{2,1,0:T(8,128)(2,1)S(1)} %bitcast.289), kind=kOutput, calls=%fused_computation.10 | convolution fusion | flops 342097920 | bytes 15077376 | tf_op jit(solution)/shard_map/ctn,cqn->ctq/dot_general | solution.py:223
  173.3 4.4 %copy.175 = bf16[8,256,640]{2,1,0:T(8,128)(2,1)} copy(bf16[8,256,640]{1,2,0:T(8,128)(2,1)} %fusion.6) | data formatting | bytes 5242880 | tf_op jit(solution)/shard_map/convert_element_type | solution.py:237
  177.7 6.5 %all-to-all-start.1 = ((bf16[128,16,640]{2,1,0:T(8,128)(2,1)}), bf16[128,16,640]{2,1,0:T(8,128)(2,1)}, u32[]{:S(2)}, u32[]{:S(2)}) async-start(bf16[128,16,640]{2,1,0:T(8,128)(2,1)} %bitcast.285), calls=%async_computation.1 | async-start | bytes 5242880 | tf_op jit(solution)/shard_map/all_to_all | solution.py:238
  184.3 3.9 %fusion.12 = f32[8,10,64,128]{3,2,1,0:T(8,128)} fusion(f32[8,10,64,128]{3,2,1,0:T(8,128)S(1)} %fusion.13, f32[10,64,128,8]{2,3,1,0:T(8,128)} %copy-done, f32[8,10]{1,0:T(8,128)S(1)} %get-tuple-element.92, pred[8]{0:T(512)(128)(4,1)S(1)} %get-tuple-element.6), kind=kLoop, calls=%fused_computation.28 | loop fusion | flops 1966080 | bytes 7864648 | tf_op jit(solution)/shard_map/jit(_where)/select_n | solution.py:219
  188.2 31.8 %all-to-all-done.1 = bf16[128,16,640]{2,1,0:T(8,128)(2,1)} async-done(((bf16[128,16,640]{2,1,0:T(8,128)(2,1)}), bf16[128,16,640]{2,1,0:T(8,128)(2,1)}, u32[]{:S(2)}, u32[]{:S(2)}) %all-to-all-start.1) | async-done | bytes 2621472 | tf_op jit(solution)/shard_map/all_to_all | solution.py:238
  220.0 1.9 fusion.65
  221.9 1.9 multiply_reduce_fusion
  223.8 13.8 %convolution_convert_fusion = bf16[512,2560]{1,0:T(8,128)(2,1)} fusion(bf16[2560,2560]{1,0:T(8,128)(2,1)} %param.22, f32[2560]{0:T(1024)S(1)} %copy-done.10, f32[512]{0:T(512)S(1)} %add_rsqrt_fusion, bf16[512,2560]{1,0:T(8,128)(2,1)S(1)} %copy-done.7, bf16[512,640]{1,0:T(8,128)(2,1)S(1)} %bitcast.296, bf16[512,640]{1,0:T(8,128)(2,1)S(1)} %bitcast.298, ...), kind=kOutput, calls=%fused_computation.17 | convolution fusion | flops 6734479360 | bytes 20983808 | tf_op jit(solution)/shard_map/dot_general | solution.py:242
  (122 shorter events, 11.3 us)
Async XLA Ops:
  0.6 3.1 %copy-start.8 = (bf16[512,256]{1,0:T(8,128)(2,1)S(1)}, bf16[512,256]{1,0:T(8,128)(2,1)}, u32[]{:S(2)}) copy-start(bf16[512,256]{1,0:T(8,128)(2,1)} %param.13) | copy-start | bytes 786436
  6.2 12.7 %copy-start.9 = (s32[64]{0:T(128)S(1)}, s32[64]{0:T(128)}, u32[]{:S(2)}) copy-start(s32[64]{0:T(128)} %param.23) | copy-start | bytes 772
  6.2 14.1 %copy-start.11 = (f32[40]{0:T(128)S(1)}, f32[40]{0:T(128)}, u32[]{:S(2)}) copy-start(f32[40]{0:T(128)} %param.18) | copy-start | bytes 484
  6.2 14.1 %copy-start.12 = (f32[40]{0:T(128)S(1)}, f32[40]{0:T(128)}, u32[]{:S(2)}) copy-start(f32[40]{0:T(128)} %param.20) | copy-start | bytes 484
  6.2 17.4 %copy-start.13 = (f32[40]{0:T(128)S(1)}, f32[40]{0:T(128)}, u32[]{:S(2)}) copy-start(f32[40]{0:T(128)} %param.19) | copy-start | bytes 484
  6.2 64.5 %all-to-all-start = ((bf16[128,16,906]{2,1,0:T(8,128)(2,1)}), bf16[128,16,906]{2,1,0:T(8,128)(2,1)}, u32[]{:S(2)}, u32[]{:S(2)}) async-start(bf16[128,16,906]{2,1,0:T(8,128)(2,1)} %bitcast.282), calls=%async_computation | async-start | bytes 8388608 | tf_op jit(solution)/shard_map/all_to_all | solution.py:147
  98.3 18.0 %collective-permute-start = (bf16[3,256]{1,0:T(4,128)(2,1)S(1)}, bf16[3,256]{1,0:T(4,128)(2,1)S(1)}, u32[]{:S(2)}, u32[]{:S(2)}) collective-permute-start(bf16[3,256]{1,0:T(4,128)(2,1)S(1)} %slice.494), channel_id=1, source_target_pairs={{0,4},{4,8},{8,12},{12,16},{16,20},{20,24},{24,28},{28,32},{32,36}... | collective-permute-start | bytes 4616 | tf_op jit(solution)/shard_map/ppermute | solution.py:13
  101.4 26.3 %collective-permute-start.1 = (bf16[3,640]{1,0:T(4,128)(2,1)S(1)}, bf16[3,640]{1,0:T(4,128)(2,1)S(1)}, u32[]{:S(2)}, u32[]{:S(2)}) collective-permute-start(bf16[3,640]{1,0:T(4,128)(2,1)S(1)} %slice.506), channel_id=1, source_target_pairs={{0,4},{4,8},{8,12},{12,16},{16,20},{20,24},{24,28},{28,32},{32,36}... | collective-permute-start | bytes 11528 | tf_op jit(solution)/shard_map/ppermute | solution.py:13
  103.4 58.4 %collective-permute-start.2 = (f32[10]{0:T(128)S(1)}, f32[10]{0:T(128)S(1)}, u32[]{:S(2)}, u32[]{:S(2)}) collective-permute-start(f32[10]{0:T(128)S(1)} %get-tuple-element.94), channel_id=1, source_target_pairs={{0,4},{4,8},{8,12},{12,16},{16,20},{20,24},{24,28},{28,32},{32,36}... | collective-permute-start | bytes 128 | tf_op jit(solution)/shard_map/ppermute | solution.py:13
  119.5 1.0 copy-start.3
  120.5 7.2 %copy-start.2 = (bf16[2048,640]{1,0:T(8,128)(2,1)S(1)}, bf16[2048,640]{1,0:T(8,128)(2,1)}, u32[]{:S(2)}) copy-start(bf16[2048,640]{1,0:T(8,128)(2,1)} %slice.507) | copy-start | bytes 7864324
  133.6 5.8 %copy-start.1 = (bf16[2048,640]{1,0:T(8,128)(2,1)}, bf16[2048,640]{1,0:T(8,128)(2,1)S(1)}, u32[]{:S(2)}) copy-start(bf16[2048,640]{1,0:T(8,128)(2,1)S(1)} %multiply_convert_fusion.3) | copy-start | bytes 7864324
  136.6 11.5 %slice-start.2 = ((s8[10485760]{0:T(1024)(128)(4,1)}), s8[2097152]{0:T(1024)(128)(4,1)S(1)}, s32[]{:S(2)}) async-start(s8[10485760]{0:T(1024)(128)(4,1)} %bitcast.283), calls=%async_computation.4 | async-start | bytes 4194304
  139.4 1.4 copy-start.4
  139.4 8.7 %slice-start.3 = ((s8[10485760]{0:T(1024)(128)(4,1)}), s8[4194304]{0:T(1024)(128)(4,1)S(1)}, s32[]{:S(2)}) async-start(s8[10485760]{0:T(1024)(128)(4,1)} %bitcast.283), calls=%async_computation.5 | async-start | bytes 8388608
  140.8 7.3 %slice-start.4 = ((s8[10485760]{0:T(1024)(128)(4,1)}), s8[4194304]{0:T(1024)(128)(4,1)S(1)}, s32[]{:S(2)}) async-start(s8[10485760]{0:T(1024)(128)(4,1)} %bitcast.283), calls=%async_computation.6 | async-start | bytes 8388608
  142.6 19.2 %collective-permute-start.4 = (f32[10,64,128]{2,1,0:T(8,128)}, f32[10,64,128]{2,1,0:T(8,128)S(1)}, u32[]{:S(2)}, u32[]{:S(2)}) collective-permute-start(f32[10,64,128]{2,1,0:T(8,128)} %fusion.26), channel_id=1, source_target_pairs={{0,4},{4,8},{8,12},{12,16},{16,20},{20,24},{24,28},{28,32},{32,36}... | collective-permute-start | bytes 983048 | tf_op jit(solution)/shard_map/ppermute | solution.py:13
  144.6 17.2 %collective-permute-start.3 = (f32[10,64,128]{2,1,0:T(8,128)}, f32[10,64,128]{2,1,0:T(8,128)S(1)}, u32[]{:S(2)}, u32[]{:S(2)}) collective-permute-start(f32[10,64,128]{2,1,0:T(8,128)} %fusion.26), channel_id=1, source_target_pairs={{0,8},{4,12},{8,16},{12,20},{16,24},{20,28},{24,32},{28,36},{32,40... | collective-permute-start | bytes 983048 | tf_op jit(solution)/shard_map/ppermute | solution.py:13
  152.1 2.3 copy-start.6
  161.9 8.7 %slice-start = ((s8[5242880]{0:T(1024)(128)(4,1)}), s8[4194304]{0:T(1024)(128)(4,1)S(1)}, s32[]{:S(2)}) async-start(s8[5242880]{0:T(1024)(128)(4,1)} %bitcast.280), calls=%async_computation.2 | async-start | bytes 8388608
  161.9 8.7 %slice-start.5 = ((s8[5242880]{0:T(1024)(128)(4,1)}), s8[4194304]{0:T(1024)(128)(4,1)S(1)}, s32[]{:S(2)}) async-start(s8[5242880]{0:T(1024)(128)(4,1)} %bitcast.290), calls=%async_computation.7 | async-start | bytes 8388608
  162.3 8.3 %slice-start.1 = ((s8[5242880]{0:T(1024)(128)(4,1)}), s8[1048576]{0:T(1024)(128)(4,1)S(1)}, s32[]{:S(2)}) async-start(s8[5242880]{0:T(1024)(128)(4,1)} %bitcast.280), calls=%async_computation.3 | async-start | bytes 2097152
  162.3 8.3 %copy-start.5 = (bf16[2048,256]{1,0:T(8,128)(2,1)S(1)}, bf16[2048,256]{1,0:T(8,128)(2,1)}, u32[]{:S(2)}) copy-start(bf16[2048,256]{1,0:T(8,128)(2,1)} %copy-done.3) | copy-start | bytes 3145732
  162.3 8.3 %slice-start.6 = ((s8[5242880]{0:T(1024)(128)(4,1)}), s8[1048576]{0:T(1024)(128)(4,1)S(1)}, s32[]{:S(2)}) async-start(s8[5242880]{0:T(1024)(128)(4,1)} %bitcast.290), calls=%async_computation.8 | async-start | bytes 2097152
  168.6 1.5 copy-start
  177.7 42.3 %all-to-all-start.1 = ((bf16[128,16,640]{2,1,0:T(8,128)(2,1)}), bf16[128,16,640]{2,1,0:T(8,128)(2,1)}, u32[]{:S(2)}, u32[]{:S(2)}) async-start(bf16[128,16,640]{2,1,0:T(8,128)(2,1)} %bitcast.285), calls=%async_computation.1 | async-start | bytes 5242880 | tf_op jit(solution)/shard_map/all_to_all | solution.py:238
  188.2 33.7 %copy-start.7 = (bf16[512,2560]{1,0:T(8,128)(2,1)S(1)}, bf16[512,2560]{1,0:T(8,128)(2,1)}, u32[]{:S(2)}) copy-start(bf16[512,2560]{1,0:T(8,128)(2,1)} %param.14) | copy-start | bytes 7864324
  188.2 35.6 %copy-start.10 = (f32[2560]{0:T(1024)S(1)}, f32[2560]{0:T(1024)}, u32[]{:S(2)}) copy-start(f32[2560]{0:T(1024)} %param.21) | copy-start | bytes 30724

commit v8 on v6

--- a/solution.py
+++ b/solution.py
@@ -211,24 +211,33 @@
         state_prev = state_out
     state_low = jnp.stack(state_ins, axis=0).astype(jnp.bfloat16)
     state_low = state_low.reshape(stretch_count, width, N)
-    y_off = jnp.repeat(jnp.exp(log_decay), head_dim, axis=-1) * jnp.einsum(
-        "ctn,cqn->ctq", c_mat, state_low, preferred_element_type=jnp.float32
-    )
-    y_diag = jnp.concatenate(
-        [
-            jnp.einsum(
-                "ctu,cup->ctp", mixing[:, h], x_heads[:, :, h], preferred_element_type=jnp.float32
-            )
-            for h in range(share)
-        ],
-        axis=-1,
-    )
-    x_flat = conv_x.reshape(stretch_count, STRETCH, width).astype(jnp.float32)
-    mixed = y_diag + y_off + jnp.repeat(skip, head_dim)[None, None, :] * x_flat
-    mixed = mixed.astype(jnp.bfloat16).reshape(n_seq * n_req, chunk, width)
-    back = lax.all_to_all(mixed, ("seq", "req"), 0, 0, tiled=True)
-    back = back.reshape(n_seq, tok_rows, width)
-    mixed_tokens = jnp.concatenate([back[g] for g in range(n_seq)], axis=1)
+    split = 4 if share > 4 else share
+    pieces = []
+    for lo, hi in ((0, split), (split, share)):
+        if lo == hi:
+            continue
+        cols = slice(lo * head_dim, hi * head_dim)
+        y_off = jnp.repeat(jnp.exp(log_decay[:, :, lo:hi]), head_dim, axis=-1) * jnp.einsum(
+            "ctn,cqn->ctq", c_mat, state_low[:, cols], preferred_element_type=jnp.float32
+        )
+        y_diag = jnp.concatenate(
+            [
+                jnp.einsum(
+                    "ctu,cup->ctp", mixing[:, h], x_heads[:, :, h],
+                    preferred_element_type=jnp.float32,
+                )
+                for h in range(lo, hi)
+            ],
+            axis=-1,
+        )
+        x_flat = conv_x.reshape(stretch_count, STRETCH, width)[:, :, cols].astype(jnp.float32)
+        mixed = y_diag + y_off + jnp.repeat(skip[lo:hi], head_dim)[None, None, :] * x_flat
+        mixed = mixed.astype(jnp.bfloat16).reshape(n_seq * n_req, chunk, (hi - lo) * head_dim)
+        back = lax.all_to_all(mixed, ("seq", "req"), 0, 0, tiled=True)
+        pieces.append(back.reshape(n_seq, tok_rows, (hi - lo) * head_dim))
+    mixed_tokens = jnp.concatenate(
+        [piece[g] for g in range(n_seq) for piece in pieces], axis=1
+    )
     normed = gate_and_norm(mixed_tokens, z_in, norm_gain)
     mixed_out = jnp.dot(normed, w_out, preferred_element_type=jnp.float32).astype(jnp.bfloat16)
     return (mixed_out, jnp.stack(ending_parts, axis=0))

time: 220 us -> 246 us (1.12)
  matrix products: 24.4 us -> 45.7 us
  waiting for transfers between devices: 81.2 us -> 70.7 us
  starting transfers between devices: 31.2 us -> 39.1 us
  local copies, waits for them, and re-layouts: 34.8 us -> 41.9 us
    dot_general x10, matrix products: 6.62 us -> 25.2 us  [per_device(): jnp.einsum('ctu,cup->ctp', mixing[:, h], x_heads[:, :, h], preferred_elem...]
    all_to_all x1 -> x2, waiting for transfers between devices: 33.7 us -> 23.4 us  [per_device(): back = lax.all_to_all(mixed, ('seq', 'req'), 0, 0, tiled=True)]
    all_to_all x1 -> x2, starting transfers between devices: 6.53 us -> 14.6 us  [per_device(): back = lax.all_to_all(mixed, ('seq', 'req'), 0, 0, tiled=True)]
    unnamed x50 -> x67, local copies, waits for them, and re-layouts: 7.25 us -> 13.3 us
    slice x3 -> x7, local copies, waits for them, and re-layouts: 2.2 us -> 5.49 us  [the longest x2 2.76 us: per_device(): piece[g]]
    convert_element_type x2, local copies, waits for them, and re-layouts: 7.61 us -> 4.88 us  [per_device(): mixed.astype(jnp.bfloat16)]
    dot_general x1 -> x2, matrix products: 2.72 us -> 5.38 us  [per_device(): jnp.einsum('ctn,cqn->ctq', c_mat, state_low[:, cols], preferred_element_t...]
    unnamed x9 -> x7, other arithmetic: 11.4 us -> 9.98 us
  transfers between devices with their start and end apart: 7 -> 8, of which waited for: 2 -> 3; matrix products, arithmetic and copies ran while one was open for 21% -> 31% of each run, Pallas kernels for 0% -> 0%
where the time goes in v8:
time: 246 us; the launch traced here: 244 us
  waiting for transfers between devices  70.7 us (29%)
  matrix products  45.7 us (19%)
  other arithmetic  45.3 us (18%)
  local copies, waits for them, and re-layouts  41.9 us (17%)
  starting transfers between devices  39.1 us (16%)
    all_to_all x1, waiting for transfers between devices, per_device(): inbound = lax.all_to_all(outbound, ('seq', 'req'), 0, 0, tiled=True)  47.3 us
    dot_general x10, matrix products, per_device(): jnp.einsum('ctu,cup->ctp', mixing[:, h], x_heads[:, :, h], preferred_elem...  25.2 us
    all_to_all x2, waiting for transfers between devices, per_device(): back = lax.all_to_all(mixed, ('seq', 'req'), 0, 0, tiled=True)  23.4 us
    all_to_all x2, starting transfers between devices, per_device(): back = lax.all_to_all(mixed, ('seq', 'req'), 0, 0, tiled=True)  14.6 us
    dot_general x1, matrix products, per_device(): jnp.dot(normed, w_out, preferred_element_type=jnp.float32)  13.8 us
    unnamed x67, local copies, waits for them, and re-layouts  13.3 us
    ppermute x5, starting transfers between devices, from_behind(): lax.ppermute(value, axis, [(source, source + steps) for source in range(l...  12.6 us
    all_to_all x1, starting transfers between devices, per_device(): inbound = lax.all_to_all(outbound, ('seq', 'req'), 0, 0, tiled=True)  12 us
  transfers between devices with their start and end apart: 8, of which 3 were waited for; matrix products, arithmetic and copies ran while one was open for 31% of the time, Pallas kernels for 0%

profile of v8, /device:TPU:1, one launch (start us, length us, event | category | flops | bytes accessed | tf_op | source)
XLA Modules:
  0.0 244.1 jit_solution(5714522452852409938)
XLA Ops:
  1.8 2.0 slice_bitcast_fusion.23
  3.9 2.3 pad_maximum_fusion
  6.2 12.0 %all-to-all-start = ((bf16[128,16,906]{2,1,0:T(8,128)(2,1)}), bf16[128,16,906]{2,1,0:T(8,128)(2,1)}, u32[]{:S(2)}, u32[]{:S(2)}) async-start(bf16[128,16,906]{2,1,0:T(8,128)(2,1)} %bitcast.307), calls=%async_computation | async-start | bytes 8388608 | tf_op jit(solution)/shard_map/all_to_all | solution.py:147
  23.5 47.3 %all-to-all-done = bf16[128,16,906]{2,1,0:T(8,128)(2,1)} async-done(((bf16[128,16,906]{2,1,0:T(8,128)(2,1)}), bf16[128,16,906]{2,1,0:T(8,128)(2,1)}, u32[]{:S(2)}, u32[]{:S(2)}) %all-to-all-start) | async-done | bytes 3711008 | tf_op jit(solution)/shard_map/all_to_all | solution.py:147
  73.7 4.6 %reduce-window.18 = f32[8,10,2,128]{3,1,2,0:T(8,128)S(1)} reduce-window(f32[8,10,2,128]{3,1,2,0:T(8,128)S(1)} %copy.147, f32[]{:T(128)} %constant.62.clone.1), window={size=1x1x1x128 pad=0_0x0_0x0_0x127_0}, to_apply=%region_2.3 | reduce-window | flops 2600960 | bytes 163844 | tf_op jit(solution)/shard_map/reduce-window.1
  79.6 2.0 slice.473
  81.6 3.1 %collective-permute-start = (bf16[3,256]{1,0:T(4,128)(2,1)S(1)}, bf16[3,256]{1,0:T(4,128)(2,1)S(1)}, u32[]{:S(2)}, u32[]{:S(2)}) collective-permute-start(bf16[3,256]{1,0:T(4,128)(2,1)S(1)} %slice.460), channel_id=1, source_target_pairs={{0,4},{4,8},{8,12},{12,16},{16,20},{20,24},{24,28},{28,32},{32,36}... | collective-permute-start | bytes 4616 | tf_op jit(solution)/shard_map/ppermute | solution.py:13
  84.7 1.9 collective-permute-start.1
  86.6 2.2 collective-permute-start.2
  90.3 3.2 %multiply_convert_fusion.5 = bf16[2048,256]{1,0:T(8,128)(2,1)S(1)} fusion(bf16[2048,256]{1,0:T(8,128)(2,1)S(1)} %slice.461, bf16[3,256]{1,0:T(4,128)(2,1)S(1)} %collective-permute-done, f32[256]{0:T(256)S(1)} %bitcast.344, f32[256]{0:T(256)S(1)} %bitcast.342, f32[256]{0:T(256)S(1)} %bitcast.343, f32[256]{0:T(256)S(1)} %bitcast.341, f32[256]{0:T(256)S(1)} %slice.351, ...), kind=kLoop, calls=%fused_computation.30 | loop fusion | flops 15728640 | bytes 2112000 | tf_op jit(solution)/shard_map/convert_element_type | solution.py:67
  94.9 7.3 %multiply_convert_fusion = bf16[8,10,256,256]{3,2,0,1:T(8,128)(2,1)} fusion(f32[8,10,256]{2,0,1:T(8,128)S(1)} %get-tuple-element.53, f32[8,10,256]{2,0,1:T(8,128)S(1)} %bitcast.320, f32[8,256,256]{2,1,0:T(8,128)S(1)} %fusion.28, pred[256,256]{1,0:T(8,128)(4,1)S(1)} %iota_compare_fusion), kind=kLoop, calls=%fused_computation | loop fusion | flops 31457280 | bytes 12812288 | tf_op jit(solution)/shard_map/convert_element_type | solution.py:199
  102.2 6.0 %multiply_convert_fusion.3 = bf16[2048,640]{1,0:T(8,128)(2,1)S(1)} fusion(bf16[2048,640]{1,0:T(8,128)(2,1)S(1)} %slice.473, bf16[3,640]{1,0:T(4,128)(2,1)S(1)} %collective-permute-done.1, f32[640]{0:T(1024)S(1)} %get-tuple-element.13, f32[640]{0:T(1024)S(1)} %get-tuple-element.11, f32[640]{0:T(1024)S(1)} %get-tuple-element.12, ...), kind=kLoop, calls=%fused_computation.10 | loop fusion | flops 39321600 | bytes 5267712 | tf_op jit(solution)/shard_map/convert_element_type | solution.py:67
  108.2 2.6 %copy.151 = bf16[2048,640]{0,1:T(8,128)(2,1)} copy(bf16[2048,640]{1,0:T(8,128)(2,1)S(1)} %multiply_convert_fusion.3) | data formatting | bytes 5242880 | tf_op jit(solution)/shard_map/convert_element_type | solution.py:67
  110.8 2.6 %copy.191 = bf16[80,8,8,256]{3,2,1,0:T(8,128)(2,1)S(1)} copy(bf16[80,8,8,256]{3,1,2,0:T(8,128)(2,1)} %bitcast.312) | data formatting | bytes 5242880
  117.8 1.9 collective-permute-start.4
  119.7 3.5 %collective-permute-start.3 = (f32[10,64,128]{2,1,0:T(8,128)}, f32[10,64,128]{2,1,0:T(8,128)S(1)}, u32[]{:S(2)}, u32[]{:S(2)}) collective-permute-start(f32[10,64,128]{2,1,0:T(8,128)} %multiply_add_fusion.7), channel_id=1, source_target_pairs={{0,8},{4,12},{8,16},{12,20},{16,24},{20,28},{24,32},{28,36},{32,40... | collective-permute-start | bytes 983048 | tf_op jit(solution)/shard_map/ppermute | solution.py:13
  123.3 2.5 %fusion.17 = f32[8,256,64]{1,2,0:T(8,128)} fusion(bf16[8,10,256,256]{3,2,0,1:T(8,128)(2,1)} %multiply_convert_fusion, bf16[8,256,1,64]{1,0,3,2:T(8,128)(2,1)S(1)} %get-tuple-element.36), kind=kOutput, calls=%fused_computation.48 | convolution fusion | flops 67108864 | bytes 1835008 | tf_op jit(solution)/shard_map/ctu,cup->ctp/dot_general | solution.py:225
  125.8 2.5 %fusion.18 = f32[8,256,64]{1,2,0:T(8,128)} fusion(bf16[8,10,256,256]{3,2,0,1:T(8,128)(2,1)} %multiply_convert_fusion, bf16[8,256,1,64]{1,0,3,2:T(8,128)(2,1)S(1)} %get-tuple-element.37), kind=kOutput, calls=%fused_computation.50 | convolution fusion | flops 67108864 | bytes 1835008 | tf_op jit(solution)/shard_map/ctu,cup->ctp/dot_general | solution.py:225
  128.2 2.5 %fusion.19 = f32[8,256,64]{1,2,0:T(8,128)} fusion(bf16[8,10,256,256]{3,2,0,1:T(8,128)(2,1)} %multiply_convert_fusion, bf16[8,256,1,64]{1,0,3,2:T(8,128)(2,1)S(1)} %get-tuple-element.38), kind=kOutput, calls=%fused_computation.52 | convolution fusion | flops 67108864 | bytes 1835008 | tf_op jit(solution)/shard_map/ctu,cup->ctp/dot_general | solution.py:225
  130.7 2.5 %fusion.20 = f32[8,256,64]{1,2,0:T(8,128)} fusion(bf16[8,10,256,256]{3,2,0,1:T(8,128)(2,1)} %multiply_convert_fusion, bf16[8,256,1,64]{1,0,3,2:T(8,128)(2,1)S(1)} %get-tuple-element.39), kind=kOutput, calls=%fused_computation.54 | convolution fusion | flops 67108864 | bytes 1835008 | tf_op jit(solution)/shard_map/ctu,cup->ctp/dot_general | solution.py:225
  133.2 2.5 %convolution_dynamic-update-slice_fusion.5 = f32[8,256,384]{1,2,0:T(8,128)} fusion(bf16[8,10,256,256]{3,2,0,1:T(8,128)(2,1)} %multiply_convert_fusion, bf16[8,256,1,64]{1,0,3,2:T(8,128)(2,1)S(1)} %get-tuple-element.35), kind=kOutput, calls=%fused_computation.38 | convolution fusion | flops 67108864 | bytes 1835008 | tf_op jit(solution)/shard_map/ctu,cup->ctp/dot_general | solution.py:225
  138.1 2.3 copy.182
  140.3 2.8 %copy.189 = bf16[8,256,384]{1,2,0:T(8,128)(2,1)} copy(bf16[8,256,384]{2,1,0:T(8,128)(2,1)} %slice.519) | data formatting | bytes 3145728
  143.1 2.6 %convolution_dynamic-update-slice_fusion.4 = f32[8,256,384]{1,2,0:T(8,128)} fusion(f32[8,256,384]{1,2,0:T(8,128)} %convolution_dynamic-update-slice_fusion.5, bf16[8,10,256,256]{3,2,0,1:T(8,128)(2,1)} %multiply_convert_fusion, bf16[8,256,1,64]{1,0,3,2:T(8,128)(2,1)} %get-tuple-element.34), kind=kOutput, calls=%fused_computation.37 | convolution fusion | flops 67108864 | bytes 1835008 | tf_op jit(solution)/shard_map/ctu,cup->ctp/dot_general | solution.py:225
  146.3 1.3 bitcast_dynamic-update-slice_fusion.7
  148.4 1.5 bitcast_dynamic-update-slice_fusion.6
  150.7 1.4 bitcast_dynamic-update-slice_fusion.5
  152.7 1.4 bitcast_dynamic-update-slice_fusion.4
  154.7 1.4 bitcast_dynamic-update-slice_fusion.3
  157.0 1.7 bitcast_dynamic-update-slice_fusion.2
  159.4 1.4 bitcast_dynamic-update-slice_fusion.1
  163.4 1.6 fusion.14
  164.9 2.3 copy.162
  167.2 6.6 %all-to-all-start.1 = ((bf16[128,16,256]{2,1,0:T(8,128)(2,1)}), bf16[128,16,256]{2,1,0:T(8,128)(2,1)}, u32[]{:S(2)}, u32[]{:S(2)}) async-start(bf16[128,16,256]{2,1,0:T(8,128)(2,1)} %bitcast.314), calls=%async_computation.1 | async-start | bytes 2097152 | tf_op jit(solution)/shard_map/all_to_all | solution.py:236
  173.8 2.6 %convolution_dynamic-update-slice_fusion.3 = f32[8,256,384]{1,2,0:T(8,128)} fusion(f32[8,256,384]{1,2,0:T(8,128)} %convolution_dynamic-update-slice_fusion.4, bf16[8,10,256,256]{3,2,0,1:T(8,128)(2,1)} %multiply_convert_fusion, bf16[8,256,1,64]{1,0,3,2:T(8,128)(2,1)} %get-tuple-element.33), kind=kOutput, calls=%fused_computation.36 | convolution fusion | flops 67108864 | bytes 1835008 | tf_op jit(solution)/shard_map/ctu,cup->ctp/dot_general | solution.py:225
  176.4 2.7 %convolution_dynamic-update-slice_fusion.2 = f32[8,256,384]{1,2,0:T(8,128)} fusion(f32[8,256,384]{1,2,0:T(8,128)} %convolution_dynamic-update-slice_fusion.3, bf16[8,10,256,256]{3,2,0,1:T(8,128)(2,1)} %multiply_convert_fusion, bf16[8,256,1,64]{1,0,3,2:T(8,128)(2,1)} %get-tuple-element.32), kind=kOutput, calls=%fused_computation.35 | convolution fusion | flops 67108864 | bytes 1835008 | tf_op jit(solution)/shard_map/ctu,cup->ctp/dot_general | solution.py:225
  179.1 2.5 %convolution_dynamic-update-slice_fusion.1 = f32[8,256,384]{1,2,0:T(8,128)} fusion(f32[8,256,384]{1,2,0:T(8,128)} %convolution_dynamic-update-slice_fusion.2, bf16[8,10,256,256]{3,2,0,1:T(8,128)(2,1)} %multiply_convert_fusion, bf16[8,256,1,64]{1,0,3,2:T(8,128)(2,1)S(1)} %copy-done.17), kind=kOutput, calls=%fused_computation.34 | convolution fusion | flops 67108864 | bytes 1835008 | tf_op jit(solution)/shard_map/ctu,cup->ctp/dot_general | solution.py:225
  181.6 2.5 %convolution_dynamic-update-slice_fusion = f32[8,256,384]{1,2,0:T(8,128)} fusion(f32[8,256,384]{1,2,0:T(8,128)} %convolution_dynamic-update-slice_fusion.1, bf16[8,10,256,256]{3,2,0,1:T(8,128)(2,1)} %multiply_convert_fusion, bf16[8,256,1,64]{1,0,3,2:T(8,128)(2,1)S(1)} %copy-done.16), kind=kOutput, calls=%fused_computation.33 | convolution fusion | flops 67108864 | bytes 1835008 | tf_op jit(solution)/shard_map/ctu,cup->ctp/dot_general | solution.py:225
  184.1 3.8 %fusion.6 = bf16[8,256,384]{1,2,0:T(8,128)(2,1)} fusion(f32[8,256,384]{1,2,0:T(8,128)} %convolution_dynamic-update-slice_fusion, bf16[8,256,384]{1,2,0:T(8,128)(2,1)S(1)} %copy-done.6, f32[384]{0:T(512)S(1)} %mul.427, f32[8,256,6]{1,2,0:T(8,128)S(1)} %copy.169, bf16[8,640,128]{2,1,0:T(8,128)(2,1)S(1)} %copy-done.10, bf16[8,256,256]{2,1,0:T(8,128)(2,1)S(1)} %bitcast.311), kind=kOutput, calls=%fused_computation.18 | convolution fusion | flops 206045184 | bytes 7669760 | tf_op jit(solution)/shard_map/ctn,cqn->ctq/dot_general | solution.py:220
  187.9 2.6 %copy.172 = bf16[8,256,384]{2,1,0:T(8,128)(2,1)} copy(bf16[8,256,384]{1,2,0:T(8,128)(2,1)} %fusion.6) | data formatting | bytes 3145728 | tf_op jit(solution)/shard_map/convert_element_type | solution.py:235
  190.5 2.2 all-to-all-done.1
  192.7 8.0 %all-to-all-start.2 = ((bf16[128,16,384]{2,1,0:T(8,128)(2,1)}), bf16[128,16,384]{2,1,0:T(8,128)(2,1)}, u32[]{:S(2)}, u32[]{:S(2)}) async-start(bf16[128,16,384]{2,1,0:T(8,128)(2,1)} %bitcast.313), calls=%async_computation.2 | async-start | bytes 3145728 | tf_op jit(solution)/shard_map/all_to_all | solution.py:236
  200.7 2.0 bitcast_dynamic-update-slice_fusion
  204.0 21.2 %all-to-all-done.2 = bf16[128,16,384]{2,1,0:T(8,128)(2,1)} async-done(((bf16[128,16,384]{2,1,0:T(8,128)(2,1)}), bf16[128,16,384]{2,1,0:T(8,128)(2,1)}, u32[]{:S(2)}, u32[]{:S(2)}) %all-to-all-start.2) | async-done | bytes 1572896 | tf_op jit(solution)/shard_map/all_to_all | solution.py:236
  225.2 1.5 fusion.66
  227.1 1.4 copy-done.8
  228.5 1.8 multiply_reduce_fusion
  230.3 13.8 %convolution_convert_fusion = bf16[512,2560]{1,0:T(8,128)(2,1)} fusion(bf16[2560,2560]{1,0:T(8,128)(2,1)} %param.22, f32[2560]{0:T(1024)S(1)} %copy-done.20, f32[512]{0:T(512)S(1)} %add_rsqrt_fusion, bf16[512,2560]{1,0:T(8,128)(2,1)S(1)} %copy-done.8, bf16[512,2560]{1,0:T(8,128)(2,1)S(1)} %constant_dynamic-update-slice_fusion), kind=kOutput, calls=%fused_computation.11 | convolution fusion | flops 6725304320 | bytes 20983808 | tf_op jit(solution)/shard_map/dot_general | solution.py:242
  (140 shorter events, 29.5 us)
Async XLA Ops:
  1.8 2.0 copy-start.15
  6.2 12.0 %copy-start.21 = (f32[40]{0:T(128)S(1)}, f32[40]{0:T(128)}, u32[]{:S(2)}) copy-start(f32[40]{0:T(128)} %param.18) | copy-start | bytes 484
  6.2 12.1 %copy-start.22 = (f32[40]{0:T(128)S(1)}, f32[40]{0:T(128)}, u32[]{:S(2)}) copy-start(f32[40]{0:T(128)} %param.20) | copy-start | bytes 484
  6.2 14.0 %copy-start.19 = (s32[64]{0:T(128)S(1)}, s32[64]{0:T(128)}, u32[]{:S(2)}) copy-start(s32[64]{0:T(128)} %param.23) | copy-start | bytes 772
  6.2 15.5 %copy-start.23 = (f32[40]{0:T(128)S(1)}, f32[40]{0:T(128)}, u32[]{:S(2)}) copy-start(f32[40]{0:T(128)} %param.19) | copy-start | bytes 484
  6.2 64.5 %all-to-all-start = ((bf16[128,16,906]{2,1,0:T(8,128)(2,1)}), bf16[128,16,906]{2,1,0:T(8,128)(2,1)}, u32[]{:S(2)}, u32[]{:S(2)}) async-start(bf16[128,16,906]{2,1,0:T(8,128)(2,1)} %bitcast.307), calls=%async_computation | async-start | bytes 8388608 | tf_op jit(solution)/shard_map/all_to_all | solution.py:147
  81.6 8.7 %collective-permute-start = (bf16[3,256]{1,0:T(4,128)(2,1)S(1)}, bf16[3,256]{1,0:T(4,128)(2,1)S(1)}, u32[]{:S(2)}, u32[]{:S(2)}) collective-permute-start(bf16[3,256]{1,0:T(4,128)(2,1)S(1)} %slice.460), channel_id=1, source_target_pairs={{0,4},{4,8},{8,12},{12,16},{16,20},{20,24},{24,28},{28,32},{32,36}... | collective-permute-start | bytes 4616 | tf_op jit(solution)/shard_map/ppermute | solution.py:13
  84.7 17.5 %collective-permute-start.1 = (bf16[3,640]{1,0:T(4,128)(2,1)S(1)}, bf16[3,640]{1,0:T(4,128)(2,1)S(1)}, u32[]{:S(2)}, u32[]{:S(2)}) collective-permute-start(bf16[3,640]{1,0:T(4,128)(2,1)S(1)} %slice.472), channel_id=1, source_target_pairs={{0,4},{4,8},{8,12},{12,16},{16,20},{20,24},{24,28},{28,32},{32,36}... | collective-permute-start | bytes 11528 | tf_op jit(solution)/shard_map/ppermute | solution.py:13
  86.6 59.0 %collective-permute-start.2 = (f32[10]{0:T(128)S(1)}, f32[10]{0:T(128)S(1)}, u32[]{:S(2)}, u32[]{:S(2)}) collective-permute-start(f32[10]{0:T(128)S(1)} %get-tuple-element.64), channel_id=1, source_target_pairs={{0,4},{4,8},{8,12},{12,16},{16,20},{20,24},{24,28},{28,32},{32,36}... | collective-permute-start | bytes 128 | tf_op jit(solution)/shard_map/ppermute | solution.py:13
  93.5 1.0 copy-start.2
  114.5 1.2 copy-start.3
  116.6 11.6 %copy-start = (f32[8,10,64,128]{3,2,1,0:T(8,128)}, f32[8,10,64,128]{3,2,1,0:T(8,128)S(1)}, u32[]{:S(2)}) copy-start(f32[8,10,64,128]{3,2,1,0:T(8,128)S(1)} %fusion.9) | copy-start | bytes 7864324
  117.8 27.8 %collective-permute-start.4 = (f32[10,64,128]{2,1,0:T(8,128)}, f32[10,64,128]{2,1,0:T(8,128)S(1)}, u32[]{:S(2)}, u32[]{:S(2)}) collective-permute-start(f32[10,64,128]{2,1,0:T(8,128)} %multiply_add_fusion.7), channel_id=1, source_target_pairs={{0,4},{4,8},{8,12},{12,16},{16,20},{20,24},{24,28},{28,32},{32,36}... | collective-permute-start | bytes 983048 | tf_op jit(solution)/shard_map/ppermute | solution.py:13
  119.7 25.9 %collective-permute-start.3 = (f32[10,64,128]{2,1,0:T(8,128)}, f32[10,64,128]{2,1,0:T(8,128)S(1)}, u32[]{:S(2)}, u32[]{:S(2)}) collective-permute-start(f32[10,64,128]{2,1,0:T(8,128)} %multiply_add_fusion.7), channel_id=1, source_target_pairs={{0,8},{4,12},{8,16},{12,20},{16,24},{20,28},{24,32},{28,36},{32,40... | collective-permute-start | bytes 983048 | tf_op jit(solution)/shard_map/ppermute | solution.py:13
  140.3 6.0 %copy-start.1 = (f32[8,10,64,128]{3,2,1,0:T(8,128)S(1)}, f32[8,10,64,128]{3,2,1,0:T(8,128)}, u32[]{:S(2)}) copy-start(f32[8,10,64,128]{3,2,1,0:T(8,128)} %copy-done) | copy-start | bytes 7864324
  156.1 7.2 %copy-start.4 = (bf16[2048,256]{1,0:T(8,128)(2,1)S(1)}, bf16[2048,256]{1,0:T(8,128)(2,1)}, u32[]{:S(2)}) copy-start(bf16[2048,256]{1,0:T(8,128)(2,1)} %copy-done.2) | copy-start | bytes 3145732
  156.1 7.2 %copy-start.7 = (bf16[8,256,256]{1,2,0:T(8,128)(2,1)S(1)}, bf16[8,256,256]{1,2,0:T(8,128)(2,1)}, u32[]{:S(2)}) copy-start(bf16[8,256,256]{1,2,0:T(8,128)(2,1)} %copy.182) | copy-start | bytes 3145732
  156.1 7.2 %copy-start.11 = (f32[8,256,64]{1,2,0:T(8,128)S(1)}, f32[8,256,64]{1,2,0:T(8,128)}, u32[]{:S(2)}) copy-start(f32[8,256,64]{1,2,0:T(8,128)} %fusion.17) | copy-start | bytes 1572868
  156.1 7.2 %copy-start.12 = (f32[8,256,64]{1,2,0:T(8,128)S(1)}, f32[8,256,64]{1,2,0:T(8,128)}, u32[]{:S(2)}) copy-start(f32[8,256,64]{1,2,0:T(8,128)} %fusion.18) | copy-start | bytes 1572868
  156.2 7.2 %copy-start.13 = (f32[8,256,64]{1,2,0:T(8,128)S(1)}, f32[8,256,64]{1,2,0:T(8,128)}, u32[]{:S(2)}) copy-start(f32[8,256,64]{1,2,0:T(8,128)} %fusion.19) | copy-start | bytes 1572868
  156.2 7.2 %copy-start.14 = (f32[8,256,64]{1,2,0:T(8,128)S(1)}, f32[8,256,64]{1,2,0:T(8,128)}, u32[]{:S(2)}) copy-start(f32[8,256,64]{1,2,0:T(8,128)} %fusion.20) | copy-start | bytes 1572868
  160.8 1.5 copy-start.18
  162.3 1.1 copy-start.9
  167.2 25.4 %all-to-all-start.1 = ((bf16[128,16,256]{2,1,0:T(8,128)(2,1)}), bf16[128,16,256]{2,1,0:T(8,128)(2,1)}, u32[]{:S(2)}, u32[]{:S(2)}) async-start(bf16[128,16,256]{2,1,0:T(8,128)(2,1)} %bitcast.314), calls=%async_computation.1 | async-start | bytes 2097152 | tf_op jit(solution)/shard_map/all_to_all | solution.py:236
  173.8 5.3 %copy-start.17 = (bf16[8,256,1,64]{1,0,3,2:T(8,128)(2,1)S(1)}, bf16[8,256,1,64]{1,0,3,2:T(8,128)(2,1)}, u32[]{:S(2)}) copy-start(bf16[8,256,1,64]{1,0,3,2:T(8,128)(2,1)} %get-tuple-element.31) | copy-start | bytes 786436
  173.8 7.8 %copy-start.16 = (bf16[8,256,1,64]{1,0,3,2:T(8,128)(2,1)S(1)}, bf16[8,256,1,64]{1,0,3,2:T(8,128)(2,1)}, u32[]{:S(2)}) copy-start(bf16[8,256,1,64]{1,0,3,2:T(8,128)(2,1)} %get-tuple-element.30) | copy-start | bytes 786436
  176.4 7.7 %copy-start.5 = (bf16[2048,256]{1,0:T(8,128)(2,1)S(1)}, bf16[2048,256]{1,0:T(8,128)(2,1)}, u32[]{:S(2)}) copy-start(bf16[2048,256]{1,0:T(8,128)(2,1)} %copy-done.2) | copy-start | bytes 3145732
  176.4 7.7 %copy-start.6 = (bf16[8,256,384]{1,2,0:T(8,128)(2,1)S(1)}, bf16[8,256,384]{1,2,0:T(8,128)(2,1)}, u32[]{:S(2)}) copy-start(bf16[8,256,384]{1,2,0:T(8,128)(2,1)} %copy.189) | copy-start | bytes 4718596
  176.4 7.7 %copy-start.10 = (bf16[8,640,128]{2,1,0:T(8,128)(2,1)S(1)}, bf16[8,640,128]{2,1,0:T(8,128)(2,1)}, u32[]{:S(2)}) copy-start(bf16[8,640,128]{2,1,0:T(8,128)(2,1)} %copy-done.9) | copy-start | bytes 3932164
  192.7 32.6 %all-to-all-start.2 = ((bf16[128,16,384]{2,1,0:T(8,128)(2,1)}), bf16[128,16,384]{2,1,0:T(8,128)(2,1)}, u32[]{:S(2)}, u32[]{:S(2)}) async-start(bf16[128,16,384]{2,1,0:T(8,128)(2,1)} %bitcast.313), calls=%async_computation.2 | async-start | bytes 3145728 | tf_op jit(solution)/shard_map/all_to_all | solution.py:236
  226.7 1.7 copy-start.8
  228.5 1.8 copy-start.20

commit v9 on v6

--- a/solution.py
+++ b/solution.py
@@ -141,14 +141,17 @@
 
     x_slabs = jnp.stack([x_in[:, g * width : (g + 1) * width] for g in range(n_seq)], axis=0)
     dt_slabs = jnp.stack([dt_raw[:, g * share : (g + 1) * share] for g in range(n_seq)], axis=0)
-    bc_slabs = jnp.broadcast_to(bc_in[None], (n_seq, tok_rows, bc_width))
+    quarter = bc_width // n_seq
+    bc_slabs = jnp.stack(
+        [bc_in[:, g * quarter : (g + 1) * quarter] for g in range(n_seq)], axis=0
+    )
     outbound = jnp.concatenate([x_slabs, bc_slabs, dt_slabs], axis=2)
     outbound = outbound.reshape(n_seq * n_req, chunk, -1)
     inbound = lax.all_to_all(outbound, ("seq", "req"), 0, 0, tiled=True)
     inbound = inbound.reshape(n_seq * tok_rows, -1)
     x_rows = inbound[:, :width]
-    bc_rows = inbound[:, width : width + bc_width]
-    dt_rows = inbound[:, width + bc_width :]
+    bc_rows = inbound[:, width : width + quarter]
+    dt_rows = inbound[:, width + quarter :]
 
     row_count = x_rows.shape[0]
     stretch_count = row_count // STRETCH
@@ -160,9 +163,11 @@
     weight_x = lax.dynamic_slice_in_dim(conv_weight, group * width, width, axis=1)
     bias_x = lax.dynamic_slice_in_dim(conv_bias, group * width, width, axis=0)
     conv_x = causal_conv(x_rows, edge_x, weight_x, bias_x, starts)
-    conv_bc = causal_conv(
-        bc_rows, edge_bc, conv_weight[:, inner_width:], conv_bias[inner_width:], starts
-    )
+    weight_bc = lax.dynamic_slice_in_dim(conv_weight, inner_width + group * quarter, quarter, axis=1)
+    bias_bc = lax.dynamic_slice_in_dim(conv_bias, inner_width + group * quarter, quarter, axis=0)
+    conv_quarter = causal_conv(bc_rows, edge_bc, weight_bc, bias_bc, starts)
+    gathered = lax.all_gather(conv_quarter, "seq", axis=0, tiled=False)
+    conv_bc = jnp.concatenate([gathered[g] for g in range(n_seq)], axis=1)
     bias_dt = lax.dynamic_slice_in_dim(dt_bias, group * share, share)
     rate_log = lax.dynamic_slice_in_dim(a_log, group * share, share)
     skip = lax.dynamic_slice_in_dim(d_skip, group * share, share)

time: 220 us -> 255 us (1.16)
  other arithmetic: 46.4 us -> 66.2 us
  between operations: 1.32 us -> 15 us
  waiting for transfers between devices: 81.2 us -> 71 us
  local copies, waits for them, and re-layouts: 34.8 us -> 42.8 us
    all_to_all x1, waiting for transfers between devices: 47.6 us -> 33.7 us  [per_device(): inbound = lax.all_to_all(outbound, ('seq', 'req'), 0, 0, tiled=True)]
    convert_element_type x0 -> x1, other arithmetic: none -> 6.88 us  [per_device(): mixed = mixed.astype(jnp.bfloat16).reshape(n_seq * n_req, chunk, width)]
    convert_element_type x2, other arithmetic: 9.14 us -> 15.7 us  [causal_conv(): return jax.nn.silu(running).astype(jnp.bfloat16)]
    another operation x14, other arithmetic: 10.2 us -> 14 us
    all_gather x0 -> x1, waiting for transfers between devices: none -> 3.69 us  [per_device(): gathered = lax.all_gather(conv_quarter, 'seq', axis=0, tiled=False)]
    unnamed x50 -> x92, local copies, waits for them, and re-layouts: 7.25 us -> 5.07 us
    unnamed x9 -> x8, other arithmetic: 11.4 us -> 9.58 us
  transfers between devices with their start and end apart: 7 -> 8, of which waited for: 2 -> 3; matrix products, arithmetic and copies ran while one was open for 21% -> 23% of each run, Pallas kernels for 0% -> 0%
where the time goes in v9:
time: 255 us; the launch traced here: 253 us
  waiting for transfers between devices  71 us (28%)
  other arithmetic  66.2 us (26%)
  local copies, waits for them, and re-layouts  42.8 us (17%)
  starting transfers between devices  33.5 us (13%)
  matrix products  24.8 us (10%)
  between operations  15 us (6%)
    all_to_all x1, waiting for transfers between devices, per_device(): inbound = lax.all_to_all(outbound, ('seq', 'req'), 0, 0, tiled=True)  33.7 us
    all_to_all x1, waiting for transfers between devices, per_device(): back = lax.all_to_all(mixed, ('seq', 'req'), 0, 0, tiled=True)  33.6 us
    convert_element_type x2, other arithmetic, causal_conv(): return jax.nn.silu(running).astype(jnp.bfloat16)  15.7 us
    ppermute x5, starting transfers between devices, from_behind(): lax.ppermute(value, axis, [(source, source + steps) for source in range(l...  14.3 us
    another operation x14, other arithmetic  14 us
    dot_general x1, matrix products, per_device(): jnp.dot(normed, w_out, preferred_element_type=jnp.float32)  13.8 us
    all_to_all x1, starting transfers between devices, per_device(): inbound = lax.all_to_all(outbound, ('seq', 'req'), 0, 0, tiled=True)  11.5 us
    unnamed x8, other arithmetic  9.58 us
  transfers between devices with their start and end apart: 8, of which 3 were waited for; matrix products, arithmetic and copies ran while one was open for 23% of the time, Pallas kernels for 0%

profile of v9, /device:TPU:1, one launch (start us, length us, event | category | flops | bytes accessed | tf_op | source)
XLA Modules:
  0.0 253.3 jit_solution(4156809867213265379)
XLA Ops:
  7.2 0.9 slice_bitcast_fusion.39
  8.4 1.2 slice_bitcast_fusion.35
  9.6 1.9 slice_bitcast_fusion.23
  11.6 4.7 %pad_maximum_fusion = bf16[4,512,714]{2,1,0:T(8,128)(2,1)} fusion(bf16[4,512,10]{2,1,0:T(8,128)(2,1)S(1)} %copy.129, bf16[1,512,64]{2,1,0:T(8,128)(2,1)S(1)} %get-tuple-element.56, bf16[1,512,64]{2,1,0:T(8,128)(2,1)S(1)} %get-tuple-element.57, bf16[1,512,64]{2,1,0:T(8,128)(2,1)S(1)} %get-tuple-element.55, bf16[1,512,64]{2,1,0:T(8,128)(2,1)S(1)} %get-tuple-element.54, ...), kind=kLoop, calls=%fused_computation.18 | loop fusion | flops 26320896 | bytes 5849088 | tf_op jit(solution)/shard_map/concatenate | solution.py:148
  16.3 11.5 %all-to-all-start = ((bf16[128,16,714]{2,1,0:T(8,128)(2,1)}), bf16[128,16,714]{2,1,0:T(8,128)(2,1)S(1)}, u32[]{:S(2)}, u32[]{:S(2)}) async-start(bf16[128,16,714]{2,1,0:T(8,128)(2,1)} %bitcast.321), calls=%async_computation | async-start | bytes 6291456 | tf_op jit(solution)/shard_map/all_to_all | solution.py:150
  28.5 1.3 dynamic_slice.21
  29.8 1.4 dynamic_slice.25
  31.5 1.5 dynamic-slice_reduce_fusion.3
  35.8 33.7 %all-to-all-done = bf16[128,16,714]{2,1,0:T(8,128)(2,1)S(1)} async-done(((bf16[128,16,714]{2,1,0:T(8,128)(2,1)}), bf16[128,16,714]{2,1,0:T(8,128)(2,1)S(1)}, u32[]{:S(2)}, u32[]{:S(2)}) %all-to-all-start) | async-done | bytes 2924576 | tf_op jit(solution)/shard_map/all_to_all | solution.py:150
  69.4 1.0 slice.441
  70.4 1.3 copy.156
  72.6 8.1 %reduce-window.18 = f32[8,10,2,128]{3,1,2,0:T(8,128)S(1)} reduce-window(f32[8,10,2,128]{3,1,2,0:T(8,128)} %copy.131, f32[]{:T(128)} %constant.69.clone.1), window={size=1x1x1x128 pad=0_0x0_0x0_0x127_0}, to_apply=%region_2.3 | reduce-window | flops 2600960 | bytes 163844 | tf_op jit(solution)/shard_map/reduce-window.1
  81.4 1.1 copy.132
  86.5 0.9 fusion.43
  87.4 1.4 exponential_multiply_fusion
  88.8 3.1 %collective-permute-start = (bf16[3,64]{1,0:T(4,128)(2,1)}, bf16[3,64]{1,0:T(4,128)(2,1)S(1)}, u32[]{:S(2)}, u32[]{:S(2)}) collective-permute-start(bf16[3,64]{1,0:T(4,128)(2,1)} %slice.431), channel_id=1, source_target_pairs={{0,4},{4,8},{8,12},{12,16},{16,20},{20,24},{24,28},{28,32},{32,36}... | collective-permute-start | bytes 1160 | tf_op jit(solution)/shard_map/ppermute | solution.py:13
  91.9 1.7 slice.446
  93.7 1.9 collective-permute-start.1
  95.6 2.2 collective-permute-start.2
  97.8 4.8 %multiply_convert_fusion.5 = bf16[2048,64]{1,0:T(8,128)(2,1)} fusion(bf16[2048,64]{1,0:T(8,128)(2,1)S(1)} %copy-done.3, bf16[3,64]{1,0:T(4,128)(2,1)S(1)} %collective-permute-done, f32[64]{0:T(128)} %get-tuple-element.78, f32[64]{0:T(128)} %get-tuple-element.79, f32[64]{0:T(128)} %get-tuple-element.80, f32[64]{0:T(128)} %get-tuple-element.77, ...), kind=kLoop, calls=%fused_computation.46 | loop fusion | flops 3932160 | bytes 534144 | tf_op jit(solution)/shard_map/convert_element_type | solution.py:67
  102.7 10.9 %multiply_convert_fusion.3 = bf16[2048,640]{1,0:T(8,128)(2,1)S(1)} fusion(bf16[2048,640]{1,0:T(8,128)(2,1)} %slice.446, bf16[3,640]{1,0:T(4,128)(2,1)S(1)} %collective-permute-done.1, f32[640]{0:T(1024)} %get-tuple-element.13, f32[640]{0:T(1024)} %get-tuple-element.11, f32[640]{0:T(1024)} %get-tuple-element.12, f32[640]{0:T(1024)S(1)} %get-tuple-element.10, ...), kind=kLoop, calls=%fused_computation.14 | loop fusion | flops 39321600 | bytes 5267712 | tf_op jit(solution)/shard_map/convert_element_type | solution.py:67
  113.6 3.0 %copy.135 = bf16[2048,640]{0,1:T(8,128)(2,1)} copy(bf16[2048,640]{1,0:T(8,128)(2,1)S(1)} %multiply_convert_fusion.3) | data formatting | bytes 5242880 | tf_op jit(solution)/shard_map/convert_element_type | solution.py:67
  116.6 2.6 %copy.168 = bf16[80,8,8,256]{3,2,1,0:T(8,128)(2,1)S(1)} copy(bf16[80,8,8,256]{3,1,2,0:T(8,128)(2,1)} %bitcast.323) | data formatting | bytes 5242880
  119.2 5.0 %copy.151 = f32[8,256,640]{1,2,0:T(8,128)} copy(bf16[8,256,640]{2,1,0:T(8,128)(2,1)} %bitcast.313) | data formatting | bytes 7864320 | tf_op jit(solution)/shard_map/convert_element_type | solution.py:231
  124.2 1.4 fusion.55
  125.6 2.0 multiply_convert_fusion.2
  127.6 3.7 %all-gather.3.cloned.1.call-done = bf16[8192,64]{1,0:T(8,128)(2,1)} async-done(((bf16[2048,64]{1,0:T(8,128)(2,1)}), bf16[8192,64]{1,0:T(8,128)(2,1)}) %all-gather.3.cloned.1.call-update) | async-done | bytes 1048592 | tf_op jit(solution)/shard_map/all_gather | solution.py:169
  131.3 1.7 fusion.56
  133.0 2.7 %fusion.9 = f32[8,10,64,128]{3,2,1,0:T(8,128)S(1)} fusion(bf16[8,256,10,64]{1,0,3,2:T(8,128)(2,1)} %multiply_convert_fusion.2, bf16[8,256,64]{2,1,0:T(8,128)(2,1)S(1)} %bitcast.326, bf16[8,256,64]{2,1,0:T(8,128)(2,1)S(1)} %bitcast.324), kind=kOutput, calls=%fused_computation.22 | convolution fusion | flops 336592896 | bytes 5767168 | tf_op jit(solution)/shard_map/cuhp,cun->chpn/dot_general | solution.py:184
  136.0 3.8 %collective-permute-start.4 = (f32[10,64,128]{2,1,0:T(8,128)S(1)}, f32[10,64,128]{2,1,0:T(8,128)S(1)}, u32[]{:S(2)}, u32[]{:S(2)}) collective-permute-start(f32[10,64,128]{2,1,0:T(8,128)S(1)} %multiply_add_fusion.7), channel_id=1, source_target_pairs={{0,4},{4,8},{8,12},{12,16},{16,20},{20,24},{24,28},{28,32},{32,36}... | collective-permute-start | bytes 983048 | tf_op jit(solution)/shard_map/ppermute | solution.py:13
  139.8 3.3 %collective-permute-start.3 = (f32[10,64,128]{2,1,0:T(8,128)S(1)}, f32[10,64,128]{2,1,0:T(8,128)S(1)}, u32[]{:S(2)}, u32[]{:S(2)}) collective-permute-start(f32[10,64,128]{2,1,0:T(8,128)S(1)} %multiply_add_fusion.7), channel_id=1, source_target_pairs={{0,8},{4,12},{8,16},{12,20},{16,24},{20,28},{24,32},{28,36},{32,40... | collective-permute-start | bytes 983048 | tf_op jit(solution)/shard_map/ppermute | solution.py:13
  143.9 6.1 %multiply_convert_fusion = bf16[8,10,256,256]{3,2,0,1:T(8,128)(2,1)S(1)} fusion(f32[8,10,256]{2,0,1:T(8,128)S(1)} %get-tuple-element.59, f32[8,10,256]{2,0,1:T(8,128)S(1)} %bitcast.340, f32[8,256,256]{2,1,0:T(8,128)S(1)} %fusion.16, pred[256,256]{1,0:T(8,128)(4,1)S(1)} %copy-done.6), kind=kLoop, calls=%fused_computation | loop fusion | flops 31457280 | bytes 12812288 | tf_op jit(solution)/shard_map/convert_element_type | solution.py:204
  155.4 1.4 bitcast_dynamic-update-slice_fusion.7
  157.5 1.4 bitcast_dynamic-update-slice_fusion.6
  159.5 1.2 bitcast_dynamic-update-slice_fusion.5
  161.5 1.3 bitcast_dynamic-update-slice_fusion.4
  163.5 1.4 bitcast_dynamic-update-slice_fusion.3
  165.7 1.4 bitcast_dynamic-update-slice_fusion.2
  167.9 1.5 bitcast_dynamic-update-slice_fusion.1
  170.9 3.3 %fusion.17 = f32[8,256,640]{1,2,0:T(8,128)} fusion(bf16[8,640,128]{2,1,0:T(8,128)(2,1)S(1)} %bitcast_dynamic-update-slice_fusion.8, bf16[8,256,64]{2,1,0:T(8,128)(2,1)S(1)} %bitcast.331, bf16[8,256,64]{2,1,0:T(8,128)(2,1)S(1)} %bitcast.329), kind=kOutput, calls=%fused_computation.119 | convolution fusion | flops 336592896 | bytes 7077888 | tf_op jit(solution)/shard_map/ctn,cqn->ctq/dot_general | solution.py:219
  174.2 6.9 %fusion.6 = bf16[8,256,640]{1,2,0:T(8,128)(2,1)} fusion(f32[8,256,640]{1,2,0:T(8,128)} %copy-done.1, f32[8,256,640]{1,2,0:T(8,128)} %fusion.17, f32[8,256,640]{1,2,0:T(8,128)S(1)} %bitcast.315, f32[640]{0:T(1024)S(1)} %mul.415, f32[8,256,10]{1,2,0:T(8,128)S(1)} %copy.146), kind=kLoop, calls=%fused_computation.10 | loop fusion | flops 6553600 | bytes 18434560 | tf_op jit(solution)/shard_map/convert_element_type | solution.py:233
  181.0 4.4 %copy.152 = bf16[8,256,640]{2,1,0:T(8,128)(2,1)} copy(bf16[8,256,640]{1,2,0:T(8,128)(2,1)} %fusion.6) | data formatting | bytes 5242880 | tf_op jit(solution)/shard_map/convert_element_type | solution.py:233
  185.4 7.6 %all-to-all-start.1 = ((bf16[128,16,640]{2,1,0:T(8,128)(2,1)}), bf16[128,16,640]{2,1,0:T(8,128)(2,1)}, u32[]{:S(2)}, u32[]{:S(2)}) async-start(bf16[128,16,640]{2,1,0:T(8,128)(2,1)} %bitcast.322), calls=%async_computation.1 | async-start | bytes 5242880 | tf_op jit(solution)/shard_map/all_to_all | solution.py:234
  193.1 2.1 bitcast_dynamic-update-slice_fusion
  195.2 33.6 %all-to-all-done.1 = bf16[128,16,640]{2,1,0:T(8,128)(2,1)} async-done(((bf16[128,16,640]{2,1,0:T(8,128)(2,1)}), bf16[128,16,640]{2,1,0:T(8,128)(2,1)}, u32[]{:S(2)}, u32[]{:S(2)}) %all-to-all-start.1) | async-done | bytes 2621472 | tf_op jit(solution)/shard_map/all_to_all | solution.py:234
  228.8 1.9 fusion.54
  230.7 1.9 multiply_reduce_fusion
  232.6 13.8 %convolution_convert_fusion = bf16[512,2560]{1,0:T(8,128)(2,1)} fusion(bf16[2560,2560]{1,0:T(8,128)(2,1)} %param.22, f32[2560]{0:T(1024)S(1)} %copy-done.35, f32[512]{0:T(512)S(1)} %add_rsqrt_fusion, bf16[512,2560]{1,0:T(8,128)(2,1)S(1)} %copy-done.2, bf16[512,640]{1,0:T(8,128)(2,1)S(1)} %bitcast.335, bf16[512,640]{1,0:T(8,128)(2,1)S(1)} %bitcast.337, ...), kind=kOutput, calls=%fused_computation.15 | convolution fusion | flops 6734479360 | bytes 20983808 | tf_op jit(solution)/shard_map/dot_general | solution.py:238
  (160 shorter events, 21.5 us)
Async XLA Ops:
  11.5 16.3 %copy-start.34 = (s32[64]{0:T(128)S(1)}, s32[64]{0:T(128)}, u32[]{:S(2)}) copy-start(s32[64]{0:T(128)} %param.23) | copy-start | bytes 772
  11.5 19.6 %copy-start.36 = (f32[40]{0:T(128)S(1)}, f32[40]{0:T(128)}, u32[]{:S(2)}) copy-start(f32[40]{0:T(128)} %param.18) | copy-start | bytes 484
  11.6 19.7 %copy-start.37 = (f32[40]{0:T(128)S(1)}, f32[40]{0:T(128)}, u32[]{:S(2)}) copy-start(f32[40]{0:T(128)} %param.20) | copy-start | bytes 484
  11.6 21.5 %copy-start.38 = (f32[40]{0:T(128)S(1)}, f32[40]{0:T(128)}, u32[]{:S(2)}) copy-start(f32[40]{0:T(128)} %param.19) | copy-start | bytes 484
  16.3 53.1 %all-to-all-start = ((bf16[128,16,714]{2,1,0:T(8,128)(2,1)}), bf16[128,16,714]{2,1,0:T(8,128)(2,1)S(1)}, u32[]{:S(2)}, u32[]{:S(2)}) async-start(bf16[128,16,714]{2,1,0:T(8,128)(2,1)} %bitcast.321), calls=%async_computation | async-start | bytes 6291456 | tf_op jit(solution)/shard_map/all_to_all | solution.py:150
  27.8 103.5 %all-gather.3.cloned.1.call-start = ((), (), s32[]{:S(2)}) async-start(), calls=%async_computation.2 | async-start | bytes 2621440 | tf_op jit(solution)/shard_map/all_gather | solution.py:169
  31.3 56.1 %copy-start.25 = (f32[10]{0:T(128)}, f32[10]{0:T(128)S(1)}, u32[]{:S(2)}) copy-start(f32[10]{0:T(128)S(1)} %dynamic_slice.24) | copy-start | bytes 124
  85.2 12.5 %copy-start.4 = (f32[8,256,10]{1,0,2:T(8,128)S(1)}, f32[8,256,10]{1,0,2:T(8,128)}, u32[]{:S(2)}) copy-start(f32[8,256,10]{1,0,2:T(8,128)} %get-tuple-element.30) | copy-start | bytes 245764
  85.2 12.6 %copy-start.3 = (bf16[2048,64]{1,0:T(8,128)(2,1)S(1)}, bf16[2048,64]{1,0:T(8,128)(2,1)}, u32[]{:S(2)}) copy-start(bf16[2048,64]{1,0:T(8,128)(2,1)} %slice.432) | copy-start | bytes 786436
  88.8 9.0 %collective-permute-start = (bf16[3,64]{1,0:T(4,128)(2,1)}, bf16[3,64]{1,0:T(4,128)(2,1)S(1)}, u32[]{:S(2)}, u32[]{:S(2)}) collective-permute-start(bf16[3,64]{1,0:T(4,128)(2,1)} %slice.431), channel_id=1, source_target_pairs={{0,4},{4,8},{8,12},{12,16},{16,20},{20,24},{24,28},{28,32},{32,36}... | collective-permute-start | bytes 1160 | tf_op jit(solution)/shard_map/ppermute | solution.py:13
  93.7 9.0 %collective-permute-start.1 = (bf16[3,640]{1,0:T(4,128)(2,1)S(1)}, bf16[3,640]{1,0:T(4,128)(2,1)S(1)}, u32[]{:S(2)}, u32[]{:S(2)}) collective-permute-start(bf16[3,640]{1,0:T(4,128)(2,1)S(1)} %slice.445), channel_id=1, source_target_pairs={{0,4},{4,8},{8,12},{12,16},{16,20},{20,24},{24,28},{28,32},{32,36}... | collective-permute-start | bytes 11528 | tf_op jit(solution)/shard_map/ppermute | solution.py:13
  95.6 59.0 %collective-permute-start.2 = (f32[10]{0:T(128)}, f32[10]{0:T(128)S(1)}, u32[]{:S(2)}, u32[]{:S(2)}) collective-permute-start(f32[10]{0:T(128)} %get-tuple-element.64), channel_id=1, source_target_pairs={{0,4},{4,8},{8,12},{12,16},{16,20},{20,24},{24,28},{28,32},{32,36}... | collective-permute-start | bytes 128 | tf_op jit(solution)/shard_map/ppermute | solution.py:13
  113.6 3.0 %copy-start = (bf16[2048,640]{1,0:T(8,128)(2,1)}, bf16[2048,640]{1,0:T(8,128)(2,1)S(1)}, u32[]{:S(2)}) copy-start(bf16[2048,640]{1,0:T(8,128)(2,1)S(1)} %multiply_convert_fusion.3) | copy-start | bytes 7864324
  119.2 6.4 %copy-start.5 = (f32[8,256,10]{1,0,2:T(8,128)S(1)}, f32[8,256,10]{1,0,2:T(8,128)}, u32[]{:S(2)}) copy-start(f32[8,256,10]{1,0,2:T(8,128)} %get-tuple-element.58) | copy-start | bytes 245764
  127.5 8.1 %copy-start.26 = (f32[10]{0:T(128)S(1)}, f32[10]{0:T(128)}, u32[]{:S(2)}) copy-start(f32[10]{0:T(128)} %get-tuple-element.66) | copy-start | bytes 124
  127.6 8.1 %copy-start.27 = (f32[10]{0:T(128)S(1)}, f32[10]{0:T(128)}, u32[]{:S(2)}) copy-start(f32[10]{0:T(128)} %get-tuple-element.67) | copy-start | bytes 124
  127.6 8.1 %copy-start.28 = (f32[10]{0:T(128)S(1)}, f32[10]{0:T(128)}, u32[]{:S(2)}) copy-start(f32[10]{0:T(128)} %get-tuple-element.68) | copy-start | bytes 124
  127.6 8.1 %copy-start.29 = (f32[10]{0:T(128)S(1)}, f32[10]{0:T(128)}, u32[]{:S(2)}) copy-start(f32[10]{0:T(128)} %get-tuple-element.69) | copy-start | bytes 124
  127.6 8.1 %copy-start.30 = (f32[10]{0:T(128)S(1)}, f32[10]{0:T(128)}, u32[]{:S(2)}) copy-start(f32[10]{0:T(128)} %get-tuple-element.70) | copy-start | bytes 124
  127.6 8.1 %copy-start.31 = (f32[10]{0:T(128)S(1)}, f32[10]{0:T(128)}, u32[]{:S(2)}) copy-start(f32[10]{0:T(128)} %get-tuple-element.71) | copy-start | bytes 124
  127.6 8.1 %copy-start.32 = (f32[10]{0:T(128)S(1)}, f32[10]{0:T(128)}, u32[]{:S(2)}) copy-start(f32[10]{0:T(128)} %get-tuple-element.72) | copy-start | bytes 124
  127.6 8.1 %copy-start.33 = (f32[10]{0:T(128)S(1)}, f32[10]{0:T(128)}, u32[]{:S(2)}) copy-start(f32[10]{0:T(128)} %get-tuple-element.65) | copy-start | bytes 124
  132.9 10.9 %copy-start.6 = (pred[256,256]{1,0:T(8,128)(4,1)S(1)}, pred[256,256]{1,0:T(8,128)(4,1)}, u32[]{:S(2)}) copy-start(pred[256,256]{1,0:T(8,128)(4,1)} %iota_compare_fusion) | copy-start | bytes 196612
  136.0 18.6 %collective-permute-start.4 = (f32[10,64,128]{2,1,0:T(8,128)S(1)}, f32[10,64,128]{2,1,0:T(8,128)S(1)}, u32[]{:S(2)}, u32[]{:S(2)}) collective-permute-start(f32[10,64,128]{2,1,0:T(8,128)S(1)} %multiply_add_fusion.7), channel_id=1, source_target_pairs={{0,4},{4,8},{8,12},{12,16},{16,20},{20,24},{24,28},{28,32},{32,36}... | collective-permute-start | bytes 983048 | tf_op jit(solution)/shard_map/ppermute | solution.py:13
  139.8 14.8 %collective-permute-start.3 = (f32[10,64,128]{2,1,0:T(8,128)S(1)}, f32[10,64,128]{2,1,0:T(8,128)S(1)}, u32[]{:S(2)}, u32[]{:S(2)}) collective-permute-start(f32[10,64,128]{2,1,0:T(8,128)S(1)} %multiply_add_fusion.7), channel_id=1, source_target_pairs={{0,8},{4,12},{8,16},{12,20},{16,24},{20,28},{24,32},{28,36},{32,40... | collective-permute-start | bytes 983048 | tf_op jit(solution)/shard_map/ppermute | solution.py:13
  143.8 6.2 %copy-start.15 = (bf16[8,256,1,64]{1,0,3,2:T(8,128)(2,1)S(1)}, bf16[8,256,1,64]{1,0,3,2:T(8,128)(2,1)}, u32[]{:S(2)}) copy-start(bf16[8,256,1,64]{1,0,3,2:T(8,128)(2,1)} %get-tuple-element.45) | copy-start | bytes 786436
  143.9 6.6 %copy-start.14 = (bf16[8,256,1,64]{1,0,3,2:T(8,128)(2,1)S(1)}, bf16[8,256,1,64]{1,0,3,2:T(8,128)(2,1)}, u32[]{:S(2)}) copy-start(bf16[8,256,1,64]{1,0,3,2:T(8,128)(2,1)} %get-tuple-element.44) | copy-start | bytes 786436
  143.9 7.1 %copy-start.13 = (bf16[8,256,1,64]{1,0,3,2:T(8,128)(2,1)S(1)}, bf16[8,256,1,64]{1,0,3,2:T(8,128)(2,1)}, u32[]{:S(2)}) copy-start(bf16[8,256,1,64]{1,0,3,2:T(8,128)(2,1)} %get-tuple-element.43) | copy-start | bytes 786436
  150.0 1.8 copy-start.11
  150.0 2.3 copy-start.10
  150.5 2.3 copy-start.9
  150.9 2.3 copy-start.8
  151.4 2.3 copy-start.7
  152.3 3.1 %copy-start.17 = (f32[10]{0:T(128)S(1)}, f32[10]{0:T(128)}, u32[]{:S(2)}) copy-start(f32[10]{0:T(128)} %get-tuple-element.9) | copy-start | bytes 124
  153.2 4.3 %copy-start.24 = (f32[10]{0:T(128)S(1)}, f32[10]{0:T(128)}, u32[]{:S(2)}) copy-start(f32[10]{0:T(128)} %get-tuple-element.8) | copy-start | bytes 124
  153.6 5.9 %copy-start.23 = (f32[10]{0:T(128)S(1)}, f32[10]{0:T(128)}, u32[]{:S(2)}) copy-start(f32[10]{0:T(128)} %get-tuple-element.7) | copy-start | bytes 124
  154.1 7.4 %copy-start.22 = (f32[10]{0:T(128)S(1)}, f32[10]{0:T(128)}, u32[]{:S(2)}) copy-start(f32[10]{0:T(128)} %get-tuple-element.6) | copy-start | bytes 124
  154.5 10.3 %copy-start.1 = (f32[8,256,640]{1,2,0:T(8,128)}, f32[8,256,640]{1,2,0:T(8,128)S(1)}, u32[]{:S(2)}) copy-start(f32[8,256,640]{1,2,0:T(8,128)S(1)} %convolution_dynamic-update-slice_fusion) | copy-start | bytes 15728644
  154.5 8.9 %copy-start.21 = (f32[10]{0:T(128)S(1)}, f32[10]{0:T(128)}, u32[]{:S(2)}) copy-start(f32[10]{0:T(128)} %get-tuple-element.5) | copy-start | bytes 124
  155.4 10.3 %copy-start.20 = (f32[10]{0:T(128)S(1)}, f32[10]{0:T(128)}, u32[]{:S(2)}) copy-start(f32[10]{0:T(128)} %get-tuple-element.4) | copy-start | bytes 124
  157.5 10.4 %copy-start.19 = (f32[10]{0:T(128)S(1)}, f32[10]{0:T(128)}, u32[]{:S(2)}) copy-start(f32[10]{0:T(128)} %get-tuple-element.3) | copy-start | bytes 124
  167.1 7.1 %slice-start = ((s8[5242880]{0:T(1024)(128)(4,1)}), s8[4194304]{0:T(1024)(128)(4,1)S(1)}, s32[]{:S(2)}) async-start(s8[5242880]{0:T(1024)(128)(4,1)} %bitcast.314), calls=%async_computation.3 | async-start | bytes 8388608
  169.4 1.5 copy-start.16
  170.9 3.3 %slice-start.1 = ((s8[5242880]{0:T(1024)(128)(4,1)}), s8[1048576]{0:T(1024)(128)(4,1)S(1)}, s32[]{:S(2)}) async-start(s8[5242880]{0:T(1024)(128)(4,1)} %bitcast.314), calls=%async_computation.4 | async-start | bytes 2097152
  181.0 12.0 %copy-start.18 = (f32[10]{0:T(128)S(1)}, f32[10]{0:T(128)}, u32[]{:S(2)}) copy-start(f32[10]{0:T(128)} %get-tuple-element.2) | copy-start | bytes 124
  185.4 43.4 %all-to-all-start.1 = ((bf16[128,16,640]{2,1,0:T(8,128)(2,1)}), bf16[128,16,640]{2,1,0:T(8,128)(2,1)}, u32[]{:S(2)}, u32[]{:S(2)}) async-start(bf16[128,16,640]{2,1,0:T(8,128)(2,1)} %bitcast.322), calls=%async_computation.1 | async-start | bytes 5242880 | tf_op jit(solution)/shard_map/all_to_all | solution.py:234
  195.1 35.6 %copy-start.2 = (bf16[512,2560]{1,0:T(8,128)(2,1)S(1)}, bf16[512,2560]{1,0:T(8,128)(2,1)}, u32[]{:S(2)}) copy-start(bf16[512,2560]{1,0:T(8,128)(2,1)} %param.14) | copy-start | bytes 7864324
  195.1 37.5 %copy-start.35 = (f32[2560]{0:T(1024)S(1)}, f32[2560]{0:T(1024)}, u32[]{:S(2)}) copy-start(f32[2560]{0:T(1024)} %param.21) | copy-start | bytes 30724
  (1 other events, 1.4 us)
Sparse Core Ops, SparseCore 0:
  102.8 28.4 all-gather.2

commit v10 on v7

--- a/solution.py
+++ b/solution.py
@@ -201,20 +201,18 @@
 
     keep = jnp.where(starts, 0.0, 1.0)
     gains = jnp.exp(log_decay[:, -1, :])
-    rows = []
-    weights = [jnp.zeros((share,), jnp.float32)] * stretch_count + [jnp.ones((share,), jnp.float32)]
-    for stretch in range(stretch_count):
-        if stretch > 0:
-            weights = [w * gains[stretch - 1] for w in weights]
-            weights[stretch - 1] = weights[stretch - 1] + 1.0
-        weights = [w * keep[stretch] for w in weights]
-        rows.append(jnp.stack(weights, axis=0))
-    mix = jnp.stack(rows, axis=0)
-    sources = jnp.concatenate([stretch_state, state_prev[None]], axis=0)
-    state_in_all = jnp.einsum(
-        "ckh,khpn->chpn", mix, sources, precision=lax.Precision.HIGHEST,
-        preferred_element_type=jnp.float32,
-    )
+    c_idx = jnp.arange(stretch_count)[:, None, None]
+    k_idx = jnp.arange(-1, stretch_count)[None, :, None]
+    m_idx = jnp.arange(stretch_count)[None, None, :]
+    keep_span = (m_idx > k_idx) & (m_idx <= c_idx)
+    gain_span = (m_idx > k_idx) & (m_idx < c_idx)
+    live = k_idx < c_idx
+    factors = jnp.where(keep_span[..., None], keep[None, None, :, None], 1.0) * jnp.where(
+        gain_span[..., None], gains[None, None, :, :], 1.0
+    )
+    weights = jnp.where(live, jnp.prod(factors, axis=2), 0.0)
+    sources = jnp.concatenate([state_prev[None], stretch_state], axis=0)
+    state_in_all = jnp.sum(weights[:, :, :, None, None] * sources[None], axis=1)
     state_out_all = gains[:, :, None, None] * state_in_all + stretch_state
     endings = jnp.where(finals[:, None, None, None], state_out_all, 0.0)
     state_ins = [state_in_all[c] for c in range(stretch_count)]

time: 239 us -> 207 us (0.87)
  blocking collectives: 0 us -> 42 us
  waiting for transfers between devices: 77.9 us -> 48.1 us
  other arithmetic: 55.8 us -> 32.6 us
  local copies, waits for them, and re-layouts: 40.4 us -> 33.5 us
  starting transfers between devices: 31.1 us -> 24.6 us
  matrix products: 30.5 us -> 24.3 us
    all_to_all x0 -> x1, blocking collectives: none -> 42 us  [per_device(): back = lax.all_to_all(mixed, ('seq', 'req'), 0, 0, tiled=True)]
    all_to_all x1 -> x0, waiting for transfers between devices: 31.8 us -> none  [per_device(): back = lax.all_to_all(mixed, ('seq', 'req'), 0, 0, tiled=True)]
    mul x6 -> x0, other arithmetic: 23.8 us -> none  [per_device(): weights = [w * keep[stretch] for w in weights]]
    all_to_all x1 -> x0, starting transfers between devices: 6.53 us -> none  [per_device(): back = lax.all_to_all(mixed, ('seq', 'req'), 0, 0, tiled=True)]
    dot_general x1 -> x0, matrix products: 6.24 us -> none  [per_device(): jnp.einsum('ckh,khpn->chpn', mix, sources, precision=lax.Precision.HIGHES...]
    unnamed x45 -> x41, local copies, waits for them, and re-layouts: 7.41 us -> 7.85 us
  transfers between devices with their start and end apart: 7 -> 6, of which waited for: 2 -> 1; matrix products, arithmetic and copies ran while one was open for 24% -> 22% of each run, Pallas kernels for 0% -> 0%
where the time goes in v10:
time: 207 us; the launch traced here: 206 us
  waiting for transfers between devices  48.1 us (23%)
  blocking collectives  42 us (20%)
  local copies, waits for them, and re-layouts  33.5 us (16%)
  other arithmetic  32.6 us (16%)
  starting transfers between devices  24.6 us (12%)
  matrix products  24.3 us (12%)
    all_to_all x1, waiting for transfers between devices, per_device(): inbound = lax.all_to_all(outbound, ('seq', 'req'), 0, 0, tiled=True)  48.1 us
    all_to_all x1, blocking collectives, per_device(): back = lax.all_to_all(mixed, ('seq', 'req'), 0, 0, tiled=True)  42 us
    dot_general x1, matrix products, per_device(): jnp.dot(normed, w_out, preferred_element_type=jnp.float32)  13.8 us
    ppermute x5, starting transfers between devices, from_behind(): lax.ppermute(value, axis, [(source, source + steps) for source in range(l...  12.6 us
    all_to_all x1, starting transfers between devices, per_device(): inbound = lax.all_to_all(outbound, ('seq', 'req'), 0, 0, tiled=True)  12 us
    convert_element_type x2, other arithmetic, causal_conv(): return jax.nn.silu(running).astype(jnp.bfloat16)  9.14 us
    unnamed x41, local copies, waits for them, and re-layouts  7.85 us
    convert_element_type x1, other arithmetic, per_device(): mixing = (scores[:, None] * decay_mask * step_size.transpose(0, 2, 1)[:,...  7.29 us
  transfers between devices with their start and end apart: 6, of which 1 were waited for; matrix products, arithmetic and copies ran while one was open for 22% of the time, Pallas kernels for 0%

profile of v10, /device:TPU:1, one launch (start us, length us, event | category | flops | bytes accessed | tf_op | source)
XLA Modules:
  0.0 206.1 jit_solution(14318621702986047735)
XLA Ops:
  0.6 0.9 slice_bitcast_fusion.35
  1.8 1.9 slice_bitcast_fusion.23
  3.8 2.4 %pad_maximum_fusion = bf16[4,512,906]{2,1,0:T(8,128)(2,1)} fusion(bf16[4,512,10]{2,1,0:T(8,128)(2,1)S(1)} %copy.102, bf16[4,512,256]{2,1,0:T(8,128)(2,1)S(1)} %broadcast_in_dim.210, bf16[1,512,640]{2,1,0:T(8,128)(2,1)S(1)} %get-tuple-element.28, bf16[1,512,640]{2,1,0:T(8,128)(2,1)S(1)} %get-tuple-element.29, bf16[1,512,640]{2,1,0:T(8,128)(2,1)S(1)} %get-tuple-element.27, ...), kind=kLoop, calls=%fused_computation.17 | loop fusion | flops 22265856 | bytes 7421952 | tf_op jit(solution)/shard_map/concatenate | solution.py:145
  6.2 12.0 %all-to-all-start = ((bf16[128,16,906]{2,1,0:T(8,128)(2,1)}), bf16[128,16,906]{2,1,0:T(8,128)(2,1)}, u32[]{:S(2)}, u32[]{:S(2)}) async-start(bf16[128,16,906]{2,1,0:T(8,128)(2,1)} %bitcast.253), calls=%async_computation | async-start | bytes 8388608 | tf_op jit(solution)/shard_map/all_to_all | solution.py:147
  18.2 0.7 slice.241
  19.5 0.8 dynamic_slice.17
  20.6 0.9 dynamic-slice_reduce_fusion.3
  21.8 0.8 fusion.62
  22.7 48.1 %all-to-all-done = bf16[128,16,906]{2,1,0:T(8,128)(2,1)} async-done(((bf16[128,16,906]{2,1,0:T(8,128)(2,1)}), bf16[128,16,906]{2,1,0:T(8,128)(2,1)}, u32[]{:S(2)}, u32[]{:S(2)}) %all-to-all-start) | async-done | bytes 3711008 | tf_op jit(solution)/shard_map/all_to_all | solution.py:147
  70.8 1.1 slice.322
  71.8 0.7 slice.314
  72.5 0.7 slice.326
  73.7 4.6 %reduce-window.18 = f32[8,10,2,128]{3,1,2,0:T(8,128)S(1)} reduce-window(f32[8,10,2,128]{3,1,2,0:T(8,128)S(1)} %copy.104, f32[]{:T(128)} %constant.64.clone.1), window={size=1x1x1x128 pad=0_0x0_0x0_0x127_0}, to_apply=%region_2.3 | reduce-window | flops 2600960 | bytes 163844 | tf_op jit(solution)/shard_map/reduce-window.1
  79.3 3.1 %collective-permute-start = (bf16[3,256]{1,0:T(4,128)(2,1)S(1)}, bf16[3,256]{1,0:T(4,128)(2,1)S(1)}, u32[]{:S(2)}, u32[]{:S(2)}) collective-permute-start(bf16[3,256]{1,0:T(4,128)(2,1)S(1)} %slice.314), channel_id=1, source_target_pairs={{0,4},{4,8},{8,12},{12,16},{16,20},{20,24},{24,28},{28,32},{32,36}... | collective-permute-start | bytes 4616 | tf_op jit(solution)/shard_map/ppermute | solution.py:13
  82.4 1.9 collective-permute-start.1
  84.4 2.2 %collective-permute-start.2 = (f32[10]{0:T(128)S(1)}, f32[10]{0:T(128)S(1)}, u32[]{:S(2)}, u32[]{:S(2)}) collective-permute-start(f32[10]{0:T(128)S(1)} %get-tuple-element.42), channel_id=1, source_target_pairs={{0,4},{4,8},{8,12},{12,16},{16,20},{20,24},{24,28},{28,32},{32,36}... | collective-permute-start | bytes 128 | tf_op jit(solution)/shard_map/ppermute | solution.py:13
  87.0 1.3 slice.315
  88.3 2.0 slice.327
  90.3 3.2 %multiply_convert_fusion.5 = bf16[2048,256]{1,0:T(8,128)(2,1)S(1)} fusion(bf16[2048,256]{1,0:T(8,128)(2,1)S(1)} %slice.315, bf16[3,256]{1,0:T(4,128)(2,1)S(1)} %collective-permute-done, f32[256]{0:T(256)S(1)} %bitcast.280, f32[256]{0:T(256)S(1)} %bitcast.278, f32[256]{0:T(256)S(1)} %bitcast.279, f32[256]{0:T(256)S(1)} %bitcast.277, f32[256]{0:T(256)S(1)} %slice.241, ...), kind=kLoop, calls=%fused_computation.29 | loop fusion | flops 15728640 | bytes 2112000 | tf_op jit(solution)/shard_map/convert_element_type | solution.py:67
  93.5 1.0 copy-done.1
  94.9 7.3 %multiply_convert_fusion = bf16[8,10,256,256]{3,2,0,1:T(8,128)(2,1)} fusion(f32[8,10,256]{2,0,1:T(8,128)S(1)} %get-tuple-element.31, f32[8,10,256]{2,0,1:T(8,128)S(1)} %bitcast.272, f32[8,256,256]{2,1,0:T(8,128)S(1)} %fusion.17, pred[256,256]{1,0:T(8,128)(4,1)S(1)} %iota_compare_fusion), kind=kLoop, calls=%fused_computation.1 | loop fusion | flops 31457280 | bytes 12812288 | tf_op jit(solution)/shard_map/convert_element_type | solution.py:199
  102.2 6.0 %multiply_convert_fusion.3 = bf16[2048,640]{1,0:T(8,128)(2,1)S(1)} fusion(bf16[2048,640]{1,0:T(8,128)(2,1)S(1)} %slice.327, bf16[3,640]{1,0:T(4,128)(2,1)S(1)} %collective-permute-done.1, f32[640]{0:T(1024)S(1)} %get-tuple-element.5, f32[640]{0:T(1024)S(1)} %get-tuple-element.3, f32[640]{0:T(1024)S(1)} %get-tuple-element.4, f32[640]{0:T(1024)S(1)} %get-tuple-element.2, ...), kind=kLoop, calls=%fused_computation.15 | loop fusion | flops 39321600 | bytes 5267712 | tf_op jit(solution)/shard_map/convert_element_type | solution.py:67
  108.2 3.0 %copy.108 = bf16[2048,640]{0,1:T(8,128)(2,1)} copy(bf16[2048,640]{1,0:T(8,128)(2,1)S(1)} %multiply_convert_fusion.3) | data formatting | bytes 5242880 | tf_op jit(solution)/shard_map/convert_element_type | solution.py:67
  111.1 2.8 %copy.141 = bf16[80,8,8,256]{3,2,1,0:T(8,128)(2,1)S(1)} copy(bf16[80,8,8,256]{3,1,2,0:T(8,128)(2,1)} %bitcast.257) | data formatting | bytes 5242880
  113.9 0.9 fusion.61
  114.9 0.5 multiply_convert_fusion.2
  115.4 0.9 fusion.9
  116.2 1.0 fusion.22
  117.2 1.9 collective-permute-start.4
  119.1 3.5 %collective-permute-start.3 = (f32[10,64,128]{2,1,0:T(8,128)}, f32[10,64,128]{2,1,0:T(8,128)S(1)}, u32[]{:S(2)}, u32[]{:S(2)}) collective-permute-start(f32[10,64,128]{2,1,0:T(8,128)} %fusion.22), channel_id=1, source_target_pairs={{0,8},{4,12},{8,16},{12,20},{16,24},{20,28},{24,32},{28,36},{32,40... | collective-permute-start | bytes 983048 | tf_op jit(solution)/shard_map/ppermute | solution.py:13
  123.1 0.4 convolution_dynamic-update-slice_fusion.8
  123.6 0.4 convolution_dynamic-update-slice_fusion.7
  124.0 0.4 convolution_dynamic-update-slice_fusion.6
  124.5 0.4 convolution_dynamic-update-slice_fusion.5
  124.9 0.4 convolution_dynamic-update-slice_fusion.4
  125.8 0.4 convolution_dynamic-update-slice_fusion.2
  126.2 0.4 convolution_dynamic-update-slice_fusion.1
  126.7 2.3 %copy-done.4 = f32[8,256,640]{1,2,0:T(8,128)} copy-done((f32[8,256,640]{1,2,0:T(8,128)}, f32[8,256,640]{1,2,0:T(8,128)S(1)}, u32[]{:S(2)}) %copy-start.4) | copy-done | bytes 5242904
  128.9 4.9 %copy.124 = f32[8,256,640]{1,2,0:T(8,128)} copy(bf16[8,256,640]{2,1,0:T(8,128)(2,1)} %bitcast.250) | data formatting | bytes 7864320 | tf_op jit(solution)/shard_map/convert_element_type | solution.py:233
  133.8 2.5 %convolution_dynamic-update-slice_fusion = f32[8,256,640]{1,2,0:T(8,128)} fusion(f32[8,256,640]{1,2,0:T(8,128)} %copy-done.4, bf16[8,10,256,256]{3,2,0,1:T(8,128)(2,1)} %multiply_convert_fusion, bf16[8,256,1,64]{1,0,3,2:T(8,128)(2,1)} %get-tuple-element.16), kind=kOutput, calls=%fused_computation.32 | convolution fusion | flops 67108864 | bytes 1835008 | tf_op jit(solution)/shard_map/ctu,cup->ctp/dot_general | solution.py:226
  136.7 2.1 %multiply_reduce_fusion = f32[8,10,64,128]{3,2,1,0:T(8,128)S(1)} fusion(f32[9,10,64,128]{3,2,1,0:T(8,128)S(1)} %pad_maximum_fusion.1, f32[8,9,10]{2,1,0:T(8,128)S(1)} %broadcast_select_fusion), kind=kLoop, calls=%fused_computation | loop fusion | flops 11141120 | bytes 5573440 | tf_op jit(solution)/shard_map/reduce_sum | solution.py:215
  138.8 2.0 add_select_fusion
  140.8 1.5 slice-done.1
  142.4 2.7 %fusion.6 = bf16[8,256,640]{1,2,0:T(8,128)(2,1)} fusion(f32[8,256,640]{1,2,0:T(8,128)S(1)} %bitcast.262, f32[8,256,640]{1,2,0:T(8,128)S(1)} %bitcast.252, f32[640]{0:T(1024)S(1)} %mul.366, f32[8,256,10]{1,2,0:T(8,128)S(1)} %copy.119, bf16[8,640,128]{2,1,0:T(8,128)(2,1)S(1)} %bitcast.263, bf16[8,256,256]{2,1,0:T(8,128)(2,1)S(1)} %bitcast.260), kind=kOutput, calls=%fused_computation.11 | convolution fusion | flops 342097920 | bytes 15077376 | tf_op jit(solution)/shard_map/ctn,cqn->ctq/dot_general | solution.py:221
  145.0 3.1 %copy.125 = bf16[8,256,640]{2,1,0:T(8,128)(2,1)S(1)} copy(bf16[8,256,640]{1,2,0:T(8,128)(2,1)} %fusion.6) | data formatting | bytes 5242880 | tf_op jit(solution)/shard_map/convert_element_type | solution.py:235
  148.2 42.0 %all_to_all.10 = bf16[128,16,640]{2,1,0:T(8,128)(2,1)S(1)} all-to-all(bf16[128,16,640]{2,1,0:T(8,128)(2,1)S(1)} %bitcast.256), channel_id=1, replica_groups=mesh['req'=32,'seq'=4] {'seq','req'}, dimensions={0} | all-to-all | bytes 5242880 | tf_op jit(solution)/shard_map/all_to_all | solution.py:236
  190.4 1.9 multiply_reduce_fusion.1
  192.3 13.8 %convolution_convert_fusion = bf16[512,2560]{1,0:T(8,128)(2,1)} fusion(bf16[2560,2560]{1,0:T(8,128)(2,1)} %param.22, f32[2560]{0:T(1024)S(1)} %copy-done.8, f32[512]{0:T(512)S(1)} %add_rsqrt_fusion, bf16[512,2560]{1,0:T(8,128)(2,1)S(1)} %copy-done.5, bf16[512,640]{1,0:T(8,128)(2,1)S(1)} %bitcast.267, bf16[512,640]{1,0:T(8,128)(2,1)S(1)} %bitcast.269, ...), kind=kOutput, calls=%fused_computation.16 | convolution fusion | flops 6734479360 | bytes 20983808 | tf_op jit(solution)/shard_map/dot_general | solution.py:240
  (99 shorter events, 5.4 us)
Async XLA Ops:
  0.6 3.1 %copy-start.6 = (bf16[512,256]{1,0:T(8,128)(2,1)S(1)}, bf16[512,256]{1,0:T(8,128)(2,1)}, u32[]{:S(2)}) copy-start(bf16[512,256]{1,0:T(8,128)(2,1)} %param.13) | copy-start | bytes 786436
  6.2 12.7 %copy-start.7 = (s32[64]{0:T(128)S(1)}, s32[64]{0:T(128)}, u32[]{:S(2)}) copy-start(s32[64]{0:T(128)} %param.23) | copy-start | bytes 772
  6.2 14.1 %copy-start.9 = (f32[40]{0:T(128)S(1)}, f32[40]{0:T(128)}, u32[]{:S(2)}) copy-start(f32[40]{0:T(128)} %param.18) | copy-start | bytes 484
  6.2 14.1 %copy-start.10 = (f32[40]{0:T(128)S(1)}, f32[40]{0:T(128)}, u32[]{:S(2)}) copy-start(f32[40]{0:T(128)} %param.20) | copy-start | bytes 484
  6.2 15.3 %copy-start.11 = (f32[40]{0:T(128)S(1)}, f32[40]{0:T(128)}, u32[]{:S(2)}) copy-start(f32[40]{0:T(128)} %param.19) | copy-start | bytes 484
  6.2 64.5 %all-to-all-start = ((bf16[128,16,906]{2,1,0:T(8,128)(2,1)}), bf16[128,16,906]{2,1,0:T(8,128)(2,1)}, u32[]{:S(2)}, u32[]{:S(2)}) async-start(bf16[128,16,906]{2,1,0:T(8,128)(2,1)} %bitcast.253), calls=%async_computation | async-start | bytes 8388608 | tf_op jit(solution)/shard_map/all_to_all | solution.py:147
  79.3 11.0 %collective-permute-start = (bf16[3,256]{1,0:T(4,128)(2,1)S(1)}, bf16[3,256]{1,0:T(4,128)(2,1)S(1)}, u32[]{:S(2)}, u32[]{:S(2)}) collective-permute-start(bf16[3,256]{1,0:T(4,128)(2,1)S(1)} %slice.314), channel_id=1, source_target_pairs={{0,4},{4,8},{8,12},{12,16},{16,20},{20,24},{24,28},{28,32},{32,36}... | collective-permute-start | bytes 4616 | tf_op jit(solution)/shard_map/ppermute | solution.py:13
  82.4 19.8 %collective-permute-start.1 = (bf16[3,640]{1,0:T(4,128)(2,1)S(1)}, bf16[3,640]{1,0:T(4,128)(2,1)S(1)}, u32[]{:S(2)}, u32[]{:S(2)}) collective-permute-start(bf16[3,640]{1,0:T(4,128)(2,1)S(1)} %slice.326), channel_id=1, source_target_pairs={{0,4},{4,8},{8,12},{12,16},{16,20},{20,24},{24,28},{28,32},{32,36}... | collective-permute-start | bytes 11528 | tf_op jit(solution)/shard_map/ppermute | solution.py:13
  84.4 51.9 %collective-permute-start.2 = (f32[10]{0:T(128)S(1)}, f32[10]{0:T(128)S(1)}, u32[]{:S(2)}, u32[]{:S(2)}) collective-permute-start(f32[10]{0:T(128)S(1)} %get-tuple-element.42), channel_id=1, source_target_pairs={{0,4},{4,8},{8,12},{12,16},{16,20},{20,24},{24,28},{28,32},{32,36}... | collective-permute-start | bytes 128 | tf_op jit(solution)/shard_map/ppermute | solution.py:13
  93.5 1.0 copy-start.1
  108.1 5.8 %copy-start = (bf16[2048,640]{1,0:T(8,128)(2,1)}, bf16[2048,640]{1,0:T(8,128)(2,1)S(1)}, u32[]{:S(2)}) copy-start(bf16[2048,640]{1,0:T(8,128)(2,1)S(1)} %multiply_convert_fusion.3) | copy-start | bytes 7864324
  111.1 11.5 %slice-start.2 = ((s8[10485760]{0:T(1024)(128)(4,1)}), s8[2097152]{0:T(1024)(128)(4,1)S(1)}, s32[]{:S(2)}) async-start(s8[10485760]{0:T(1024)(128)(4,1)} %bitcast.254), calls=%async_computation.4 | async-start | bytes 4194304
  113.9 1.4 copy-start.2
  113.9 8.7 %slice-start.3 = ((s8[10485760]{0:T(1024)(128)(4,1)}), s8[4194304]{0:T(1024)(128)(4,1)S(1)}, s32[]{:S(2)}) async-start(s8[10485760]{0:T(1024)(128)(4,1)} %bitcast.254), calls=%async_computation.5 | async-start | bytes 8388608
  115.4 7.3 %slice-start.4 = ((s8[10485760]{0:T(1024)(128)(4,1)}), s8[4194304]{0:T(1024)(128)(4,1)S(1)}, s32[]{:S(2)}) async-start(s8[10485760]{0:T(1024)(128)(4,1)} %bitcast.254), calls=%async_computation.6 | async-start | bytes 8388608
  117.2 19.1 %collective-permute-start.4 = (f32[10,64,128]{2,1,0:T(8,128)}, f32[10,64,128]{2,1,0:T(8,128)S(1)}, u32[]{:S(2)}, u32[]{:S(2)}) collective-permute-start(f32[10,64,128]{2,1,0:T(8,128)} %fusion.22), channel_id=1, source_target_pairs={{0,4},{4,8},{8,12},{12,16},{16,20},{20,24},{24,28},{28,32},{32,36}... | collective-permute-start | bytes 983048 | tf_op jit(solution)/shard_map/ppermute | solution.py:13
  119.1 17.2 %collective-permute-start.3 = (f32[10,64,128]{2,1,0:T(8,128)}, f32[10,64,128]{2,1,0:T(8,128)S(1)}, u32[]{:S(2)}, u32[]{:S(2)}) collective-permute-start(f32[10,64,128]{2,1,0:T(8,128)} %fusion.22), channel_id=1, source_target_pairs={{0,8},{4,12},{8,16},{12,20},{16,24},{20,28},{24,32},{28,36},{32,40... | collective-permute-start | bytes 983048 | tf_op jit(solution)/shard_map/ppermute | solution.py:13
  126.7 2.3 %copy-start.4 = (f32[8,256,640]{1,2,0:T(8,128)}, f32[8,256,640]{1,2,0:T(8,128)S(1)}, u32[]{:S(2)}) copy-start(f32[8,256,640]{1,2,0:T(8,128)S(1)} %convolution_dynamic-update-slice_fusion.1) | copy-start | bytes 15728644
  136.4 4.4 %slice-start.5 = ((s8[5242880]{0:T(1024)(128)(4,1)}), s8[4194304]{0:T(1024)(128)(4,1)S(1)}, s32[]{:S(2)}) async-start(s8[5242880]{0:T(1024)(128)(4,1)} %bitcast.261), calls=%async_computation.7 | async-start | bytes 8388608
  136.7 4.2 %slice-start = ((s8[5242880]{0:T(1024)(128)(4,1)}), s8[1048576]{0:T(1024)(128)(4,1)S(1)}, s32[]{:S(2)}) async-start(s8[5242880]{0:T(1024)(128)(4,1)} %bitcast.251), calls=%async_computation.2 | async-start | bytes 2097152
  136.7 4.1 %slice-start.6 = ((s8[5242880]{0:T(1024)(128)(4,1)}), s8[1048576]{0:T(1024)(128)(4,1)S(1)}, s32[]{:S(2)}) async-start(s8[5242880]{0:T(1024)(128)(4,1)} %bitcast.261), calls=%async_computation.8 | async-start | bytes 2097152
  138.8 2.0 copy-start.3
  138.8 3.6 %slice-start.1 = ((s8[5242880]{0:T(1024)(128)(4,1)}), s8[4194304]{0:T(1024)(128)(4,1)S(1)}, s32[]{:S(2)}) async-start(s8[5242880]{0:T(1024)(128)(4,1)} %bitcast.251), calls=%async_computation.3 | async-start | bytes 8388608
  148.2 42.2 %copy-start.5 = (bf16[512,2560]{1,0:T(8,128)(2,1)S(1)}, bf16[512,2560]{1,0:T(8,128)(2,1)}, u32[]{:S(2)}) copy-start(bf16[512,2560]{1,0:T(8,128)(2,1)} %param.14) | copy-start | bytes 7864324
  190.2 2.2 %copy-start.8 = (f32[2560]{0:T(1024)S(1)}, f32[2560]{0:T(1024)}, u32[]{:S(2)}) copy-start(f32[2560]{0:T(1024)} %param.21) | copy-start | bytes 30724

commit v11 on v10

--- a/solution.py
+++ b/solution.py
@@ -173,7 +173,12 @@
     c_mat = bcs[:, :, state_size:]
     dts = dt_rows.reshape(stretch_count, STRETCH, share)
     step_size = jax.nn.softplus(dts.astype(jnp.float32) + bias_dt[None, None, :])
-    log_decay = jnp.cumsum(-jnp.exp(rate_log)[None, None, :] * step_size, axis=1)
+    rates = -jnp.exp(rate_log)[None, None, :] * step_size
+    lower = (jnp.arange(STRETCH)[:, None] >= jnp.arange(STRETCH)[None, :]).astype(jnp.float32)
+    log_decay = jnp.einsum(
+        "tu,cuh->cth", lower, rates, precision=lax.Precision.HIGHEST,
+        preferred_element_type=jnp.float32,
+    )
     tail_weight = jnp.exp(log_decay[:, -1:, :] - log_decay) * step_size
     weighted_x = (x_heads.astype(jnp.float32) * tail_weight[..., None]).astype(jnp.bfloat16)
     stretch_state = jnp.einsum(
@@ -197,7 +202,6 @@
     mixing = (
         scores[:, None] * decay_mask * step_size.transpose(0, 2, 1)[:, :, None, :]
     ).astype(jnp.bfloat16)
-    y_diag = jnp.einsum("chtu,cuhp->cthp", mixing, x_heads, preferred_element_type=jnp.float32)
 
     keep = jnp.where(starts, 0.0, 1.0)
     gains = jnp.exp(log_decay[:, -1, :])

time: 207 us -> 202 us (0.976)
  other arithmetic: 32.6 us -> 27.8 us
    another operation x6 -> x2, other arithmetic: 5.03 us -> 0.2 us
  transfers between devices with their start and end apart: 6 -> 6, of which waited for: 1 -> 1; matrix products, arithmetic and copies ran while one was open for 22% -> 23% of each run, Pallas kernels for 0% -> 0%
where the time goes in v11:
time: 202 us; the launch traced here: 201 us
  waiting for transfers between devices  48.1 us (24%)
  blocking collectives  42 us (21%)
  local copies, waits for them, and re-layouts  32.9 us (16%)
  other arithmetic  27.8 us (14%)
  matrix products  24.6 us (12%)
  starting transfers between devices  24.5 us (12%)
    all_to_all x1, waiting for transfers between devices, per_device(): inbound = lax.all_to_all(outbound, ('seq', 'req'), 0, 0, tiled=True)  48.1 us
    all_to_all x1, blocking collectives, per_device(): back = lax.all_to_all(mixed, ('seq', 'req'), 0, 0, tiled=True)  42 us
    dot_general x1, matrix products, per_device(): jnp.dot(normed, w_out, preferred_element_type=jnp.float32)  13.8 us
    ppermute x5, starting transfers between devices, from_behind(): lax.ppermute(value, axis, [(source, source + steps) for source in range(l...  12.6 us
    all_to_all x1, starting transfers between devices, per_device(): inbound = lax.all_to_all(outbound, ('seq', 'req'), 0, 0, tiled=True)  12 us
    convert_element_type x2, other arithmetic, causal_conv(): return jax.nn.silu(running).astype(jnp.bfloat16)  9.13 us
    unnamed x41, local copies, waits for them, and re-layouts  7.87 us
    convert_element_type x1, other arithmetic, per_device(): mixing = (scores[:, None] * decay_mask * step_size.transpose(0, 2, 1)[:,...  7.36 us
  transfers between devices with their start and end apart: 6, of which 1 were waited for; matrix products, arithmetic and copies ran while one was open for 23% of the time, Pallas kernels for 0%

profile of v11, /device:TPU:1, one launch (start us, length us, event | category | flops | bytes accessed | tf_op | source)
XLA Modules:
  0.0 201.1 jit_solution(12045885725806749472)
XLA Ops:
  0.6 0.9 slice_bitcast_fusion.36
  1.8 1.9 slice_bitcast_fusion.23
  3.8 2.3 %pad_maximum_fusion = bf16[4,512,906]{2,1,0:T(8,128)(2,1)} fusion(bf16[4,512,10]{2,1,0:T(8,128)(2,1)S(1)} %copy.94, bf16[4,512,256]{2,1,0:T(8,128)(2,1)S(1)} %broadcast_in_dim.212, bf16[1,512,640]{2,1,0:T(8,128)(2,1)S(1)} %get-tuple-element.26, bf16[1,512,640]{2,1,0:T(8,128)(2,1)S(1)} %get-tuple-element.27, bf16[1,512,640]{2,1,0:T(8,128)(2,1)S(1)} %get-tuple-element.25, ...), kind=kLoop, calls=%fused_computation.17 | loop fusion | flops 22265856 | bytes 7421952 | tf_op jit(solution)/shard_map/concatenate | solution.py:145
  6.2 12.0 %all-to-all-start = ((bf16[128,16,906]{2,1,0:T(8,128)(2,1)}), bf16[128,16,906]{2,1,0:T(8,128)(2,1)}, u32[]{:S(2)}, u32[]{:S(2)}) async-start(bf16[128,16,906]{2,1,0:T(8,128)(2,1)} %bitcast.232), calls=%async_computation | async-start | bytes 8388608 | tf_op jit(solution)/shard_map/all_to_all | solution.py:147
  18.2 0.7 slice.235
  19.5 0.8 dynamic_slice.17
  20.6 0.9 dynamic-slice_reduce_fusion.3
  21.8 0.8 fusion.69
  22.7 48.1 %all-to-all-done = bf16[128,16,906]{2,1,0:T(8,128)(2,1)} async-done(((bf16[128,16,906]{2,1,0:T(8,128)(2,1)}), bf16[128,16,906]{2,1,0:T(8,128)(2,1)}, u32[]{:S(2)}, u32[]{:S(2)}) %all-to-all-start) | async-done | bytes 3711008 | tf_op jit(solution)/shard_map/all_to_all | solution.py:147
  70.7 1.1 slice.314
  71.8 0.7 slice.306
  72.5 0.7 slice.316
  74.3 3.1 %collective-permute-start = (bf16[3,256]{1,0:T(4,128)(2,1)S(1)}, bf16[3,256]{1,0:T(4,128)(2,1)S(1)}, u32[]{:S(2)}, u32[]{:S(2)}) collective-permute-start(bf16[3,256]{1,0:T(4,128)(2,1)S(1)} %slice.306), channel_id=1, source_target_pairs={{0,4},{4,8},{8,12},{12,16},{16,20},{20,24},{24,28},{28,32},{32,36}... | collective-permute-start | bytes 4616 | tf_op jit(solution)/shard_map/ppermute | solution.py:13
  77.3 1.9 collective-permute-start.1
  79.3 2.2 %collective-permute-start.2 = (f32[10]{0:T(128)S(1)}, f32[10]{0:T(128)S(1)}, u32[]{:S(2)}, u32[]{:S(2)}) collective-permute-start(f32[10]{0:T(128)S(1)} %get-tuple-element.41), channel_id=1, source_target_pairs={{0,4},{4,8},{8,12},{12,16},{16,20},{20,24},{24,28},{28,32},{32,36}... | collective-permute-start | bytes 128 | tf_op jit(solution)/shard_map/ppermute | solution.py:13
  81.9 1.3 slice.307
  83.2 2.0 slice.317
  85.3 3.2 %multiply_convert_fusion.5 = bf16[2048,256]{1,0:T(8,128)(2,1)S(1)} fusion(bf16[2048,256]{1,0:T(8,128)(2,1)S(1)} %slice.307, bf16[3,256]{1,0:T(4,128)(2,1)S(1)} %collective-permute-done, f32[256]{0:T(256)S(1)} %bitcast.257, f32[256]{0:T(256)S(1)} %bitcast.255, f32[256]{0:T(256)S(1)} %bitcast.256, f32[256]{0:T(256)S(1)} %bitcast.254, f32[256]{0:T(256)S(1)} %slice.235, ...), kind=kLoop, calls=%fused_computation.29 | loop fusion | flops 15728640 | bytes 2112000 | tf_op jit(solution)/shard_map/convert_element_type | solution.py:67
  88.4 1.0 copy-done.1
  89.8 7.4 %multiply_convert_fusion = bf16[8,10,256,256]{3,2,0,1:T(8,128)(2,1)} fusion(f32[8,10,256]{2,0,1:T(8,128)S(1)} %copy.99, f32[8,10,256]{2,0,1:T(8,128)S(1)} %copy.97, f32[8,256,256]{2,1,0:T(8,128)S(1)} %fusion.17, pred[256,256]{1,0:T(8,128)(4,1)S(1)} %iota_compare_fusion), kind=kLoop, calls=%fused_computation.1 | loop fusion | flops 31457280 | bytes 12812288 | tf_op jit(solution)/shard_map/convert_element_type | solution.py:204
  97.2 6.0 %multiply_convert_fusion.3 = bf16[2048,640]{1,0:T(8,128)(2,1)S(1)} fusion(bf16[2048,640]{1,0:T(8,128)(2,1)S(1)} %slice.317, bf16[3,640]{1,0:T(4,128)(2,1)S(1)} %collective-permute-done.1, f32[640]{0:T(1024)S(1)} %get-tuple-element.5, f32[640]{0:T(1024)S(1)} %get-tuple-element.3, f32[640]{0:T(1024)S(1)} %get-tuple-element.4, f32[640]{0:T(1024)S(1)} %get-tuple-element.2, ...), kind=kLoop, calls=%fused_computation.15 | loop fusion | flops 39321600 | bytes 5267712 | tf_op jit(solution)/shard_map/convert_element_type | solution.py:67
  103.2 3.0 %copy.100 = bf16[2048,640]{0,1:T(8,128)(2,1)} copy(bf16[2048,640]{1,0:T(8,128)(2,1)S(1)} %multiply_convert_fusion.3) | data formatting | bytes 5242880 | tf_op jit(solution)/shard_map/convert_element_type | solution.py:67
  106.2 2.8 %copy.130 = bf16[80,8,8,256]{3,2,1,0:T(8,128)(2,1)S(1)} copy(bf16[80,8,8,256]{3,1,2,0:T(8,128)(2,1)} %bitcast.236) | data formatting | bytes 5242880
  109.0 0.9 fusion.68
  109.9 0.5 multiply_convert_fusion.2
  110.4 0.9 fusion.9
  111.2 1.0 fusion.22
  112.2 1.9 collective-permute-start.4
  114.1 3.5 %collective-permute-start.3 = (f32[10,64,128]{2,1,0:T(8,128)}, f32[10,64,128]{2,1,0:T(8,128)S(1)}, u32[]{:S(2)}, u32[]{:S(2)}) collective-permute-start(f32[10,64,128]{2,1,0:T(8,128)} %fusion.22), channel_id=1, source_target_pairs={{0,8},{4,12},{8,16},{12,20},{16,24},{20,28},{24,32},{28,36},{32,40... | collective-permute-start | bytes 983048 | tf_op jit(solution)/shard_map/ppermute | solution.py:13
  118.1 0.4 convolution_dynamic-update-slice_fusion.8
  118.6 0.4 convolution_dynamic-update-slice_fusion.7
  119.0 0.4 convolution_dynamic-update-slice_fusion.6
  119.5 0.4 convolution_dynamic-update-slice_fusion.5
  119.9 0.4 convolution_dynamic-update-slice_fusion.4
  120.4 0.4 convolution_dynamic-update-slice_fusion.3
  120.8 0.4 convolution_dynamic-update-slice_fusion.2
  121.2 0.4 convolution_dynamic-update-slice_fusion.1
  121.7 2.3 %copy-done.4 = f32[8,256,640]{1,2,0:T(8,128)} copy-done((f32[8,256,640]{1,2,0:T(8,128)}, f32[8,256,640]{1,2,0:T(8,128)S(1)}, u32[]{:S(2)}) %copy-start.4) | copy-done | bytes 5242904
  123.9 4.9 %copy.114 = f32[8,256,640]{1,2,0:T(8,128)} copy(bf16[8,256,640]{2,1,0:T(8,128)(2,1)} %bitcast.229) | data formatting | bytes 7864320 | tf_op jit(solution)/shard_map/convert_element_type | solution.py:237
  128.8 2.5 %convolution_dynamic-update-slice_fusion = f32[8,256,640]{1,2,0:T(8,128)} fusion(f32[8,256,640]{1,2,0:T(8,128)} %copy-done.4, bf16[8,10,256,256]{3,2,0,1:T(8,128)(2,1)} %multiply_convert_fusion, bf16[8,256,1,64]{1,0,3,2:T(8,128)(2,1)} %get-tuple-element.14), kind=kOutput, calls=%fused_computation.32 | convolution fusion | flops 67108864 | bytes 1835008 | tf_op jit(solution)/shard_map/ctu,cup->ctp/dot_general | solution.py:230
  131.7 2.1 %multiply_reduce_fusion = f32[8,10,64,128]{3,2,1,0:T(8,128)S(1)} fusion(f32[9,10,64,128]{3,2,1,0:T(8,128)S(1)} %pad_maximum_fusion.1, f32[8,9,10]{2,1,0:T(8,128)S(1)} %broadcast_select_fusion), kind=kLoop, calls=%fused_computation | loop fusion | flops 11141120 | bytes 5573440 | tf_op jit(solution)/shard_map/reduce_sum | solution.py:219
  133.8 2.0 add_select_fusion
  135.8 1.5 slice-done.1
  137.4 2.7 %fusion.6 = bf16[8,256,640]{1,2,0:T(8,128)(2,1)} fusion(f32[8,256,640]{1,2,0:T(8,128)S(1)} %bitcast.241, f32[8,256,640]{1,2,0:T(8,128)S(1)} %bitcast.231, f32[640]{0:T(1024)S(1)} %mul.366, f32[8,256,10]{1,2,0:T(8,128)S(1)} %get-tuple-element.28, bf16[8,640,128]{2,1,0:T(8,128)(2,1)S(1)} %bitcast.242, bf16[8,256,256]{2,1,0:T(8,128)(2,1)S(1)} %bitcast.239), kind=kOutput, calls=%fused_computation.11 | convolution fusion | flops 342097920 | bytes 15077376 | tf_op jit(solution)/shard_map/ctn,cqn->ctq/dot_general | solution.py:225
  140.1 3.1 %copy.115 = bf16[8,256,640]{2,1,0:T(8,128)(2,1)S(1)} copy(bf16[8,256,640]{1,2,0:T(8,128)(2,1)} %fusion.6) | data formatting | bytes 5242880 | tf_op jit(solution)/shard_map/convert_element_type | solution.py:239
  143.2 42.0 %all_to_all.10 = bf16[128,16,640]{2,1,0:T(8,128)(2,1)S(1)} all-to-all(bf16[128,16,640]{2,1,0:T(8,128)(2,1)S(1)} %bitcast.235), channel_id=1, replica_groups=mesh['req'=32,'seq'=4] {'seq','req'}, dimensions={0} | all-to-all | bytes 5242880 | tf_op jit(solution)/shard_map/all_to_all | solution.py:240
  185.4 1.9 multiply_reduce_fusion.1
  187.3 13.8 %convolution_convert_fusion = bf16[512,2560]{1,0:T(8,128)(2,1)} fusion(bf16[2560,2560]{1,0:T(8,128)(2,1)} %param.22, f32[2560]{0:T(1024)S(1)} %copy-done.8, f32[512]{0:T(512)S(1)} %add_rsqrt_fusion, bf16[512,2560]{1,0:T(8,128)(2,1)S(1)} %copy-done.5, bf16[512,640]{1,0:T(8,128)(2,1)S(1)} %bitcast.246, bf16[512,640]{1,0:T(8,128)(2,1)S(1)} %bitcast.248, ...), kind=kOutput, calls=%fused_computation.16 | convolution fusion | flops 6734479360 | bytes 20983808 | tf_op jit(solution)/shard_map/dot_general | solution.py:244
  (90 shorter events, 4.5 us)
Async XLA Ops:
  0.6 3.1 %copy-start.6 = (bf16[512,256]{1,0:T(8,128)(2,1)S(1)}, bf16[512,256]{1,0:T(8,128)(2,1)}, u32[]{:S(2)}) copy-start(bf16[512,256]{1,0:T(8,128)(2,1)} %param.13) | copy-start | bytes 786436
  6.2 12.7 %copy-start.7 = (s32[64]{0:T(128)S(1)}, s32[64]{0:T(128)}, u32[]{:S(2)}) copy-start(s32[64]{0:T(128)} %param.23) | copy-start | bytes 772
  6.2 14.1 %copy-start.9 = (f32[40]{0:T(128)S(1)}, f32[40]{0:T(128)}, u32[]{:S(2)}) copy-start(f32[40]{0:T(128)} %param.18) | copy-start | bytes 484
  6.2 14.1 %copy-start.10 = (f32[40]{0:T(128)S(1)}, f32[40]{0:T(128)}, u32[]{:S(2)}) copy-start(f32[40]{0:T(128)} %param.20) | copy-start | bytes 484
  6.2 15.3 %copy-start.11 = (f32[40]{0:T(128)S(1)}, f32[40]{0:T(128)}, u32[]{:S(2)}) copy-start(f32[40]{0:T(128)} %param.19) | copy-start | bytes 484
  6.2 64.5 %all-to-all-start = ((bf16[128,16,906]{2,1,0:T(8,128)(2,1)}), bf16[128,16,906]{2,1,0:T(8,128)(2,1)}, u32[]{:S(2)}, u32[]{:S(2)}) async-start(bf16[128,16,906]{2,1,0:T(8,128)(2,1)} %bitcast.232), calls=%async_computation | async-start | bytes 8388608 | tf_op jit(solution)/shard_map/all_to_all | solution.py:147
  74.3 11.0 %collective-permute-start = (bf16[3,256]{1,0:T(4,128)(2,1)S(1)}, bf16[3,256]{1,0:T(4,128)(2,1)S(1)}, u32[]{:S(2)}, u32[]{:S(2)}) collective-permute-start(bf16[3,256]{1,0:T(4,128)(2,1)S(1)} %slice.306), channel_id=1, source_target_pairs={{0,4},{4,8},{8,12},{12,16},{16,20},{20,24},{24,28},{28,32},{32,36}... | collective-permute-start | bytes 4616 | tf_op jit(solution)/shard_map/ppermute | solution.py:13
  77.3 19.9 %collective-permute-start.1 = (bf16[3,640]{1,0:T(4,128)(2,1)S(1)}, bf16[3,640]{1,0:T(4,128)(2,1)S(1)}, u32[]{:S(2)}, u32[]{:S(2)}) collective-permute-start(bf16[3,640]{1,0:T(4,128)(2,1)S(1)} %slice.316), channel_id=1, source_target_pairs={{0,4},{4,8},{8,12},{12,16},{16,20},{20,24},{24,28},{28,32},{32,36}... | collective-permute-start | bytes 11528 | tf_op jit(solution)/shard_map/ppermute | solution.py:13
  79.3 52.0 %collective-permute-start.2 = (f32[10]{0:T(128)S(1)}, f32[10]{0:T(128)S(1)}, u32[]{:S(2)}, u32[]{:S(2)}) collective-permute-start(f32[10]{0:T(128)S(1)} %get-tuple-element.41), channel_id=1, source_target_pairs={{0,4},{4,8},{8,12},{12,16},{16,20},{20,24},{24,28},{28,32},{32,36}... | collective-permute-start | bytes 128 | tf_op jit(solution)/shard_map/ppermute | solution.py:13
  88.4 1.0 copy-start.1
  103.2 5.8 %copy-start = (bf16[2048,640]{1,0:T(8,128)(2,1)}, bf16[2048,640]{1,0:T(8,128)(2,1)S(1)}, u32[]{:S(2)}) copy-start(bf16[2048,640]{1,0:T(8,128)(2,1)S(1)} %multiply_convert_fusion.3) | copy-start | bytes 7864324
  106.2 11.5 %slice-start.2 = ((s8[10485760]{0:T(1024)(128)(4,1)}), s8[2097152]{0:T(1024)(128)(4,1)S(1)}, s32[]{:S(2)}) async-start(s8[10485760]{0:T(1024)(128)(4,1)} %bitcast.233), calls=%async_computation.4 | async-start | bytes 4194304
  108.9 1.4 copy-start.2
  109.0 8.7 %slice-start.3 = ((s8[10485760]{0:T(1024)(128)(4,1)}), s8[4194304]{0:T(1024)(128)(4,1)S(1)}, s32[]{:S(2)}) async-start(s8[10485760]{0:T(1024)(128)(4,1)} %bitcast.233), calls=%async_computation.5 | async-start | bytes 8388608
  110.4 7.3 %slice-start.4 = ((s8[10485760]{0:T(1024)(128)(4,1)}), s8[4194304]{0:T(1024)(128)(4,1)S(1)}, s32[]{:S(2)}) async-start(s8[10485760]{0:T(1024)(128)(4,1)} %bitcast.233), calls=%async_computation.6 | async-start | bytes 8388608
  112.2 19.1 %collective-permute-start.4 = (f32[10,64,128]{2,1,0:T(8,128)}, f32[10,64,128]{2,1,0:T(8,128)S(1)}, u32[]{:S(2)}, u32[]{:S(2)}) collective-permute-start(f32[10,64,128]{2,1,0:T(8,128)} %fusion.22), channel_id=1, source_target_pairs={{0,4},{4,8},{8,12},{12,16},{16,20},{20,24},{24,28},{28,32},{32,36}... | collective-permute-start | bytes 983048 | tf_op jit(solution)/shard_map/ppermute | solution.py:13
  114.1 17.2 %collective-permute-start.3 = (f32[10,64,128]{2,1,0:T(8,128)}, f32[10,64,128]{2,1,0:T(8,128)S(1)}, u32[]{:S(2)}, u32[]{:S(2)}) collective-permute-start(f32[10,64,128]{2,1,0:T(8,128)} %fusion.22), channel_id=1, source_target_pairs={{0,8},{4,12},{8,16},{12,20},{16,24},{20,28},{24,32},{28,36},{32,40... | collective-permute-start | bytes 983048 | tf_op jit(solution)/shard_map/ppermute | solution.py:13
  121.7 2.3 %copy-start.4 = (f32[8,256,640]{1,2,0:T(8,128)}, f32[8,256,640]{1,2,0:T(8,128)S(1)}, u32[]{:S(2)}) copy-start(f32[8,256,640]{1,2,0:T(8,128)S(1)} %convolution_dynamic-update-slice_fusion.1) | copy-start | bytes 15728644
  131.4 4.4 %slice-start.5 = ((s8[5242880]{0:T(1024)(128)(4,1)}), s8[4194304]{0:T(1024)(128)(4,1)S(1)}, s32[]{:S(2)}) async-start(s8[5242880]{0:T(1024)(128)(4,1)} %bitcast.240), calls=%async_computation.7 | async-start | bytes 8388608
  131.7 4.2 %slice-start = ((s8[5242880]{0:T(1024)(128)(4,1)}), s8[1048576]{0:T(1024)(128)(4,1)S(1)}, s32[]{:S(2)}) async-start(s8[5242880]{0:T(1024)(128)(4,1)} %bitcast.230), calls=%async_computation.2 | async-start | bytes 2097152
  131.7 4.1 %slice-start.6 = ((s8[5242880]{0:T(1024)(128)(4,1)}), s8[1048576]{0:T(1024)(128)(4,1)S(1)}, s32[]{:S(2)}) async-start(s8[5242880]{0:T(1024)(128)(4,1)} %bitcast.240), calls=%async_computation.8 | async-start | bytes 2097152
  133.8 2.0 %copy-start.3 = (bf16[2048,256]{1,0:T(8,128)(2,1)S(1)}, bf16[2048,256]{1,0:T(8,128)(2,1)}, u32[]{:S(2)}) copy-start(bf16[2048,256]{1,0:T(8,128)(2,1)} %copy-done.1) | copy-start | bytes 3145732
  133.8 3.6 %slice-start.1 = ((s8[5242880]{0:T(1024)(128)(4,1)}), s8[4194304]{0:T(1024)(128)(4,1)S(1)}, s32[]{:S(2)}) async-start(s8[5242880]{0:T(1024)(128)(4,1)} %bitcast.230), calls=%async_computation.3 | async-start | bytes 8388608
  143.2 42.2 %copy-start.5 = (bf16[512,2560]{1,0:T(8,128)(2,1)S(1)}, bf16[512,2560]{1,0:T(8,128)(2,1)}, u32[]{:S(2)}) copy-start(bf16[512,2560]{1,0:T(8,128)(2,1)} %param.14) | copy-start | bytes 7864324
  185.2 2.2 %copy-start.8 = (f32[2560]{0:T(1024)S(1)}, f32[2560]{0:T(1024)}, u32[]{:S(2)}) copy-start(f32[2560]{0:T(1024)} %param.21) | copy-start | bytes 30724

commit v12 on v11

--- a/solution.py
+++ b/solution.py
@@ -154,9 +154,9 @@
     stretch_count = row_count // STRETCH
     stretch_ids = block * stretch_count + jnp.arange(stretch_count, dtype=jnp.int32)
     starts, finals = stretch_flags(prompt_stretches, stretch_ids)
-    edge_x, edge_bc = from_behind(
-        (x_rows[row_count - conv_span + 1 :], bc_rows[row_count - conv_span + 1 :]), "req", 1
-    )
+    edge = from_behind(inbound[row_count - conv_span + 1 :, : width + bc_width], "req", 1)
+    edge_x = edge[:, :width]
+    edge_bc = edge[:, width:]
     weight_x = lax.dynamic_slice_in_dim(conv_weight, group * width, width, axis=1)
     bias_x = lax.dynamic_slice_in_dim(conv_bias, group * width, width, axis=0)
     conv_x = causal_conv(x_rows, edge_x, weight_x, bias_x, starts)
@@ -189,9 +189,18 @@
     for stretch in range(stretch_count):
         total = chain_states(total, (carried[stretch], stretch_state[stretch]))
     reach = -(-(LMAX_CH - 1) // stretch_count)
-    behind = from_behind(total, "req", reach)
+    cells = head_dim * N
+    packed = jnp.concatenate(
+        [total[1].reshape(share, cells), jnp.broadcast_to(total[0][:, None], (share, 128))],
+        axis=1,
+    )
+
+    def unpack(moved):
+        return (moved[:, cells], moved[:, :cells].reshape(share, head_dim, N))
+
+    behind = unpack(from_behind(packed, "req", reach))
     for step in range(reach - 1, 0, -1):
-        behind = chain_states(behind, from_behind(total, "req", step))
+        behind = chain_states(behind, unpack(from_behind(packed, "req", step)))
     state_prev = behind[1]
 
     scores = jnp.einsum("ctn,cun->ctu", c_mat, b_mat, preferred_element_type=jnp.float32)

time: 202 us -> 202 us (level)
  starting transfers between devices: 24.5 us -> 19.5 us
  local copies, waits for them, and re-layouts: 32.9 us -> 36.1 us
    ppermute x5 -> x3, starting transfers between devices: 12.6 us -> 7.57 us  [from_behind(): lax.ppermute(value, axis, [(source, source + steps) for source in range(l...]
    unnamed x41 -> x60, local copies, waits for them, and re-layouts: 7.87 us -> 10.4 us
  transfers between devices with their start and end apart: 6 -> 4, of which waited for: 1 -> 1; matrix products, arithmetic and copies ran while one was open for 23% -> 13% of each run, Pallas kernels for 0% -> 0%
where the time goes in v12:
time: 202 us; the launch traced here: 201 us
  waiting for transfers between devices  48.1 us (24%)
  blocking collectives  42.2 us (21%)
  local copies, waits for them, and re-layouts  36.1 us (18%)
  other arithmetic  27.5 us (14%)
  matrix products  25.9 us (13%)
  starting transfers between devices  19.5 us (10%)
    all_to_all x1, waiting for transfers between devices, per_device(): inbound = lax.all_to_all(outbound, ('seq', 'req'), 0, 0, tiled=True)  48.1 us
    all_to_all x1, blocking collectives, per_device(): back = lax.all_to_all(mixed, ('seq', 'req'), 0, 0, tiled=True)  42.2 us
    dot_general x1, matrix products, per_device(): jnp.dot(normed, w_out, preferred_element_type=jnp.float32)  13.8 us
    all_to_all x1, starting transfers between devices, per_device(): inbound = lax.all_to_all(outbound, ('seq', 'req'), 0, 0, tiled=True)  12 us
    unnamed x60, local copies, waits for them, and re-layouts  10.4 us
    convert_element_type x2, other arithmetic, causal_conv(): return jax.nn.silu(running).astype(jnp.bfloat16)  9.16 us
    ppermute x3, starting transfers between devices, from_behind(): lax.ppermute(value, axis, [(source, source + steps) for source in range(l...  7.57 us
    dot_general x10, matrix products, per_device(): jnp.einsum('ctu,cup->ctp', mixing[:, h], x_heads[:, :, h], preferred_elem...  6.48 us
  transfers between devices with their start and end apart: 4, of which 1 were waited for; matrix products, arithmetic and copies ran while one was open for 13% of the time, Pallas kernels for 0%

profile of v12, /device:TPU:1, one launch (start us, length us, event | category | flops | bytes accessed | tf_op | source)
XLA Modules:
  0.0 200.7 jit_solution(15751483340583911642)
XLA Ops:
  0.6 0.9 slice_bitcast_fusion.36
  1.8 1.9 slice_bitcast_fusion.23
  3.8 2.4 %pad_maximum_fusion = bf16[4,512,906]{2,1,0:T(8,128)(2,1)} fusion(bf16[4,512,10]{2,1,0:T(8,128)(2,1)S(1)} %copy.160, bf16[4,512,256]{2,1,0:T(8,128)(2,1)S(1)} %broadcast_in_dim.215, bf16[1,512,640]{2,1,0:T(8,128)(2,1)S(1)} %get-tuple-element.34, bf16[1,512,640]{2,1,0:T(8,128)(2,1)S(1)} %get-tuple-element.35, bf16[1,512,640]{2,1,0:T(8,128)(2,1)S(1)} %get-tuple-element.33, ...), kind=kLoop, calls=%fused_computation.17 | loop fusion | flops 22265856 | bytes 7421952 | tf_op jit(solution)/shard_map/concatenate | solution.py:145
  6.2 12.0 %all-to-all-start = ((bf16[128,16,906]{2,1,0:T(8,128)(2,1)}), bf16[128,16,906]{2,1,0:T(8,128)(2,1)}, u32[]{:S(2)}, u32[]{:S(2)}) async-start(bf16[128,16,906]{2,1,0:T(8,128)(2,1)} %bitcast.222), calls=%async_computation | async-start | bytes 8388608 | tf_op jit(solution)/shard_map/all_to_all | solution.py:147
  18.2 0.7 slice.245
  19.5 0.8 dynamic_slice.17
  20.6 0.9 dynamic-slice_reduce_fusion.3
  21.8 0.8 fusion.54
  22.7 48.1 %all-to-all-done = bf16[128,16,906]{2,1,0:T(8,128)(2,1)} async-done(((bf16[128,16,906]{2,1,0:T(8,128)(2,1)}), bf16[128,16,906]{2,1,0:T(8,128)(2,1)}, u32[]{:S(2)}, u32[]{:S(2)}) %all-to-all-start) | async-done | bytes 3711008 | tf_op jit(solution)/shard_map/all_to_all | solution.py:147
  70.8 1.1 slice.329
  71.8 0.7 slice.320
  73.6 3.1 %collective-permute-start = (bf16[3,896]{1,0:T(4,128)(2,1)S(1)}, bf16[3,896]{1,0:T(4,128)(2,1)S(1)}, u32[]{:S(2)}, u32[]{:S(2)}) collective-permute-start(bf16[3,896]{1,0:T(4,128)(2,1)S(1)} %slice.320), channel_id=1, source_target_pairs={{0,4},{4,8},{8,12},{12,16},{16,20},{20,24},{24,28},{28,32},{32,36}... | collective-permute-start | bytes 16136 | tf_op jit(solution)/shard_map/ppermute | solution.py:13
  76.9 0.7 broadcast_select_fusion
  77.7 1.3 slice.322
  79.0 2.0 slice.332
  81.1 3.2 %multiply_convert_fusion.5 = bf16[2048,256]{1,0:T(8,128)(2,1)S(1)} fusion(bf16[2048,256]{1,0:T(8,128)(2,1)S(1)} %slice.322, bf16[3,256]{1,0:T(4,128)(2,1)S(1)} %slice.321, f32[256]{0:T(256)S(1)} %bitcast.265, f32[256]{0:T(256)S(1)} %bitcast.263, f32[256]{0:T(256)S(1)} %bitcast.264, f32[256]{0:T(256)S(1)} %bitcast.262, f32[256]{0:T(256)S(1)} %slice.245, ...), kind=kLoop, calls=%fused_computation.29 | loop fusion | flops 15728640 | bytes 2112000 | tf_op jit(solution)/shard_map/convert_element_type | solution.py:67
  84.3 1.8 fusion.17
  86.1 6.0 %multiply_convert_fusion.3 = bf16[2048,640]{1,0:T(8,128)(2,1)S(1)} fusion(bf16[2048,640]{1,0:T(8,128)(2,1)S(1)} %slice.332, bf16[3,640]{1,0:T(4,128)(2,1)S(1)} %slice.331, f32[640]{0:T(1024)S(1)} %get-tuple-element.5, f32[640]{0:T(1024)S(1)} %get-tuple-element.3, f32[640]{0:T(1024)S(1)} %get-tuple-element.4, f32[640]{0:T(1024)S(1)} %get-tuple-element.2, ...), kind=kLoop, calls=%fused_computation.15 | loop fusion | flops 39321600 | bytes 5267712 | tf_op jit(solution)/shard_map/convert_element_type | solution.py:67
  92.1 3.0 %copy.166 = bf16[2048,640]{0,1:T(8,128)(2,1)} copy(bf16[2048,640]{1,0:T(8,128)(2,1)S(1)} %multiply_convert_fusion.3) | data formatting | bytes 5242880 | tf_op jit(solution)/shard_map/convert_element_type | solution.py:67
  95.1 2.6 %copy.196 = bf16[80,8,8,256]{3,2,1,0:T(8,128)(2,1)S(1)} copy(bf16[80,8,8,256]{3,1,2,0:T(8,128)(2,1)} %bitcast.224) | data formatting | bytes 5242880
  97.7 0.9 fusion.53
  98.6 0.5 multiply_convert_fusion.2
  99.1 0.9 fusion.9
  103.5 0.8 pad_maximum_fusion.4
  104.4 1.9 collective-permute-start.1
  106.3 2.6 %collective-permute-start.2 = (f32[10,8320]{1,0:T(8,128)}, f32[10,8320]{1,0:T(8,128)}, u32[]{:S(2)}, u32[]{:S(2)}) collective-permute-start(f32[10,8320]{1,0:T(8,128)} %pad_maximum_fusion.4), channel_id=1, source_target_pairs={{0,8},{4,12},{8,16},{12,20},{16,24},{20,28},{24,32},{28,36},{32,40... | collective-permute-start | bytes 998408 | tf_op jit(solution)/shard_map/ppermute | solution.py:13
  108.9 6.1 %multiply_convert_fusion = bf16[8,10,256,256]{3,2,0,1:T(8,128)(2,1)S(1)} fusion(f32[8,10,256]{2,0,1:T(8,128)S(1)} %copy.165, f32[8,10,256]{2,0,1:T(8,128)S(1)} %copy.163, f32[8,256,256]{2,1,0:T(8,128)S(1)} %copy-done.5, pred[256,256]{1,0:T(8,128)(4,1)S(1)} %iota_compare_fusion), kind=kLoop, calls=%fused_computation.1 | loop fusion | flops 31457280 | bytes 12812288 | tf_op jit(solution)/shard_map/convert_element_type | solution.py:213
  115.1 0.4 convolution_dynamic-update-slice_fusion.9
  115.5 0.4 convolution_dynamic-update-slice_fusion.8
  115.9 0.4 convolution_dynamic-update-slice_fusion.7
  116.4 0.4 convolution_dynamic-update-slice_fusion.6
  116.8 0.4 convolution_dynamic-update-slice_fusion.5
  117.3 0.4 convolution_dynamic-update-slice_fusion.4
  117.7 0.4 convolution_dynamic-update-slice_fusion.3
  118.2 0.4 convolution_dynamic-update-slice_fusion.2
  119.0 0.4 convolution_dynamic-update-slice_fusion.1
  119.5 2.2 %copy-done.6 = f32[8,256,640]{1,2,0:T(8,128)} copy-done((f32[8,256,640]{1,2,0:T(8,128)}, f32[8,256,640]{1,2,0:T(8,128)S(1)}, u32[]{:S(2)}) %copy-start.6) | copy-done | bytes 5242904
  121.7 4.9 %copy.180 = f32[8,256,640]{1,2,0:T(8,128)} copy(bf16[8,256,640]{2,1,0:T(8,128)(2,1)} %bitcast.219) | data formatting | bytes 7864320 | tf_op jit(solution)/shard_map/convert_element_type | solution.py:246
  126.6 2.5 %convolution_dynamic-update-slice_fusion = f32[8,256,640]{1,2,0:T(8,128)} fusion(f32[8,256,640]{1,2,0:T(8,128)} %copy-done.6, bf16[8,10,256,256]{3,2,0,1:T(8,128)(2,1)} %copy-done.1, bf16[8,256,1,64]{1,0,3,2:T(8,128)(2,1)} %get-tuple-element.22), kind=kOutput, calls=%fused_computation.32 | convolution fusion | flops 67108864 | bytes 1835008 | tf_op jit(solution)/shard_map/ctu,cup->ctp/dot_general | solution.py:239
  129.3 1.1 slice.366
  131.0 2.1 %multiply_reduce_fusion = f32[8,10,64,128]{3,2,1,0:T(8,128)S(1)} fusion(f32[9,10,64,128]{3,2,1,0:T(8,128)S(1)} %pad_maximum_fusion.1, f32[8,9,10]{2,1,0:T(8,128)S(1)} %copy-done.8), kind=kLoop, calls=%fused_computation | loop fusion | flops 11141120 | bytes 5573440 | tf_op jit(solution)/shard_map/reduce_sum | solution.py:228
  133.1 2.0 add_select_fusion
  135.1 1.5 slice-done.1
  136.6 2.7 %fusion.6 = bf16[8,256,640]{1,2,0:T(8,128)(2,1)} fusion(f32[8,256,640]{1,2,0:T(8,128)S(1)} %bitcast.229, f32[8,256,640]{1,2,0:T(8,128)S(1)} %bitcast.221, f32[640]{0:T(1024)S(1)} %mul.435, f32[8,256,10]{1,2,0:T(8,128)S(1)} %get-tuple-element.36, bf16[8,640,128]{2,1,0:T(8,128)(2,1)S(1)} %bitcast.230, bf16[8,256,256]{2,1,0:T(8,128)(2,1)S(1)} %bitcast.227), kind=kOutput, calls=%fused_computation.11 | convolution fusion | flops 342097920 | bytes 15077376 | tf_op jit(solution)/shard_map/ctn,cqn->ctq/dot_general | solution.py:234
  139.3 3.1 %copy.181 = bf16[8,256,640]{2,1,0:T(8,128)(2,1)S(1)} copy(bf16[8,256,640]{1,2,0:T(8,128)(2,1)} %fusion.6) | data formatting | bytes 5242880 | tf_op jit(solution)/shard_map/convert_element_type | solution.py:248
  142.5 42.2 %all_to_all.10 = bf16[128,16,640]{2,1,0:T(8,128)(2,1)S(1)} all-to-all(bf16[128,16,640]{2,1,0:T(8,128)(2,1)S(1)} %bitcast.223), channel_id=1, replica_groups=mesh['req'=32,'seq'=4] {'seq','req'}, dimensions={0} | all-to-all | bytes 5242880 | tf_op jit(solution)/shard_map/all_to_all | solution.py:249
  184.9 1.9 multiply_reduce_fusion.1
  186.9 13.8 %convolution_convert_fusion = bf16[512,2560]{1,0:T(8,128)(2,1)} fusion(bf16[2560,2560]{1,0:T(8,128)(2,1)} %param.22, f32[2560]{0:T(1024)S(1)} %copy-done.11, f32[512]{0:T(512)S(1)} %add_rsqrt_fusion, bf16[512,2560]{1,0:T(8,128)(2,1)S(1)} %copy-done.7, bf16[512,640]{1,0:T(8,128)(2,1)S(1)} %bitcast.234, bf16[512,640]{1,0:T(8,128)(2,1)S(1)} %bitcast.236, ...), kind=kOutput, calls=%fused_computation.16 | convolution fusion | flops 6734479360 | bytes 20983808 | tf_op jit(solution)/shard_map/dot_general | solution.py:253
  (110 shorter events, 7.8 us)
Async XLA Ops:
  0.6 3.1 %copy-start.9 = (bf16[512,256]{1,0:T(8,128)(2,1)S(1)}, bf16[512,256]{1,0:T(8,128)(2,1)}, u32[]{:S(2)}) copy-start(bf16[512,256]{1,0:T(8,128)(2,1)} %param.13) | copy-start | bytes 786436
  6.2 12.7 %copy-start.10 = (s32[64]{0:T(128)S(1)}, s32[64]{0:T(128)}, u32[]{:S(2)}) copy-start(s32[64]{0:T(128)} %param.23) | copy-start | bytes 772
  6.2 14.1 %copy-start.12 = (f32[40]{0:T(128)S(1)}, f32[40]{0:T(128)}, u32[]{:S(2)}) copy-start(f32[40]{0:T(128)} %param.18) | copy-start | bytes 484
  6.2 14.1 %copy-start.13 = (f32[40]{0:T(128)S(1)}, f32[40]{0:T(128)}, u32[]{:S(2)}) copy-start(f32[40]{0:T(128)} %param.20) | copy-start | bytes 484
  6.2 15.3 %copy-start.14 = (f32[40]{0:T(128)S(1)}, f32[40]{0:T(128)}, u32[]{:S(2)}) copy-start(f32[40]{0:T(128)} %param.19) | copy-start | bytes 484
  6.2 64.5 %all-to-all-start = ((bf16[128,16,906]{2,1,0:T(8,128)(2,1)}), bf16[128,16,906]{2,1,0:T(8,128)(2,1)}, u32[]{:S(2)}, u32[]{:S(2)}) async-start(bf16[128,16,906]{2,1,0:T(8,128)(2,1)} %bitcast.222), calls=%async_computation | async-start | bytes 8388608 | tf_op jit(solution)/shard_map/all_to_all | solution.py:147
  73.6 7.5 %collective-permute-start = (bf16[3,896]{1,0:T(4,128)(2,1)S(1)}, bf16[3,896]{1,0:T(4,128)(2,1)S(1)}, u32[]{:S(2)}, u32[]{:S(2)}) collective-permute-start(bf16[3,896]{1,0:T(4,128)(2,1)S(1)} %slice.320), channel_id=1, source_target_pairs={{0,4},{4,8},{8,12},{12,16},{16,20},{20,24},{24,28},{28,32},{32,36}... | collective-permute-start | bytes 16136 | tf_op jit(solution)/shard_map/ppermute | solution.py:13
  84.3 1.8 copy-start.2
  92.1 5.6 %copy-start = (bf16[2048,640]{1,0:T(8,128)(2,1)}, bf16[2048,640]{1,0:T(8,128)(2,1)S(1)}, u32[]{:S(2)}) copy-start(bf16[2048,640]{1,0:T(8,128)(2,1)S(1)} %multiply_convert_fusion.3) | copy-start | bytes 7864324
  97.7 1.4 copy-start.3
  102.1 6.8 %copy-start.5 = (f32[8,256,256]{2,1,0:T(8,128)S(1)}, f32[8,256,256]{2,1,0:T(8,128)}, u32[]{:S(2)}) copy-start(f32[8,256,256]{2,1,0:T(8,128)} %fusion.17) | copy-start | bytes 6291460
  104.4 24.7 %collective-permute-start.1 = (f32[10,8320]{1,0:T(8,128)}, f32[10,8320]{1,0:T(8,128)S(1)}, u32[]{:S(2)}, u32[]{:S(2)}) collective-permute-start(f32[10,8320]{1,0:T(8,128)} %pad_maximum_fusion.4), channel_id=1, source_target_pairs={{0,4},{4,8},{8,12},{12,16},{16,20},{20,24},{24,28},{28,32},{32,36}... | collective-permute-start | bytes 998408 | tf_op jit(solution)/shard_map/ppermute | solution.py:13
  106.3 23.0 %collective-permute-start.2 = (f32[10,8320]{1,0:T(8,128)}, f32[10,8320]{1,0:T(8,128)}, u32[]{:S(2)}, u32[]{:S(2)}) collective-permute-start(f32[10,8320]{1,0:T(8,128)} %pad_maximum_fusion.4), channel_id=1, source_target_pairs={{0,8},{4,12},{8,16},{12,20},{16,24},{20,28},{24,32},{28,36},{32,40... | collective-permute-start | bytes 998408 | tf_op jit(solution)/shard_map/ppermute | solution.py:13
  115.1 4.0 %copy-start.1 = (bf16[8,10,256,256]{3,2,0,1:T(8,128)(2,1)}, bf16[8,10,256,256]{3,2,0,1:T(8,128)(2,1)S(1)}, u32[]{:S(2)}) copy-start(bf16[8,10,256,256]{3,2,0,1:T(8,128)(2,1)S(1)} %multiply_convert_fusion) | copy-start | bytes 31457284
  119.5 2.3 %copy-start.6 = (f32[8,256,640]{1,2,0:T(8,128)}, f32[8,256,640]{1,2,0:T(8,128)S(1)}, u32[]{:S(2)}) copy-start(f32[8,256,640]{1,2,0:T(8,128)S(1)} %convolution_dynamic-update-slice_fusion.1) | copy-start | bytes 15728644
  129.2 1.8 copy-start.8
  130.7 4.4 %slice-start.2 = ((s8[5242880]{0:T(1024)(128)(4,1)}), s8[4194304]{0:T(1024)(128)(4,1)S(1)}, s32[]{:S(2)}) async-start(s8[5242880]{0:T(1024)(128)(4,1)} %bitcast.228), calls=%async_computation.4 | async-start | bytes 8388608
  130.9 4.2 %slice-start = ((s8[5242880]{0:T(1024)(128)(4,1)}), s8[1048576]{0:T(1024)(128)(4,1)S(1)}, s32[]{:S(2)}) async-start(s8[5242880]{0:T(1024)(128)(4,1)} %bitcast.220), calls=%async_computation.2 | async-start | bytes 2097152
  131.0 4.1 %slice-start.3 = ((s8[5242880]{0:T(1024)(128)(4,1)}), s8[1048576]{0:T(1024)(128)(4,1)S(1)}, s32[]{:S(2)}) async-start(s8[5242880]{0:T(1024)(128)(4,1)} %bitcast.228), calls=%async_computation.5 | async-start | bytes 2097152
  133.1 2.0 %copy-start.4 = (bf16[2048,256]{1,0:T(8,128)(2,1)S(1)}, bf16[2048,256]{1,0:T(8,128)(2,1)}, u32[]{:S(2)}) copy-start(bf16[2048,256]{1,0:T(8,128)(2,1)} %copy-done.2) | copy-start | bytes 3145732
  133.1 3.6 %slice-start.1 = ((s8[5242880]{0:T(1024)(128)(4,1)}), s8[4194304]{0:T(1024)(128)(4,1)S(1)}, s32[]{:S(2)}) async-start(s8[5242880]{0:T(1024)(128)(4,1)} %bitcast.220), calls=%async_computation.3 | async-start | bytes 8388608
  142.5 42.5 %copy-start.7 = (bf16[512,2560]{1,0:T(8,128)(2,1)S(1)}, bf16[512,2560]{1,0:T(8,128)(2,1)}, u32[]{:S(2)}) copy-start(bf16[512,2560]{1,0:T(8,128)(2,1)} %param.14) | copy-start | bytes 7864324
  184.7 2.2 %copy-start.11 = (f32[2560]{0:T(1024)S(1)}, f32[2560]{0:T(1024)}, u32[]{:S(2)}) copy-start(f32[2560]{0:T(1024)} %param.21) | copy-start | bytes 30724

commit v13 on v12

--- a/solution.py
+++ b/solution.py
@@ -180,27 +180,31 @@
         preferred_element_type=jnp.float32,
     )
     tail_weight = jnp.exp(log_decay[:, -1:, :] - log_decay) * step_size
-    weighted_x = (x_heads.astype(jnp.float32) * tail_weight[..., None]).astype(jnp.bfloat16)
+    weighted_x = (
+        x_heads.astype(jnp.float32) * tail_weight[..., None]
+    ).astype(jnp.bfloat16).reshape(stretch_count, STRETCH, width)
     stretch_state = jnp.einsum(
-        "cuhp,cun->chpn", weighted_x, b_mat, preferred_element_type=jnp.float32
-    )
-    carried = jnp.where(starts[:, None], 0.0, jnp.exp(log_decay[:, -1, :]))
-    total = (jnp.ones((share,), jnp.float32), jnp.zeros((share, head_dim, N), jnp.float32))
+        "cun,cuq->cnq", b_mat, weighted_x, preferred_element_type=jnp.float32
+    )
+    carried = jnp.repeat(
+        jnp.where(starts[:, None], 0.0, jnp.exp(log_decay[:, -1, :])), head_dim, axis=-1
+    )
+
+    def chain_cols(earlier, later):
+        return (earlier[0] * later[0], later[0][None, :] * earlier[1] + later[1])
+
+    total = (jnp.ones((width,), jnp.float32), jnp.zeros((N, width), jnp.float32))
     for stretch in range(stretch_count):
-        total = chain_states(total, (carried[stretch], stretch_state[stretch]))
+        total = chain_cols(total, (carried[stretch], stretch_state[stretch]))
     reach = -(-(LMAX_CH - 1) // stretch_count)
-    cells = head_dim * N
-    packed = jnp.concatenate(
-        [total[1].reshape(share, cells), jnp.broadcast_to(total[0][:, None], (share, 128))],
-        axis=1,
-    )
+    packed = jnp.concatenate([total[1], total[0][None, :]], axis=0)
 
     def unpack(moved):
-        return (moved[:, cells], moved[:, :cells].reshape(share, head_dim, N))
+        return (moved[N], moved[:N])
 
     behind = unpack(from_behind(packed, "req", reach))
     for step in range(reach - 1, 0, -1):
-        behind = chain_states(behind, unpack(from_behind(packed, "req", step)))
+        behind = chain_cols(behind, unpack(from_behind(packed, "req", step)))
     state_prev = behind[1]
 
     scores = jnp.einsum("ctn,cun->ctu", c_mat, b_mat, preferred_element_type=jnp.float32)
@@ -225,14 +229,15 @@
     )
     weights = jnp.where(live, jnp.prod(factors, axis=2), 0.0)
     sources = jnp.concatenate([state_prev[None], stretch_state], axis=0)
-    state_in_all = jnp.sum(weights[:, :, :, None, None] * sources[None], axis=1)
-    state_out_all = gains[:, :, None, None] * state_in_all + stretch_state
-    endings = jnp.where(finals[:, None, None, None], state_out_all, 0.0)
-    state_ins = [state_in_all[c] for c in range(stretch_count)]
-    state_low = jnp.stack(state_ins, axis=0).astype(jnp.bfloat16)
-    state_low = state_low.reshape(stretch_count, width, N)
+    weights = jnp.repeat(weights, head_dim, axis=-1)
+    state_in_all = jnp.sum(weights[:, :, None, :] * sources[None], axis=1)
+    gains_cols = jnp.repeat(gains, head_dim, axis=-1)
+    state_out_all = gains_cols[:, None, :] * state_in_all + stretch_state
+    endings = jnp.where(finals[:, None, None], state_out_all, 0.0)
+    endings = endings.reshape(stretch_count, N, share, head_dim).transpose(0, 2, 3, 1)
+    state_low = state_in_all.astype(jnp.bfloat16)
     y_off = jnp.repeat(jnp.exp(log_decay), head_dim, axis=-1) * jnp.einsum(
-        "ctn,cqn->ctq", c_mat, state_low, preferred_element_type=jnp.float32
+        "ctn,cnq->ctq", c_mat, state_low, preferred_element_type=jnp.float32
     )
     y_diag = jnp.concatenate(
         [

time: 202 us -> 213 us (1.054)
  blocking collectives: 42.2 us -> 0 us
  waiting for transfers between devices: 48.1 us -> 76.7 us
  local copies, waits for them, and re-layouts: 36.1 us -> 46.1 us
  starting transfers between devices: 19.5 us -> 26.3 us
  matrix products: 25.9 us -> 30.1 us
  other arithmetic: 27.5 us -> 31.4 us
    all_to_all x1 -> x0, blocking collectives: 42.2 us -> none  [per_device(): back = lax.all_to_all(mixed, ('seq', 'req'), 0, 0, tiled=True)]
    all_to_all x0 -> x1, waiting for transfers between devices: none -> 28.6 us  [per_device(): back = lax.all_to_all(mixed, ('seq', 'req'), 0, 0, tiled=True)]
    mul x2 -> x7, local copies, waits for them, and re-layouts: 0.06 us -> 9.1 us  [the longest x2 8.68 us: per_device(): x_heads.astype(jnp.float32) * tail_weight[..., None]]
    all_to_all x0 -> x1, starting transfers between devices: none -> 7.36 us  [per_device(): back = lax.all_to_all(mixed, ('seq', 'req'), 0, 0, tiled=True)]
    dot_general x2, matrix products: 3.53 us -> 9.81 us  [the longest x1 5.48 us: per_device(): jnp.einsum('ctn,cnq->ctq', c_mat, state_low, preferred_element_type=jnp.f...]
    convert_element_type x2, other arithmetic: 9.16 us -> 14 us  [causal_conv(): return jax.nn.silu(running).astype(jnp.bfloat16)]
    unnamed x60 -> x35, local copies, waits for them, and re-layouts: 10.4 us -> 5.78 us
    select_n x0 -> x2, local copies, waits for them, and re-layouts: none -> 3.38 us  [the longest x1 3.36 us: per_device(): endings = jnp.where(finals[:, None, None], state_out_all, 0.0)]
  transfers between devices with their start and end apart: 4 -> 5, of which waited for: 1 -> 2; matrix products, arithmetic and copies ran while one was open for 13% -> 18% of each run, Pallas kernels for 0% -> 0%
where the time goes in v13:
time: 213 us; the launch traced here: 212 us
  waiting for transfers between devices  76.7 us (36%)
  local copies, waits for them, and re-layouts  46.1 us (22%)
  other arithmetic  31.4 us (15%)
  matrix products  30.1 us (14%)
  starting transfers between devices  26.3 us (12%)
    all_to_all x1, waiting for transfers between devices, per_device(): inbound = lax.all_to_all(outbound, ('seq', 'req'), 0, 0, tiled=True)  48.1 us
    all_to_all x1, waiting for transfers between devices, per_device(): back = lax.all_to_all(mixed, ('seq', 'req'), 0, 0, tiled=True)  28.6 us
    convert_element_type x2, other arithmetic, causal_conv(): return jax.nn.silu(running).astype(jnp.bfloat16)  14 us
    dot_general x1, matrix products, per_device(): jnp.dot(normed, w_out, preferred_element_type=jnp.float32)  13.8 us
    all_to_all x1, starting transfers between devices, per_device(): inbound = lax.all_to_all(outbound, ('seq', 'req'), 0, 0, tiled=True)  12 us
    mul x2, local copies, waits for them, and re-layouts, per_device(): x_heads.astype(jnp.float32) * tail_weight[..., None]  8.68 us
    all_to_all x1, starting transfers between devices, per_device(): back = lax.all_to_all(mixed, ('seq', 'req'), 0, 0, tiled=True)  7.36 us
    ppermute x3, starting transfers between devices, from_behind(): lax.ppermute(value, axis, [(source, source + steps) for source in range(l...  6.96 us
  transfers between devices with their start and end apart: 5, of which 2 were waited for; matrix products, arithmetic and copies ran while one was open for 18% of the time, Pallas kernels for 0%

profile of v13, /device:TPU:1, one launch (start us, length us, event | category | flops | bytes accessed | tf_op | source)
XLA Modules:
  0.0 211.7 jit_solution(3212775833443646161)
XLA Ops:
  0.6 0.9 slice_bitcast_fusion.36
  1.8 1.9 slice_bitcast_fusion.23
  3.8 2.3 %pad_maximum_fusion = bf16[4,512,906]{2,1,0:T(8,128)(2,1)} fusion(bf16[4,512,10]{2,1,0:T(8,128)(2,1)S(1)} %copy.128, bf16[4,512,256]{2,1,0:T(8,128)(2,1)S(1)} %broadcast_in_dim.255, bf16[1,512,640]{2,1,0:T(8,128)(2,1)S(1)} %get-tuple-element.24, bf16[1,512,640]{2,1,0:T(8,128)(2,1)S(1)} %get-tuple-element.25, bf16[1,512,640]{2,1,0:T(8,128)(2,1)S(1)} %get-tuple-element.23, ...), kind=kLoop, calls=%fused_computation.17 | loop fusion | flops 22265856 | bytes 7421952 | tf_op jit(solution)/shard_map/concatenate | solution.py:145
  6.2 12.0 %all-to-all-start = ((bf16[128,16,906]{2,1,0:T(8,128)(2,1)}), bf16[128,16,906]{2,1,0:T(8,128)(2,1)}, u32[]{:S(2)}, u32[]{:S(2)}) async-start(bf16[128,16,906]{2,1,0:T(8,128)(2,1)} %bitcast.231), calls=%async_computation | async-start | bytes 8388608 | tf_op jit(solution)/shard_map/all_to_all | solution.py:147
  18.2 0.7 slice.268
  19.5 0.8 dynamic_slice.17
  20.5 0.9 dynamic-slice_reduce_fusion.3
  21.8 0.8 fusion.70
  22.7 48.1 %all-to-all-done = bf16[128,16,906]{2,1,0:T(8,128)(2,1)} async-done(((bf16[128,16,906]{2,1,0:T(8,128)(2,1)}), bf16[128,16,906]{2,1,0:T(8,128)(2,1)}, u32[]{:S(2)}, u32[]{:S(2)}) %all-to-all-start) | async-done | bytes 3711008 | tf_op jit(solution)/shard_map/all_to_all | solution.py:147
  70.7 1.1 slice.360
  71.8 0.7 slice.351
  73.6 3.1 %collective-permute-start = (bf16[3,896]{1,0:T(4,128)(2,1)S(1)}, bf16[3,896]{1,0:T(4,128)(2,1)S(1)}, u32[]{:S(2)}, u32[]{:S(2)}) collective-permute-start(bf16[3,896]{1,0:T(4,128)(2,1)S(1)} %slice.351), channel_id=1, source_target_pairs={{0,4},{4,8},{8,12},{12,16},{16,20},{20,24},{24,28},{28,32},{32,36}... | collective-permute-start | bytes 16136 | tf_op jit(solution)/shard_map/ppermute | solution.py:13
  77.1 1.3 slice.353
  78.4 3.5 %slice.363 = bf16[2048,640]{1,0:T(8,128)(2,1)} slice(bf16[2048,906]{1,0:T(8,128)(2,1)} %bitcast.11), slice={[0:2048], [0:640]} | slice | bytes 5242880 | tf_op jit(solution)/shard_map/slice | solution.py:149
  81.9 2.7 %mul.419 = f32[8,256,10,64]{1,3,2,0:T(8,128)} broadcast(f32[8,256,10]{1,2,0:T(8,128)S(1)} %get-tuple-element.27), dimensions={0,1,2} | broadcast | bytes 5324800 | tf_op jit(solution)/shard_map/mul | solution.py:184
  84.6 6.0 %copy.147 = f32[8,256,640]{2,1,0:T(8,128)} copy(f32[8,256,640]{1,2,0:T(8,128)} %bitcast.230) | data formatting | bytes 10485760 | tf_op jit(solution)/shard_map/mul | solution.py:184
  92.3 3.2 %multiply_convert_fusion.6 = bf16[2048,256]{1,0:T(8,128)(2,1)S(1)} fusion(bf16[2048,256]{1,0:T(8,128)(2,1)S(1)} %slice.353, bf16[3,256]{1,0:T(4,128)(2,1)S(1)} %slice.352, f32[256]{0:T(256)S(1)} %bitcast.253, f32[256]{0:T(256)S(1)} %bitcast.251, f32[256]{0:T(256)S(1)} %bitcast.252, f32[256]{0:T(256)S(1)} %bitcast.250, f32[256]{0:T(256)S(1)} %slice.268, ...), kind=kLoop, calls=%fused_computation.28 | loop fusion | flops 15728640 | bytes 2112000 | tf_op jit(solution)/shard_map/convert_element_type | solution.py:67
  95.5 1.7 fusion.18
  97.3 10.8 %multiply_convert_fusion.3 = bf16[2048,640]{1,0:T(8,128)(2,1)S(1)} fusion(bf16[2048,640]{1,0:T(8,128)(2,1)} %slice.363, bf16[3,640]{1,0:T(4,128)(2,1)S(1)} %slice.362, f32[640]{0:T(1024)S(1)} %get-tuple-element.5, f32[640]{0:T(1024)S(1)} %get-tuple-element.3, f32[640]{0:T(1024)S(1)} %get-tuple-element.4, f32[640]{0:T(1024)S(1)} %get-tuple-element.2, ...), kind=kLoop, calls=%fused_computation.15 | loop fusion | flops 39321600 | bytes 5267712 | tf_op jit(solution)/shard_map/convert_element_type | solution.py:67
  108.1 3.0 %copy.134 = bf16[2048,640]{0,1:T(8,128)(2,1)} copy(bf16[2048,640]{1,0:T(8,128)(2,1)S(1)} %multiply_convert_fusion.3) | data formatting | bytes 5242880 | tf_op jit(solution)/shard_map/convert_element_type | solution.py:67
  111.1 3.3 %copy.150 = f32[8,256,640]{1,2,0:T(8,128)} copy(bf16[8,256,640]{2,1,0:T(8,128)(2,1)S(1)} %bitcast.226) | data formatting | bytes 7864320 | tf_op jit(solution)/shard_map/convert_element_type | solution.py:184
  114.4 4.3 %fusion.9 = f32[8,128,640]{2,1,0:T(8,128)S(1)} fusion(f32[8,256,640]{2,1,0:T(8,128)} %copy.147, bf16[8,256,640]{2,1,0:T(8,128)(2,1)} %bitcast.227, bf16[8,256,256]{2,1,0:T(8,128)(2,1)} %bitcast.236), kind=kOutput, calls=%fused_computation.23 | convolution fusion | flops 339476480 | bytes 11010048 | tf_op jit(solution)/shard_map/cun,cuq->cnq/dot_general | solution.py:186
  118.9 1.9 collective-permute-start.1
  120.8 2.0 collective-permute-start.2
  122.9 0.9 copy.167
  123.9 0.5 copy-done.5
  124.4 6.1 %multiply_convert_fusion = bf16[8,10,256,256]{3,2,0,1:T(8,128)(2,1)S(1)} fusion(f32[8,10,256]{2,0,1:T(8,128)S(1)} %copy.133, f32[8,10,256]{2,0,1:T(8,128)S(1)} %copy.131, f32[8,256,256]{2,1,0:T(8,128)S(1)} %copy-done.5, pred[256,256]{1,0:T(8,128)(4,1)S(1)} %iota_compare_fusion), kind=kLoop, calls=%fused_computation.1 | loop fusion | flops 31457280 | bytes 12812288 | tf_op jit(solution)/shard_map/convert_element_type | solution.py:217
  131.0 0.4 convolution_dynamic-update-slice_fusion.8
  131.4 0.4 convolution_dynamic-update-slice_fusion.7
  131.8 0.4 convolution_dynamic-update-slice_fusion.6
  132.3 0.4 convolution_dynamic-update-slice_fusion.5
  132.7 0.4 convolution_dynamic-update-slice_fusion.4
  133.2 0.4 convolution_dynamic-update-slice_fusion.3
  133.6 0.4 convolution_dynamic-update-slice_fusion.2
  134.1 0.4 convolution_dynamic-update-slice_fusion.1
  134.5 0.4 convolution_dynamic-update-slice_fusion
  135.0 2.6 %copy-done.6 = f32[8,256,640]{1,2,0:T(8,128)} copy-done((f32[8,256,640]{1,2,0:T(8,128)}, f32[8,256,640]{1,2,0:T(8,128)S(1)}, u32[]{:S(2)}) %copy-start.6) | copy-done | bytes 5242904
  137.8 1.8 multiply_reduce_fusion
  139.7 1.5 copy-done.1
  141.2 5.5 %fusion.6 = bf16[8,256,640]{1,2,0:T(8,128)(2,1)} fusion(f32[8,256,640]{1,2,0:T(8,128)} %copy-done.6, f32[8,256,640]{1,2,0:T(8,128)S(1)} %bitcast.229, f32[640]{0:T(1024)S(1)} %mul.443, f32[8,256,10]{1,2,0:T(8,128)S(1)} %get-tuple-element.26, f32[8,128,640]{2,1,0:T(8,128)S(1)} %multiply_reduce_fusion, bf16[8,256,256]{2,1,0:T(8,128)(2,1)S(1)} %bitcast.237), kind=kOutput, calls=%fused_computation.11 | convolution fusion | flops 342753280 | bytes 16388096 | tf_op jit(solution)/shard_map/ctn,cnq->ctq/dot_general | solution.py:239
  146.6 4.4 %copy.151 = bf16[8,256,640]{2,1,0:T(8,128)(2,1)} copy(bf16[8,256,640]{1,2,0:T(8,128)(2,1)} %fusion.6) | data formatting | bytes 5242880 | tf_op jit(solution)/shard_map/convert_element_type | solution.py:253
  151.0 7.4 %all-to-all-start.1 = ((bf16[128,16,640]{2,1,0:T(8,128)(2,1)}), bf16[128,16,640]{2,1,0:T(8,128)(2,1)}, u32[]{:S(2)}, u32[]{:S(2)}) async-start(bf16[128,16,640]{2,1,0:T(8,128)(2,1)} %bitcast.233), calls=%async_computation.1 | async-start | bytes 5242880 | tf_op jit(solution)/shard_map/all_to_all | solution.py:254
  158.5 3.6 %add_select_fusion = f32[8,128,640]{2,1,0:T(8,128)} fusion(f32[8,128,640]{2,1,0:T(8,128)S(1)} %fusion.9, f32[8,128,640]{2,1,0:T(8,128)} %copy-done.1, f32[8,640]{1,0:T(8,128)S(1)} %mul.453, pred[8]{0:T(512)(128)(4,1)S(1)} %get-tuple-element.6), kind=kLoop, calls=%fused_computation.25 | loop fusion | flops 1966080 | bytes 7884808 | tf_op jit(solution)/shard_map/jit(_where)/select_n | solution.py:236
  162.1 3.4 %copy.152 = f32[8,128,640]{1,2,0:T(8,128)} copy(f32[8,128,640]{2,1,0:T(8,128)} %add_select_fusion) | data formatting | bytes 5242880 | tf_op jit(solution)/shard_map/jit(_where)/select_n | solution.py:236
  165.5 28.6 %all-to-all-done.1 = bf16[128,16,640]{2,1,0:T(8,128)(2,1)} async-done(((bf16[128,16,640]{2,1,0:T(8,128)(2,1)}), bf16[128,16,640]{2,1,0:T(8,128)(2,1)}, u32[]{:S(2)}, u32[]{:S(2)}) %all-to-all-start.1) | async-done | bytes 2621472 | tf_op jit(solution)/shard_map/all_to_all | solution.py:254
  194.1 1.9 fusion.68
  196.0 1.9 multiply_reduce_fusion.1
  198.0 13.8 %convolution_convert_fusion = bf16[512,2560]{1,0:T(8,128)(2,1)} fusion(bf16[2560,2560]{1,0:T(8,128)(2,1)} %param.22, f32[2560]{0:T(1024)S(1)} %copy-done.10, f32[512]{0:T(512)S(1)} %add_rsqrt_fusion, bf16[512,2560]{1,0:T(8,128)(2,1)S(1)} %copy-done.7, bf16[512,640]{1,0:T(8,128)(2,1)S(1)} %bitcast.241, bf16[512,640]{1,0:T(8,128)(2,1)S(1)} %bitcast.243, ...), kind=kOutput, calls=%fused_computation.16 | convolution fusion | flops 6734479360 | bytes 20983808 | tf_op jit(solution)/shard_map/dot_general | solution.py:258
  (107 shorter events, 6.0 us)
Async XLA Ops:
  0.6 3.1 %copy-start.8 = (bf16[512,256]{1,0:T(8,128)(2,1)S(1)}, bf16[512,256]{1,0:T(8,128)(2,1)}, u32[]{:S(2)}) copy-start(bf16[512,256]{1,0:T(8,128)(2,1)} %param.13) | copy-start | bytes 786436
  6.2 12.7 %copy-start.9 = (s32[64]{0:T(128)S(1)}, s32[64]{0:T(128)}, u32[]{:S(2)}) copy-start(s32[64]{0:T(128)} %param.23) | copy-start | bytes 772
  6.2 14.1 %copy-start.11 = (f32[40]{0:T(128)S(1)}, f32[40]{0:T(128)}, u32[]{:S(2)}) copy-start(f32[40]{0:T(128)} %param.18) | copy-start | bytes 484
  6.2 14.1 %copy-start.12 = (f32[40]{0:T(128)S(1)}, f32[40]{0:T(128)}, u32[]{:S(2)}) copy-start(f32[40]{0:T(128)} %param.20) | copy-start | bytes 484
  6.2 15.3 %copy-start.13 = (f32[40]{0:T(128)S(1)}, f32[40]{0:T(128)}, u32[]{:S(2)}) copy-start(f32[40]{0:T(128)} %param.19) | copy-start | bytes 484
  6.2 64.5 %all-to-all-start = ((bf16[128,16,906]{2,1,0:T(8,128)(2,1)}), bf16[128,16,906]{2,1,0:T(8,128)(2,1)}, u32[]{:S(2)}, u32[]{:S(2)}) async-start(bf16[128,16,906]{2,1,0:T(8,128)(2,1)} %bitcast.231), calls=%async_computation | async-start | bytes 8388608 | tf_op jit(solution)/shard_map/all_to_all | solution.py:147
  73.6 18.7 %collective-permute-start = (bf16[3,896]{1,0:T(4,128)(2,1)S(1)}, bf16[3,896]{1,0:T(4,128)(2,1)S(1)}, u32[]{:S(2)}, u32[]{:S(2)}) collective-permute-start(bf16[3,896]{1,0:T(4,128)(2,1)S(1)} %slice.351), channel_id=1, source_target_pairs={{0,4},{4,8},{8,12},{12,16},{16,20},{20,24},{24,28},{28,32},{32,36}... | collective-permute-start | bytes 16136 | tf_op jit(solution)/shard_map/ppermute | solution.py:13
  95.5 1.7 copy-start.3
  108.1 3.0 %copy-start = (bf16[2048,640]{1,0:T(8,128)(2,1)}, bf16[2048,640]{1,0:T(8,128)(2,1)S(1)}, u32[]{:S(2)}) copy-start(bf16[2048,640]{1,0:T(8,128)(2,1)S(1)} %multiply_convert_fusion.3) | copy-start | bytes 7864324
  114.4 8.5 %copy-start.2 = (bf16[2048,640]{0,1:T(8,128)(2,1)S(1)}, bf16[2048,640]{0,1:T(8,128)(2,1)}, u32[]{:S(2)}) copy-start(bf16[2048,640]{0,1:T(8,128)(2,1)} %copy.134) | copy-start | bytes 7864324
  118.9 16.0 %collective-permute-start.1 = (f32[129,640]{1,0:T(8,128)S(1)}, f32[129,640]{1,0:T(8,128)S(1)}, u32[]{:S(2)}, u32[]{:S(2)}) collective-permute-start(f32[129,640]{1,0:T(8,128)S(1)} %pad_maximum_fusion.4), channel_id=1, source_target_pairs={{0,4},{4,8},{8,12},{12,16},{16,20},{20,24},{24,28},{28,32},{32,36}... | collective-permute-start | bytes 990728 | tf_op jit(solution)/shard_map/ppermute | solution.py:13
  120.8 14.1 %collective-permute-start.2 = (f32[129,640]{1,0:T(8,128)S(1)}, f32[129,640]{1,0:T(8,128)S(1)}, u32[]{:S(2)}, u32[]{:S(2)}) collective-permute-start(f32[129,640]{1,0:T(8,128)S(1)} %pad_maximum_fusion.4), channel_id=1, source_target_pairs={{0,8},{4,12},{8,16},{12,20},{16,24},{20,28},{24,32},{28,36},{32,40... | collective-permute-start | bytes 990728 | tf_op jit(solution)/shard_map/ppermute | solution.py:13
  122.8 1.6 copy-start.5
  134.9 2.7 %copy-start.6 = (f32[8,256,640]{1,2,0:T(8,128)}, f32[8,256,640]{1,2,0:T(8,128)S(1)}, u32[]{:S(2)}) copy-start(f32[8,256,640]{1,2,0:T(8,128)S(1)} %convolution_dynamic-update-slice_fusion) | copy-start | bytes 15728644
  135.0 6.2 %slice-start = ((s8[5242880]{0:T(1024)(128)(4,1)}), s8[4194304]{0:T(1024)(128)(4,1)S(1)}, s32[]{:S(2)}) async-start(s8[5242880]{0:T(1024)(128)(4,1)} %bitcast.228), calls=%async_computation.2 | async-start | bytes 8388608
  137.6 3.5 %slice-start.1 = ((s8[5242880]{0:T(1024)(128)(4,1)}), s8[1048576]{0:T(1024)(128)(4,1)S(1)}, s32[]{:S(2)}) async-start(s8[5242880]{0:T(1024)(128)(4,1)} %bitcast.228), calls=%async_computation.3 | async-start | bytes 2097152
  137.6 3.5 %copy-start.4 = (bf16[2048,256]{1,0:T(8,128)(2,1)S(1)}, bf16[2048,256]{1,0:T(8,128)(2,1)}, u32[]{:S(2)}) copy-start(bf16[2048,256]{1,0:T(8,128)(2,1)} %copy-done.3) | copy-start | bytes 3145732
  139.6 1.5 copy-start.1
  151.0 43.1 %all-to-all-start.1 = ((bf16[128,16,640]{2,1,0:T(8,128)(2,1)}), bf16[128,16,640]{2,1,0:T(8,128)(2,1)}, u32[]{:S(2)}, u32[]{:S(2)}) async-start(bf16[128,16,640]{2,1,0:T(8,128)(2,1)} %bitcast.233), calls=%async_computation.1 | async-start | bytes 5242880 | tf_op jit(solution)/shard_map/all_to_all | solution.py:254
  162.1 33.9 %copy-start.7 = (bf16[512,2560]{1,0:T(8,128)(2,1)S(1)}, bf16[512,2560]{1,0:T(8,128)(2,1)}, u32[]{:S(2)}) copy-start(bf16[512,2560]{1,0:T(8,128)(2,1)} %param.14) | copy-start | bytes 7864324
  165.5 32.5 %copy-start.10 = (f32[2560]{0:T(1024)S(1)}, f32[2560]{0:T(1024)}, u32[]{:S(2)}) copy-start(f32[2560]{0:T(1024)} %param.21) | copy-start | bytes 30724

commit v14 on v12

--- a/solution.py
+++ b/solution.py
@@ -140,15 +140,17 @@
     block = lax.axis_index("req")
 
     x_slabs = jnp.stack([x_in[:, g * width : (g + 1) * width] for g in range(n_seq)], axis=0)
-    dt_slabs = jnp.stack([dt_raw[:, g * share : (g + 1) * share] for g in range(n_seq)], axis=0)
     bc_slabs = jnp.broadcast_to(bc_in[None], (n_seq, tok_rows, bc_width))
-    outbound = jnp.concatenate([x_slabs, bc_slabs, dt_slabs], axis=2)
+    outbound = jnp.concatenate([x_slabs, bc_slabs], axis=2)
+    dt_chunks = dt_raw.reshape(n_req, chunk, n_seq, share).transpose(2, 0, 1, 3)
+    dt_chunks = dt_chunks.reshape(n_seq * n_req, chunk * share)
+    dt_rows = lax.all_to_all(dt_chunks, ("seq", "req"), 0, 0, tiled=True)
+    dt_rows = dt_rows.reshape(n_seq * tok_rows, share)
     outbound = outbound.reshape(n_seq * n_req, chunk, -1)
     inbound = lax.all_to_all(outbound, ("seq", "req"), 0, 0, tiled=True)
     inbound = inbound.reshape(n_seq * tok_rows, -1)
     x_rows = inbound[:, :width]
     bc_rows = inbound[:, width : width + bc_width]
-    dt_rows = inbound[:, width + bc_width :]
 
     row_count = x_rows.shape[0]
     stretch_count = row_count // STRETCH

time: 202 us -> 208 us (1.030)
  starting transfers between devices: 19.5 us -> 26.8 us
  waiting for transfers between devices: 48.1 us -> 45.4 us
    all_to_all x0 -> x1, starting transfers between devices: none -> 11.5 us  [per_device(): dt_rows = lax.all_to_all(dt_chunks, ('seq', 'req'), 0, 0, tiled=True)]
    all_to_all x1, waiting for transfers between devices: 48.1 us -> 42.8 us  [per_device(): inbound = lax.all_to_all(outbound, ('seq', 'req'), 0, 0, tiled=True)]
    all_to_all x1, starting transfers between devices: 12 us -> 7.58 us  [per_device(): inbound = lax.all_to_all(outbound, ('seq', 'req'), 0, 0, tiled=True)]
    all_to_all x0 -> x1, waiting for transfers between devices: none -> 2.6 us  [per_device(): dt_rows = lax.all_to_all(dt_chunks, ('seq', 'req'), 0, 0, tiled=True)]
    unnamed x60 -> x58, local copies, waits for them, and re-layouts: 10.4 us -> 10.1 us
  transfers between devices with their start and end apart: 4 -> 5, of which waited for: 1 -> 2; matrix products, arithmetic and copies ran while one was open for 13% -> 16% of each run, Pallas kernels for 0% -> 0%
where the time goes in v14:
time: 208 us; the launch traced here: 207 us
  waiting for transfers between devices  45.4 us (22%)
  blocking collectives  42.9 us (21%)
  local copies, waits for them, and re-layouts  36.8 us (18%)
  other arithmetic  27.5 us (13%)
  starting transfers between devices  26.8 us (13%)
  matrix products  26 us (12%)
    all_to_all x1, blocking collectives, per_device(): back = lax.all_to_all(mixed, ('seq', 'req'), 0, 0, tiled=True)  42.9 us
    all_to_all x1, waiting for transfers between devices, per_device(): inbound = lax.all_to_all(outbound, ('seq', 'req'), 0, 0, tiled=True)  42.8 us
    dot_general x1, matrix products, per_device(): jnp.dot(normed, w_out, preferred_element_type=jnp.float32)  13.8 us
    all_to_all x1, starting transfers between devices, per_device(): dt_rows = lax.all_to_all(dt_chunks, ('seq', 'req'), 0, 0, tiled=True)  11.5 us
    unnamed x58, local copies, waits for them, and re-layouts  10.1 us
    convert_element_type x2, other arithmetic, causal_conv(): return jax.nn.silu(running).astype(jnp.bfloat16)  9.17 us
    ppermute x3, starting transfers between devices, from_behind(): lax.ppermute(value, axis, [(source, source + steps) for source in range(l...  7.68 us
    all_to_all x1, starting transfers between devices, per_device(): inbound = lax.all_to_all(outbound, ('seq', 'req'), 0, 0, tiled=True)  7.58 us
  transfers between devices with their start and end apart: 5, of which 2 were waited for; matrix products, arithmetic and copies ran while one was open for 16% of the time, Pallas kernels for 0%

profile of v14, /device:TPU:1, one launch (start us, length us, event | category | flops | bytes accessed | tf_op | source)
XLA Modules:
  0.0 206.7 jit_solution(7878601279740978176)
XLA Ops:
  0.7 1.1 reshape.323
  2.1 0.8 copy.112
  2.9 11.5 %all-to-all-start.1 = ((bf16[128,1,160]{2,1,0:T(2,128)(2,1)}), bf16[128,1,160]{2,1,0:T(2,128)(2,1)S(1)}, u32[]{:S(2)}, u32[]{:S(2)}) async-start(bf16[128,1,160]{2,1,0:T(2,128)(2,1)} %copy.112), calls=%async_computation.1 | async-start | bytes 262144 | tf_op jit(solution)/shard_map/all_to_all | solution.py:147
  14.4 1.9 slice_bitcast_fusion.23
  16.8 2.0 pad_maximum_fusion
  18.9 0.7 slice.230
  19.7 0.8 dynamic_slice.17
  20.8 0.9 dynamic-slice_reduce_fusion.3
  21.8 2.6 %all-to-all-done.1 = bf16[128,1,160]{2,1,0:T(2,128)(2,1)S(1)} async-done(((bf16[128,1,160]{2,1,0:T(2,128)(2,1)}), bf16[128,1,160]{2,1,0:T(2,128)(2,1)S(1)}, u32[]{:S(2)}, u32[]{:S(2)}) %all-to-all-start.1) | async-done | bytes 40992 | tf_op jit(solution)/shard_map/all_to_all | solution.py:147
  24.4 7.6 %all-to-all-start = ((bf16[128,16,896]{2,1,0:T(8,128)(2,1)}), bf16[128,16,896]{2,1,0:T(8,128)(2,1)}, u32[]{:S(2)}, u32[]{:S(2)}) async-start(bf16[128,16,896]{2,1,0:T(8,128)(2,1)} %bitcast.213), calls=%async_computation | async-start | bytes 7340032 | tf_op jit(solution)/shard_map/all_to_all | solution.py:150
  32.1 0.6 iota_compare_fusion
  32.8 0.8 fusion.48
  34.1 0.6 reshape.329
  36.1 42.8 %all-to-all-done = bf16[128,16,896]{2,1,0:T(8,128)(2,1)} async-done(((bf16[128,16,896]{2,1,0:T(8,128)(2,1)}), bf16[128,16,896]{2,1,0:T(8,128)(2,1)}, u32[]{:S(2)}, u32[]{:S(2)}) %all-to-all-start) | async-done | bytes 3670048 | tf_op jit(solution)/shard_map/all_to_all | solution.py:150
  79.0 0.7 slice.300
  79.7 3.2 %collective-permute-start = (bf16[3,896]{1,0:T(4,128)(2,1)S(1)}, bf16[3,896]{1,0:T(4,128)(2,1)S(1)}, u32[]{:S(2)}, u32[]{:S(2)}) collective-permute-start(bf16[3,896]{1,0:T(4,128)(2,1)S(1)} %slice.300), channel_id=1, source_target_pairs={{0,4},{4,8},{8,12},{12,16},{16,20},{20,24},{24,28},{28,32},{32,36}... | collective-permute-start | bytes 16136 | tf_op jit(solution)/shard_map/ppermute | solution.py:13
  83.1 1.3 slice.302
  84.4 2.0 slice.311
  86.4 3.2 %multiply_convert_fusion.5 = bf16[2048,256]{1,0:T(8,128)(2,1)S(1)} fusion(bf16[2048,256]{1,0:T(8,128)(2,1)S(1)} %slice.302, bf16[3,256]{1,0:T(4,128)(2,1)S(1)} %slice.301, f32[256]{0:T(256)S(1)} %bitcast.255, f32[256]{0:T(256)S(1)} %bitcast.253, f32[256]{0:T(256)S(1)} %bitcast.254, f32[256]{0:T(256)S(1)} %bitcast.252, f32[256]{0:T(256)S(1)} %slice.230, ...), kind=kLoop, calls=%fused_computation.29 | loop fusion | flops 15728640 | bytes 2112000 | tf_op jit(solution)/shard_map/convert_element_type | solution.py:67
  89.6 1.8 fusion.17
  91.4 6.0 %multiply_convert_fusion.3 = bf16[2048,640]{1,0:T(8,128)(2,1)S(1)} fusion(bf16[2048,640]{1,0:T(8,128)(2,1)S(1)} %slice.311, bf16[3,640]{1,0:T(4,128)(2,1)S(1)} %slice.310, f32[640]{0:T(1024)S(1)} %get-tuple-element.5, f32[640]{0:T(1024)S(1)} %get-tuple-element.3, f32[640]{0:T(1024)S(1)} %get-tuple-element.4, f32[640]{0:T(1024)S(1)} %get-tuple-element.2, ...), kind=kLoop, calls=%fused_computation.15 | loop fusion | flops 39321600 | bytes 5267712 | tf_op jit(solution)/shard_map/convert_element_type | solution.py:67
  97.4 3.0 %copy.117 = bf16[2048,640]{0,1:T(8,128)(2,1)} copy(bf16[2048,640]{1,0:T(8,128)(2,1)S(1)} %multiply_convert_fusion.3) | data formatting | bytes 5242880 | tf_op jit(solution)/shard_map/convert_element_type | solution.py:67
  100.4 2.6 %copy.145 = bf16[80,8,8,256]{3,2,1,0:T(8,128)(2,1)S(1)} copy(bf16[80,8,8,256]{3,1,2,0:T(8,128)(2,1)} %bitcast.215) | data formatting | bytes 5242880
  103.0 0.9 fusion.47
  103.9 0.5 multiply_convert_fusion.2
  104.4 0.8 fusion.9
  108.9 0.8 pad_maximum_fusion.4
  109.7 1.9 collective-permute-start.1
  111.6 2.5 %collective-permute-start.2 = (f32[10,8320]{1,0:T(8,128)}, f32[10,8320]{1,0:T(8,128)}, u32[]{:S(2)}, u32[]{:S(2)}) collective-permute-start(f32[10,8320]{1,0:T(8,128)} %pad_maximum_fusion.4), channel_id=1, source_target_pairs={{0,8},{4,12},{8,16},{12,20},{16,24},{20,28},{24,32},{28,36},{32,40... | collective-permute-start | bytes 998408 | tf_op jit(solution)/shard_map/ppermute | solution.py:13
  114.2 6.1 %multiply_convert_fusion = bf16[8,10,256,256]{3,2,0,1:T(8,128)(2,1)S(1)} fusion(f32[8,10,256]{2,0,1:T(8,128)S(1)} %copy.116, f32[8,10,256]{2,0,1:T(8,128)S(1)} %copy.114, f32[8,256,256]{2,1,0:T(8,128)S(1)} %copy-done.5, pred[256,256]{1,0:T(8,128)(4,1)S(1)} %copy-done.8), kind=kLoop, calls=%fused_computation.1 | loop fusion | flops 31457280 | bytes 12812288 | tf_op jit(solution)/shard_map/convert_element_type | solution.py:215
  120.8 0.4 convolution_dynamic-update-slice_fusion.8
  121.2 0.4 convolution_dynamic-update-slice_fusion.7
  121.6 0.4 convolution_dynamic-update-slice_fusion.6
  122.5 0.4 convolution_dynamic-update-slice_fusion.4
  123.0 0.4 convolution_dynamic-update-slice_fusion.3
  123.4 0.4 convolution_dynamic-update-slice_fusion.2
  124.7 2.2 %copy-done.6 = f32[8,256,640]{1,2,0:T(8,128)} copy-done((f32[8,256,640]{1,2,0:T(8,128)}, f32[8,256,640]{1,2,0:T(8,128)S(1)}, u32[]{:S(2)}) %copy-start.6) | copy-done | bytes 5242904
  127.0 4.9 %copy.131 = f32[8,256,640]{1,2,0:T(8,128)} copy(bf16[8,256,640]{2,1,0:T(8,128)(2,1)} %bitcast.210) | data formatting | bytes 7864320 | tf_op jit(solution)/shard_map/convert_element_type | solution.py:248
  131.9 2.6 %convolution_dynamic-update-slice_fusion = f32[8,256,640]{1,2,0:T(8,128)} fusion(f32[8,256,640]{1,2,0:T(8,128)} %copy-done.6, bf16[8,10,256,256]{3,2,0,1:T(8,128)(2,1)} %copy-done.1, bf16[8,256,1,64]{1,0,3,2:T(8,128)(2,1)} %get-tuple-element.22), kind=kOutput, calls=%fused_computation.32 | convolution fusion | flops 67108864 | bytes 1835008 | tf_op jit(solution)/shard_map/ctu,cup->ctp/dot_general | solution.py:241
  134.6 1.1 slice.345
  136.3 2.1 %multiply_reduce_fusion = f32[8,10,64,128]{3,2,1,0:T(8,128)S(1)} fusion(f32[9,10,64,128]{3,2,1,0:T(8,128)S(1)} %pad_maximum_fusion.1, f32[8,9,10]{2,1,0:T(8,128)S(1)} %broadcast_select_fusion), kind=kLoop, calls=%fused_computation | loop fusion | flops 11141120 | bytes 5573440 | tf_op jit(solution)/shard_map/reduce_sum | solution.py:230
  138.4 2.0 add_select_fusion
  140.4 1.5 slice-done.1
  142.0 2.7 %fusion.6 = bf16[8,256,640]{1,2,0:T(8,128)(2,1)} fusion(f32[8,256,640]{1,2,0:T(8,128)S(1)} %bitcast.220, f32[8,256,640]{1,2,0:T(8,128)S(1)} %bitcast.212, f32[640]{0:T(1024)S(1)} %mul.435, f32[8,256,10]{1,2,0:T(8,128)S(1)} %get-tuple-element.38, bf16[8,640,128]{2,1,0:T(8,128)(2,1)S(1)} %bitcast.221, bf16[8,256,256]{2,1,0:T(8,128)(2,1)S(1)} %bitcast.218), kind=kOutput, calls=%fused_computation.11 | convolution fusion | flops 342097920 | bytes 15077376 | tf_op jit(solution)/shard_map/ctn,cqn->ctq/dot_general | solution.py:236
  144.6 3.1 %copy.132 = bf16[8,256,640]{2,1,0:T(8,128)(2,1)S(1)} copy(bf16[8,256,640]{1,2,0:T(8,128)(2,1)} %fusion.6) | data formatting | bytes 5242880 | tf_op jit(solution)/shard_map/convert_element_type | solution.py:250
  147.8 42.9 %all_to_all.19 = bf16[128,16,640]{2,1,0:T(8,128)(2,1)S(1)} all-to-all(bf16[128,16,640]{2,1,0:T(8,128)(2,1)S(1)} %bitcast.214), channel_id=1, replica_groups=mesh['req'=32,'seq'=4] {'seq','req'}, dimensions={0} | all-to-all | bytes 5242880 | tf_op jit(solution)/shard_map/all_to_all | solution.py:251
  190.9 1.9 multiply_reduce_fusion.1
  192.9 13.8 %convolution_convert_fusion = bf16[512,2560]{1,0:T(8,128)(2,1)} fusion(bf16[2560,2560]{1,0:T(8,128)(2,1)} %param.22, f32[2560]{0:T(1024)S(1)} %copy-done.11, f32[512]{0:T(512)S(1)} %add_rsqrt_fusion, bf16[512,2560]{1,0:T(8,128)(2,1)S(1)} %copy-done.7, bf16[512,640]{1,0:T(8,128)(2,1)S(1)} %bitcast.225, bf16[512,640]{1,0:T(8,128)(2,1)S(1)} %bitcast.227, ...), kind=kOutput, calls=%fused_computation.16 | convolution fusion | flops 6734479360 | bytes 20983808 | tf_op jit(solution)/shard_map/dot_general | solution.py:255
  (111 shorter events, 9.6 us)
Async XLA Ops:
  0.6 15.7 %copy-start.10 = (s32[64]{0:T(128)S(1)}, s32[64]{0:T(128)}, u32[]{:S(2)}) copy-start(s32[64]{0:T(128)} %param.23) | copy-start | bytes 772
  0.6 16.0 %copy-start.9 = (bf16[512,256]{1,0:T(8,128)(2,1)S(1)}, bf16[512,256]{1,0:T(8,128)(2,1)}, u32[]{:S(2)}) copy-start(bf16[512,256]{1,0:T(8,128)(2,1)} %param.13) | copy-start | bytes 786436
  2.9 21.5 %all-to-all-start.1 = ((bf16[128,1,160]{2,1,0:T(2,128)(2,1)}), bf16[128,1,160]{2,1,0:T(2,128)(2,1)S(1)}, u32[]{:S(2)}, u32[]{:S(2)}) async-start(bf16[128,1,160]{2,1,0:T(2,128)(2,1)} %copy.112), calls=%async_computation.1 | async-start | bytes 262144 | tf_op jit(solution)/shard_map/all_to_all | solution.py:147
  16.3 4.2 %copy-start.12 = (f32[40]{0:T(128)S(1)}, f32[40]{0:T(128)}, u32[]{:S(2)}) copy-start(f32[40]{0:T(128)} %param.18) | copy-start | bytes 484
  16.3 4.3 %copy-start.13 = (f32[40]{0:T(128)S(1)}, f32[40]{0:T(128)}, u32[]{:S(2)}) copy-start(f32[40]{0:T(128)} %param.20) | copy-start | bytes 484
  18.8 13.2 %copy-start.14 = (f32[40]{0:T(128)S(1)}, f32[40]{0:T(128)}, u32[]{:S(2)}) copy-start(f32[40]{0:T(128)} %param.19) | copy-start | bytes 484
  24.4 54.6 %all-to-all-start = ((bf16[128,16,896]{2,1,0:T(8,128)(2,1)}), bf16[128,16,896]{2,1,0:T(8,128)(2,1)}, u32[]{:S(2)}, u32[]{:S(2)}) async-start(bf16[128,16,896]{2,1,0:T(8,128)(2,1)} %bitcast.213), calls=%async_computation | async-start | bytes 7340032 | tf_op jit(solution)/shard_map/all_to_all | solution.py:150
  79.7 6.7 %collective-permute-start = (bf16[3,896]{1,0:T(4,128)(2,1)S(1)}, bf16[3,896]{1,0:T(4,128)(2,1)S(1)}, u32[]{:S(2)}, u32[]{:S(2)}) collective-permute-start(bf16[3,896]{1,0:T(4,128)(2,1)S(1)} %slice.300), channel_id=1, source_target_pairs={{0,4},{4,8},{8,12},{12,16},{16,20},{20,24},{24,28},{28,32},{32,36}... | collective-permute-start | bytes 16136 | tf_op jit(solution)/shard_map/ppermute | solution.py:13
  89.6 1.8 copy-start.2
  97.4 5.6 %copy-start = (bf16[2048,640]{1,0:T(8,128)(2,1)}, bf16[2048,640]{1,0:T(8,128)(2,1)S(1)}, u32[]{:S(2)}) copy-start(bf16[2048,640]{1,0:T(8,128)(2,1)S(1)} %multiply_convert_fusion.3) | copy-start | bytes 7864324
  103.0 1.4 copy-start.3
  107.4 6.8 %copy-start.5 = (f32[8,256,256]{2,1,0:T(8,128)S(1)}, f32[8,256,256]{2,1,0:T(8,128)}, u32[]{:S(2)}) copy-start(f32[8,256,256]{2,1,0:T(8,128)} %fusion.17) | copy-start | bytes 6291460
  107.4 6.8 %copy-start.8 = (pred[256,256]{1,0:T(8,128)(4,1)S(1)}, pred[256,256]{1,0:T(8,128)(4,1)}, u32[]{:S(2)}) copy-start(pred[256,256]{1,0:T(8,128)(4,1)} %iota_compare_fusion) | copy-start | bytes 196612
  109.7 24.7 %collective-permute-start.1 = (f32[10,8320]{1,0:T(8,128)}, f32[10,8320]{1,0:T(8,128)S(1)}, u32[]{:S(2)}, u32[]{:S(2)}) collective-permute-start(f32[10,8320]{1,0:T(8,128)} %pad_maximum_fusion.4), channel_id=1, source_target_pairs={{0,4},{4,8},{8,12},{12,16},{16,20},{20,24},{24,28},{28,32},{32,36}... | collective-permute-start | bytes 998408 | tf_op jit(solution)/shard_map/ppermute | solution.py:13
  111.6 23.0 %collective-permute-start.2 = (f32[10,8320]{1,0:T(8,128)}, f32[10,8320]{1,0:T(8,128)}, u32[]{:S(2)}, u32[]{:S(2)}) collective-permute-start(f32[10,8320]{1,0:T(8,128)} %pad_maximum_fusion.4), channel_id=1, source_target_pairs={{0,8},{4,12},{8,16},{12,20},{16,24},{20,28},{24,32},{28,36},{32,40... | collective-permute-start | bytes 998408 | tf_op jit(solution)/shard_map/ppermute | solution.py:13
  120.3 4.0 %copy-start.1 = (bf16[8,10,256,256]{3,2,0,1:T(8,128)(2,1)}, bf16[8,10,256,256]{3,2,0,1:T(8,128)(2,1)S(1)}, u32[]{:S(2)}) copy-start(bf16[8,10,256,256]{3,2,0,1:T(8,128)(2,1)S(1)} %multiply_convert_fusion) | copy-start | bytes 31457284
  124.7 2.3 %copy-start.6 = (f32[8,256,640]{1,2,0:T(8,128)}, f32[8,256,640]{1,2,0:T(8,128)S(1)}, u32[]{:S(2)}) copy-start(f32[8,256,640]{1,2,0:T(8,128)S(1)} %convolution_dynamic-update-slice_fusion.1) | copy-start | bytes 15728644
  136.0 4.4 %slice-start.2 = ((s8[5242880]{0:T(1024)(128)(4,1)}), s8[4194304]{0:T(1024)(128)(4,1)S(1)}, s32[]{:S(2)}) async-start(s8[5242880]{0:T(1024)(128)(4,1)} %bitcast.219), calls=%async_computation.5 | async-start | bytes 8388608
  136.2 4.2 %slice-start = ((s8[5242880]{0:T(1024)(128)(4,1)}), s8[1048576]{0:T(1024)(128)(4,1)S(1)}, s32[]{:S(2)}) async-start(s8[5242880]{0:T(1024)(128)(4,1)} %bitcast.211), calls=%async_computation.3 | async-start | bytes 2097152
  136.3 4.2 %slice-start.3 = ((s8[5242880]{0:T(1024)(128)(4,1)}), s8[1048576]{0:T(1024)(128)(4,1)S(1)}, s32[]{:S(2)}) async-start(s8[5242880]{0:T(1024)(128)(4,1)} %bitcast.219), calls=%async_computation.6 | async-start | bytes 2097152
  138.4 2.0 copy-start.4
  138.4 3.5 %slice-start.1 = ((s8[5242880]{0:T(1024)(128)(4,1)}), s8[4194304]{0:T(1024)(128)(4,1)S(1)}, s32[]{:S(2)}) async-start(s8[5242880]{0:T(1024)(128)(4,1)} %bitcast.211), calls=%async_computation.4 | async-start | bytes 8388608
  147.8 43.1 %copy-start.7 = (bf16[512,2560]{1,0:T(8,128)(2,1)S(1)}, bf16[512,2560]{1,0:T(8,128)(2,1)}, u32[]{:S(2)}) copy-start(bf16[512,2560]{1,0:T(8,128)(2,1)} %param.14) | copy-start | bytes 7864324
  190.7 2.2 %copy-start.11 = (f32[2560]{0:T(1024)S(1)}, f32[2560]{0:T(1024)}, u32[]{:S(2)}) copy-start(f32[2560]{0:T(1024)} %param.21) | copy-start | bytes 30724
